TPU v7x, 32 devices: a whole 2x2x4 slice. The times are simulated.
32 devices in a mesh: row: 8 (over y, x, core), col: 4 (over z).
Axes of the slice: x: 2, y: 2, z: 4, core: 2. Of those that a mesh axis runs over, the one named last changes fastest.
Arguments:
- out_grads: bfloat16 [64, 28672], P('col', 'row'), may hold values from -6 to 6
- in_acts: bfloat16 [64, 8192], P('row', 'col'), may hold values from -6 to 6
- out_basis: bfloat16 [28672, 28672], P('row', 'col'), may hold values from -0.03125 to 0.03125
- in_basis: bfloat16 [8192, 8192], P('col', 'row'), may hold values from -0.0625 to 0.0625
- eigenvalues: bfloat16 [28672, 8192], P('col', 'row'), may hold values from 0.019897461 to 2
- queries: bfloat16 [2, 28672, 8192], P(None, 'col', 'row'), may hold values from -0.00015640259 to 0.00015640259
Outputs:
- scores: float32 [2, 64], replicated
All inputs are finite; a program needn't handle non-finite values.
Results may differ from a plain program's by a relative error of at most 0.0045.
Values may be sent and summed in bfloat16 or wider, within the bound.
No kernel may reach another device: no remote copies, remote signals or barrier semaphores. Data moves between devices by JAX's collectives and lax.ppermute only.
A program may use at most 192 MiB of HBM per device.

v0:
```python
import jax
import jax.numpy as jnp
from jax import lax
from jax.sharding import PartitionSpec as P

DAMPING = 0.1


def local(out_grads, in_acts, out_basis, in_basis, eigenvalues, queries):
    grads_all = lax.all_gather(out_grads, "col", axis=0, tiled=True)
    grad_mine = lax.psum_scatter(
        jnp.dot(grads_all, out_basis, preferred_element_type=jnp.float32),
        "row",
        scatter_dimension=0,
        tiled=True,
    ).astype(jnp.bfloat16)
    grad_rot = lax.all_gather(grad_mine, "row", axis=0, tiled=True)
    acts_all = lax.all_gather(in_acts, "row", axis=0, tiled=True)
    act_part = jnp.dot(acts_all, in_basis, preferred_element_type=jnp.float32)
    act_rot = lax.psum(act_part, "col").astype(jnp.bfloat16)
    shifted = eigenvalues.astype(jnp.float32) + DAMPING
    scaled = queries.astype(jnp.float32) / shifted[None]
    lifted = jnp.einsum(
        "qkj,tj->qkt",
        scaled,
        act_rot.astype(jnp.float32),
        precision=lax.Precision.HIGHEST,
        preferred_element_type=jnp.float32,
    )
    partial_scores = jnp.einsum(
        "qkt,tk->qt", lifted, grad_rot.astype(jnp.float32), precision=lax.Precision.HIGHEST
    )
    return lax.psum(partial_scores, ("row", "col"))


def solution(mesh):
    in_specs = (
        P("col", "row"),
        P("row", "col"),
        P("row", "col"),
        P("col", "row"),
        P("col", "row"),
        P(None, "col", "row"),
    )
    out_specs = P()
    return jax.shard_map(local, mesh=mesh, in_specs=in_specs, out_specs=out_specs, check_vma=False)
```

profile of v0, /device:TPU:0, one launch (start us, length us, event | category | flops | bytes accessed | tf_op | source)
XLA Modules:
  0.0 220.7 jit_solution(7782558009660924071)
XLA Ops:
  6.5 0.0 reduce-scatter.2.cloned.1.call-start
  6.5 17.0 %all_gather.9 = bf16[64,3584]{1,0:T(8,128)(2,1)S(1)} all-gather(bf16[16,3584]{1,0:T(8,128)(2,1)} %param.6), channel_id=1, replica_groups=mesh['row'=8,'col'=4] {'col'}, dimensions={0}, use_global_device_ids=true | all-gather | bytes 573440 | tf_op jit(solution)/shard_map/all_gather | solution.py:10
  23.5 21.8 %fusion.7 = f32[64,7168]{1,0:T(8,128)} fusion(bf16[64,3584]{1,0:T(8,128)(2,1)S(1)} %all_gather.9, bf16[3584,7168]{1,0:T(8,128)(2,1)} %param.8), kind=kOutput, calls=%fused_computation.9 | convolution fusion | flops 3288334336 | bytes 53673984 | tf_op jit(solution)/shard_map/dot_general | solution.py:12
  45.3 0.0 copy-start.1
  45.3 0.0 reduce-scatter.2.cloned.1.call-update
  45.4 0.0 copy-start
  45.4 17.4 %convert_add_fusion = f32[7168,1024]{1,0:T(8,128)} fusion(bf16[7168,1024]{1,0:T(8,128)(2,1)} %param.10), kind=kLoop, calls=%fused_computation.3 | loop fusion | flops 14680064 | bytes 44040192 | tf_op jit(solution)/shard_map/add | solution.py:21
  62.8 0.0 copy-done.1
  62.8 9.4 %all_gather.11 = bf16[64,2048]{1,0:T(8,128)(2,1)S(1)} all-gather(bf16[8,2048]{1,0:T(8,128)(2,1)S(1)} %copy-done.1), channel_id=1, replica_groups=mesh['row'=8,'col'=4] {'row'}, dimensions={0}, use_global_device_ids=true | all-gather | bytes 294912 | tf_op jit(solution)/shard_map/all_gather | solution.py:18
  72.2 0.0 copy-done
  72.2 0.8 fusion.8
  73.1 25.6 %all-reduce.1 = bf16[64,1024]{1,0:T(8,128)(2,1)S(1)} all-reduce(f32[64,1024]{1,0:T(8,128)S(1)} %fusion.8), channel_id=1, replica_groups=mesh['row'=8,'col'=4] {'col'}, use_global_device_ids=true, to_apply=%region_1.0 | all-reduce | flops 65536 | bytes 393216 | tf_op jit(solution)/shard_map/psum | solution.py:20
  98.7 45.4 %fusion = f32[2,7168,64]{1,2,0:T(8,128)} fusion(bf16[2,7168,1024]{2,1,0:T(8,128)(2,1)} %param.11, f32[7168,1024]{1,0:T(8,128)} %convert_add_fusion, bf16[64,1024]{1,0:T(8,128)(2,1)S(1)} %all-reduce.1), kind=kOutput, calls=%fused_computation.1 | convolution fusion | flops 11303649280 | bytes 62521344 | tf_op jit(solution)/shard_map/qkj,tj->qkt/dot_general | solution.py:23
  144.1 0.0 reduce-scatter.2.cloned.1.call-done
  144.1 1.0 convert_element_type.14
  145.1 11.0 %all_gather.10 = bf16[64,7168]{1,0:T(8,128)(2,1)S(1)} all-gather(bf16[8,7168]{1,0:T(8,128)(2,1)S(1)} %convert_element_type.14), channel_id=1, replica_groups=mesh['row'=8,'col'=4] {'row'}, dimensions={0}, use_global_device_ids=true | all-gather | bytes 1032192 | tf_op jit(solution)/shard_map/all_gather | solution.py:17
  156.0 19.9 %fusion.2 = f32[64,1,2]{2,1,0:T(1,128)S(1)} fusion(f32[2,7168,64]{1,2,0:T(8,128)} %fusion, bf16[64,7168,1]{1,0,2:T(8,128)(2,1)S(1)} %bitcast.11), kind=kOutput, calls=%fused_computation.4 | convolution fusion | flops 11010048 | bytes 4588032 | tf_op jit(solution)/shard_map/qkt,tk->qt/dot_general | solution.py:30
  175.9 0.1 copy.9
  176.0 37.8 %psum.15 = f32[2,64]{1,0:T(2,128)} all-reduce(f32[2,64]{1,0:T(2,128)S(1)} %bitcast.12), channel_id=1, replica_groups=mesh['row'=8,'col'=4] {'row','col'}, use_global_device_ids=true, to_apply=%region_2.0 | all-reduce | flops 128 | bytes 1024 | tf_op jit(solution)/shard_map/psum | solution.py:33
Async XLA Ops:
  6.5 137.6 %reduce-scatter.2.cloned.1.call-start = ((), (), s32[]{:S(2)}) async-start(), calls=%async_computation.1 | async-start | bytes 2064384 | tf_op jit(solution)/shard_map/reduce_scatter | solution.py:11
  45.3 17.4 %copy-start.1 = (bf16[8,2048]{1,0:T(8,128)(2,1)S(1)}, bf16[8,2048]{1,0:T(8,128)(2,1)}, u32[]{:S(2)}) copy-start(bf16[8,2048]{1,0:T(8,128)(2,1)} %param.7) | copy-start | bytes 98308
  45.4 26.8 %copy-start = (bf16[2048,1024]{1,0:T(8,128)(2,1)S(1)}, bf16[2048,1024]{1,0:T(8,128)(2,1)}, u32[]{:S(2)}) copy-start(bf16[2048,1024]{1,0:T(8,128)(2,1)} %param.9) | copy-start | bytes 12582916
Sparse Core Ops, SparseCore 0:
  45.5 42.0 reduce-scatter.1
where the time goes:
time: 221 us
  blocking collectives  101 us (46%)
  matrix products  88 us (40%)
  other arithmetic  18.3 us (8%)
  between operations  13.4 us (6%)
    dot_general x1, matrix products, local(): jnp.einsum('qkj,tj->qkt', scaled, act_rot.astype(jnp.float32), precision=...  45.4 us
    psum x1, blocking collectives, local(): return lax.psum(partial_scores, ('row', 'col'))  37.8 us
    psum x1, blocking collectives, local(): act_rot = lax.psum(act_part, 'col').astype(jnp.bfloat16)  25.6 us
    dot_general x1, matrix products, local(): jnp.dot(grads_all, out_basis, preferred_element_type=jnp.float32)  21.8 us
    dot_general x1, matrix products, local(): jnp.einsum('qkt,tk->qt', lifted, grad_rot.astype(jnp.float32), precision=...  19.9 us
    add x1, other arithmetic, local(): shifted = eigenvalues.astype(jnp.float32) + DAMPING  17.4 us
    all_gather x1, blocking collectives, local(): grads_all = lax.all_gather(out_grads, 'col', axis=0, tiled=True)  17 us
    all_gather x1, blocking collectives, local(): grad_rot = lax.all_gather(grad_mine, 'row', axis=0, tiled=True)  11 us
  transfers between devices with their start and end apart: 1, of which 0 were waited for; matrix products, arithmetic and copies ran while one was open for 29% of the time, Pallas kernels for 0%

commit v1 on v0

v1 whole, which is shorter than its diff:
```python
import functools

import jax
import jax.numpy as jnp
from jax import lax
from jax.experimental import pallas as pl
from jax.experimental.pallas import tpu as pltpu
from jax.sharding import PartitionSpec as P

DAMPING = 0.1
F32 = jnp.float32
BF16 = jnp.bfloat16


def _swap(x, axis, n, b):
    return lax.ppermute(x, axis, [(i, i ^ b) for i in range(n)])


def _gather(x, axis, n, dim):
    me = lax.axis_index(axis)
    b = 1
    while b < n:
        other = _swap(x, axis, n, b)
        first = (me // b) % 2 == 0
        x = jnp.where(first, jnp.concatenate([x, other], dim), jnp.concatenate([other, x], dim))
        b *= 2
    return x


def _allreduce_bf16(x, axis, n, dim):
    me = lax.axis_index(axis)
    b = 1
    while b < n:
        half = x.shape[dim] // 2
        upper = (me // b) % 2 == 1
        lo = lax.slice_in_dim(x, 0, half, axis=dim)
        hi = lax.slice_in_dim(x, half, 2 * half, axis=dim)
        keep = jnp.where(upper, hi, lo)
        send = jnp.where(upper, lo, hi)
        x = keep + _swap(send, axis, n, b)
        b *= 2
    x = x.astype(BF16)
    b = n // 2
    while b >= 1:
        other = _swap(x, axis, n, b)
        first = (me // b) % 2 == 0
        x = jnp.where(first, jnp.concatenate([x, other], dim), jnp.concatenate([other, x], dim))
        b //= 2
    return x


def _allreduce_small(x, axis, n):
    b = 1
    while b < n:
        x = x + _swap(x, axis, n, b)
        b *= 2
    return x


def _lifted_kernel(a_ref, e_ref, q_ref, o_ref):
    recip = 1.0 / (e_ref[...].astype(F32) + DAMPING)
    a = a_ref[...]
    dims = (((1,), (1,)), ((), ()))
    for qi in range(q_ref.shape[0]):
        s = q_ref[qi].astype(F32) * recip
        hi = s.astype(BF16)
        lo = (s - hi.astype(F32)).astype(BF16)
        o_ref[qi] = lax.dot_general(a, hi, dims, preferred_element_type=F32) + lax.dot_general(
            a, lo, dims, preferred_element_type=F32
        )


def _lifted(act_rot, eigenvalues, queries):
    nq, kk, jj = queries.shape
    tt = act_rot.shape[0]
    tk = next(c for c in (512, 256, 128, kk) if kk % c == 0)
    return pl.pallas_call(
        _lifted_kernel,
        grid=(kk // tk,),
        in_specs=[
            pl.BlockSpec((tt, jj), lambda i: (0, 0)),
            pl.BlockSpec((tk, jj), lambda i: (i, 0)),
            pl.BlockSpec((nq, tk, jj), lambda i: (0, i, 0)),
        ],
        out_specs=pl.BlockSpec((nq, tt, tk), lambda i: (0, 0, i)),
        out_shape=jax.ShapeDtypeStruct((nq, tt, kk), F32),
        compiler_params=pltpu.CompilerParams(dimension_semantics=("arbitrary",)),
        cost_estimate=pl.CostEstimate(
            flops=4 * nq * kk * jj * tt,
            bytes_accessed=(nq + 1) * kk * jj * 2 + nq * tt * kk * 4,
            transcendentals=0,
        ),
    )(act_rot, eigenvalues, queries)


def local(out_grads, in_acts, out_basis, in_basis, eigenvalues, queries, *, nr, nc):
    acts_all = _gather(in_acts, "row", nr, 0)
    grads_all = _gather(out_grads, "col", nc, 0)
    act_part = jnp.dot(acts_all, in_basis, preferred_element_type=F32)
    act_rot = _allreduce_bf16(act_part, "col", nc, 1)
    grad_part = jnp.dot(grads_all, out_basis, preferred_element_type=F32)
    grad_rot = _allreduce_bf16(grad_part, "row", nr, 1)
    lifted = _lifted(act_rot, eigenvalues, queries)
    partial = jnp.sum(lifted * grad_rot.astype(F32)[None], axis=2)
    return _allreduce_small(_allreduce_small(partial, "col", nc), "row", nr)


def solution(mesh):
    in_specs = (
        P("col", "row"),
        P("row", "col"),
        P("row", "col"),
        P("col", "row"),
        P("col", "row"),
        P(None, "col", "row"),
    )
    fn = functools.partial(local, nr=mesh.shape["row"], nc=mesh.shape["col"])
    return jax.shard_map(fn, mesh=mesh, in_specs=in_specs, out_specs=P(), check_vma=False)
```

time: 221 us -> 134 us (0.61)
  blocking collectives: 101 us -> 0 us
  matrix products: 88 us -> 21.3 us
  waiting for transfers between devices: 0.02 us -> 57.9 us
  Pallas kernels: 0 us -> 28.3 us
  starting transfers between devices: 0.01 us -> 18.9 us
  between operations: 13.4 us -> 0.16 us
  other arithmetic: 18.3 us -> 6.79 us
    dot_general x4 -> x2, matrix products: 88 us -> 21.3 us  [the longest x1 20.4 us: local(): grad_part = jnp.dot(grads_all, out_basis, preferred_element_type=F32)]
    psum x2 -> x0, blocking collectives: 63.4 us -> none  [the longest x1 37.8 us: local(): return lax.psum(partial_scores, ('row', 'col'))]
    ppermute x0 -> x20, waiting for transfers between devices: none -> 57.9 us  [_swap(): return lax.ppermute(x, axis, [(i, i ^ b) for i in range(n)])]
    all_gather x3 -> x0, blocking collectives: 37.4 us -> none  [the longest x1 17 us: local(): grads_all = lax.all_gather(out_grads, 'col', axis=0, tiled=True)]
    pallas_call x0 -> x1, Pallas kernels: none -> 28.3 us  [_lifted(): pl.pallas_call(_lifted_kernel, grid=(kk // tk,), in_specs=[pl.BlockSpec((...]
    ppermute x0 -> x20, starting transfers between devices: none -> 18.9 us  [_swap(): return lax.ppermute(x, axis, [(i, i ^ b) for i in range(n)])]
    add x1 -> x8, other arithmetic: 17.4 us -> 1.98 us  [the longest x3 1.41 us: _allreduce_bf16(): x = keep + _swap(send, axis, n, b)]
    reduce_sum x0 -> x1, other arithmetic: none -> 2.41 us  [local(): partial = jnp.sum(lifted * grad_rot.astype(F32)[None], axis=2)]
  transfers between devices with their start and end apart: 1 -> 20, of which waited for: 0 -> 16; matrix products, arithmetic and copies ran while one was open for 29% -> 2% of each run, Pallas kernels for 0% -> 21%
where the time goes in v1:
time: 134 us; the launch traced here: 133 us
  waiting for transfers between devices  57.9 us (43%)
  Pallas kernels  28.3 us (21%)
  matrix products  21.3 us (16%)
  starting transfers between devices  18.9 us (14%)
  other arithmetic  6.79 us (5%)
    ppermute x20, waiting for transfers between devices, _swap(): return lax.ppermute(x, axis, [(i, i ^ b) for i in range(n)])  57.9 us
    pallas_call x1, Pallas kernels, _lifted(): pl.pallas_call(_lifted_kernel, grid=(kk // tk,), in_specs=[pl.BlockSpec((...  28.3 us
    dot_general x1, matrix products, local(): grad_part = jnp.dot(grads_all, out_basis, preferred_element_type=F32)  20.4 us
    ppermute x20, starting transfers between devices, _swap(): return lax.ppermute(x, axis, [(i, i ^ b) for i in range(n)])  18.9 us
  transfers between devices with their start and end apart: 20, of which 16 were waited for; matrix products, arithmetic and copies ran while one was open for 2% of the time, Pallas kernels for 21%

profile of v1, /device:TPU:0, one launch (start us, length us, event | category | flops | bytes accessed | tf_op | source)
XLA Modules:
  0.0 133.3 jit_solution(5992535416185544926)
XLA Ops:
  0.0 3.0 %collective-permute-start.7 = (bf16[16,3584]{1,0:T(8,128)(2,1)}, bf16[16,3584]{1,0:T(8,128)(2,1)S(1)}, u32[]{:S(2)}, u32[]{:S(2)}) collective-permute-start(bf16[16,3584]{1,0:T(8,128)(2,1)} %param.6), channel_id=1, source_target_pairs={{0,1},{1,0},{2,3},{3,2},{4,5},{5,4},{6,7},{7,6},{8,9},{9,8},{10,11... | collective-permute-start | bytes 344072 | tf_op jit(solution)/shard_map/ppermute | solution.py:16
  3.0 3.4 %collective-permute-done.7 = bf16[16,3584]{1,0:T(8,128)(2,1)S(1)} collective-permute-done((bf16[16,3584]{1,0:T(8,128)(2,1)}, bf16[16,3584]{1,0:T(8,128)(2,1)S(1)}, u32[]{:S(2)}, u32[]{:S(2)}) %collective-permute-start.7) | collective-permute-done | bytes 114720 | tf_op jit(solution)/shard_map/ppermute | solution.py:16
  6.4 1.0 maximum_select_fusion.6
  7.4 2.8 %collective-permute-start.8 = (bf16[32,3584]{1,0:T(8,128)(2,1)S(1)}, bf16[32,3584]{1,0:T(8,128)(2,1)S(1)}, u32[]{:S(2)}, u32[]{:S(2)}) collective-permute-start(bf16[32,3584]{1,0:T(8,128)(2,1)S(1)} %maximum_select_fusion.6), channel_id=1, source_target_pairs={{0,2},{1,3},{2,0},{3,1},{4,6},{5,7},{6,4},{7,5},{8,10},{9,11},{10,... | collective-permute-start | bytes 688136 | tf_op jit(solution)/shard_map/ppermute | solution.py:16
  10.2 9.8 %collective-permute-done.8 = bf16[32,3584]{1,0:T(8,128)(2,1)S(1)} collective-permute-done((bf16[32,3584]{1,0:T(8,128)(2,1)S(1)}, bf16[32,3584]{1,0:T(8,128)(2,1)S(1)}, u32[]{:S(2)}, u32[]{:S(2)}) %collective-permute-start.8) | collective-permute-done | bytes 229408 | tf_op jit(solution)/shard_map/ppermute | solution.py:16
  20.1 20.4 %fusion.1 = f32[64,7168]{1,0:T(8,128)S(1)} fusion(bf16[3584,7168]{1,0:T(8,128)(2,1)} %param.8, bf16[32,3584]{1,0:T(8,128)(2,1)S(1)} %collective-permute-done.8, bf16[32,3584]{1,0:T(8,128)(2,1)S(1)} %maximum_select_fusion.6, pred[]{:T(512)S(6)} %eq.52), kind=kOutput, calls=%fused_computation.6 | convolution fusion | flops 3290398720 | bytes 53673984 | tf_op jit(solution)/shard_map/dot_general | solution.py:101
  41.2 1.6 %collective-permute-done = bf16[8,2048]{1,0:T(8,128)(2,1)S(1)} collective-permute-done((bf16[8,2048]{1,0:T(8,128)(2,1)S(1)}, bf16[8,2048]{1,0:T(8,128)(2,1)S(1)}, u32[]{:S(2)}, u32[]{:S(2)}) %collective-permute-start) | collective-permute-done | bytes 32800 | tf_op jit(solution)/shard_map/ppermute | solution.py:16
  42.8 1.4 %collective-permute-start.1 = (bf16[16,2048]{1,0:T(8,128)(2,1)S(1)}, bf16[16,2048]{1,0:T(8,128)(2,1)S(1)}, u32[]{:S(2)}, u32[]{:S(2)}) collective-permute-start(bf16[16,2048]{1,0:T(8,128)(2,1)S(1)} %maximum_select_fusion.10), channel_id=1, source_target_pairs={{0,8},{4,12},{8,0},{12,4},{16,24},{20,28},{24,16},{28,20},{1,9},{5... | collective-permute-start | bytes 196616 | tf_op jit(solution)/shard_map/ppermute | solution.py:16
  44.3 3.0 %collective-permute-done.1 = bf16[16,2048]{1,0:T(8,128)(2,1)S(1)} collective-permute-done((bf16[16,2048]{1,0:T(8,128)(2,1)S(1)}, bf16[16,2048]{1,0:T(8,128)(2,1)S(1)}, u32[]{:S(2)}, u32[]{:S(2)}) %collective-permute-start.1) | collective-permute-done | bytes 65568 | tf_op jit(solution)/shard_map/ppermute | solution.py:16
  47.3 1.4 %collective-permute-start.2 = (bf16[32,2048]{1,0:T(8,128)(2,1)S(1)}, bf16[32,2048]{1,0:T(8,128)(2,1)S(1)}, u32[]{:S(2)}, u32[]{:S(2)}) collective-permute-start(bf16[32,2048]{1,0:T(8,128)(2,1)S(1)} %maximum_select_fusion.8), channel_id=1, source_target_pairs={{0,16},{4,20},{8,24},{12,28},{16,0},{20,4},{24,8},{28,12},{1,17},{... | collective-permute-start | bytes 393224 | tf_op jit(solution)/shard_map/ppermute | solution.py:16
  48.7 1.3 select_add_fusion
  50.1 1.6 %collective-permute-start.10 = (f32[64,1792]{1,0:T(8,128)S(1)}, f32[64,1792]{1,0:T(8,128)S(1)}, u32[]{:S(2)}, u32[]{:S(2)}) collective-permute-start(f32[64,1792]{1,0:T(8,128)S(1)} %slice_select_fusion.1), channel_id=1, source_target_pairs={{0,8},{4,12},{8,0},{12,4},{16,24},{20,28},{24,16},{28,20},{1,9},{5... | collective-permute-start | bytes 1376264 | tf_op jit(solution)/shard_map/ppermute | solution.py:16
  52.3 0.8 fusion.8
  53.8 8.1 %collective-permute-done.10 = f32[64,1792]{1,0:T(8,128)S(1)} collective-permute-done((f32[64,1792]{1,0:T(8,128)S(1)}, f32[64,1792]{1,0:T(8,128)S(1)}, u32[]{:S(2)}, u32[]{:S(2)}) %collective-permute-start.10) | collective-permute-done | bytes 458784 | tf_op jit(solution)/shard_map/ppermute | solution.py:16
  62.0 0.7 collective-permute-start.11
  62.7 5.3 %collective-permute-done.11 = f32[64,896]{1,0:T(8,128)S(1)} collective-permute-done((f32[64,896]{1,0:T(8,128)S(1)}, f32[64,896]{1,0:T(8,128)S(1)}, u32[]{:S(2)}, u32[]{:S(2)}) %collective-permute-start.11) | collective-permute-done | bytes 229408 | tf_op jit(solution)/shard_map/ppermute | solution.py:16
  68.1 0.7 collective-permute-start.12
  68.9 4.0 %collective-permute-done.12 = bf16[64,896]{1,0:T(8,128)(2,1)S(1)} collective-permute-done((bf16[64,896]{1,0:T(8,128)(2,1)S(1)}, bf16[64,896]{1,0:T(8,128)(2,1)S(1)}, u32[]{:S(2)}, u32[]{:S(2)}) %collective-permute-start.12) | collective-permute-done | bytes 114720 | tf_op jit(solution)/shard_map/ppermute | solution.py:16
  73.1 1.6 %collective-permute-start.13 = (bf16[64,1792]{1,0:T(8,128)(2,1)S(1)}, bf16[64,1792]{1,0:T(8,128)(2,1)S(1)}, u32[]{:S(2)}, u32[]{:S(2)}) collective-permute-start(bf16[64,1792]{1,0:T(8,128)(2,1)S(1)} %maximum_select_fusion.7), channel_id=1, source_target_pairs={{0,8},{4,12},{8,0},{12,4},{16,24},{20,28},{24,16},{28,20},{1,9},{5... | collective-permute-start | bytes 688136 | tf_op jit(solution)/shard_map/ppermute | solution.py:16
  74.6 0.8 collective-permute-done.4
  75.5 5.0 %collective-permute-done.5 = bf16[64,256]{1,0:T(8,128)(2,1)S(1)} collective-permute-done((bf16[64,256]{1,0:T(8,128)(2,1)S(1)}, bf16[64,256]{1,0:T(8,128)(2,1)S(1)}, u32[]{:S(2)}, u32[]{:S(2)}) %collective-permute-start.5) | collective-permute-done | bytes 32800 | tf_op jit(solution)/shard_map/ppermute | solution.py:16
  80.9 3.8 %collective-permute-done.6 = bf16[64,512]{1,0:T(8,128)(2,1)S(1)} collective-permute-done((bf16[64,512]{1,0:T(8,128)(2,1)S(1)}, bf16[64,512]{1,0:T(8,128)(2,1)S(1)}, u32[]{:S(2)}, u32[]{:S(2)}) %collective-permute-start.6) | collective-permute-done | bytes 65568 | tf_op jit(solution)/shard_map/ppermute | solution.py:16
  85.5 28.3 %shard_map.64 = f32[2,64,7168]{2,1,0:T(8,128)} custom-call(bf16[64,1024]{1,0:T(8,128)(2,1)} %maximum_select_fusion.9.a_ref, bf16[7168,1024]{1,0:T(8,128)(2,1)} %e_ref.1, bf16[2,7168,1024]{2,1,0:T(8,128)(2,1)} %q_ref.1), custom_call_target="tpu_custom_call" | custom-call | flops 3758096384 | bytes 47710208 | tf_op jit(solution)/shard_map/pallas_call | solution.py:77
  114.0 2.4 %multiply_reduce_fusion = f32[2,64]{1,0:T(2,128)S(1)} fusion(f32[2,64,7168]{2,1,0:T(8,128)} %shard_map.64, f32[64,7168]{1,0:T(8,128)S(1)} %fusion), kind=kLoop, calls=%fused_computation | loop fusion | flops 1834880 | bytes 5505536 | tf_op jit(solution)/shard_map/reduce_sum | solution.py:104
  116.7 3.3 %collective-permute-done.15 = f32[2,64]{1,0:T(2,128)S(1)} collective-permute-done((f32[2,64]{1,0:T(2,128)S(1)}, f32[2,64]{1,0:T(2,128)S(1)}, u32[]{:S(2)}, u32[]{:S(2)}) %collective-permute-start.15) | collective-permute-done | bytes 544 | tf_op jit(solution)/shard_map/ppermute | solution.py:16
  120.0 1.1 collective-permute-start.16
  121.1 3.4 %collective-permute-done.16 = f32[2,64]{1,0:T(2,128)S(1)} collective-permute-done((f32[2,64]{1,0:T(2,128)S(1)}, f32[2,64]{1,0:T(2,128)S(1)}, u32[]{:S(2)}, u32[]{:S(2)}) %collective-permute-start.16) | collective-permute-done | bytes 544 | tf_op jit(solution)/shard_map/ppermute | solution.py:16
  124.5 1.1 collective-permute-done.17
  125.6 1.3 collective-permute-start.18
  126.9 2.3 %collective-permute-done.18 = f32[2,64]{1,0:T(2,128)S(1)} collective-permute-done((f32[2,64]{1,0:T(2,128)S(1)}, f32[2,64]{1,0:T(2,128)S(1)}, u32[]{:S(2)}, u32[]{:S(2)}) %collective-permute-start.18) | collective-permute-done | bytes 544 | tf_op jit(solution)/shard_map/ppermute | solution.py:16
  129.2 1.3 collective-permute-start.19
  130.5 2.2 %collective-permute-done.19 = f32[2,64]{1,0:T(2,128)S(1)} collective-permute-done((f32[2,64]{1,0:T(2,128)S(1)}, f32[2,64]{1,0:T(2,128)S(1)}, u32[]{:S(2)}, u32[]{:S(2)}) %collective-permute-start.19) | collective-permute-done | bytes 544 | tf_op jit(solution)/shard_map/ppermute | solution.py:16
  (39 shorter events, 4.6 us)
Async XLA Ops:
  0.0 6.4 %collective-permute-start.7 = (bf16[16,3584]{1,0:T(8,128)(2,1)}, bf16[16,3584]{1,0:T(8,128)(2,1)S(1)}, u32[]{:S(2)}, u32[]{:S(2)}) collective-permute-start(bf16[16,3584]{1,0:T(8,128)(2,1)} %param.6), channel_id=1, source_target_pairs={{0,1},{1,0},{2,3},{3,2},{4,5},{5,4},{6,7},{7,6},{8,9},{9,8},{10,11... | collective-permute-start | bytes 344072 | tf_op jit(solution)/shard_map/ppermute | solution.py:16
  7.4 12.7 %collective-permute-start.8 = (bf16[32,3584]{1,0:T(8,128)(2,1)S(1)}, bf16[32,3584]{1,0:T(8,128)(2,1)S(1)}, u32[]{:S(2)}, u32[]{:S(2)}) collective-permute-start(bf16[32,3584]{1,0:T(8,128)(2,1)S(1)} %maximum_select_fusion.6), channel_id=1, source_target_pairs={{0,2},{1,3},{2,0},{3,1},{4,6},{5,7},{6,4},{7,5},{8,10},{9,11},{10,... | collective-permute-start | bytes 688136 | tf_op jit(solution)/shard_map/ppermute | solution.py:16
  10.2 30.5 %copy-start.1 = (bf16[8,2048]{1,0:T(8,128)(2,1)S(1)}, bf16[8,2048]{1,0:T(8,128)(2,1)}, u32[]{:S(2)}) copy-start(bf16[8,2048]{1,0:T(8,128)(2,1)} %param.7) | copy-start | bytes 98308
  40.6 8.1 %collective-permute-start.9 = (f32[64,3584]{1,0:T(8,128)S(1)}, f32[64,3584]{1,0:T(8,128)}, u32[]{:S(2)}, u32[]{:S(2)}) collective-permute-start(f32[64,3584]{1,0:T(8,128)S(1)} %slice_select_fusion), channel_id=1, source_target_pairs={{0,4},{4,0},{8,12},{12,8},{16,20},{20,16},{24,28},{28,24},{1,5},{5... | collective-permute-start | bytes 2752520 | tf_op jit(solution)/shard_map/ppermute | solution.py:16
  40.7 2.1 %collective-permute-start = (bf16[8,2048]{1,0:T(8,128)(2,1)S(1)}, bf16[8,2048]{1,0:T(8,128)(2,1)S(1)}, u32[]{:S(2)}, u32[]{:S(2)}) collective-permute-start(bf16[8,2048]{1,0:T(8,128)(2,1)S(1)} %copy-done.1), channel_id=1, source_target_pairs={{0,4},{4,0},{8,12},{12,8},{16,20},{20,16},{24,28},{28,24},{1,5},{5... | collective-permute-start | bytes 98312 | tf_op jit(solution)/shard_map/ppermute | solution.py:16
  42.8 4.4 %collective-permute-start.1 = (bf16[16,2048]{1,0:T(8,128)(2,1)S(1)}, bf16[16,2048]{1,0:T(8,128)(2,1)S(1)}, u32[]{:S(2)}, u32[]{:S(2)}) collective-permute-start(bf16[16,2048]{1,0:T(8,128)(2,1)S(1)} %maximum_select_fusion.10), channel_id=1, source_target_pairs={{0,8},{4,12},{8,0},{12,4},{16,24},{20,28},{24,16},{28,20},{1,9},{5... | collective-permute-start | bytes 196616 | tf_op jit(solution)/shard_map/ppermute | solution.py:16
  44.3 8.1 %copy-start = (bf16[2048,1024]{1,0:T(8,128)(2,1)S(1)}, bf16[2048,1024]{1,0:T(8,128)(2,1)}, u32[]{:S(2)}) copy-start(bf16[2048,1024]{1,0:T(8,128)(2,1)} %param.9) | copy-start | bytes 12582916
  47.3 5.0 %collective-permute-start.2 = (bf16[32,2048]{1,0:T(8,128)(2,1)S(1)}, bf16[32,2048]{1,0:T(8,128)(2,1)S(1)}, u32[]{:S(2)}, u32[]{:S(2)}) collective-permute-start(bf16[32,2048]{1,0:T(8,128)(2,1)S(1)} %maximum_select_fusion.8), channel_id=1, source_target_pairs={{0,16},{4,20},{8,24},{12,28},{16,0},{20,4},{24,8},{28,12},{1,17},{... | collective-permute-start | bytes 393224 | tf_op jit(solution)/shard_map/ppermute | solution.py:16
  50.1 11.8 %collective-permute-start.10 = (f32[64,1792]{1,0:T(8,128)S(1)}, f32[64,1792]{1,0:T(8,128)S(1)}, u32[]{:S(2)}, u32[]{:S(2)}) collective-permute-start(f32[64,1792]{1,0:T(8,128)S(1)} %slice_select_fusion.1), channel_id=1, source_target_pairs={{0,8},{4,12},{8,0},{12,4},{16,24},{20,28},{24,16},{28,20},{1,9},{5... | collective-permute-start | bytes 1376264 | tf_op jit(solution)/shard_map/ppermute | solution.py:16
  53.2 9.5 %collective-permute-start.3 = (f32[64,512]{1,0:T(8,128)S(1)}, f32[64,512]{1,0:T(8,128)S(1)}, u32[]{:S(2)}, u32[]{:S(2)}) collective-permute-start(f32[64,512]{1,0:T(8,128)S(1)} %slice_select_fusion.3), channel_id=1, source_target_pairs={{0,1},{1,0},{2,3},{3,2},{4,5},{5,4},{6,7},{7,6},{8,9},{9,8},{10,11... | collective-permute-start | bytes 393224 | tf_op jit(solution)/shard_map/ppermute | solution.py:16
  62.0 6.1 %collective-permute-start.11 = (f32[64,896]{1,0:T(8,128)S(1)}, f32[64,896]{1,0:T(8,128)S(1)}, u32[]{:S(2)}, u32[]{:S(2)}) collective-permute-start(f32[64,896]{1,0:T(8,128)S(1)} %slice_select_fusion.2), channel_id=1, source_target_pairs={{0,16},{4,20},{8,24},{12,28},{16,0},{20,4},{24,8},{28,12},{1,17},{... | collective-permute-start | bytes 688136 | tf_op jit(solution)/shard_map/ppermute | solution.py:16
  68.1 4.9 %collective-permute-start.12 = (bf16[64,896]{1,0:T(8,128)(2,1)S(1)}, bf16[64,896]{1,0:T(8,128)(2,1)S(1)}, u32[]{:S(2)}, u32[]{:S(2)}) collective-permute-start(bf16[64,896]{1,0:T(8,128)(2,1)S(1)} %add_convert_fusion), channel_id=1, source_target_pairs={{0,16},{4,20},{8,24},{12,28},{16,0},{20,4},{24,8},{28,12},{1,17},{... | collective-permute-start | bytes 344072 | tf_op jit(solution)/shard_map/ppermute | solution.py:16
  68.9 6.5 %collective-permute-start.4 = (f32[64,256]{1,0:T(8,128)S(1)}, f32[64,256]{1,0:T(8,128)S(1)}, u32[]{:S(2)}, u32[]{:S(2)}) collective-permute-start(f32[64,256]{1,0:T(8,128)S(1)} %slice_select_fusion.4), channel_id=1, source_target_pairs={{0,2},{1,3},{2,0},{3,1},{4,6},{5,7},{6,4},{7,5},{8,10},{9,11},{10,... | collective-permute-start | bytes 196616 | tf_op jit(solution)/shard_map/ppermute | solution.py:16
  73.1 7.7 %collective-permute-start.13 = (bf16[64,1792]{1,0:T(8,128)(2,1)S(1)}, bf16[64,1792]{1,0:T(8,128)(2,1)S(1)}, u32[]{:S(2)}, u32[]{:S(2)}) collective-permute-start(bf16[64,1792]{1,0:T(8,128)(2,1)S(1)} %maximum_select_fusion.7), channel_id=1, source_target_pairs={{0,8},{4,12},{8,0},{12,4},{16,24},{20,28},{24,16},{28,20},{1,9},{5... | collective-permute-start | bytes 688136 | tf_op jit(solution)/shard_map/ppermute | solution.py:16
  75.4 5.0 %collective-permute-start.5 = (bf16[64,256]{1,0:T(8,128)(2,1)S(1)}, bf16[64,256]{1,0:T(8,128)(2,1)S(1)}, u32[]{:S(2)}, u32[]{:S(2)}) collective-permute-start(bf16[64,256]{1,0:T(8,128)(2,1)S(1)} %add_convert_fusion.1), channel_id=1, source_target_pairs={{0,2},{1,3},{2,0},{3,1},{4,6},{5,7},{6,4},{7,5},{8,10},{9,11},{10,... | collective-permute-start | bytes 98312 | tf_op jit(solution)/shard_map/ppermute | solution.py:16
  80.5 4.3 %collective-permute-start.6 = (bf16[64,512]{1,0:T(8,128)(2,1)S(1)}, bf16[64,512]{1,0:T(8,128)(2,1)S(1)}, u32[]{:S(2)}, u32[]{:S(2)}) collective-permute-start(bf16[64,512]{1,0:T(8,128)(2,1)S(1)} %maximum_select_fusion.11), channel_id=1, source_target_pairs={{0,1},{1,0},{2,3},{3,2},{4,5},{5,4},{6,7},{7,6},{8,9},{9,8},{10,11... | collective-permute-start | bytes 196616 | tf_op jit(solution)/shard_map/ppermute | solution.py:16
  80.9 33.0 %collective-permute-start.14 = (bf16[64,3584]{1,0:T(8,128)(2,1)S(1)}, bf16[64,3584]{1,0:T(8,128)(2,1)S(1)}, u32[]{:S(2)}, u32[]{:S(2)}) collective-permute-start(bf16[64,3584]{1,0:T(8,128)(2,1)S(1)} %maximum_select_fusion.3), channel_id=1, source_target_pairs={{0,4},{4,0},{8,12},{12,8},{16,20},{20,16},{24,28},{28,24},{1,5},{5... | collective-permute-start | bytes 1376264 | tf_op jit(solution)/shard_map/ppermute | solution.py:16
  116.4 3.6 %collective-permute-start.15 = (f32[2,64]{1,0:T(2,128)S(1)}, f32[2,64]{1,0:T(2,128)S(1)}, u32[]{:S(2)}, u32[]{:S(2)}) collective-permute-start(f32[2,64]{1,0:T(2,128)S(1)} %multiply_reduce_fusion), channel_id=1, source_target_pairs={{0,1},{1,0},{2,3},{3,2},{4,5},{5,4},{6,7},{7,6},{8,9},{9,8},{10,11... | collective-permute-start | bytes 1544 | tf_op jit(solution)/shard_map/ppermute | solution.py:16
  120.0 4.5 %collective-permute-start.16 = (f32[2,64]{1,0:T(2,128)S(1)}, f32[2,64]{1,0:T(2,128)S(1)}, u32[]{:S(2)}, u32[]{:S(2)}) collective-permute-start(f32[2,64]{1,0:T(2,128)S(1)} %add.71), channel_id=1, source_target_pairs={{0,2},{1,3},{2,0},{3,1},{4,6},{5,7},{6,4},{7,5},{8,10},{9,11},{10,... | collective-permute-start | bytes 1544 | tf_op jit(solution)/shard_map/ppermute | solution.py:16
  124.5 1.1 collective-permute-start.17
  125.6 3.6 %collective-permute-start.18 = (f32[2,64]{1,0:T(2,128)S(1)}, f32[2,64]{1,0:T(2,128)S(1)}, u32[]{:S(2)}, u32[]{:S(2)}) collective-permute-start(f32[2,64]{1,0:T(2,128)S(1)} %add.73), channel_id=1, source_target_pairs={{0,8},{4,12},{8,0},{12,4},{16,24},{20,28},{24,16},{28,20},{1,9},{5... | collective-permute-start | bytes 1544 | tf_op jit(solution)/shard_map/ppermute | solution.py:16
  129.2 3.6 %collective-permute-start.19 = (f32[2,64]{1,0:T(2,128)S(1)}, f32[2,64]{1,0:T(2,128)S(1)}, u32[]{:S(2)}, u32[]{:S(2)}) collective-permute-start(f32[2,64]{1,0:T(2,128)S(1)} %add.74), channel_id=1, source_target_pairs={{0,16},{4,20},{8,24},{12,28},{16,0},{20,4},{24,8},{28,12},{1,17},{... | collective-permute-start | bytes 1544 | tf_op jit(solution)/shard_map/ppermute | solution.py:16

commit v2 on v1

v2 whole, which is shorter than its diff:
```python
import functools

import jax
import jax.numpy as jnp
from jax import lax
from jax.experimental import pallas as pl
from jax.experimental.pallas import tpu as pltpu
from jax.sharding import PartitionSpec as P

DAMPING = 0.1
F32 = jnp.float32
BF16 = jnp.bfloat16


def _shift(x, axis, n, s):
    return lax.ppermute(x, axis, [(i, (i + s) % n) for i in range(n)])


def _place(parts, me, n, dim):
    w = parts[0].shape[dim]
    shape = list(parts[0].shape)
    shape[dim] = n * w
    out = jnp.zeros(shape, parts[0].dtype)
    for s, p in enumerate(parts):
        out = lax.dynamic_update_slice_in_dim(out, p, ((me - s) % n) * w, axis=dim)
    return out


def _gather(x, axis, n, dim):
    me = lax.axis_index(axis)
    return _place([x] + [_shift(x, axis, n, s) for s in range(1, n)], me, n, dim)


def _allreduce_bf16(x, axis, n):
    me = lax.axis_index(axis)
    w = x.shape[1] // n
    total = lax.dynamic_slice_in_dim(x, me * w, w, axis=1)
    for s in range(1, n):
        piece = lax.dynamic_slice_in_dim(x, ((me + s) % n) * w, w, axis=1)
        total = total + _shift(piece, axis, n, s)
    return _gather(total.astype(BF16), axis, n, 1)


def _allreduce_small(x, axis, n):
    stacked = _gather(x[None], axis, n, 0)
    return jnp.sum(stacked, axis=0)


def _lifted_kernel(a_ref, e_ref, q_ref, o_ref):
    recip = 1.0 / (e_ref[...].astype(F32) + DAMPING)
    a = a_ref[...]
    dims = (((1,), (1,)), ((), ()))
    for qi in range(q_ref.shape[0]):
        s = q_ref[qi].astype(F32) * recip
        hi = s.astype(BF16)
        lo = (s - hi.astype(F32)).astype(BF16)
        o_ref[qi] = lax.dot_general(a, hi, dims, preferred_element_type=F32) + lax.dot_general(
            a, lo, dims, preferred_element_type=F32
        )


def _lifted(act_rot, eigenvalues, queries, chunk, nchunks):
    nq, kk, jj = queries.shape
    tt = act_rot.shape[0]
    kc = kk // nchunks
    tk = next(c for c in (512, 256, 128, kc) if kc % c == 0)
    base = chunk * (kc // tk)
    return pl.pallas_call(
        _lifted_kernel,
        grid=(kc // tk,),
        in_specs=[
            pl.BlockSpec((tt, jj), lambda i: (0, 0)),
            pl.BlockSpec((tk, jj), lambda i: (base + i, 0)),
            pl.BlockSpec((nq, tk, jj), lambda i: (0, base + i, 0)),
        ],
        out_specs=pl.BlockSpec((nq, tt, tk), lambda i: (0, 0, i)),
        out_shape=jax.ShapeDtypeStruct((nq, tt, kc), F32),
        compiler_params=pltpu.CompilerParams(dimension_semantics=("arbitrary",)),
        cost_estimate=pl.CostEstimate(
            flops=4 * nq * kc * jj * tt,
            bytes_accessed=(nq + 1) * kc * jj * 2 + nq * tt * kc * 4,
            transcendentals=0,
        ),
    )(act_rot, eigenvalues, queries)


def local(out_grads, in_acts, out_basis, in_basis, eigenvalues, queries, *, nr, nc, ng, nl):
    acts_all = _gather(in_acts, "row", nr, 0)
    grads_all = _gather(out_grads, "col", nc, 0)
    act_part = jnp.dot(acts_all, in_basis, preferred_element_type=F32)
    act_rot = _allreduce_bf16(act_part, "col", nc)
    kk = out_basis.shape[1]
    kg = kk // ng
    grad_part = jnp.concatenate(
        [
            jnp.dot(grads_all, out_basis[:, g * kg : (g + 1) * kg], preferred_element_type=F32)
            for g in range(ng)
        ],
        axis=1,
    )
    grad_rot = _allreduce_bf16(grad_part, "row", nr)
    kc = kk // nl
    partial = None
    for c in range(nl):
        lifted = _lifted(act_rot, eigenvalues, queries, c, nl)
        g = grad_rot[:, c * kc : (c + 1) * kc].astype(F32)
        term = jnp.sum(lifted * g[None], axis=2)
        partial = term if partial is None else partial + term
    return _allreduce_small(_allreduce_small(partial, "col", nc), "row", nr)


def solution(mesh):
    in_specs = (
        P("col", "row"),
        P("row", "col"),
        P("row", "col"),
        P("col", "row"),
        P("col", "row"),
        P(None, "col", "row"),
    )
    fn = functools.partial(local, nr=mesh.shape["row"], nc=mesh.shape["col"], ng=4, nl=4)
    return jax.shard_map(fn, mesh=mesh, in_specs=in_specs, out_specs=P(), check_vma=False)
```

time: 134 us -> 150 us (1.12)
  waiting for transfers between devices: 57.9 us -> 13.2 us
  starting transfers between devices: 18.9 us -> 53.1 us
  Pallas kernels: 28.3 us -> 40.7 us
  local copies, waits for them, and re-layouts: 0.01 us -> 9.19 us
  matrix products: 21.3 us -> 26.8 us
    ppermute x20 -> x40, waiting for transfers between devices: 57.9 us -> 13.2 us  [_shift(): return lax.ppermute(x, axis, [(i, (i + s) % n) for i in range(n)])]
    ppermute x20 -> x40, starting transfers between devices: 18.9 us -> 53.1 us  [_shift(): return lax.ppermute(x, axis, [(i, (i + s) % n) for i in range(n)])]
    pallas_call x1 -> x4, Pallas kernels: 28.3 us -> 40.7 us  [_lifted(): pl.pallas_call(_lifted_kernel, grid=(kc // tk,), in_specs=[pl.BlockSpec((...]
    dynamic_update_slice x0 -> x33, local copies, waits for them, and re-layouts: none -> 6.51 us  [_place(): out = lax.dynamic_update_slice_in_dim(out, p, (me - s) % n * w, axis=dim)]
    dot_general x1 -> x4, matrix products: 20.4 us -> 23.7 us  [local(): jnp.dot(grads_all, out_basis[:, g * kg:(g + 1) * kg], preferred_element_t...]
    dot_general x1, matrix products: 0.84 us -> 3.02 us  [local(): act_part = jnp.dot(acts_all, in_basis, preferred_element_type=F32)]
    select_n x12 -> x0, other arithmetic: 2.12 us -> none  [the longest x3 1.06 us: _gather(): jnp.where(first, jnp.concatenate([x, other], dim), jnp.concatenate([other...]
    add x8 -> x0, other arithmetic: 1.98 us -> none  [the longest x3 1.41 us: _allreduce_bf16(): x = keep + _swap(send, axis, n, b)]
  transfers between devices with their start and end apart: 20 -> 40, of which waited for: 16 -> 14; matrix products, arithmetic and copies ran while one was open for 2% -> 23% of each run, Pallas kernels for 21% -> 27%
where the time goes in v2:
time: 150 us; the launch traced here: 149 us
  starting transfers between devices  53.1 us (35%)
  Pallas kernels  40.7 us (27%)
  matrix products  26.8 us (18%)
  waiting for transfers between devices  13.2 us (9%)
  local copies, waits for them, and re-layouts  9.19 us (6%)
  other arithmetic  5.31 us (4%)
    ppermute x40, starting transfers between devices, _shift(): return lax.ppermute(x, axis, [(i, (i + s) % n) for i in range(n)])  53.1 us
    pallas_call x4, Pallas kernels, _lifted(): pl.pallas_call(_lifted_kernel, grid=(kc // tk,), in_specs=[pl.BlockSpec((...  40.7 us
    dot_general x4, matrix products, local(): jnp.dot(grads_all, out_basis[:, g * kg:(g + 1) * kg], preferred_element_t...  23.7 us
    ppermute x40, waiting for transfers between devices, _shift(): return lax.ppermute(x, axis, [(i, (i + s) % n) for i in range(n)])  13.2 us
    dynamic_update_slice x33, local copies, waits for them, and re-layouts, _place(): out = lax.dynamic_update_slice_in_dim(out, p, (me - s) % n * w, axis=dim)  6.51 us
    dot_general x1, matrix products, local(): act_part = jnp.dot(acts_all, in_basis, preferred_element_type=F32)  3.02 us
  transfers between devices with their start and end apart: 40, of which 14 were waited for; matrix products, arithmetic and copies ran while one was open for 23% of the time, Pallas kernels for 27%

profile of v2, /device:TPU:0, one launch (start us, length us, event | category | flops | bytes accessed | tf_op | source)
XLA Modules:
  0.0 148.7 jit_solution(9914123023309777616)
XLA Ops:
  0.0 3.0 %collective-permute-start.13 = (bf16[16,3584]{1,0:T(8,128)(2,1)}, bf16[16,3584]{1,0:T(8,128)(2,1)S(1)}, u32[]{:S(2)}, u32[]{:S(2)}) collective-permute-start(bf16[16,3584]{1,0:T(8,128)(2,1)} %param.6), channel_id=1, source_target_pairs={{0,1},{1,2},{2,3},{3,0},{4,5},{5,6},{6,7},{7,4},{8,9},{9,10},{10,1... | collective-permute-start | bytes 344072 | tf_op jit(solution)/shard_map/ppermute | solution.py:16
  3.0 2.6 %collective-permute-start.14 = (bf16[16,3584]{1,0:T(8,128)(2,1)}, bf16[16,3584]{1,0:T(8,128)(2,1)S(1)}, u32[]{:S(2)}, u32[]{:S(2)}) collective-permute-start(bf16[16,3584]{1,0:T(8,128)(2,1)} %param.6), channel_id=1, source_target_pairs={{0,2},{1,3},{2,0},{3,1},{4,6},{5,7},{6,4},{7,5},{8,10},{9,11},{10,... | collective-permute-start | bytes 344072 | tf_op jit(solution)/shard_map/ppermute | solution.py:16
  5.6 1.5 %collective-permute-start.1 = (bf16[8,2048]{1,0:T(8,128)(2,1)}, bf16[8,2048]{1,0:T(8,128)(2,1)S(1)}, u32[]{:S(2)}, u32[]{:S(2)}) collective-permute-start(bf16[8,2048]{1,0:T(8,128)(2,1)} %param.7), channel_id=1, source_target_pairs={{0,8},{4,12},{8,16},{12,20},{16,24},{20,28},{24,0},{28,4},{1,9},{5... | collective-permute-start | bytes 98312 | tf_op jit(solution)/shard_map/ppermute | solution.py:16
  7.1 2.4 %collective-permute-start.2 = (bf16[8,2048]{1,0:T(8,128)(2,1)}, bf16[8,2048]{1,0:T(8,128)(2,1)S(1)}, u32[]{:S(2)}, u32[]{:S(2)}) collective-permute-start(bf16[8,2048]{1,0:T(8,128)(2,1)} %param.7), channel_id=1, source_target_pairs={{0,12},{4,16},{8,20},{12,24},{16,28},{20,0},{24,4},{28,8},{1,13},{... | collective-permute-start | bytes 98312 | tf_op jit(solution)/shard_map/ppermute | solution.py:16
  15.2 1.5 %collective-permute-done.5 = bf16[8,2048]{1,0:T(8,128)(2,1)S(1)} collective-permute-done((bf16[8,2048]{1,0:T(8,128)(2,1)}, bf16[8,2048]{1,0:T(8,128)(2,1)S(1)}, u32[]{:S(2)}, u32[]{:S(2)}) %collective-permute-start.5) | collective-permute-done | bytes 32800 | tf_op jit(solution)/shard_map/ppermute | solution.py:16
  16.8 3.0 %fusion.8 = f32[64,1024]{1,0:T(8,128)S(1)} fusion(bf16[64,2048]{1,0:T(8,128)(2,1)S(1)} %constant_dynamic-update-slice_fusion.28, bf16[2048,1024]{1,0:T(8,128)(2,1)} %param.9), kind=kOutput, calls=%fused_computation.66 | convolution fusion | flops 268435456 | bytes 4718592 | tf_op jit(solution)/shard_map/dot_general | solution.py:90
  20.1 1.7 %collective-permute-start.8 = (f32[64,256]{1,0:T(8,128)S(1)}, f32[64,256]{1,0:T(8,128)S(1)}, u32[]{:S(2)}, u32[]{:S(2)}) collective-permute-start(f32[64,256]{1,0:T(8,128)S(1)} %get-tuple-element.24), channel_id=1, source_target_pairs={{0,2},{1,3},{2,0},{3,1},{4,6},{5,7},{6,4},{7,5},{8,10},{9,11},{10,... | collective-permute-start | bytes 196616 | tf_op jit(solution)/shard_map/ppermute | solution.py:16
  21.8 1.9 %collective-permute-start.9 = (f32[64,256]{1,0:T(8,128)S(1)}, f32[64,256]{1,0:T(8,128)S(1)}, u32[]{:S(2)}, u32[]{:S(2)}) collective-permute-start(f32[64,256]{1,0:T(8,128)S(1)} %get-tuple-element.23), channel_id=1, source_target_pairs={{0,3},{1,0},{2,1},{3,2},{4,7},{5,4},{6,5},{7,6},{8,11},{9,8},{10,9... | collective-permute-start | bytes 196616 | tf_op jit(solution)/shard_map/ppermute | solution.py:16
  24.9 1.8 %collective-permute-done.7 = f32[64,256]{1,0:T(8,128)S(1)} collective-permute-done((f32[64,256]{1,0:T(8,128)S(1)}, f32[64,256]{1,0:T(8,128)S(1)}, u32[]{:S(2)}, u32[]{:S(2)}) %collective-permute-start.7) | collective-permute-done | bytes 65568 | tf_op jit(solution)/shard_map/ppermute | solution.py:16
  26.7 2.0 %collective-permute-done.8 = f32[64,256]{1,0:T(8,128)S(1)} collective-permute-done((f32[64,256]{1,0:T(8,128)S(1)}, f32[64,256]{1,0:T(8,128)S(1)}, u32[]{:S(2)}, u32[]{:S(2)}) %collective-permute-start.8) | collective-permute-done | bytes 65568 | tf_op jit(solution)/shard_map/ppermute | solution.py:16
  28.8 2.0 %collective-permute-start.10 = (bf16[64,256]{1,0:T(8,128)(2,1)S(1)}, bf16[64,256]{1,0:T(8,128)(2,1)S(1)}, u32[]{:S(2)}, u32[]{:S(2)}) collective-permute-start(bf16[64,256]{1,0:T(8,128)(2,1)S(1)} %get-tuple-element.10), channel_id=1, source_target_pairs={{0,1},{1,2},{2,3},{3,0},{4,5},{5,6},{6,7},{7,4},{8,9},{9,10},{10,1... | collective-permute-start | bytes 98312 | tf_op jit(solution)/shard_map/ppermute | solution.py:16
  31.7 5.9 %fusion = f32[64,1792]{1,0:T(8,128)S(1)} fusion(bf16[64,3584]{1,0:T(8,128)(2,1)S(1)} %constant_dynamic-update-slice_fusion.20, bf16[3584,7168]{1,0:T(8,128)(2,1)} %param.8), kind=kOutput, calls=%fused_computation | convolution fusion | flops 822083584 | bytes 13762560 | tf_op jit(solution)/shard_map/dot_general | solution.py:96
  37.6 6.0 %fusion.2 = f32[64,1792]{1,0:T(8,128)S(1)} fusion(bf16[64,3584]{1,0:T(8,128)(2,1)S(1)} %constant_dynamic-update-slice_fusion.20, bf16[3584,7168]{1,0:T(8,128)(2,1)} %param.8), kind=kOutput, calls=%fused_computation.2 | convolution fusion | flops 822083584 | bytes 13762560 | tf_op jit(solution)/shard_map/dot_general | solution.py:96
  43.6 5.9 %fusion.4 = f32[64,1792]{1,0:T(8,128)S(1)} fusion(bf16[64,3584]{1,0:T(8,128)(2,1)S(1)} %constant_dynamic-update-slice_fusion.20, bf16[3584,7168]{1,0:T(8,128)(2,1)} %param.8), kind=kOutput, calls=%fused_computation.4 | convolution fusion | flops 822083584 | bytes 13762560 | tf_op jit(solution)/shard_map/dot_general | solution.py:96
  49.5 5.9 %fusion.6 = f32[64,1792]{1,0:T(8,128)S(1)} fusion(bf16[64,3584]{1,0:T(8,128)(2,1)S(1)} %constant_dynamic-update-slice_fusion.20, bf16[3584,7168]{1,0:T(8,128)(2,1)} %param.8), kind=kOutput, calls=%fused_computation.6 | convolution fusion | flops 822083584 | bytes 13762560 | tf_op jit(solution)/shard_map/dot_general | solution.py:96
  58.8 2.2 %collective-permute-start.12 = (bf16[64,256]{1,0:T(8,128)(2,1)S(1)}, bf16[64,256]{1,0:T(8,128)(2,1)S(1)}, u32[]{:S(2)}, u32[]{:S(2)}) collective-permute-start(bf16[64,256]{1,0:T(8,128)(2,1)S(1)} %get-tuple-element.10), channel_id=1, source_target_pairs={{0,3},{1,0},{2,1},{3,2},{4,7},{5,4},{6,5},{7,6},{8,11},{9,8},{10,9... | collective-permute-start | bytes 98312 | tf_op jit(solution)/shard_map/ppermute | solution.py:16
  61.0 1.9 %collective-permute-start.18 = (f32[64,896]{1,0:T(8,128)}, f32[64,896]{1,0:T(8,128)}, u32[]{:S(2)}, u32[]{:S(2)}) collective-permute-start(f32[64,896]{1,0:T(8,128)} %get-tuple-element.16), channel_id=1, source_target_pairs={{0,12},{4,16},{8,20},{12,24},{16,28},{20,0},{24,4},{28,8},{1,13},{... | collective-permute-start | bytes 688136 | tf_op jit(solution)/shard_map/ppermute | solution.py:16
  63.0 2.0 %collective-permute-start.19 = (f32[64,896]{1,0:T(8,128)S(1)}, f32[64,896]{1,0:T(8,128)}, u32[]{:S(2)}, u32[]{:S(2)}) collective-permute-start(f32[64,896]{1,0:T(8,128)S(1)} %get-tuple-element.15), channel_id=1, source_target_pairs={{0,16},{4,20},{8,24},{12,28},{16,0},{20,4},{24,8},{28,12},{1,17},{... | collective-permute-start | bytes 688136 | tf_op jit(solution)/shard_map/ppermute | solution.py:16
  66.7 4.3 %collective-permute-start.22 = (f32[64,896]{1,0:T(8,128)S(1)}, f32[64,896]{1,0:T(8,128)}, u32[]{:S(2)}, u32[]{:S(2)}) collective-permute-start(f32[64,896]{1,0:T(8,128)S(1)} %get-tuple-element.12), channel_id=1, source_target_pairs={{0,28},{4,0},{8,4},{12,8},{16,12},{20,16},{24,20},{28,24},{1,29},{... | collective-permute-start | bytes 688136 | tf_op jit(solution)/shard_map/ppermute | solution.py:16
  71.6 10.1 %shard_map.64 = f32[2,64,1792]{2,1,0:T(8,128)} custom-call(bf16[64,1024]{1,0:T(8,128)(2,1)} %copy-done.4, bf16[7168,1024]{1,0:T(8,128)(2,1)} %e_ref.7, bf16[2,7168,1024]{2,1,0:T(8,128)(2,1)} %q_ref.7), custom_call_target="tpu_custom_call" | custom-call | flops 939524096 | bytes 11927552 | tf_op jit(solution)/shard_map/pallas_call | solution.py:68
  81.8 10.1 %shard_map.65 = f32[2,64,1792]{2,1,0:T(8,128)} custom-call(bf16[64,1024]{1,0:T(8,128)(2,1)} %copy-done.4, bf16[7168,1024]{1,0:T(8,128)(2,1)} %e_ref.7, bf16[2,7168,1024]{2,1,0:T(8,128)(2,1)} %q_ref.7), custom_call_target="tpu_custom_call" | custom-call | flops 939524096 | bytes 11927552 | tf_op jit(solution)/shard_map/pallas_call | solution.py:68
  92.0 1.5 constant_dynamic-update-slice_fusion.19
  94.4 10.1 %shard_map.66 = f32[2,64,1792]{2,1,0:T(8,128)} custom-call(bf16[64,1024]{1,0:T(8,128)(2,1)} %copy-done.4, bf16[7168,1024]{1,0:T(8,128)(2,1)} %e_ref.7, bf16[2,7168,1024]{2,1,0:T(8,128)(2,1)} %q_ref.7), custom_call_target="tpu_custom_call" | custom-call | flops 939524096 | bytes 11927552 | tf_op jit(solution)/shard_map/pallas_call | solution.py:68
  104.5 10.3 %shard_map.67 = f32[2,64,1792]{2,1,0:T(8,128)} custom-call(bf16[64,1024]{1,0:T(8,128)(2,1)} %copy-done.4, bf16[7168,1024]{1,0:T(8,128)(2,1)} %e_ref.7, bf16[2,7168,1024]{2,1,0:T(8,128)(2,1)} %q_ref.7), custom_call_target="tpu_custom_call" | custom-call | flops 939524096 | bytes 11927552 | tf_op jit(solution)/shard_map/pallas_call | solution.py:68
  115.2 2.3 %collective-permute-start.25 = (bf16[64,896]{1,0:T(8,128)(2,1)S(1)}, bf16[64,896]{1,0:T(8,128)(2,1)S(1)}, u32[]{:S(2)}, u32[]{:S(2)}) collective-permute-start(bf16[64,896]{1,0:T(8,128)(2,1)S(1)} %get-tuple-element.8), channel_id=1, source_target_pairs={{0,12},{4,16},{8,20},{12,24},{16,28},{20,0},{24,4},{28,8},{1,13},{... | collective-permute-start | bytes 344072 | tf_op jit(solution)/shard_map/ppermute | solution.py:16
  118.2 2.6 %collective-permute-start.28 = (bf16[64,896]{1,0:T(8,128)(2,1)S(1)}, bf16[64,896]{1,0:T(8,128)(2,1)S(1)}, u32[]{:S(2)}, u32[]{:S(2)}) collective-permute-start(bf16[64,896]{1,0:T(8,128)(2,1)S(1)} %get-tuple-element.8), channel_id=1, source_target_pairs={{0,24},{4,28},{8,0},{12,4},{16,8},{20,12},{24,16},{28,20},{1,25},{... | collective-permute-start | bytes 344072 | tf_op jit(solution)/shard_map/ppermute | solution.py:16
  123.3 1.6 %collective-permute-done.25 = bf16[64,896]{1,0:T(8,128)(2,1)S(1)} collective-permute-done((bf16[64,896]{1,0:T(8,128)(2,1)S(1)}, bf16[64,896]{1,0:T(8,128)(2,1)S(1)}, u32[]{:S(2)}, u32[]{:S(2)}) %collective-permute-start.25) | collective-permute-done | bytes 114720 | tf_op jit(solution)/shard_map/ppermute | solution.py:16
  132.5 1.6 %collective-permute-start.31 = (f32[1,2,64]{2,1,0:T(2,128)S(1)}, f32[1,2,64]{2,1,0:T(2,128)S(1)}, u32[]{:S(2)}, u32[]{:S(2)}) collective-permute-start(f32[1,2,64]{2,1,0:T(2,128)S(1)} %get-tuple-element.6), channel_id=1, source_target_pairs={{0,2},{1,3},{2,0},{3,1},{4,6},{5,7},{6,4},{7,5},{8,10},{9,11},{10,... | collective-permute-start | bytes 1544 | tf_op jit(solution)/shard_map/ppermute | solution.py:16
  135.2 1.5 %collective-permute-done.30 = f32[1,2,64]{2,1,0:T(2,128)S(1)} collective-permute-done((f32[1,2,64]{2,1,0:T(2,128)S(1)}, f32[1,2,64]{2,1,0:T(2,128)S(1)}, u32[]{:S(2)}, u32[]{:S(2)}) %collective-permute-start.30) | collective-permute-done | bytes 544 | tf_op jit(solution)/shard_map/ppermute | solution.py:16
  137.8 3.4 %collective-permute-start.34 = (f32[1,2,64]{2,1,0:T(2,128)S(1)}, f32[1,2,64]{2,1,0:T(2,128)S(1)}, u32[]{:S(2)}, u32[]{:S(2)}) collective-permute-start(f32[1,2,64]{2,1,0:T(2,128)S(1)} %bitcast.12), channel_id=1, source_target_pairs={{0,8},{4,12},{8,16},{12,20},{16,24},{20,28},{24,0},{28,4},{1,9},{5... | collective-permute-start | bytes 1544 | tf_op jit(solution)/shard_map/ppermute | solution.py:16
  142.1 1.9 %collective-permute-start.36 = (f32[1,2,64]{2,1,0:T(2,128)S(1)}, f32[1,2,64]{2,1,0:T(2,128)S(1)}, u32[]{:S(2)}, u32[]{:S(2)}) collective-permute-start(f32[1,2,64]{2,1,0:T(2,128)S(1)} %bitcast.14), channel_id=1, source_target_pairs={{0,16},{4,20},{8,24},{12,28},{16,0},{20,4},{24,8},{28,12},{1,17},{... | collective-permute-start | bytes 1544 | tf_op jit(solution)/shard_map/ppermute | solution.py:16
  145.3 1.5 %collective-permute-start.39 = (f32[1,2,64]{2,1,0:T(2,128)S(1)}, f32[1,2,64]{2,1,0:T(2,128)S(1)}, u32[]{:S(2)}, u32[]{:S(2)}) collective-permute-start(f32[1,2,64]{2,1,0:T(2,128)S(1)} %bitcast.17), channel_id=1, source_target_pairs={{0,28},{4,0},{8,4},{12,8},{16,12},{20,16},{24,20},{28,24},{1,29},{... | collective-permute-start | bytes 1544 | tf_op jit(solution)/shard_map/ppermute | solution.py:16
  (117 shorter events, 32.1 us)
Async XLA Ops:
  0.0 30.8 %collective-permute-start.13 = (bf16[16,3584]{1,0:T(8,128)(2,1)}, bf16[16,3584]{1,0:T(8,128)(2,1)S(1)}, u32[]{:S(2)}, u32[]{:S(2)}) collective-permute-start(bf16[16,3584]{1,0:T(8,128)(2,1)} %param.6), channel_id=1, source_target_pairs={{0,1},{1,2},{2,3},{3,0},{4,5},{5,6},{6,7},{7,4},{8,9},{9,10},{10,1... | collective-permute-start | bytes 344072 | tf_op jit(solution)/shard_map/ppermute | solution.py:16
  3.0 27.8 %collective-permute-start.14 = (bf16[16,3584]{1,0:T(8,128)(2,1)}, bf16[16,3584]{1,0:T(8,128)(2,1)S(1)}, u32[]{:S(2)}, u32[]{:S(2)}) collective-permute-start(bf16[16,3584]{1,0:T(8,128)(2,1)} %param.6), channel_id=1, source_target_pairs={{0,2},{1,3},{2,0},{3,1},{4,6},{5,7},{6,4},{7,5},{8,10},{9,11},{10,... | collective-permute-start | bytes 344072 | tf_op jit(solution)/shard_map/ppermute | solution.py:16
  5.6 4.7 %collective-permute-start = (bf16[8,2048]{1,0:T(8,128)(2,1)}, bf16[8,2048]{1,0:T(8,128)(2,1)S(1)}, u32[]{:S(2)}, u32[]{:S(2)}) collective-permute-start(bf16[8,2048]{1,0:T(8,128)(2,1)} %param.7), channel_id=1, source_target_pairs={{0,4},{4,8},{8,12},{12,16},{16,20},{20,24},{24,28},{28,0},{1,5},{5... | collective-permute-start | bytes 98312 | tf_op jit(solution)/shard_map/ppermute | solution.py:16
  5.6 6.0 %collective-permute-start.1 = (bf16[8,2048]{1,0:T(8,128)(2,1)}, bf16[8,2048]{1,0:T(8,128)(2,1)S(1)}, u32[]{:S(2)}, u32[]{:S(2)}) collective-permute-start(bf16[8,2048]{1,0:T(8,128)(2,1)} %param.7), channel_id=1, source_target_pairs={{0,8},{4,12},{8,16},{12,20},{16,24},{20,28},{24,0},{28,4},{1,9},{5... | collective-permute-start | bytes 98312 | tf_op jit(solution)/shard_map/ppermute | solution.py:16
  7.1 5.4 %collective-permute-start.2 = (bf16[8,2048]{1,0:T(8,128)(2,1)}, bf16[8,2048]{1,0:T(8,128)(2,1)S(1)}, u32[]{:S(2)}, u32[]{:S(2)}) collective-permute-start(bf16[8,2048]{1,0:T(8,128)(2,1)} %param.7), channel_id=1, source_target_pairs={{0,12},{4,16},{8,20},{12,24},{16,28},{20,0},{24,4},{28,8},{1,13},{... | collective-permute-start | bytes 98312 | tf_op jit(solution)/shard_map/ppermute | solution.py:16
  19.8 6.8 %collective-permute-start.7 = (f32[64,256]{1,0:T(8,128)S(1)}, f32[64,256]{1,0:T(8,128)S(1)}, u32[]{:S(2)}, u32[]{:S(2)}) collective-permute-start(f32[64,256]{1,0:T(8,128)S(1)} %get-tuple-element.22), channel_id=1, source_target_pairs={{0,1},{1,2},{2,3},{3,0},{4,5},{5,6},{6,7},{7,4},{8,9},{9,10},{10,1... | collective-permute-start | bytes 196616 | tf_op jit(solution)/shard_map/ppermute | solution.py:16
  20.1 8.6 %collective-permute-start.8 = (f32[64,256]{1,0:T(8,128)S(1)}, f32[64,256]{1,0:T(8,128)S(1)}, u32[]{:S(2)}, u32[]{:S(2)}) collective-permute-start(f32[64,256]{1,0:T(8,128)S(1)} %get-tuple-element.24), channel_id=1, source_target_pairs={{0,2},{1,3},{2,0},{3,1},{4,6},{5,7},{6,4},{7,5},{8,10},{9,11},{10,... | collective-permute-start | bytes 196616 | tf_op jit(solution)/shard_map/ppermute | solution.py:16
  21.8 6.9 %collective-permute-start.9 = (f32[64,256]{1,0:T(8,128)S(1)}, f32[64,256]{1,0:T(8,128)S(1)}, u32[]{:S(2)}, u32[]{:S(2)}) collective-permute-start(f32[64,256]{1,0:T(8,128)S(1)} %get-tuple-element.23), channel_id=1, source_target_pairs={{0,3},{1,0},{2,1},{3,2},{4,7},{5,4},{6,5},{7,6},{8,11},{9,8},{10,9... | collective-permute-start | bytes 196616 | tf_op jit(solution)/shard_map/ppermute | solution.py:16
  26.7 5.0 %collective-permute-start.15 = (bf16[16,3584]{1,0:T(8,128)(2,1)}, bf16[16,3584]{1,0:T(8,128)(2,1)S(1)}, u32[]{:S(2)}, u32[]{:S(2)}) collective-permute-start(bf16[16,3584]{1,0:T(8,128)(2,1)} %param.6), channel_id=1, source_target_pairs={{0,3},{1,0},{2,1},{3,2},{4,7},{5,4},{6,5},{7,6},{8,11},{9,8},{10,9... | collective-permute-start | bytes 344072 | tf_op jit(solution)/shard_map/ppermute | solution.py:16
  28.8 32.3 %collective-permute-start.10 = (bf16[64,256]{1,0:T(8,128)(2,1)S(1)}, bf16[64,256]{1,0:T(8,128)(2,1)S(1)}, u32[]{:S(2)}, u32[]{:S(2)}) collective-permute-start(bf16[64,256]{1,0:T(8,128)(2,1)S(1)} %get-tuple-element.10), channel_id=1, source_target_pairs={{0,1},{1,2},{2,3},{3,0},{4,5},{5,6},{6,7},{7,4},{8,9},{9,10},{10,1... | collective-permute-start | bytes 98312 | tf_op jit(solution)/shard_map/ppermute | solution.py:16
  56.5 8.8 %collective-permute-start.16 = (f32[64,896]{1,0:T(8,128)}, f32[64,896]{1,0:T(8,128)S(1)}, u32[]{:S(2)}, u32[]{:S(2)}) collective-permute-start(f32[64,896]{1,0:T(8,128)} %get-tuple-element.11), channel_id=1, source_target_pairs={{0,4},{4,8},{8,12},{12,16},{16,20},{20,24},{24,28},{28,0},{1,5},{5... | collective-permute-start | bytes 688136 | tf_op jit(solution)/shard_map/ppermute | solution.py:16
  56.5 10.2 %collective-permute-start.17 = (f32[64,896]{1,0:T(8,128)}, f32[64,896]{1,0:T(8,128)S(1)}, u32[]{:S(2)}, u32[]{:S(2)}) collective-permute-start(f32[64,896]{1,0:T(8,128)} %get-tuple-element.17), channel_id=1, source_target_pairs={{0,8},{4,12},{8,16},{12,20},{16,24},{20,28},{24,0},{28,4},{1,9},{5... | collective-permute-start | bytes 688136 | tf_op jit(solution)/shard_map/ppermute | solution.py:16
  57.7 5.2 %collective-permute-start.11 = (bf16[64,256]{1,0:T(8,128)(2,1)S(1)}, bf16[64,256]{1,0:T(8,128)(2,1)S(1)}, u32[]{:S(2)}, u32[]{:S(2)}) collective-permute-start(bf16[64,256]{1,0:T(8,128)(2,1)S(1)} %get-tuple-element.10), channel_id=1, source_target_pairs={{0,2},{1,3},{2,0},{3,1},{4,6},{5,7},{6,4},{7,5},{8,10},{9,11},{10,... | collective-permute-start | bytes 98312 | tf_op jit(solution)/shard_map/ppermute | solution.py:16
  58.8 6.1 %collective-permute-start.12 = (bf16[64,256]{1,0:T(8,128)(2,1)S(1)}, bf16[64,256]{1,0:T(8,128)(2,1)S(1)}, u32[]{:S(2)}, u32[]{:S(2)}) collective-permute-start(bf16[64,256]{1,0:T(8,128)(2,1)S(1)} %get-tuple-element.10), channel_id=1, source_target_pairs={{0,3},{1,0},{2,1},{3,2},{4,7},{5,4},{6,5},{7,6},{8,11},{9,8},{10,9... | collective-permute-start | bytes 98312 | tf_op jit(solution)/shard_map/ppermute | solution.py:16
  61.0 30.9 %collective-permute-start.18 = (f32[64,896]{1,0:T(8,128)}, f32[64,896]{1,0:T(8,128)}, u32[]{:S(2)}, u32[]{:S(2)}) collective-permute-start(f32[64,896]{1,0:T(8,128)} %get-tuple-element.16), channel_id=1, source_target_pairs={{0,12},{4,16},{8,20},{12,24},{16,28},{20,0},{24,4},{28,8},{1,13},{... | collective-permute-start | bytes 688136 | tf_op jit(solution)/shard_map/ppermute | solution.py:16
  63.0 28.9 %collective-permute-start.19 = (f32[64,896]{1,0:T(8,128)S(1)}, f32[64,896]{1,0:T(8,128)}, u32[]{:S(2)}, u32[]{:S(2)}) collective-permute-start(f32[64,896]{1,0:T(8,128)S(1)} %get-tuple-element.15), channel_id=1, source_target_pairs={{0,16},{4,20},{8,24},{12,28},{16,0},{20,4},{24,8},{28,12},{1,17},{... | collective-permute-start | bytes 688136 | tf_op jit(solution)/shard_map/ppermute | solution.py:16
  64.9 27.0 %collective-permute-start.20 = (f32[64,896]{1,0:T(8,128)S(1)}, f32[64,896]{1,0:T(8,128)}, u32[]{:S(2)}, u32[]{:S(2)}) collective-permute-start(f32[64,896]{1,0:T(8,128)S(1)} %get-tuple-element.14), channel_id=1, source_target_pairs={{0,20},{4,24},{8,28},{12,0},{16,4},{20,8},{24,12},{28,16},{1,21},{... | collective-permute-start | bytes 688136 | tf_op jit(solution)/shard_map/ppermute | solution.py:16
  65.3 26.6 %collective-permute-start.21 = (f32[64,896]{1,0:T(8,128)S(1)}, f32[64,896]{1,0:T(8,128)}, u32[]{:S(2)}, u32[]{:S(2)}) collective-permute-start(f32[64,896]{1,0:T(8,128)S(1)} %get-tuple-element.13), channel_id=1, source_target_pairs={{0,24},{4,28},{8,0},{12,4},{16,8},{20,12},{24,16},{28,20},{1,25},{... | collective-permute-start | bytes 688136 | tf_op jit(solution)/shard_map/ppermute | solution.py:16
  66.7 25.2 %collective-permute-start.22 = (f32[64,896]{1,0:T(8,128)S(1)}, f32[64,896]{1,0:T(8,128)}, u32[]{:S(2)}, u32[]{:S(2)}) collective-permute-start(f32[64,896]{1,0:T(8,128)S(1)} %get-tuple-element.12), channel_id=1, source_target_pairs={{0,28},{4,0},{8,4},{12,8},{16,12},{20,16},{24,20},{28,24},{1,29},{... | collective-permute-start | bytes 688136 | tf_op jit(solution)/shard_map/ppermute | solution.py:16
  94.4 23.8 %collective-permute-start.23 = (bf16[64,896]{1,0:T(8,128)(2,1)S(1)}, bf16[64,896]{1,0:T(8,128)(2,1)S(1)}, u32[]{:S(2)}, u32[]{:S(2)}) collective-permute-start(bf16[64,896]{1,0:T(8,128)(2,1)S(1)} %get-tuple-element.8), channel_id=1, source_target_pairs={{0,4},{4,8},{8,12},{12,16},{16,20},{20,24},{24,28},{28,0},{1,5},{5... | collective-permute-start | bytes 344072 | tf_op jit(solution)/shard_map/ppermute | solution.py:16
  114.8 6.6 %collective-permute-start.24 = (bf16[64,896]{1,0:T(8,128)(2,1)S(1)}, bf16[64,896]{1,0:T(8,128)(2,1)S(1)}, u32[]{:S(2)}, u32[]{:S(2)}) collective-permute-start(bf16[64,896]{1,0:T(8,128)(2,1)S(1)} %get-tuple-element.8), channel_id=1, source_target_pairs={{0,8},{4,12},{8,16},{12,20},{16,24},{20,28},{24,0},{28,4},{1,9},{5... | collective-permute-start | bytes 344072 | tf_op jit(solution)/shard_map/ppermute | solution.py:16
  115.2 9.7 %collective-permute-start.25 = (bf16[64,896]{1,0:T(8,128)(2,1)S(1)}, bf16[64,896]{1,0:T(8,128)(2,1)S(1)}, u32[]{:S(2)}, u32[]{:S(2)}) collective-permute-start(bf16[64,896]{1,0:T(8,128)(2,1)S(1)} %get-tuple-element.8), channel_id=1, source_target_pairs={{0,12},{4,16},{8,20},{12,24},{16,28},{20,0},{24,4},{28,8},{1,13},{... | collective-permute-start | bytes 344072 | tf_op jit(solution)/shard_map/ppermute | solution.py:16
  117.5 8.0 %collective-permute-start.26 = (bf16[64,896]{1,0:T(8,128)(2,1)S(1)}, bf16[64,896]{1,0:T(8,128)(2,1)S(1)}, u32[]{:S(2)}, u32[]{:S(2)}) collective-permute-start(bf16[64,896]{1,0:T(8,128)(2,1)S(1)} %get-tuple-element.8), channel_id=1, source_target_pairs={{0,16},{4,20},{8,24},{12,28},{16,0},{20,4},{24,8},{28,12},{1,17},{... | collective-permute-start | bytes 344072 | tf_op jit(solution)/shard_map/ppermute | solution.py:16
  118.1 8.1 %collective-permute-start.27 = (bf16[64,896]{1,0:T(8,128)(2,1)S(1)}, bf16[64,896]{1,0:T(8,128)(2,1)S(1)}, u32[]{:S(2)}, u32[]{:S(2)}) collective-permute-start(bf16[64,896]{1,0:T(8,128)(2,1)S(1)} %get-tuple-element.8), channel_id=1, source_target_pairs={{0,20},{4,24},{8,28},{12,0},{16,4},{20,8},{24,12},{28,16},{1,21},{... | collective-permute-start | bytes 344072 | tf_op jit(solution)/shard_map/ppermute | solution.py:16
  118.2 8.7 %collective-permute-start.28 = (bf16[64,896]{1,0:T(8,128)(2,1)S(1)}, bf16[64,896]{1,0:T(8,128)(2,1)S(1)}, u32[]{:S(2)}, u32[]{:S(2)}) collective-permute-start(bf16[64,896]{1,0:T(8,128)(2,1)S(1)} %get-tuple-element.8), channel_id=1, source_target_pairs={{0,24},{4,28},{8,0},{12,4},{16,8},{20,12},{24,16},{28,20},{1,25},{... | collective-permute-start | bytes 344072 | tf_op jit(solution)/shard_map/ppermute | solution.py:16
  121.4 6.1 %collective-permute-start.29 = (bf16[64,896]{1,0:T(8,128)(2,1)S(1)}, bf16[64,896]{1,0:T(8,128)(2,1)S(1)}, u32[]{:S(2)}, u32[]{:S(2)}) collective-permute-start(bf16[64,896]{1,0:T(8,128)(2,1)S(1)} %get-tuple-element.8), channel_id=1, source_target_pairs={{0,28},{4,0},{8,4},{12,8},{16,12},{20,16},{24,20},{28,24},{1,29},{... | collective-permute-start | bytes 344072 | tf_op jit(solution)/shard_map/ppermute | solution.py:16
  131.3 5.4 %collective-permute-start.30 = (f32[1,2,64]{2,1,0:T(2,128)S(1)}, f32[1,2,64]{2,1,0:T(2,128)S(1)}, u32[]{:S(2)}, u32[]{:S(2)}) collective-permute-start(f32[1,2,64]{2,1,0:T(2,128)S(1)} %get-tuple-element.6), channel_id=1, source_target_pairs={{0,1},{1,2},{2,3},{3,0},{4,5},{5,6},{6,7},{7,4},{8,9},{9,10},{10,1... | collective-permute-start | bytes 1544 | tf_op jit(solution)/shard_map/ppermute | solution.py:16
  132.5 4.5 %collective-permute-start.31 = (f32[1,2,64]{2,1,0:T(2,128)S(1)}, f32[1,2,64]{2,1,0:T(2,128)S(1)}, u32[]{:S(2)}, u32[]{:S(2)}) collective-permute-start(f32[1,2,64]{2,1,0:T(2,128)S(1)} %get-tuple-element.6), channel_id=1, source_target_pairs={{0,2},{1,3},{2,0},{3,1},{4,6},{5,7},{6,4},{7,5},{8,10},{9,11},{10,... | collective-permute-start | bytes 1544 | tf_op jit(solution)/shard_map/ppermute | solution.py:16
  137.6 6.4 %collective-permute-start.33 = (f32[1,2,64]{2,1,0:T(2,128)S(1)}, f32[1,2,64]{2,1,0:T(2,128)S(1)}, u32[]{:S(2)}, u32[]{:S(2)}) collective-permute-start(f32[1,2,64]{2,1,0:T(2,128)S(1)} %bitcast.11), channel_id=1, source_target_pairs={{0,4},{4,8},{8,12},{12,16},{16,20},{20,24},{24,28},{28,0},{1,5},{5... | collective-permute-start | bytes 1544 | tf_op jit(solution)/shard_map/ppermute | solution.py:16
  137.8 7.5 %collective-permute-start.34 = (f32[1,2,64]{2,1,0:T(2,128)S(1)}, f32[1,2,64]{2,1,0:T(2,128)S(1)}, u32[]{:S(2)}, u32[]{:S(2)}) collective-permute-start(f32[1,2,64]{2,1,0:T(2,128)S(1)} %bitcast.12), channel_id=1, source_target_pairs={{0,8},{4,12},{8,16},{12,20},{16,24},{20,28},{24,0},{28,4},{1,9},{5... | collective-permute-start | bytes 1544 | tf_op jit(solution)/shard_map/ppermute | solution.py:16
  141.2 5.6 %collective-permute-start.35 = (f32[1,2,64]{2,1,0:T(2,128)S(1)}, f32[1,2,64]{2,1,0:T(2,128)S(1)}, u32[]{:S(2)}, u32[]{:S(2)}) collective-permute-start(f32[1,2,64]{2,1,0:T(2,128)S(1)} %bitcast.13), channel_id=1, source_target_pairs={{0,12},{4,16},{8,20},{12,24},{16,28},{20,0},{24,4},{28,8},{1,13},{... | collective-permute-start | bytes 1544 | tf_op jit(solution)/shard_map/ppermute | solution.py:16
  142.1 4.7 %collective-permute-start.36 = (f32[1,2,64]{2,1,0:T(2,128)S(1)}, f32[1,2,64]{2,1,0:T(2,128)S(1)}, u32[]{:S(2)}, u32[]{:S(2)}) collective-permute-start(f32[1,2,64]{2,1,0:T(2,128)S(1)} %bitcast.14), channel_id=1, source_target_pairs={{0,16},{4,20},{8,24},{12,28},{16,0},{20,4},{24,8},{28,12},{1,17},{... | collective-permute-start | bytes 1544 | tf_op jit(solution)/shard_map/ppermute | solution.py:16
  (13 other events, 104.4 us)

commit v3 on v1

--- a/solution.py
+++ b/solution.py
@@ -27,8 +27,22 @@
     return x
 
 
-def _allreduce_bf16(x, axis, n, dim):
+def _allreduce_bf16(x, axis, n, dim, works=()):
     me = lax.axis_index(axis)
+    works = list(works)
+    done = []
+
+    def swap(v, b):
+        if not works:
+            return _swap(v, axis, n, b)
+        work, arg = works.pop(0)
+        v, arg = lax.optimization_barrier((v, arg))
+        result = work(arg)
+        other = _swap(v, axis, n, b)
+        other, result = lax.optimization_barrier((other, result))
+        done.append(result)
+        return other
+
     b = 1
     while b < n:
         half = x.shape[dim] // 2
@@ -37,16 +51,17 @@
         hi = lax.slice_in_dim(x, half, 2 * half, axis=dim)
         keep = jnp.where(upper, hi, lo)
         send = jnp.where(upper, lo, hi)
-        x = keep + _swap(send, axis, n, b)
+        x = keep + swap(send, b)
         b *= 2
     x = x.astype(BF16)
     b = n // 2
     while b >= 1:
-        other = _swap(x, axis, n, b)
+        other = swap(x, b)
         first = (me // b) % 2 == 0
         x = jnp.where(first, jnp.concatenate([x, other], dim), jnp.concatenate([other, x], dim))
         b //= 2
-    return x
+    done += [work(arg) for work, arg in works]
+    return x, done
 
 
 def _allreduce_small(x, axis, n):
@@ -70,38 +85,53 @@
         )
 
 
-def _lifted(act_rot, eigenvalues, queries):
+def _lifted(act_rot, eigenvalues, queries, t0, t1, tk):
     nq, kk, jj = queries.shape
     tt = act_rot.shape[0]
-    tk = next(c for c in (512, 256, 128, kk) if kk % c == 0)
+    kc = (t1 - t0) * tk
     return pl.pallas_call(
         _lifted_kernel,
-        grid=(kk // tk,),
+        grid=(t1 - t0,),
         in_specs=[
             pl.BlockSpec((tt, jj), lambda i: (0, 0)),
-            pl.BlockSpec((tk, jj), lambda i: (i, 0)),
-            pl.BlockSpec((nq, tk, jj), lambda i: (0, i, 0)),
+            pl.BlockSpec((tk, jj), lambda i: (t0 + i, 0)),
+            pl.BlockSpec((nq, tk, jj), lambda i: (0, t0 + i, 0)),
         ],
         out_specs=pl.BlockSpec((nq, tt, tk), lambda i: (0, 0, i)),
-        out_shape=jax.ShapeDtypeStruct((nq, tt, kk), F32),
-        compiler_params=pltpu.CompilerParams(dimension_semantics=("arbitrary",)),
+        out_shape=jax.ShapeDtypeStruct((nq, tt, kc), F32),
+        compiler_params=pltpu.CompilerParams(
+            dimension_semantics=("arbitrary",), vmem_limit_bytes=48 * 1024 * 1024
+        ),
         cost_estimate=pl.CostEstimate(
-            flops=4 * nq * kk * jj * tt,
-            bytes_accessed=(nq + 1) * kk * jj * 2 + nq * tt * kk * 4,
+            flops=4 * nq * kc * jj * tt,
+            bytes_accessed=(nq + 1) * kc * jj * 2 + nq * tt * kc * 4,
             transcendentals=0,
         ),
     )(act_rot, eigenvalues, queries)
 
 
-def local(out_grads, in_acts, out_basis, in_basis, eigenvalues, queries, *, nr, nc):
+def local(out_grads, in_acts, out_basis, in_basis, eigenvalues, queries, *, nr, nc, nl):
     acts_all = _gather(in_acts, "row", nr, 0)
     grads_all = _gather(out_grads, "col", nc, 0)
     act_part = jnp.dot(acts_all, in_basis, preferred_element_type=F32)
-    act_rot = _allreduce_bf16(act_part, "col", nc, 1)
+    act_rot, _ = _allreduce_bf16(act_part, "col", nc, 1)
+    grads_all, act_rot = lax.optimization_barrier((grads_all, act_rot))
     grad_part = jnp.dot(grads_all, out_basis, preferred_element_type=F32)
-    grad_rot = _allreduce_bf16(grad_part, "row", nr, 1)
-    lifted = _lifted(act_rot, eigenvalues, queries)
-    partial = jnp.sum(lifted * grad_rot.astype(F32)[None], axis=2)
+    kk = queries.shape[1]
+    tk = next(c for c in (512, 256, 128, kk) if kk % c == 0)
+    nt = kk // tk
+    bounds = [round(i * nt / nl) for i in range(nl + 1)]
+    spans = [(t0, t1) for t0, t1 in zip(bounds[:-1], bounds[1:]) if t1 > t0]
+    works = [
+        (functools.partial(lambda a, t0, t1: _lifted(a, eigenvalues, queries, t0, t1, tk), t0=t0, t1=t1), act_rot)
+        for t0, t1 in spans
+    ]
+    grad_rot, lifted = _allreduce_bf16(grad_part, "row", nr, 1, works)
+    partial = None
+    for (t0, t1), piece in zip(spans, lifted):
+        g = grad_rot[:, t0 * tk : t1 * tk].astype(F32)
+        term = jnp.sum(piece * g[None], axis=2)
+        partial = term if partial is None else partial + term
     return _allreduce_small(_allreduce_small(partial, "col", nc), "row", nr)
 
 
@@ -114,5 +144,5 @@
         P("col", "row"),
         P(None, "col", "row"),
     )
-    fn = functools.partial(local, nr=mesh.shape["row"], nc=mesh.shape["col"])
+    fn = functools.partial(local, nr=mesh.shape["row"], nc=mesh.shape["col"], nl=6)
     return jax.shard_map(fn, mesh=mesh, in_specs=in_specs, out_specs=P(), check_vma=False)

time: 134 us -> 129 us (0.963)
  waiting for transfers between devices: 57.9 us -> 45.5 us
  Pallas kernels: 28.3 us -> 35.6 us
  other arithmetic: 6.79 us -> 4.36 us
  matrix products: 21.3 us -> 23.4 us
    ppermute x20, waiting for transfers between devices: 57.9 us -> 45.5 us  [_swap(): return lax.ppermute(x, axis, [(i, i ^ b) for i in range(n)])]
    pallas_call x1 -> x6, Pallas kernels: 28.3 us -> 35.6 us  [_lifted(): pl.pallas_call(_lifted_kernel, grid=(t1 - t0,), in_specs=[pl.BlockSpec((t...]
    dot_general x1, matrix products: 0.84 us -> 3.03 us  [local(): act_part = jnp.dot(acts_all, in_basis, preferred_element_type=F32)]
    reduce_sum x1 -> x3, other arithmetic: 2.41 us -> 0.51 us  [local(): term = jnp.sum(piece * g[None], axis=2)]
  transfers between devices with their start and end apart: 20 -> 20, of which waited for: 16 -> 14; matrix products, arithmetic and copies ran while one was open for 2% -> 0% of each run, Pallas kernels for 21% -> 28%
where the time goes in v3:
time: 129 us
  waiting for transfers between devices  45.5 us (35%)
  Pallas kernels  35.6 us (28%)
  matrix products  23.4 us (18%)
  starting transfers between devices  19.7 us (15%)
  other arithmetic  4.36 us (3%)
    ppermute x20, waiting for transfers between devices, _swap(): return lax.ppermute(x, axis, [(i, i ^ b) for i in range(n)])  45.5 us
    pallas_call x6, Pallas kernels, _lifted(): pl.pallas_call(_lifted_kernel, grid=(t1 - t0,), in_specs=[pl.BlockSpec((t...  35.6 us
    dot_general x1, matrix products, local(): grad_part = jnp.dot(grads_all, out_basis, preferred_element_type=F32)  20.4 us
    ppermute x20, starting transfers between devices, _swap(): return lax.ppermute(x, axis, [(i, i ^ b) for i in range(n)])  19.7 us
    dot_general x1, matrix products, local(): act_part = jnp.dot(acts_all, in_basis, preferred_element_type=F32)  3.03 us
  transfers between devices with their start and end apart: 20, of which 14 were waited for; matrix products, arithmetic and copies ran while one was open for 0% of the time, Pallas kernels for 28%

profile of v3, /device:TPU:0, one launch (start us, length us, event | category | flops | bytes accessed | tf_op | source)
XLA Modules:
  0.0 129.0 jit_solution(7164001107098319386)
XLA Ops:
  0.5 1.1 collective-permute-done.2
  1.5 0.8 maximum_select_fusion.9
  2.4 2.9 %collective-permute-start.3 = (bf16[16,2048]{1,0:T(8,128)(2,1)S(1)}, bf16[16,2048]{1,0:T(8,128)(2,1)S(1)}, u32[]{:S(2)}, u32[]{:S(2)}) collective-permute-start(bf16[16,2048]{1,0:T(8,128)(2,1)S(1)} %maximum_select_fusion.9), channel_id=1, source_target_pairs={{0,8},{4,12},{8,0},{12,4},{16,24},{20,28},{24,16},{28,20},{1,9},{5... | collective-permute-start | bytes 196616 | tf_op jit(solution)/shard_map/ppermute | solution.py:16
  5.3 2.4 %collective-permute-done.3 = bf16[16,2048]{1,0:T(8,128)(2,1)S(1)} collective-permute-done((bf16[16,2048]{1,0:T(8,128)(2,1)S(1)}, bf16[16,2048]{1,0:T(8,128)(2,1)S(1)}, u32[]{:S(2)}, u32[]{:S(2)}) %collective-permute-start.3) | collective-permute-done | bytes 65568 | tf_op jit(solution)/shard_map/ppermute | solution.py:16
  7.7 1.9 %collective-permute-start.4 = (bf16[32,2048]{1,0:T(8,128)(2,1)S(1)}, bf16[32,2048]{1,0:T(8,128)(2,1)S(1)}, u32[]{:S(2)}, u32[]{:S(2)}) collective-permute-start(bf16[32,2048]{1,0:T(8,128)(2,1)S(1)} %maximum_select_fusion.7), channel_id=1, source_target_pairs={{0,16},{4,20},{8,24},{12,28},{16,0},{20,4},{24,8},{28,12},{1,17},{... | collective-permute-start | bytes 393224 | tf_op jit(solution)/shard_map/ppermute | solution.py:16
  9.7 3.2 %collective-permute-done.4 = bf16[32,2048]{1,0:T(8,128)(2,1)S(1)} collective-permute-done((bf16[32,2048]{1,0:T(8,128)(2,1)S(1)}, bf16[32,2048]{1,0:T(8,128)(2,1)S(1)}, u32[]{:S(2)}, u32[]{:S(2)}) %collective-permute-start.4) | collective-permute-done | bytes 131104 | tf_op jit(solution)/shard_map/ppermute | solution.py:16
  12.8 3.0 %fusion = f32[64,1024]{1,0:T(8,128)S(1)} fusion(bf16[2048,1024]{1,0:T(8,128)(2,1)} %param.9, bf16[32,2048]{1,0:T(8,128)(2,1)S(1)} %collective-permute-done.4, bf16[32,2048]{1,0:T(8,128)(2,1)S(1)} %maximum_select_fusion.7, pred[]{:T(512)S(6)} %eq.56), kind=kOutput, calls=%fused_computation.14 | convolution fusion | flops 269615104 | bytes 4718593 | tf_op jit(solution)/shard_map/dot_general | solution.py:116
  15.9 1.9 %collective-permute-start.5 = (f32[64,512]{1,0:T(8,128)S(1)}, f32[64,512]{1,0:T(8,128)S(1)}, u32[]{:S(2)}, u32[]{:S(2)}) collective-permute-start(f32[64,512]{1,0:T(8,128)S(1)} %slice_select_fusion.3), channel_id=1, source_target_pairs={{0,1},{1,0},{2,3},{3,2},{4,5},{5,4},{6,7},{7,6},{8,9},{9,8},{10,11... | collective-permute-start | bytes 393224 | tf_op jit(solution)/shard_map/ppermute | solution.py:16
  18.0 3.4 %collective-permute-done.5 = f32[64,512]{1,0:T(8,128)S(1)} collective-permute-done((f32[64,512]{1,0:T(8,128)S(1)}, f32[64,512]{1,0:T(8,128)S(1)}, u32[]{:S(2)}, u32[]{:S(2)}) %collective-permute-start.5) | collective-permute-done | bytes 131104 | tf_op jit(solution)/shard_map/ppermute | solution.py:16
  21.4 3.2 %collective-permute-start.6 = (f32[64,256]{1,0:T(8,128)S(1)}, f32[64,256]{1,0:T(8,128)S(1)}, u32[]{:S(2)}, u32[]{:S(2)}) collective-permute-start(f32[64,256]{1,0:T(8,128)S(1)} %slice_select_fusion.4), channel_id=1, source_target_pairs={{0,2},{1,3},{2,0},{3,1},{4,6},{5,7},{6,4},{7,5},{8,10},{9,11},{10,... | collective-permute-start | bytes 196616 | tf_op jit(solution)/shard_map/ppermute | solution.py:16
  24.7 1.3 %collective-permute-start.1 = (bf16[32,3584]{1,0:T(8,128)(2,1)S(1)}, bf16[32,3584]{1,0:T(8,128)(2,1)S(1)}, u32[]{:S(2)}, u32[]{:S(2)}) collective-permute-start(bf16[32,3584]{1,0:T(8,128)(2,1)S(1)} %maximum_select_fusion.5), channel_id=1, source_target_pairs={{0,2},{1,3},{2,0},{3,1},{4,6},{5,7},{6,4},{7,5},{8,10},{9,11},{10,... | collective-permute-start | bytes 688136 | tf_op jit(solution)/shard_map/ppermute | solution.py:16
  26.0 6.7 %collective-permute-done.6 = f32[64,256]{1,0:T(8,128)S(1)} collective-permute-done((f32[64,256]{1,0:T(8,128)S(1)}, f32[64,256]{1,0:T(8,128)S(1)}, u32[]{:S(2)}, u32[]{:S(2)}) %collective-permute-start.6) | collective-permute-done | bytes 65568 | tf_op jit(solution)/shard_map/ppermute | solution.py:16
  32.8 4.9 %collective-permute-done.7 = bf16[64,256]{1,0:T(8,128)(2,1)S(1)} collective-permute-done((bf16[64,256]{1,0:T(8,128)(2,1)S(1)}, bf16[64,256]{1,0:T(8,128)(2,1)S(1)}, u32[]{:S(2)}, u32[]{:S(2)}) %collective-permute-start.7) | collective-permute-done | bytes 32800 | tf_op jit(solution)/shard_map/ppermute | solution.py:16
  37.9 4.2 %collective-permute-done.8 = bf16[64,512]{1,0:T(8,128)(2,1)S(1)} collective-permute-done((bf16[64,512]{1,0:T(8,128)(2,1)S(1)}, bf16[64,512]{1,0:T(8,128)(2,1)S(1)}, u32[]{:S(2)}, u32[]{:S(2)}) %collective-permute-start.8) | collective-permute-done | bytes 65568 | tf_op jit(solution)/shard_map/ppermute | solution.py:16
  42.1 20.4 %fusion.8 = f32[64,7168]{1,0:T(8,128)S(1)} fusion(bf16[64,3584]{1,0:T(8,128)(2,1)S(1)} %maximum_select_fusion.1, bf16[3584,7168]{1,0:T(8,128)(2,1)} %param.8), kind=kOutput, calls=%fused_computation.41 | convolution fusion | flops 3288334336 | bytes 53673984 | tf_op jit(solution)/shard_map/dot_general | solution.py:119
  62.7 5.3 %shard_map.64 = f32[2,64,1024]{2,1,0:T(8,128)S(1)} custom-call(bf16[64,1024]{1,0:T(8,128)(2,1)S(1)} %maximum_select_fusion.8.a_ref, bf16[7168,1024]{1,0:T(8,128)(2,1)} %e_ref.11, bf16[2,7168,1024]{2,1,0:T(8,128)(2,1)} %q_ref.11), custom_call_target="tpu_custom_call" | custom-call | flops 536870912 | bytes 6815744 | tf_op jit(solution)/shard_map/pallas_call | solution.py:92
  68.0 1.3 %select_add_fusion = f32[64,3584]{1,0:T(8,128)S(1)} fusion(f32[64,3584]{1,0:T(8,128)} %collective-permute-done.9, f32[64,7168]{1,0:T(8,128)S(1)} %fusion.8, pred[]{:T(512)S(6)} %eq.51), kind=kLoop, calls=%fused_computation.1 | loop fusion | flops 458752 | bytes 3670017 | tf_op jit(solution)/shard_map/add | solution.py:54
  69.4 1.6 %collective-permute-start.10 = (f32[64,1792]{1,0:T(8,128)S(1)}, f32[64,1792]{1,0:T(8,128)S(1)}, u32[]{:S(2)}, u32[]{:S(2)}) collective-permute-start(f32[64,1792]{1,0:T(8,128)S(1)} %slice_select_fusion.1), channel_id=1, source_target_pairs={{0,8},{4,12},{8,0},{12,4},{16,24},{20,28},{24,16},{28,20},{1,9},{5... | collective-permute-start | bytes 1376264 | tf_op jit(solution)/shard_map/ppermute | solution.py:16
  71.0 7.2 %shard_map.65 = f32[2,64,1536]{2,1,0:T(8,128)S(1)} custom-call(bf16[64,1024]{1,0:T(8,128)(2,1)S(1)} %maximum_select_fusion.8.a_ref, bf16[7168,1024]{1,0:T(8,128)(2,1)} %e_ref.11, bf16[2,7168,1024]{2,1,0:T(8,128)(2,1)} %q_ref.11), custom_call_target="tpu_custom_call" | custom-call | flops 805306368 | bytes 10223616 | tf_op jit(solution)/shard_map/pallas_call | solution.py:92
  78.2 4.2 %collective-permute-done.10 = f32[64,1792]{1,0:T(8,128)S(1)} collective-permute-done((f32[64,1792]{1,0:T(8,128)S(1)}, f32[64,1792]{1,0:T(8,128)S(1)}, u32[]{:S(2)}, u32[]{:S(2)}) %collective-permute-start.10) | collective-permute-done | bytes 458784 | tf_op jit(solution)/shard_map/ppermute | solution.py:16
  82.5 1.6 %collective-permute-start.11 = (f32[64,896]{1,0:T(8,128)S(1)}, f32[64,896]{1,0:T(8,128)S(1)}, u32[]{:S(2)}, u32[]{:S(2)}) collective-permute-start(f32[64,896]{1,0:T(8,128)S(1)} %slice_select_fusion.2), channel_id=1, source_target_pairs={{0,16},{4,20},{8,24},{12,28},{16,0},{20,4},{24,8},{28,12},{1,17},{... | collective-permute-start | bytes 688136 | tf_op jit(solution)/shard_map/ppermute | solution.py:16
  84.1 5.3 %shard_map.66 = f32[2,64,1024]{2,1,0:T(8,128)S(1)} custom-call(bf16[64,1024]{1,0:T(8,128)(2,1)S(1)} %maximum_select_fusion.8.a_ref, bf16[7168,1024]{1,0:T(8,128)(2,1)} %e_ref.11, bf16[2,7168,1024]{2,1,0:T(8,128)(2,1)} %q_ref.11), custom_call_target="tpu_custom_call" | custom-call | flops 536870912 | bytes 6815744 | tf_op jit(solution)/shard_map/pallas_call | solution.py:92
  89.8 1.6 %collective-permute-start.12 = (bf16[64,896]{1,0:T(8,128)(2,1)S(1)}, bf16[64,896]{1,0:T(8,128)(2,1)S(1)}, u32[]{:S(2)}, u32[]{:S(2)}) collective-permute-start(bf16[64,896]{1,0:T(8,128)(2,1)S(1)} %add_convert_fusion), channel_id=1, source_target_pairs={{0,16},{4,20},{8,24},{12,28},{16,0},{20,4},{24,8},{28,12},{1,17},{... | collective-permute-start | bytes 344072 | tf_op jit(solution)/shard_map/ppermute | solution.py:16
  91.4 5.3 %shard_map.67 = f32[2,64,1024]{2,1,0:T(8,128)S(1)} custom-call(bf16[64,1024]{1,0:T(8,128)(2,1)S(1)} %maximum_select_fusion.8.a_ref, bf16[7168,1024]{1,0:T(8,128)(2,1)} %e_ref.11, bf16[2,7168,1024]{2,1,0:T(8,128)(2,1)} %q_ref.11), custom_call_target="tpu_custom_call" | custom-call | flops 536870912 | bytes 6815744 | tf_op jit(solution)/shard_map/pallas_call | solution.py:92
  96.7 1.6 %collective-permute-start.13 = (bf16[64,1792]{1,0:T(8,128)(2,1)S(1)}, bf16[64,1792]{1,0:T(8,128)(2,1)S(1)}, u32[]{:S(2)}, u32[]{:S(2)}) collective-permute-start(bf16[64,1792]{1,0:T(8,128)(2,1)S(1)} %maximum_select_fusion.6), channel_id=1, source_target_pairs={{0,8},{4,12},{8,0},{12,4},{16,24},{20,28},{24,16},{28,20},{1,9},{5... | collective-permute-start | bytes 688136 | tf_op jit(solution)/shard_map/ppermute | solution.py:16
  98.3 7.2 %shard_map.68 = f32[2,64,1536]{2,1,0:T(8,128)S(1)} custom-call(bf16[64,1024]{1,0:T(8,128)(2,1)S(1)} %maximum_select_fusion.8.a_ref, bf16[7168,1024]{1,0:T(8,128)(2,1)} %e_ref.11, bf16[2,7168,1024]{2,1,0:T(8,128)(2,1)} %q_ref.11), custom_call_target="tpu_custom_call" | custom-call | flops 805306368 | bytes 10223616 | tf_op jit(solution)/shard_map/pallas_call | solution.py:92
  105.7 5.3 %shard_map.69 = f32[2,64,1024]{2,1,0:T(8,128)S(1)} custom-call(bf16[64,1024]{1,0:T(8,128)(2,1)S(1)} %maximum_select_fusion.8.a_ref, bf16[7168,1024]{1,0:T(8,128)(2,1)} %e_ref.11, bf16[2,7168,1024]{2,1,0:T(8,128)(2,1)} %q_ref.11), custom_call_target="tpu_custom_call" | custom-call | flops 536870912 | bytes 6815744 | tf_op jit(solution)/shard_map/pallas_call | solution.py:92
  112.1 3.6 %collective-permute-done.15 = f32[2,64]{1,0:T(2,128)S(1)} collective-permute-done((f32[2,64]{1,0:T(2,128)S(1)}, f32[2,64]{1,0:T(2,128)S(1)}, u32[]{:S(2)}, u32[]{:S(2)}) %collective-permute-start.15) | collective-permute-done | bytes 544 | tf_op jit(solution)/shard_map/ppermute | solution.py:16
  115.7 4.4 %collective-permute-done.16 = f32[2,64]{1,0:T(2,128)S(1)} collective-permute-done((f32[2,64]{1,0:T(2,128)S(1)}, f32[2,64]{1,0:T(2,128)S(1)}, u32[]{:S(2)}, u32[]{:S(2)}) %collective-permute-start.16) | collective-permute-done | bytes 544 | tf_op jit(solution)/shard_map/ppermute | solution.py:16
  120.1 1.1 collective-permute-done.17
  121.8 3.0 %collective-permute-done.18 = f32[2,64]{1,0:T(2,128)S(1)} collective-permute-done((f32[2,64]{1,0:T(2,128)S(1)}, f32[2,64]{1,0:T(2,128)S(1)}, u32[]{:S(2)}, u32[]{:S(2)}) %collective-permute-start.18) | collective-permute-done | bytes 544 | tf_op jit(solution)/shard_map/ppermute | solution.py:16
  125.3 3.1 %collective-permute-done.19 = f32[2,64]{1,0:T(2,128)S(1)} collective-permute-done((f32[2,64]{1,0:T(2,128)S(1)}, f32[2,64]{1,0:T(2,128)S(1)}, u32[]{:S(2)}, u32[]{:S(2)}) %collective-permute-start.19) | collective-permute-done | bytes 544 | tf_op jit(solution)/shard_map/ppermute | solution.py:16
  (48 shorter events, 4.7 us)
Async XLA Ops:
  0.0 17.8 %copy-start = (bf16[16,3584]{1,0:T(8,128)(2,1)S(1)}, bf16[16,3584]{1,0:T(8,128)(2,1)}, u32[]{:S(2)}) copy-start(bf16[16,3584]{1,0:T(8,128)(2,1)} %param.6) | copy-start | bytes 344068
  0.0 1.5 %collective-permute-start.2 = (bf16[8,2048]{1,0:T(8,128)(2,1)}, bf16[8,2048]{1,0:T(8,128)(2,1)S(1)}, u32[]{:S(2)}, u32[]{:S(2)}) collective-permute-start(bf16[8,2048]{1,0:T(8,128)(2,1)} %param.7), channel_id=1, source_target_pairs={{0,4},{4,0},{8,12},{12,8},{16,20},{20,16},{24,28},{28,24},{1,5},{5... | collective-permute-start | bytes 98312 | tf_op jit(solution)/shard_map/ppermute | solution.py:16
  2.4 5.3 %collective-permute-start.3 = (bf16[16,2048]{1,0:T(8,128)(2,1)S(1)}, bf16[16,2048]{1,0:T(8,128)(2,1)S(1)}, u32[]{:S(2)}, u32[]{:S(2)}) collective-permute-start(bf16[16,2048]{1,0:T(8,128)(2,1)S(1)} %maximum_select_fusion.9), channel_id=1, source_target_pairs={{0,8},{4,12},{8,0},{12,4},{16,24},{20,28},{24,16},{28,20},{1,9},{5... | collective-permute-start | bytes 196616 | tf_op jit(solution)/shard_map/ppermute | solution.py:16
  7.7 5.1 %collective-permute-start.4 = (bf16[32,2048]{1,0:T(8,128)(2,1)S(1)}, bf16[32,2048]{1,0:T(8,128)(2,1)S(1)}, u32[]{:S(2)}, u32[]{:S(2)}) collective-permute-start(bf16[32,2048]{1,0:T(8,128)(2,1)S(1)} %maximum_select_fusion.7), channel_id=1, source_target_pairs={{0,16},{4,20},{8,24},{12,28},{16,0},{20,4},{24,8},{28,12},{1,17},{... | collective-permute-start | bytes 393224 | tf_op jit(solution)/shard_map/ppermute | solution.py:16
  15.9 5.4 %collective-permute-start.5 = (f32[64,512]{1,0:T(8,128)S(1)}, f32[64,512]{1,0:T(8,128)S(1)}, u32[]{:S(2)}, u32[]{:S(2)}) collective-permute-start(f32[64,512]{1,0:T(8,128)S(1)} %slice_select_fusion.3), channel_id=1, source_target_pairs={{0,1},{1,0},{2,3},{3,2},{4,5},{5,4},{6,7},{7,6},{8,9},{9,8},{10,11... | collective-permute-start | bytes 393224 | tf_op jit(solution)/shard_map/ppermute | solution.py:16
  17.8 6.8 %collective-permute-start = (bf16[16,3584]{1,0:T(8,128)(2,1)S(1)}, bf16[16,3584]{1,0:T(8,128)(2,1)S(1)}, u32[]{:S(2)}, u32[]{:S(2)}) collective-permute-start(bf16[16,3584]{1,0:T(8,128)(2,1)S(1)} %copy-done), channel_id=1, source_target_pairs={{0,1},{1,0},{2,3},{3,2},{4,5},{5,4},{6,7},{7,6},{8,9},{9,8},{10,11... | collective-permute-start | bytes 344072 | tf_op jit(solution)/shard_map/ppermute | solution.py:16
  21.4 11.3 %collective-permute-start.6 = (f32[64,256]{1,0:T(8,128)S(1)}, f32[64,256]{1,0:T(8,128)S(1)}, u32[]{:S(2)}, u32[]{:S(2)}) collective-permute-start(f32[64,256]{1,0:T(8,128)S(1)} %slice_select_fusion.4), channel_id=1, source_target_pairs={{0,2},{1,3},{2,0},{3,1},{4,6},{5,7},{6,4},{7,5},{8,10},{9,11},{10,... | collective-permute-start | bytes 196616 | tf_op jit(solution)/shard_map/ppermute | solution.py:16
  24.7 13.1 %collective-permute-start.1 = (bf16[32,3584]{1,0:T(8,128)(2,1)S(1)}, bf16[32,3584]{1,0:T(8,128)(2,1)S(1)}, u32[]{:S(2)}, u32[]{:S(2)}) collective-permute-start(bf16[32,3584]{1,0:T(8,128)(2,1)S(1)} %maximum_select_fusion.5), channel_id=1, source_target_pairs={{0,2},{1,3},{2,0},{3,1},{4,6},{5,7},{6,4},{7,5},{8,10},{9,11},{10,... | collective-permute-start | bytes 688136 | tf_op jit(solution)/shard_map/ppermute | solution.py:16
  32.7 5.0 %collective-permute-start.7 = (bf16[64,256]{1,0:T(8,128)(2,1)S(1)}, bf16[64,256]{1,0:T(8,128)(2,1)S(1)}, u32[]{:S(2)}, u32[]{:S(2)}) collective-permute-start(bf16[64,256]{1,0:T(8,128)(2,1)S(1)} %add_convert_fusion.1), channel_id=1, source_target_pairs={{0,2},{1,3},{2,0},{3,1},{4,6},{5,7},{6,4},{7,5},{8,10},{9,11},{10,... | collective-permute-start | bytes 98312 | tf_op jit(solution)/shard_map/ppermute | solution.py:16
  37.7 4.3 %collective-permute-start.8 = (bf16[64,512]{1,0:T(8,128)(2,1)S(1)}, bf16[64,512]{1,0:T(8,128)(2,1)S(1)}, u32[]{:S(2)}, u32[]{:S(2)}) collective-permute-start(bf16[64,512]{1,0:T(8,128)(2,1)S(1)} %maximum_select_fusion.10), channel_id=1, source_target_pairs={{0,1},{1,0},{2,3},{3,2},{4,5},{5,4},{6,7},{7,6},{8,9},{9,8},{10,11... | collective-permute-start | bytes 196616 | tf_op jit(solution)/shard_map/ppermute | solution.py:16
  62.6 5.4 %collective-permute-start.9 = (f32[64,3584]{1,0:T(8,128)S(1)}, f32[64,3584]{1,0:T(8,128)}, u32[]{:S(2)}, u32[]{:S(2)}) collective-permute-start(f32[64,3584]{1,0:T(8,128)S(1)} %slice_select_fusion), channel_id=1, source_target_pairs={{0,4},{4,0},{8,12},{12,8},{16,20},{20,16},{24,28},{28,24},{1,5},{5... | collective-permute-start | bytes 2752520 | tf_op jit(solution)/shard_map/ppermute | solution.py:16
  69.4 13.0 %collective-permute-start.10 = (f32[64,1792]{1,0:T(8,128)S(1)}, f32[64,1792]{1,0:T(8,128)S(1)}, u32[]{:S(2)}, u32[]{:S(2)}) collective-permute-start(f32[64,1792]{1,0:T(8,128)S(1)} %slice_select_fusion.1), channel_id=1, source_target_pairs={{0,8},{4,12},{8,0},{12,4},{16,24},{20,28},{24,16},{28,20},{1,9},{5... | collective-permute-start | bytes 1376264 | tf_op jit(solution)/shard_map/ppermute | solution.py:16
  82.5 7.3 %collective-permute-start.11 = (f32[64,896]{1,0:T(8,128)S(1)}, f32[64,896]{1,0:T(8,128)S(1)}, u32[]{:S(2)}, u32[]{:S(2)}) collective-permute-start(f32[64,896]{1,0:T(8,128)S(1)} %slice_select_fusion.2), channel_id=1, source_target_pairs={{0,16},{4,20},{8,24},{12,28},{16,0},{20,4},{24,8},{28,12},{1,17},{... | collective-permute-start | bytes 688136 | tf_op jit(solution)/shard_map/ppermute | solution.py:16
  89.8 6.9 %collective-permute-start.12 = (bf16[64,896]{1,0:T(8,128)(2,1)S(1)}, bf16[64,896]{1,0:T(8,128)(2,1)S(1)}, u32[]{:S(2)}, u32[]{:S(2)}) collective-permute-start(bf16[64,896]{1,0:T(8,128)(2,1)S(1)} %add_convert_fusion), channel_id=1, source_target_pairs={{0,16},{4,20},{8,24},{12,28},{16,0},{20,4},{24,8},{28,12},{1,17},{... | collective-permute-start | bytes 344072 | tf_op jit(solution)/shard_map/ppermute | solution.py:16
  96.7 8.8 %collective-permute-start.13 = (bf16[64,1792]{1,0:T(8,128)(2,1)S(1)}, bf16[64,1792]{1,0:T(8,128)(2,1)S(1)}, u32[]{:S(2)}, u32[]{:S(2)}) collective-permute-start(bf16[64,1792]{1,0:T(8,128)(2,1)S(1)} %maximum_select_fusion.6), channel_id=1, source_target_pairs={{0,8},{4,12},{8,0},{12,4},{16,24},{20,28},{24,16},{28,20},{1,9},{5... | collective-permute-start | bytes 688136 | tf_op jit(solution)/shard_map/ppermute | solution.py:16
  105.6 5.4 %collective-permute-start.14 = (bf16[64,3584]{1,0:T(8,128)(2,1)S(1)}, bf16[64,3584]{1,0:T(8,128)(2,1)S(1)}, u32[]{:S(2)}, u32[]{:S(2)}) collective-permute-start(bf16[64,3584]{1,0:T(8,128)(2,1)S(1)} %maximum_select_fusion.2), channel_id=1, source_target_pairs={{0,4},{4,0},{8,12},{12,8},{16,20},{20,16},{24,28},{28,24},{1,5},{5... | collective-permute-start | bytes 1376264 | tf_op jit(solution)/shard_map/ppermute | solution.py:16
  112.0 3.6 %collective-permute-start.15 = (f32[2,64]{1,0:T(2,128)S(1)}, f32[2,64]{1,0:T(2,128)S(1)}, u32[]{:S(2)}, u32[]{:S(2)}) collective-permute-start(f32[2,64]{1,0:T(2,128)S(1)} %add_add_fusion), channel_id=1, source_target_pairs={{0,1},{1,0},{2,3},{3,2},{4,5},{5,4},{6,7},{7,6},{8,9},{9,8},{10,11... | collective-permute-start | bytes 1544 | tf_op jit(solution)/shard_map/ppermute | solution.py:16
  115.6 4.5 %collective-permute-start.16 = (f32[2,64]{1,0:T(2,128)S(1)}, f32[2,64]{1,0:T(2,128)S(1)}, u32[]{:S(2)}, u32[]{:S(2)}) collective-permute-start(f32[2,64]{1,0:T(2,128)S(1)} %add.91), channel_id=1, source_target_pairs={{0,2},{1,3},{2,0},{3,1},{4,6},{5,7},{6,4},{7,5},{8,10},{9,11},{10,... | collective-permute-start | bytes 1544 | tf_op jit(solution)/shard_map/ppermute | solution.py:16
  120.1 1.1 collective-permute-start.17
  121.2 3.6 %collective-permute-start.18 = (f32[2,64]{1,0:T(2,128)S(1)}, f32[2,64]{1,0:T(2,128)S(1)}, u32[]{:S(2)}, u32[]{:S(2)}) collective-permute-start(f32[2,64]{1,0:T(2,128)S(1)} %add.93), channel_id=1, source_target_pairs={{0,8},{4,12},{8,0},{12,4},{16,24},{20,28},{24,16},{28,20},{1,9},{5... | collective-permute-start | bytes 1544 | tf_op jit(solution)/shard_map/ppermute | solution.py:16
  124.8 3.6 %collective-permute-start.19 = (f32[2,64]{1,0:T(2,128)S(1)}, f32[2,64]{1,0:T(2,128)S(1)}, u32[]{:S(2)}, u32[]{:S(2)}) collective-permute-start(f32[2,64]{1,0:T(2,128)S(1)} %add.94), channel_id=1, source_target_pairs={{0,16},{4,20},{8,24},{12,28},{16,0},{20,4},{24,8},{28,12},{1,17},{... | collective-permute-start | bytes 1544 | tf_op jit(solution)/shard_map/ppermute | solution.py:16

commit v4 on v3

--- a/solution.py
+++ b/solution.py
@@ -110,13 +110,17 @@
     )(act_rot, eigenvalues, queries)
 
 
-def local(out_grads, in_acts, out_basis, in_basis, eigenvalues, queries, *, nr, nc, nl):
+def local(out_grads, in_acts, out_basis, in_basis, eigenvalues, queries, *, nr, nc, nl, ng):
     acts_all = _gather(in_acts, "row", nr, 0)
     grads_all = _gather(out_grads, "col", nc, 0)
     act_part = jnp.dot(acts_all, in_basis, preferred_element_type=F32)
-    act_rot, _ = _allreduce_bf16(act_part, "col", nc, 1)
-    grads_all, act_rot = lax.optimization_barrier((grads_all, act_rot))
-    grad_part = jnp.dot(grads_all, out_basis, preferred_element_type=F32)
+    kg = out_basis.shape[1] // ng
+    grad_works = [
+        (functools.partial(lambda g, c: jnp.dot(g, out_basis[:, c * kg : (c + 1) * kg], preferred_element_type=F32), c=c), grads_all)
+        for c in range(ng)
+    ]
+    act_rot, grad_parts = _allreduce_bf16(act_part, "col", nc, 1, grad_works)
+    grad_part = jnp.concatenate(grad_parts, axis=1)
     kk = queries.shape[1]
     tk = next(c for c in (512, 256, 128, kk) if kk % c == 0)
     nt = kk // tk
@@ -144,5 +148,5 @@
         P("col", "row"),
         P(None, "col", "row"),
     )
-    fn = functools.partial(local, nr=mesh.shape["row"], nc=mesh.shape["col"], nl=6)
+    fn = functools.partial(local, nr=mesh.shape["row"], nc=mesh.shape["col"], nl=6, ng=4)
     return jax.shard_map(fn, mesh=mesh, in_specs=in_specs, out_specs=P(), check_vma=False)

time: 129 us -> 120 us (0.930)
  waiting for transfers between devices: 45.5 us -> 25.7 us
  starting transfers between devices: 19.7 us -> 24.8 us
  matrix products: 23.4 us -> 26.9 us
    ppermute x20, waiting for transfers between devices: 45.5 us -> 25.7 us  [_swap(): return lax.ppermute(x, axis, [(i, i ^ b) for i in range(n)])]
    ppermute x20, starting transfers between devices: 19.7 us -> 24.8 us  [_swap(): return lax.ppermute(x, axis, [(i, i ^ b) for i in range(n)])]
    dot_general x1 -> x4, matrix products: 20.4 us -> 23.9 us  [local(): jnp.dot(g, out_basis[:, c * kg:(c + 1) * kg], preferred_element_type=F32)]
  transfers between devices with their start and end apart: 20 -> 20, of which waited for: 14 -> 11; matrix products, arithmetic and copies ran while one was open for 0% -> 23% of each run, Pallas kernels for 28% -> 30%
where the time goes in v4:
time: 120 us; the launch traced here: 119 us
  Pallas kernels  35.8 us (30%)
  matrix products  26.9 us (22%)
  waiting for transfers between devices  25.7 us (21%)
  starting transfers between devices  24.8 us (21%)
  other arithmetic  5.61 us (5%)
    pallas_call x6, Pallas kernels, _lifted(): pl.pallas_call(_lifted_kernel, grid=(t1 - t0,), in_specs=[pl.BlockSpec((t...  35.8 us
    ppermute x20, waiting for transfers between devices, _swap(): return lax.ppermute(x, axis, [(i, i ^ b) for i in range(n)])  25.7 us
    ppermute x20, starting transfers between devices, _swap(): return lax.ppermute(x, axis, [(i, i ^ b) for i in range(n)])  24.8 us
    dot_general x4, matrix products, local(): jnp.dot(g, out_basis[:, c * kg:(c + 1) * kg], preferred_element_type=F32)  23.9 us
    dot_general x1, matrix products, local(): act_part = jnp.dot(acts_all, in_basis, preferred_element_type=F32)  3.03 us
  transfers between devices with their start and end apart: 20, of which 11 were waited for; matrix products, arithmetic and copies ran while one was open for 23% of the time, Pallas kernels for 30%

profile of v4, /device:TPU:0, one launch (start us, length us, event | category | flops | bytes accessed | tf_op | source)
XLA Modules:
  0.0 119.3 jit_solution(9942349908477294212)
XLA Ops:
  0.5 1.1 collective-permute-done
  2.4 2.9 %collective-permute-start.1 = (bf16[16,2048]{1,0:T(8,128)(2,1)S(1)}, bf16[16,2048]{1,0:T(8,128)(2,1)S(1)}, u32[]{:S(2)}, u32[]{:S(2)}) collective-permute-start(bf16[16,2048]{1,0:T(8,128)(2,1)S(1)} %maximum_select_fusion.9), channel_id=1, source_target_pairs={{0,8},{4,12},{8,0},{12,4},{16,24},{20,28},{24,16},{28,20},{1,9},{5... | collective-permute-start | bytes 196616 | tf_op jit(solution)/shard_map/ppermute | solution.py:16
  5.3 1.6 %collective-permute-start.3 = (bf16[16,3584]{1,0:T(8,128)(2,1)}, bf16[16,3584]{1,0:T(8,128)(2,1)S(1)}, u32[]{:S(2)}, u32[]{:S(2)}) collective-permute-start(bf16[16,3584]{1,0:T(8,128)(2,1)} %param.6), channel_id=1, source_target_pairs={{0,1},{1,0},{2,3},{3,2},{4,5},{5,4},{6,7},{7,6},{8,9},{9,8},{10,11... | collective-permute-start | bytes 344072 | tf_op jit(solution)/shard_map/ppermute | solution.py:16
  7.7 1.9 %collective-permute-start.2 = (bf16[32,2048]{1,0:T(8,128)(2,1)S(1)}, bf16[32,2048]{1,0:T(8,128)(2,1)S(1)}, u32[]{:S(2)}, u32[]{:S(2)}) collective-permute-start(bf16[32,2048]{1,0:T(8,128)(2,1)S(1)} %maximum_select_fusion.7), channel_id=1, source_target_pairs={{0,16},{4,20},{8,24},{12,28},{16,0},{20,4},{24,8},{28,12},{1,17},{... | collective-permute-start | bytes 393224 | tf_op jit(solution)/shard_map/ppermute | solution.py:16
  10.4 1.0 maximum_select_fusion.5
  11.4 2.7 %collective-permute-start.4 = (bf16[32,3584]{1,0:T(8,128)(2,1)S(1)}, bf16[32,3584]{1,0:T(8,128)(2,1)S(1)}, u32[]{:S(2)}, u32[]{:S(2)}) collective-permute-start(bf16[32,3584]{1,0:T(8,128)(2,1)S(1)} %maximum_select_fusion.5), channel_id=1, source_target_pairs={{0,2},{1,3},{2,0},{3,1},{4,6},{5,7},{6,4},{7,5},{8,10},{9,11},{10,... | collective-permute-start | bytes 688136 | tf_op jit(solution)/shard_map/ppermute | solution.py:16
  14.1 3.0 %fusion.8 = f32[64,1024]{1,0:T(8,128)S(1)} fusion(bf16[2048,1024]{1,0:T(8,128)(2,1)} %param.9, bf16[32,2048]{1,0:T(8,128)(2,1)S(1)} %collective-permute-done.2, bf16[32,2048]{1,0:T(8,128)(2,1)S(1)} %maximum_select_fusion.7, pred[]{:T(512)S(6)} %eq.53), kind=kOutput, calls=%fused_computation.22 | convolution fusion | flops 269615104 | bytes 4718593 | tf_op jit(solution)/shard_map/dot_general | solution.py:116
  17.2 6.7 %collective-permute-done.4 = bf16[32,3584]{1,0:T(8,128)(2,1)S(1)} collective-permute-done((bf16[32,3584]{1,0:T(8,128)(2,1)S(1)}, bf16[32,3584]{1,0:T(8,128)(2,1)S(1)}, u32[]{:S(2)}, u32[]{:S(2)}) %collective-permute-start.4) | collective-permute-done | bytes 229408 | tf_op jit(solution)/shard_map/ppermute | solution.py:16
  24.7 6.0 %fusion.6 = f32[64,1792]{1,0:T(8,128)S(1)} fusion(bf16[64,3584]{1,0:T(8,128)(2,1)S(1)} %maximum_select_fusion.1, bf16[3584,7168]{1,0:T(8,128)(2,1)} %param.8), kind=kOutput, calls=%fused_computation.6 | convolution fusion | flops 822083584 | bytes 13762560 | tf_op jit(solution)/shard_map/dot_general | solution.py:119
  30.7 3.4 %collective-permute-start.6 = (f32[64,256]{1,0:T(8,128)S(1)}, f32[64,256]{1,0:T(8,128)S(1)}, u32[]{:S(2)}, u32[]{:S(2)}) collective-permute-start(f32[64,256]{1,0:T(8,128)S(1)} %slice_select_fusion.3), channel_id=1, source_target_pairs={{0,2},{1,3},{2,0},{3,1},{4,6},{5,7},{6,4},{7,5},{8,10},{9,11},{10,... | collective-permute-start | bytes 196616 | tf_op jit(solution)/shard_map/ppermute | solution.py:16
  34.1 6.0 %fusion.4 = f32[64,1792]{1,0:T(8,128)S(1)} fusion(bf16[64,3584]{1,0:T(8,128)(2,1)S(1)} %maximum_select_fusion.1, bf16[3584,7168]{1,0:T(8,128)(2,1)} %param.8), kind=kOutput, calls=%fused_computation.4 | convolution fusion | flops 822083584 | bytes 13762560 | tf_op jit(solution)/shard_map/dot_general | solution.py:119
  40.3 6.0 %fusion.2 = f32[64,1792]{1,0:T(8,128)S(1)} fusion(bf16[64,3584]{1,0:T(8,128)(2,1)S(1)} %maximum_select_fusion.1, bf16[3584,7168]{1,0:T(8,128)(2,1)} %param.8), kind=kOutput, calls=%fused_computation.2 | convolution fusion | flops 822083584 | bytes 13762560 | tf_op jit(solution)/shard_map/dot_general | solution.py:119
  46.3 0.9 collective-permute-start.8
  47.2 6.0 %fusion = f32[64,1792]{1,0:T(8,128)S(1)} fusion(bf16[64,3584]{1,0:T(8,128)(2,1)S(1)} %maximum_select_fusion.1, bf16[3584,7168]{1,0:T(8,128)(2,1)} %param.8), kind=kOutput, calls=%fused_computation | convolution fusion | flops 822083584 | bytes 13762560 | tf_op jit(solution)/shard_map/dot_general | solution.py:119
  53.6 5.3 %shard_map.64 = f32[2,64,1024]{2,1,0:T(8,128)S(1)} custom-call(bf16[64,1024]{1,0:T(8,128)(2,1)S(1)} %maximum_select_fusion.8.a_ref, bf16[7168,1024]{1,0:T(8,128)(2,1)} %e_ref.11, bf16[2,7168,1024]{2,1,0:T(8,128)(2,1)} %q_ref.11), custom_call_target="tpu_custom_call" | custom-call | flops 536870912 | bytes 6815744 | tf_op jit(solution)/shard_map/pallas_call | solution.py:92
  58.9 1.3 %select_add_fusion = f32[64,3584]{1,0:T(8,128)S(1)} fusion(f32[64,3584]{1,0:T(8,128)} %collective-permute-done.9, f32[64,3584]{1,0:T(8,128)S(1)} %get-tuple-element.92, f32[64,3584]{1,0:T(8,128)S(1)} %get-tuple-element.91, pred[]{:T(512)S(6)} %eq.51), kind=kLoop, calls=%fused_computation.9 | loop fusion | flops 458752 | bytes 3670017 | tf_op jit(solution)/shard_map/add | solution.py:54
  61.0 7.2 %shard_map.65 = f32[2,64,1536]{2,1,0:T(8,128)S(1)} custom-call(bf16[64,1024]{1,0:T(8,128)(2,1)S(1)} %maximum_select_fusion.8.a_ref, bf16[7168,1024]{1,0:T(8,128)(2,1)} %e_ref.11, bf16[2,7168,1024]{2,1,0:T(8,128)(2,1)} %q_ref.11), custom_call_target="tpu_custom_call" | custom-call | flops 805306368 | bytes 10223616 | tf_op jit(solution)/shard_map/pallas_call | solution.py:92
  68.2 5.0 %collective-permute-done.10 = f32[64,1792]{1,0:T(8,128)S(1)} collective-permute-done((f32[64,1792]{1,0:T(8,128)S(1)}, f32[64,1792]{1,0:T(8,128)S(1)}, u32[]{:S(2)}, u32[]{:S(2)}) %collective-permute-start.10) | collective-permute-done | bytes 458784 | tf_op jit(solution)/shard_map/ppermute | solution.py:16
  73.3 1.6 %collective-permute-start.11 = (f32[64,896]{1,0:T(8,128)S(1)}, f32[64,896]{1,0:T(8,128)S(1)}, u32[]{:S(2)}, u32[]{:S(2)}) collective-permute-start(f32[64,896]{1,0:T(8,128)S(1)} %slice_select_fusion.1), channel_id=1, source_target_pairs={{0,16},{4,20},{8,24},{12,28},{16,0},{20,4},{24,8},{28,12},{1,17},{... | collective-permute-start | bytes 688136 | tf_op jit(solution)/shard_map/ppermute | solution.py:16
  74.9 5.3 %shard_map.66 = f32[2,64,1024]{2,1,0:T(8,128)S(1)} custom-call(bf16[64,1024]{1,0:T(8,128)(2,1)S(1)} %maximum_select_fusion.8.a_ref, bf16[7168,1024]{1,0:T(8,128)(2,1)} %e_ref.11, bf16[2,7168,1024]{2,1,0:T(8,128)(2,1)} %q_ref.11), custom_call_target="tpu_custom_call" | custom-call | flops 536870912 | bytes 6815744 | tf_op jit(solution)/shard_map/pallas_call | solution.py:92
  80.6 1.6 %collective-permute-start.12 = (bf16[64,896]{1,0:T(8,128)(2,1)S(1)}, bf16[64,896]{1,0:T(8,128)(2,1)S(1)}, u32[]{:S(2)}, u32[]{:S(2)}) collective-permute-start(bf16[64,896]{1,0:T(8,128)(2,1)S(1)} %add_convert_fusion), channel_id=1, source_target_pairs={{0,16},{4,20},{8,24},{12,28},{16,0},{20,4},{24,8},{28,12},{1,17},{... | collective-permute-start | bytes 344072 | tf_op jit(solution)/shard_map/ppermute | solution.py:16
  82.2 5.3 %shard_map.67 = f32[2,64,1024]{2,1,0:T(8,128)S(1)} custom-call(bf16[64,1024]{1,0:T(8,128)(2,1)S(1)} %maximum_select_fusion.8.a_ref, bf16[7168,1024]{1,0:T(8,128)(2,1)} %e_ref.11, bf16[2,7168,1024]{2,1,0:T(8,128)(2,1)} %q_ref.11), custom_call_target="tpu_custom_call" | custom-call | flops 536870912 | bytes 6815744 | tf_op jit(solution)/shard_map/pallas_call | solution.py:92
  88.2 7.2 %shard_map.68 = f32[2,64,1536]{2,1,0:T(8,128)S(1)} custom-call(bf16[64,1024]{1,0:T(8,128)(2,1)S(1)} %maximum_select_fusion.8.a_ref, bf16[7168,1024]{1,0:T(8,128)(2,1)} %e_ref.11, bf16[2,7168,1024]{2,1,0:T(8,128)(2,1)} %q_ref.11), custom_call_target="tpu_custom_call" | custom-call | flops 805306368 | bytes 10223616 | tf_op jit(solution)/shard_map/pallas_call | solution.py:92
  95.6 5.5 %shard_map.69 = f32[2,64,1024]{2,1,0:T(8,128)S(1)} custom-call(bf16[64,1024]{1,0:T(8,128)(2,1)S(1)} %maximum_select_fusion.8.a_ref, bf16[7168,1024]{1,0:T(8,128)(2,1)} %e_ref.11, bf16[2,7168,1024]{2,1,0:T(8,128)(2,1)} %q_ref.11), custom_call_target="tpu_custom_call" | custom-call | flops 536870912 | bytes 6815744 | tf_op jit(solution)/shard_map/pallas_call | solution.py:92
  102.4 1.2 %collective-permute-start.15 = (f32[2,64]{1,0:T(2,128)S(1)}, f32[2,64]{1,0:T(2,128)S(1)}, u32[]{:S(2)}, u32[]{:S(2)}) collective-permute-start(f32[2,64]{1,0:T(2,128)S(1)} %add_add_fusion), channel_id=1, source_target_pairs={{0,1},{1,0},{2,3},{3,2},{4,5},{5,4},{6,7},{7,6},{8,9},{9,8},{10,11... | collective-permute-start | bytes 1544 | tf_op jit(solution)/shard_map/ppermute | solution.py:16
  103.6 2.4 %collective-permute-done.15 = f32[2,64]{1,0:T(2,128)S(1)} collective-permute-done((f32[2,64]{1,0:T(2,128)S(1)}, f32[2,64]{1,0:T(2,128)S(1)}, u32[]{:S(2)}, u32[]{:S(2)}) %collective-permute-start.15) | collective-permute-done | bytes 544 | tf_op jit(solution)/shard_map/ppermute | solution.py:16
  106.0 2.1 %collective-permute-start.16 = (f32[2,64]{1,0:T(2,128)S(1)}, f32[2,64]{1,0:T(2,128)S(1)}, u32[]{:S(2)}, u32[]{:S(2)}) collective-permute-start(f32[2,64]{1,0:T(2,128)S(1)} %add.91), channel_id=1, source_target_pairs={{0,2},{1,3},{2,0},{3,1},{4,6},{5,7},{6,4},{7,5},{8,10},{9,11},{10,... | collective-permute-start | bytes 1544 | tf_op jit(solution)/shard_map/ppermute | solution.py:16
  108.1 2.4 %collective-permute-done.16 = f32[2,64]{1,0:T(2,128)S(1)} collective-permute-done((f32[2,64]{1,0:T(2,128)S(1)}, f32[2,64]{1,0:T(2,128)S(1)}, u32[]{:S(2)}, u32[]{:S(2)}) %collective-permute-start.16) | collective-permute-done | bytes 544 | tf_op jit(solution)/shard_map/ppermute | solution.py:16
  110.5 1.1 collective-permute-done.17
  111.6 1.5 %collective-permute-start.18 = (f32[2,64]{1,0:T(2,128)S(1)}, f32[2,64]{1,0:T(2,128)S(1)}, u32[]{:S(2)}, u32[]{:S(2)}) collective-permute-start(f32[2,64]{1,0:T(2,128)S(1)} %add.93), channel_id=1, source_target_pairs={{0,8},{4,12},{8,0},{12,4},{16,24},{20,28},{24,16},{28,20},{1,9},{5... | collective-permute-start | bytes 1544 | tf_op jit(solution)/shard_map/ppermute | solution.py:16
  113.1 2.1 %collective-permute-done.18 = f32[2,64]{1,0:T(2,128)S(1)} collective-permute-done((f32[2,64]{1,0:T(2,128)S(1)}, f32[2,64]{1,0:T(2,128)S(1)}, u32[]{:S(2)}, u32[]{:S(2)}) %collective-permute-start.18) | collective-permute-done | bytes 544 | tf_op jit(solution)/shard_map/ppermute | solution.py:16
  115.9 2.9 %collective-permute-done.19 = f32[2,64]{1,0:T(2,128)S(1)} collective-permute-done((f32[2,64]{1,0:T(2,128)S(1)}, f32[2,64]{1,0:T(2,128)S(1)}, u32[]{:S(2)}, u32[]{:S(2)}) %collective-permute-start.19) | collective-permute-done | bytes 544 | tf_op jit(solution)/shard_map/ppermute | solution.py:16
  (55 shorter events, 8.9 us)
Async XLA Ops:
  0.0 1.5 %collective-permute-start = (bf16[8,2048]{1,0:T(8,128)(2,1)}, bf16[8,2048]{1,0:T(8,128)(2,1)S(1)}, u32[]{:S(2)}, u32[]{:S(2)}) collective-permute-start(bf16[8,2048]{1,0:T(8,128)(2,1)} %param.7), channel_id=1, source_target_pairs={{0,4},{4,0},{8,12},{12,8},{16,20},{20,16},{24,28},{28,24},{1,5},{5... | collective-permute-start | bytes 98312 | tf_op jit(solution)/shard_map/ppermute | solution.py:16
  2.4 5.3 %collective-permute-start.1 = (bf16[16,2048]{1,0:T(8,128)(2,1)S(1)}, bf16[16,2048]{1,0:T(8,128)(2,1)S(1)}, u32[]{:S(2)}, u32[]{:S(2)}) collective-permute-start(bf16[16,2048]{1,0:T(8,128)(2,1)S(1)} %maximum_select_fusion.9), channel_id=1, source_target_pairs={{0,8},{4,12},{8,0},{12,4},{16,24},{20,28},{24,16},{28,20},{1,9},{5... | collective-permute-start | bytes 196616 | tf_op jit(solution)/shard_map/ppermute | solution.py:16
  5.3 5.1 %collective-permute-start.3 = (bf16[16,3584]{1,0:T(8,128)(2,1)}, bf16[16,3584]{1,0:T(8,128)(2,1)S(1)}, u32[]{:S(2)}, u32[]{:S(2)}) collective-permute-start(bf16[16,3584]{1,0:T(8,128)(2,1)} %param.6), channel_id=1, source_target_pairs={{0,1},{1,0},{2,3},{3,2},{4,5},{5,4},{6,7},{7,6},{8,9},{9,8},{10,11... | collective-permute-start | bytes 344072 | tf_op jit(solution)/shard_map/ppermute | solution.py:16
  7.7 6.4 %collective-permute-start.2 = (bf16[32,2048]{1,0:T(8,128)(2,1)S(1)}, bf16[32,2048]{1,0:T(8,128)(2,1)S(1)}, u32[]{:S(2)}, u32[]{:S(2)}) collective-permute-start(bf16[32,2048]{1,0:T(8,128)(2,1)S(1)} %maximum_select_fusion.7), channel_id=1, source_target_pairs={{0,16},{4,20},{8,24},{12,28},{16,0},{20,4},{24,8},{28,12},{1,17},{... | collective-permute-start | bytes 393224 | tf_op jit(solution)/shard_map/ppermute | solution.py:16
  11.4 12.4 %collective-permute-start.4 = (bf16[32,3584]{1,0:T(8,128)(2,1)S(1)}, bf16[32,3584]{1,0:T(8,128)(2,1)S(1)}, u32[]{:S(2)}, u32[]{:S(2)}) collective-permute-start(bf16[32,3584]{1,0:T(8,128)(2,1)S(1)} %maximum_select_fusion.5), channel_id=1, source_target_pairs={{0,2},{1,3},{2,0},{3,1},{4,6},{5,7},{6,4},{7,5},{8,10},{9,11},{10,... | collective-permute-start | bytes 688136 | tf_op jit(solution)/shard_map/ppermute | solution.py:16
  23.9 6.7 %collective-permute-start.5 = (f32[64,512]{1,0:T(8,128)S(1)}, f32[64,512]{1,0:T(8,128)S(1)}, u32[]{:S(2)}, u32[]{:S(2)}) collective-permute-start(f32[64,512]{1,0:T(8,128)S(1)} %slice_select_fusion.2), channel_id=1, source_target_pairs={{0,1},{1,0},{2,3},{3,2},{4,5},{5,4},{6,7},{7,6},{8,9},{9,8},{10,11... | collective-permute-start | bytes 393224 | tf_op jit(solution)/shard_map/ppermute | solution.py:16
  30.7 9.4 %collective-permute-start.6 = (f32[64,256]{1,0:T(8,128)S(1)}, f32[64,256]{1,0:T(8,128)S(1)}, u32[]{:S(2)}, u32[]{:S(2)}) collective-permute-start(f32[64,256]{1,0:T(8,128)S(1)} %slice_select_fusion.3), channel_id=1, source_target_pairs={{0,2},{1,3},{2,0},{3,1},{4,6},{5,7},{6,4},{7,5},{8,10},{9,11},{10,... | collective-permute-start | bytes 196616 | tf_op jit(solution)/shard_map/ppermute | solution.py:16
  40.2 6.1 %collective-permute-start.7 = (bf16[64,256]{1,0:T(8,128)(2,1)S(1)}, bf16[64,256]{1,0:T(8,128)(2,1)S(1)}, u32[]{:S(2)}, u32[]{:S(2)}) collective-permute-start(bf16[64,256]{1,0:T(8,128)(2,1)S(1)} %add_convert_fusion.1), channel_id=1, source_target_pairs={{0,2},{1,3},{2,0},{3,1},{4,6},{5,7},{6,4},{7,5},{8,10},{9,11},{10,... | collective-permute-start | bytes 98312 | tf_op jit(solution)/shard_map/ppermute | solution.py:16
  46.3 6.9 %collective-permute-start.8 = (bf16[64,512]{1,0:T(8,128)(2,1)S(1)}, bf16[64,512]{1,0:T(8,128)(2,1)S(1)}, u32[]{:S(2)}, u32[]{:S(2)}) collective-permute-start(bf16[64,512]{1,0:T(8,128)(2,1)S(1)} %maximum_select_fusion.10), channel_id=1, source_target_pairs={{0,1},{1,0},{2,3},{3,2},{4,5},{5,4},{6,7},{7,6},{8,9},{9,8},{10,11... | collective-permute-start | bytes 196616 | tf_op jit(solution)/shard_map/ppermute | solution.py:16
  53.5 5.4 %collective-permute-start.9 = (f32[64,3584]{1,0:T(8,128)S(1)}, f32[64,3584]{1,0:T(8,128)}, u32[]{:S(2)}, u32[]{:S(2)}) collective-permute-start(f32[64,3584]{1,0:T(8,128)S(1)} %broadcast_select_fusion), channel_id=1, source_target_pairs={{0,4},{4,0},{8,12},{12,8},{16,20},{20,16},{24,28},{28,24},{1,5},{5... | collective-permute-start | bytes 2752520 | tf_op jit(solution)/shard_map/ppermute | solution.py:16
  60.3 13.0 %collective-permute-start.10 = (f32[64,1792]{1,0:T(8,128)S(1)}, f32[64,1792]{1,0:T(8,128)S(1)}, u32[]{:S(2)}, u32[]{:S(2)}) collective-permute-start(f32[64,1792]{1,0:T(8,128)S(1)} %slice_select_fusion), channel_id=1, source_target_pairs={{0,8},{4,12},{8,0},{12,4},{16,24},{20,28},{24,16},{28,20},{1,9},{5... | collective-permute-start | bytes 1376264 | tf_op jit(solution)/shard_map/ppermute | solution.py:16
  73.3 7.3 %collective-permute-start.11 = (f32[64,896]{1,0:T(8,128)S(1)}, f32[64,896]{1,0:T(8,128)S(1)}, u32[]{:S(2)}, u32[]{:S(2)}) collective-permute-start(f32[64,896]{1,0:T(8,128)S(1)} %slice_select_fusion.1), channel_id=1, source_target_pairs={{0,16},{4,20},{8,24},{12,28},{16,0},{20,4},{24,8},{28,12},{1,17},{... | collective-permute-start | bytes 688136 | tf_op jit(solution)/shard_map/ppermute | solution.py:16
  80.6 6.9 %collective-permute-start.12 = (bf16[64,896]{1,0:T(8,128)(2,1)S(1)}, bf16[64,896]{1,0:T(8,128)(2,1)S(1)}, u32[]{:S(2)}, u32[]{:S(2)}) collective-permute-start(bf16[64,896]{1,0:T(8,128)(2,1)S(1)} %add_convert_fusion), channel_id=1, source_target_pairs={{0,16},{4,20},{8,24},{12,28},{16,0},{20,4},{24,8},{28,12},{1,17},{... | collective-permute-start | bytes 344072 | tf_op jit(solution)/shard_map/ppermute | solution.py:16
  87.6 7.8 %collective-permute-start.13 = (bf16[64,1792]{1,0:T(8,128)(2,1)S(1)}, bf16[64,1792]{1,0:T(8,128)(2,1)S(1)}, u32[]{:S(2)}, u32[]{:S(2)}) collective-permute-start(bf16[64,1792]{1,0:T(8,128)(2,1)S(1)} %maximum_select_fusion.6), channel_id=1, source_target_pairs={{0,8},{4,12},{8,0},{12,4},{16,24},{20,28},{24,16},{28,20},{1,9},{5... | collective-permute-start | bytes 688136 | tf_op jit(solution)/shard_map/ppermute | solution.py:16
  95.6 5.6 %collective-permute-start.14 = (bf16[64,3584]{1,0:T(8,128)(2,1)S(1)}, bf16[64,3584]{1,0:T(8,128)(2,1)S(1)}, u32[]{:S(2)}, u32[]{:S(2)}) collective-permute-start(bf16[64,3584]{1,0:T(8,128)(2,1)S(1)} %maximum_select_fusion.2), channel_id=1, source_target_pairs={{0,4},{4,0},{8,12},{12,8},{16,20},{20,16},{24,28},{28,24},{1,5},{5... | collective-permute-start | bytes 1376264 | tf_op jit(solution)/shard_map/ppermute | solution.py:16
  102.4 3.6 %collective-permute-start.15 = (f32[2,64]{1,0:T(2,128)S(1)}, f32[2,64]{1,0:T(2,128)S(1)}, u32[]{:S(2)}, u32[]{:S(2)}) collective-permute-start(f32[2,64]{1,0:T(2,128)S(1)} %add_add_fusion), channel_id=1, source_target_pairs={{0,1},{1,0},{2,3},{3,2},{4,5},{5,4},{6,7},{7,6},{8,9},{9,8},{10,11... | collective-permute-start | bytes 1544 | tf_op jit(solution)/shard_map/ppermute | solution.py:16
  106.0 4.5 %collective-permute-start.16 = (f32[2,64]{1,0:T(2,128)S(1)}, f32[2,64]{1,0:T(2,128)S(1)}, u32[]{:S(2)}, u32[]{:S(2)}) collective-permute-start(f32[2,64]{1,0:T(2,128)S(1)} %add.91), channel_id=1, source_target_pairs={{0,2},{1,3},{2,0},{3,1},{4,6},{5,7},{6,4},{7,5},{8,10},{9,11},{10,... | collective-permute-start | bytes 1544 | tf_op jit(solution)/shard_map/ppermute | solution.py:16
  110.5 1.1 collective-permute-start.17
  111.6 3.6 %collective-permute-start.18 = (f32[2,64]{1,0:T(2,128)S(1)}, f32[2,64]{1,0:T(2,128)S(1)}, u32[]{:S(2)}, u32[]{:S(2)}) collective-permute-start(f32[2,64]{1,0:T(2,128)S(1)} %add.93), channel_id=1, source_target_pairs={{0,8},{4,12},{8,0},{12,4},{16,24},{20,28},{24,16},{28,20},{1,9},{5... | collective-permute-start | bytes 1544 | tf_op jit(solution)/shard_map/ppermute | solution.py:16
  115.2 3.6 %collective-permute-start.19 = (f32[2,64]{1,0:T(2,128)S(1)}, f32[2,64]{1,0:T(2,128)S(1)}, u32[]{:S(2)}, u32[]{:S(2)}) collective-permute-start(f32[2,64]{1,0:T(2,128)S(1)} %add.94), channel_id=1, source_target_pairs={{0,16},{4,20},{8,24},{12,28},{16,0},{20,4},{24,8},{28,12},{1,17},{... | collective-permute-start | bytes 1544 | tf_op jit(solution)/shard_map/ppermute | solution.py:16

commit v5 on v4

--- a/solution.py
+++ b/solution.py
@@ -36,6 +36,8 @@
         if not works:
             return _swap(v, axis, n, b)
         work, arg = works.pop(0)
+        if work is None:
+            return _swap(v, axis, n, b)
         v, arg = lax.optimization_barrier((v, arg))
         result = work(arg)
         other = _swap(v, axis, n, b)
@@ -60,7 +62,7 @@
         first = (me // b) % 2 == 0
         x = jnp.where(first, jnp.concatenate([x, other], dim), jnp.concatenate([other, x], dim))
         b //= 2
-    done += [work(arg) for work, arg in works]
+    done += [work(arg) for work, arg in works if work is not None]
     return x, done
 
 
@@ -114,10 +116,11 @@
     acts_all = _gather(in_acts, "row", nr, 0)
     grads_all = _gather(out_grads, "col", nc, 0)
     act_part = jnp.dot(acts_all, in_basis, preferred_element_type=F32)
-    kg = out_basis.shape[1] // ng
-    grad_works = [
-        (functools.partial(lambda g, c: jnp.dot(g, out_basis[:, c * kg : (c + 1) * kg], preferred_element_type=F32), c=c), grads_all)
-        for c in range(ng)
+    nb = out_basis.shape[1] // 128
+    cuts = [128 * round(i * nb / ng) for i in range(ng + 1)]
+    grad_works = [(None, None)] + [
+        (functools.partial(lambda g, c0, c1: jnp.dot(g, out_basis[:, c0:c1], preferred_element_type=F32), c0=c0, c1=c1), grads_all)
+        for c0, c1 in zip(cuts[:-1], cuts[1:])
     ]
     act_rot, grad_parts = _allreduce_bf16(act_part, "col", nc, 1, grad_works)
     grad_part = jnp.concatenate(grad_parts, axis=1)
@@ -148,5 +151,5 @@
         P("col", "row"),
         P(None, "col", "row"),
     )
-    fn = functools.partial(local, nr=mesh.shape["row"], nc=mesh.shape["col"], nl=6, ng=4)
+    fn = functools.partial(local, nr=mesh.shape["row"], nc=mesh.shape["col"], nl=6, ng=3)
     return jax.shard_map(fn, mesh=mesh, in_specs=in_specs, out_specs=P(), check_vma=False)

time: 120 us -> 119 us (level)
    dot_general x4 -> x3, matrix products: 23.9 us -> 23.1 us  [local(): jnp.dot(g, out_basis[:, c0:c1], preferred_element_type=F32)]
  transfers between devices with their start and end apart: 20 -> 20, of which waited for: 11 -> 12; matrix products, arithmetic and copies ran while one was open for 23% -> 23% of each run, Pallas kernels for 30% -> 30%
where the time goes in v5:
time: 119 us
  Pallas kernels  35.8 us (30%)
  matrix products  26.1 us (22%)
  starting transfers between devices  25.9 us (22%)
  waiting for transfers between devices  25.2 us (21%)
  other arithmetic  5.36 us (5%)
    pallas_call x6, Pallas kernels, _lifted(): pl.pallas_call(_lifted_kernel, grid=(t1 - t0,), in_specs=[pl.BlockSpec((t...  35.8 us
    ppermute x20, starting transfers between devices, _swap(): return lax.ppermute(x, axis, [(i, i ^ b) for i in range(n)])  25.9 us
    ppermute x20, waiting for transfers between devices, _swap(): return lax.ppermute(x, axis, [(i, i ^ b) for i in range(n)])  25.2 us
    dot_general x3, matrix products, local(): jnp.dot(g, out_basis[:, c0:c1], preferred_element_type=F32)  23.1 us
    dot_general x1, matrix products, local(): act_part = jnp.dot(acts_all, in_basis, preferred_element_type=F32)  3.03 us
  transfers between devices with their start and end apart: 20, of which 12 were waited for; matrix products, arithmetic and copies ran while one was open for 23% of the time, Pallas kernels for 30%

profile of v5, /device:TPU:0, one launch (start us, length us, event | category | flops | bytes accessed | tf_op | source)
XLA Modules:
  0.0 118.7 jit_solution(1102263874961670427)
XLA Ops:
  0.5 1.1 collective-permute-done
  2.4 2.9 %collective-permute-start.1 = (bf16[16,2048]{1,0:T(8,128)(2,1)S(1)}, bf16[16,2048]{1,0:T(8,128)(2,1)S(1)}, u32[]{:S(2)}, u32[]{:S(2)}) collective-permute-start(bf16[16,2048]{1,0:T(8,128)(2,1)S(1)} %maximum_select_fusion.9), channel_id=1, source_target_pairs={{0,8},{4,12},{8,0},{12,4},{16,24},{20,28},{24,16},{28,20},{1,9},{5... | collective-permute-start | bytes 196616 | tf_op jit(solution)/shard_map/ppermute | solution.py:16
  5.3 1.6 %collective-permute-start.4 = (bf16[16,3584]{1,0:T(8,128)(2,1)}, bf16[16,3584]{1,0:T(8,128)(2,1)S(1)}, u32[]{:S(2)}, u32[]{:S(2)}) collective-permute-start(bf16[16,3584]{1,0:T(8,128)(2,1)} %param.6), channel_id=1, source_target_pairs={{0,1},{1,0},{2,3},{3,2},{4,5},{5,4},{6,7},{7,6},{8,9},{9,8},{10,11... | collective-permute-start | bytes 344072 | tf_op jit(solution)/shard_map/ppermute | solution.py:16
  7.7 1.9 %collective-permute-start.2 = (bf16[32,2048]{1,0:T(8,128)(2,1)S(1)}, bf16[32,2048]{1,0:T(8,128)(2,1)S(1)}, u32[]{:S(2)}, u32[]{:S(2)}) collective-permute-start(bf16[32,2048]{1,0:T(8,128)(2,1)S(1)} %maximum_select_fusion.7), channel_id=1, source_target_pairs={{0,16},{4,20},{8,24},{12,28},{16,0},{20,4},{24,8},{28,12},{1,17},{... | collective-permute-start | bytes 393224 | tf_op jit(solution)/shard_map/ppermute | solution.py:16
  11.4 2.7 %collective-permute-start.5 = (bf16[32,3584]{1,0:T(8,128)(2,1)S(1)}, bf16[32,3584]{1,0:T(8,128)(2,1)S(1)}, u32[]{:S(2)}, u32[]{:S(2)}) collective-permute-start(bf16[32,3584]{1,0:T(8,128)(2,1)S(1)} %maximum_select_fusion.5), channel_id=1, source_target_pairs={{0,2},{1,3},{2,0},{3,1},{4,6},{5,7},{6,4},{7,5},{8,10},{9,11},{10,... | collective-permute-start | bytes 688136 | tf_op jit(solution)/shard_map/ppermute | solution.py:16
  14.1 3.0 %fusion.7 = f32[64,1024]{1,0:T(8,128)S(1)} fusion(bf16[2048,1024]{1,0:T(8,128)(2,1)} %param.9, bf16[32,2048]{1,0:T(8,128)(2,1)S(1)} %collective-permute-done.2, bf16[32,2048]{1,0:T(8,128)(2,1)S(1)} %maximum_select_fusion.7, pred[]{:T(512)S(6)} %eq.54), kind=kOutput, calls=%fused_computation.22 | convolution fusion | flops 269615104 | bytes 4718593 | tf_op jit(solution)/shard_map/dot_general | solution.py:118
  17.2 1.6 %collective-permute-start.3 = (f32[64,512]{1,0:T(8,128)S(1)}, f32[64,512]{1,0:T(8,128)S(1)}, u32[]{:S(2)}, u32[]{:S(2)}) collective-permute-start(f32[64,512]{1,0:T(8,128)S(1)} %slice_select_fusion.2), channel_id=1, source_target_pairs={{0,1},{1,0},{2,3},{3,2},{4,5},{5,4},{6,7},{7,6},{8,9},{9,8},{10,11... | collective-permute-start | bytes 393224 | tf_op jit(solution)/shard_map/ppermute | solution.py:16
  18.8 5.1 %collective-permute-done.5 = bf16[32,3584]{1,0:T(8,128)(2,1)S(1)} collective-permute-done((bf16[32,3584]{1,0:T(8,128)(2,1)S(1)}, bf16[32,3584]{1,0:T(8,128)(2,1)S(1)}, u32[]{:S(2)}, u32[]{:S(2)}) %collective-permute-start.5) | collective-permute-done | bytes 229408 | tf_op jit(solution)/shard_map/ppermute | solution.py:16
  24.0 1.1 collective-permute-done.3
  25.2 1.7 %collective-permute-start.6 = (f32[64,256]{1,0:T(8,128)S(1)}, f32[64,256]{1,0:T(8,128)S(1)}, u32[]{:S(2)}, u32[]{:S(2)}) collective-permute-start(f32[64,256]{1,0:T(8,128)S(1)} %slice_select_fusion.3), channel_id=1, source_target_pairs={{0,2},{1,3},{2,0},{3,1},{4,6},{5,7},{6,4},{7,5},{8,10},{9,11},{10,... | collective-permute-start | bytes 196616 | tf_op jit(solution)/shard_map/ppermute | solution.py:16
  26.9 8.0 %fusion.2 = f32[64,2432]{1,0:T(8,128)S(1)} fusion(bf16[64,3584]{1,0:T(8,128)(2,1)S(1)} %maximum_select_fusion.1, bf16[3584,7168]{1,0:T(8,128)(2,1)} %param.8), kind=kOutput, calls=%fused_computation.2 | convolution fusion | flops 1115684864 | bytes 18513920 | tf_op jit(solution)/shard_map/dot_general | solution.py:122
  34.9 1.3 %collective-permute-start.7 = (bf16[64,256]{1,0:T(8,128)(2,1)S(1)}, bf16[64,256]{1,0:T(8,128)(2,1)S(1)}, u32[]{:S(2)}, u32[]{:S(2)}) collective-permute-start(bf16[64,256]{1,0:T(8,128)(2,1)S(1)} %add_convert_fusion.1), channel_id=1, source_target_pairs={{0,2},{1,3},{2,0},{3,1},{4,6},{5,7},{6,4},{7,5},{8,10},{9,11},{10,... | collective-permute-start | bytes 98312 | tf_op jit(solution)/shard_map/ppermute | solution.py:16
  36.3 7.3 %fusion.4 = f32[64,2304]{1,0:T(8,128)S(1)} fusion(bf16[64,3584]{1,0:T(8,128)(2,1)S(1)} %maximum_select_fusion.1, bf16[3584,7168]{1,0:T(8,128)(2,1)} %param.8), kind=kOutput, calls=%fused_computation.4 | convolution fusion | flops 1056964608 | bytes 17563648 | tf_op jit(solution)/shard_map/dot_general | solution.py:122
  43.7 1.3 %collective-permute-start.8 = (bf16[64,512]{1,0:T(8,128)(2,1)S(1)}, bf16[64,512]{1,0:T(8,128)(2,1)S(1)}, u32[]{:S(2)}, u32[]{:S(2)}) collective-permute-start(bf16[64,512]{1,0:T(8,128)(2,1)S(1)} %maximum_select_fusion.10), channel_id=1, source_target_pairs={{0,1},{1,0},{2,3},{3,2},{4,5},{5,4},{6,7},{7,6},{8,9},{9,8},{10,11... | collective-permute-start | bytes 196616 | tf_op jit(solution)/shard_map/ppermute | solution.py:16
  45.0 7.8 %fusion = f32[64,2432]{1,0:T(8,128)S(1)} fusion(bf16[64,3584]{1,0:T(8,128)(2,1)S(1)} %maximum_select_fusion.1, bf16[3584,7168]{1,0:T(8,128)(2,1)} %param.8), kind=kOutput, calls=%fused_computation | convolution fusion | flops 1115684864 | bytes 18513920 | tf_op jit(solution)/shard_map/dot_general | solution.py:122
  53.0 5.3 %shard_map.64 = f32[2,64,1024]{2,1,0:T(8,128)S(1)} custom-call(bf16[64,1024]{1,0:T(8,128)(2,1)S(1)} %maximum_select_fusion.8.a_ref, bf16[7168,1024]{1,0:T(8,128)(2,1)} %e_ref.11, bf16[2,7168,1024]{2,1,0:T(8,128)(2,1)} %q_ref.11), custom_call_target="tpu_custom_call" | custom-call | flops 536870912 | bytes 6815744 | tf_op jit(solution)/shard_map/pallas_call | solution.py:94
  58.3 1.3 %select_add_fusion = f32[64,3584]{1,0:T(8,128)S(1)} fusion(f32[64,3584]{1,0:T(8,128)} %collective-permute-done.9, f32[64,2304]{1,0:T(8,128)S(1)} %fusion.4, f32[64,2432]{1,0:T(8,128)S(1)} %fusion.2, f32[64,2432]{1,0:T(8,128)S(1)} %fusion, pred[]{:T(512)S(6)} %eq.51), kind=kLoop, calls=%fused_computation.9 | loop fusion | flops 917504 | bytes 3670017 | tf_op jit(solution)/shard_map/add | solution.py:56
  60.5 7.2 %shard_map.65 = f32[2,64,1536]{2,1,0:T(8,128)S(1)} custom-call(bf16[64,1024]{1,0:T(8,128)(2,1)S(1)} %maximum_select_fusion.8.a_ref, bf16[7168,1024]{1,0:T(8,128)(2,1)} %e_ref.11, bf16[2,7168,1024]{2,1,0:T(8,128)(2,1)} %q_ref.11), custom_call_target="tpu_custom_call" | custom-call | flops 805306368 | bytes 10223616 | tf_op jit(solution)/shard_map/pallas_call | solution.py:94
  67.7 5.0 %collective-permute-done.10 = f32[64,1792]{1,0:T(8,128)S(1)} collective-permute-done((f32[64,1792]{1,0:T(8,128)S(1)}, f32[64,1792]{1,0:T(8,128)S(1)}, u32[]{:S(2)}, u32[]{:S(2)}) %collective-permute-start.10) | collective-permute-done | bytes 458784 | tf_op jit(solution)/shard_map/ppermute | solution.py:16
  72.8 1.6 %collective-permute-start.11 = (f32[64,896]{1,0:T(8,128)S(1)}, f32[64,896]{1,0:T(8,128)S(1)}, u32[]{:S(2)}, u32[]{:S(2)}) collective-permute-start(f32[64,896]{1,0:T(8,128)S(1)} %slice_select_fusion.1), channel_id=1, source_target_pairs={{0,16},{4,20},{8,24},{12,28},{16,0},{20,4},{24,8},{28,12},{1,17},{... | collective-permute-start | bytes 688136 | tf_op jit(solution)/shard_map/ppermute | solution.py:16
  74.4 5.3 %shard_map.66 = f32[2,64,1024]{2,1,0:T(8,128)S(1)} custom-call(bf16[64,1024]{1,0:T(8,128)(2,1)S(1)} %maximum_select_fusion.8.a_ref, bf16[7168,1024]{1,0:T(8,128)(2,1)} %e_ref.11, bf16[2,7168,1024]{2,1,0:T(8,128)(2,1)} %q_ref.11), custom_call_target="tpu_custom_call" | custom-call | flops 536870912 | bytes 6815744 | tf_op jit(solution)/shard_map/pallas_call | solution.py:94
  80.1 1.6 %collective-permute-start.12 = (bf16[64,896]{1,0:T(8,128)(2,1)S(1)}, bf16[64,896]{1,0:T(8,128)(2,1)S(1)}, u32[]{:S(2)}, u32[]{:S(2)}) collective-permute-start(bf16[64,896]{1,0:T(8,128)(2,1)S(1)} %add_convert_fusion), channel_id=1, source_target_pairs={{0,16},{4,20},{8,24},{12,28},{16,0},{20,4},{24,8},{28,12},{1,17},{... | collective-permute-start | bytes 344072 | tf_op jit(solution)/shard_map/ppermute | solution.py:16
  81.7 5.3 %shard_map.67 = f32[2,64,1024]{2,1,0:T(8,128)S(1)} custom-call(bf16[64,1024]{1,0:T(8,128)(2,1)S(1)} %maximum_select_fusion.8.a_ref, bf16[7168,1024]{1,0:T(8,128)(2,1)} %e_ref.11, bf16[2,7168,1024]{2,1,0:T(8,128)(2,1)} %q_ref.11), custom_call_target="tpu_custom_call" | custom-call | flops 536870912 | bytes 6815744 | tf_op jit(solution)/shard_map/pallas_call | solution.py:94
  87.8 7.2 %shard_map.68 = f32[2,64,1536]{2,1,0:T(8,128)S(1)} custom-call(bf16[64,1024]{1,0:T(8,128)(2,1)S(1)} %maximum_select_fusion.8.a_ref, bf16[7168,1024]{1,0:T(8,128)(2,1)} %e_ref.11, bf16[2,7168,1024]{2,1,0:T(8,128)(2,1)} %q_ref.11), custom_call_target="tpu_custom_call" | custom-call | flops 805306368 | bytes 10223616 | tf_op jit(solution)/shard_map/pallas_call | solution.py:94
  95.2 5.5 %shard_map.69 = f32[2,64,1024]{2,1,0:T(8,128)S(1)} custom-call(bf16[64,1024]{1,0:T(8,128)(2,1)S(1)} %maximum_select_fusion.8.a_ref, bf16[7168,1024]{1,0:T(8,128)(2,1)} %e_ref.11, bf16[2,7168,1024]{2,1,0:T(8,128)(2,1)} %q_ref.11), custom_call_target="tpu_custom_call" | custom-call | flops 536870912 | bytes 6815744 | tf_op jit(solution)/shard_map/pallas_call | solution.py:94
  102.5 2.8 %collective-permute-done.15 = f32[2,64]{1,0:T(2,128)S(1)} collective-permute-done((f32[2,64]{1,0:T(2,128)S(1)}, f32[2,64]{1,0:T(2,128)S(1)}, u32[]{:S(2)}, u32[]{:S(2)}) %collective-permute-start.15) | collective-permute-done | bytes 544 | tf_op jit(solution)/shard_map/ppermute | solution.py:16
  105.3 2.9 %collective-permute-start.16 = (f32[2,64]{1,0:T(2,128)S(1)}, f32[2,64]{1,0:T(2,128)S(1)}, u32[]{:S(2)}, u32[]{:S(2)}) collective-permute-start(f32[2,64]{1,0:T(2,128)S(1)} %add.91), channel_id=1, source_target_pairs={{0,2},{1,3},{2,0},{3,1},{4,6},{5,7},{6,4},{7,5},{8,10},{9,11},{10,... | collective-permute-start | bytes 1544 | tf_op jit(solution)/shard_map/ppermute | solution.py:16
  108.2 1.6 %collective-permute-done.16 = f32[2,64]{1,0:T(2,128)S(1)} collective-permute-done((f32[2,64]{1,0:T(2,128)S(1)}, f32[2,64]{1,0:T(2,128)S(1)}, u32[]{:S(2)}, u32[]{:S(2)}) %collective-permute-start.16) | collective-permute-done | bytes 544 | tf_op jit(solution)/shard_map/ppermute | solution.py:16
  109.8 1.1 collective-permute-done.17
  110.9 1.3 %collective-permute-start.18 = (f32[2,64]{1,0:T(2,128)S(1)}, f32[2,64]{1,0:T(2,128)S(1)}, u32[]{:S(2)}, u32[]{:S(2)}) collective-permute-start(f32[2,64]{1,0:T(2,128)S(1)} %add.93), channel_id=1, source_target_pairs={{0,8},{4,12},{8,0},{12,4},{16,24},{20,28},{24,16},{28,20},{1,9},{5... | collective-permute-start | bytes 1544 | tf_op jit(solution)/shard_map/ppermute | solution.py:16
  112.3 2.2 %collective-permute-done.18 = f32[2,64]{1,0:T(2,128)S(1)} collective-permute-done((f32[2,64]{1,0:T(2,128)S(1)}, f32[2,64]{1,0:T(2,128)S(1)}, u32[]{:S(2)}, u32[]{:S(2)}) %collective-permute-start.18) | collective-permute-done | bytes 544 | tf_op jit(solution)/shard_map/ppermute | solution.py:16
  115.0 3.1 %collective-permute-done.19 = f32[2,64]{1,0:T(2,128)S(1)} collective-permute-done((f32[2,64]{1,0:T(2,128)S(1)}, f32[2,64]{1,0:T(2,128)S(1)}, u32[]{:S(2)}, u32[]{:S(2)}) %collective-permute-start.19) | collective-permute-done | bytes 544 | tf_op jit(solution)/shard_map/ppermute | solution.py:16
  (48 shorter events, 9.4 us)
Async XLA Ops:
  0.0 1.5 %collective-permute-start = (bf16[8,2048]{1,0:T(8,128)(2,1)}, bf16[8,2048]{1,0:T(8,128)(2,1)S(1)}, u32[]{:S(2)}, u32[]{:S(2)}) collective-permute-start(bf16[8,2048]{1,0:T(8,128)(2,1)} %param.7), channel_id=1, source_target_pairs={{0,4},{4,0},{8,12},{12,8},{16,20},{20,16},{24,28},{28,24},{1,5},{5... | collective-permute-start | bytes 98312 | tf_op jit(solution)/shard_map/ppermute | solution.py:16
  2.4 5.3 %collective-permute-start.1 = (bf16[16,2048]{1,0:T(8,128)(2,1)S(1)}, bf16[16,2048]{1,0:T(8,128)(2,1)S(1)}, u32[]{:S(2)}, u32[]{:S(2)}) collective-permute-start(bf16[16,2048]{1,0:T(8,128)(2,1)S(1)} %maximum_select_fusion.9), channel_id=1, source_target_pairs={{0,8},{4,12},{8,0},{12,4},{16,24},{20,28},{24,16},{28,20},{1,9},{5... | collective-permute-start | bytes 196616 | tf_op jit(solution)/shard_map/ppermute | solution.py:16
  5.3 5.1 %collective-permute-start.4 = (bf16[16,3584]{1,0:T(8,128)(2,1)}, bf16[16,3584]{1,0:T(8,128)(2,1)S(1)}, u32[]{:S(2)}, u32[]{:S(2)}) collective-permute-start(bf16[16,3584]{1,0:T(8,128)(2,1)} %param.6), channel_id=1, source_target_pairs={{0,1},{1,0},{2,3},{3,2},{4,5},{5,4},{6,7},{7,6},{8,9},{9,8},{10,11... | collective-permute-start | bytes 344072 | tf_op jit(solution)/shard_map/ppermute | solution.py:16
  7.7 6.4 %collective-permute-start.2 = (bf16[32,2048]{1,0:T(8,128)(2,1)S(1)}, bf16[32,2048]{1,0:T(8,128)(2,1)S(1)}, u32[]{:S(2)}, u32[]{:S(2)}) collective-permute-start(bf16[32,2048]{1,0:T(8,128)(2,1)S(1)} %maximum_select_fusion.7), channel_id=1, source_target_pairs={{0,16},{4,20},{8,24},{12,28},{16,0},{20,4},{24,8},{28,12},{1,17},{... | collective-permute-start | bytes 393224 | tf_op jit(solution)/shard_map/ppermute | solution.py:16
  11.4 12.5 %collective-permute-start.5 = (bf16[32,3584]{1,0:T(8,128)(2,1)S(1)}, bf16[32,3584]{1,0:T(8,128)(2,1)S(1)}, u32[]{:S(2)}, u32[]{:S(2)}) collective-permute-start(bf16[32,3584]{1,0:T(8,128)(2,1)S(1)} %maximum_select_fusion.5), channel_id=1, source_target_pairs={{0,2},{1,3},{2,0},{3,1},{4,6},{5,7},{6,4},{7,5},{8,10},{9,11},{10,... | collective-permute-start | bytes 688136 | tf_op jit(solution)/shard_map/ppermute | solution.py:16
  17.2 8.0 %collective-permute-start.3 = (f32[64,512]{1,0:T(8,128)S(1)}, f32[64,512]{1,0:T(8,128)S(1)}, u32[]{:S(2)}, u32[]{:S(2)}) collective-permute-start(f32[64,512]{1,0:T(8,128)S(1)} %slice_select_fusion.2), channel_id=1, source_target_pairs={{0,1},{1,0},{2,3},{3,2},{4,5},{5,4},{6,7},{7,6},{8,9},{9,8},{10,11... | collective-permute-start | bytes 393224 | tf_op jit(solution)/shard_map/ppermute | solution.py:16
  25.2 9.7 %collective-permute-start.6 = (f32[64,256]{1,0:T(8,128)S(1)}, f32[64,256]{1,0:T(8,128)S(1)}, u32[]{:S(2)}, u32[]{:S(2)}) collective-permute-start(f32[64,256]{1,0:T(8,128)S(1)} %slice_select_fusion.3), channel_id=1, source_target_pairs={{0,2},{1,3},{2,0},{3,1},{4,6},{5,7},{6,4},{7,5},{8,10},{9,11},{10,... | collective-permute-start | bytes 196616 | tf_op jit(solution)/shard_map/ppermute | solution.py:16
  34.9 8.7 %collective-permute-start.7 = (bf16[64,256]{1,0:T(8,128)(2,1)S(1)}, bf16[64,256]{1,0:T(8,128)(2,1)S(1)}, u32[]{:S(2)}, u32[]{:S(2)}) collective-permute-start(bf16[64,256]{1,0:T(8,128)(2,1)S(1)} %add_convert_fusion.1), channel_id=1, source_target_pairs={{0,2},{1,3},{2,0},{3,1},{4,6},{5,7},{6,4},{7,5},{8,10},{9,11},{10,... | collective-permute-start | bytes 98312 | tf_op jit(solution)/shard_map/ppermute | solution.py:16
  43.7 9.1 %collective-permute-start.8 = (bf16[64,512]{1,0:T(8,128)(2,1)S(1)}, bf16[64,512]{1,0:T(8,128)(2,1)S(1)}, u32[]{:S(2)}, u32[]{:S(2)}) collective-permute-start(bf16[64,512]{1,0:T(8,128)(2,1)S(1)} %maximum_select_fusion.10), channel_id=1, source_target_pairs={{0,1},{1,0},{2,3},{3,2},{4,5},{5,4},{6,7},{7,6},{8,9},{9,8},{10,11... | collective-permute-start | bytes 196616 | tf_op jit(solution)/shard_map/ppermute | solution.py:16
  52.9 5.4 %collective-permute-start.9 = (f32[64,3584]{1,0:T(8,128)S(1)}, f32[64,3584]{1,0:T(8,128)}, u32[]{:S(2)}, u32[]{:S(2)}) collective-permute-start(f32[64,3584]{1,0:T(8,128)S(1)} %fusion.6), channel_id=1, source_target_pairs={{0,4},{4,0},{8,12},{12,8},{16,20},{20,16},{24,28},{28,24},{1,5},{5... | collective-permute-start | bytes 2752520 | tf_op jit(solution)/shard_map/ppermute | solution.py:16
  59.7 13.0 %collective-permute-start.10 = (f32[64,1792]{1,0:T(8,128)S(1)}, f32[64,1792]{1,0:T(8,128)S(1)}, u32[]{:S(2)}, u32[]{:S(2)}) collective-permute-start(f32[64,1792]{1,0:T(8,128)S(1)} %slice_select_fusion), channel_id=1, source_target_pairs={{0,8},{4,12},{8,0},{12,4},{16,24},{20,28},{24,16},{28,20},{1,9},{5... | collective-permute-start | bytes 1376264 | tf_op jit(solution)/shard_map/ppermute | solution.py:16
  72.8 7.3 %collective-permute-start.11 = (f32[64,896]{1,0:T(8,128)S(1)}, f32[64,896]{1,0:T(8,128)S(1)}, u32[]{:S(2)}, u32[]{:S(2)}) collective-permute-start(f32[64,896]{1,0:T(8,128)S(1)} %slice_select_fusion.1), channel_id=1, source_target_pairs={{0,16},{4,20},{8,24},{12,28},{16,0},{20,4},{24,8},{28,12},{1,17},{... | collective-permute-start | bytes 688136 | tf_op jit(solution)/shard_map/ppermute | solution.py:16
  80.1 6.9 %collective-permute-start.12 = (bf16[64,896]{1,0:T(8,128)(2,1)S(1)}, bf16[64,896]{1,0:T(8,128)(2,1)S(1)}, u32[]{:S(2)}, u32[]{:S(2)}) collective-permute-start(bf16[64,896]{1,0:T(8,128)(2,1)S(1)} %add_convert_fusion), channel_id=1, source_target_pairs={{0,16},{4,20},{8,24},{12,28},{16,0},{20,4},{24,8},{28,12},{1,17},{... | collective-permute-start | bytes 344072 | tf_op jit(solution)/shard_map/ppermute | solution.py:16
  87.0 8.0 %collective-permute-start.13 = (bf16[64,1792]{1,0:T(8,128)(2,1)S(1)}, bf16[64,1792]{1,0:T(8,128)(2,1)S(1)}, u32[]{:S(2)}, u32[]{:S(2)}) collective-permute-start(bf16[64,1792]{1,0:T(8,128)(2,1)S(1)} %maximum_select_fusion.6), channel_id=1, source_target_pairs={{0,8},{4,12},{8,0},{12,4},{16,24},{20,28},{24,16},{28,20},{1,9},{5... | collective-permute-start | bytes 688136 | tf_op jit(solution)/shard_map/ppermute | solution.py:16
  95.1 5.6 %collective-permute-start.14 = (bf16[64,3584]{1,0:T(8,128)(2,1)S(1)}, bf16[64,3584]{1,0:T(8,128)(2,1)S(1)}, u32[]{:S(2)}, u32[]{:S(2)}) collective-permute-start(bf16[64,3584]{1,0:T(8,128)(2,1)S(1)} %maximum_select_fusion.2), channel_id=1, source_target_pairs={{0,4},{4,0},{8,12},{12,8},{16,20},{20,16},{24,28},{28,24},{1,5},{5... | collective-permute-start | bytes 1376264 | tf_op jit(solution)/shard_map/ppermute | solution.py:16
  101.7 3.6 %collective-permute-start.15 = (f32[2,64]{1,0:T(2,128)S(1)}, f32[2,64]{1,0:T(2,128)S(1)}, u32[]{:S(2)}, u32[]{:S(2)}) collective-permute-start(f32[2,64]{1,0:T(2,128)S(1)} %add_add_fusion), channel_id=1, source_target_pairs={{0,1},{1,0},{2,3},{3,2},{4,5},{5,4},{6,7},{7,6},{8,9},{9,8},{10,11... | collective-permute-start | bytes 1544 | tf_op jit(solution)/shard_map/ppermute | solution.py:16
  105.3 4.5 %collective-permute-start.16 = (f32[2,64]{1,0:T(2,128)S(1)}, f32[2,64]{1,0:T(2,128)S(1)}, u32[]{:S(2)}, u32[]{:S(2)}) collective-permute-start(f32[2,64]{1,0:T(2,128)S(1)} %add.91), channel_id=1, source_target_pairs={{0,2},{1,3},{2,0},{3,1},{4,6},{5,7},{6,4},{7,5},{8,10},{9,11},{10,... | collective-permute-start | bytes 1544 | tf_op jit(solution)/shard_map/ppermute | solution.py:16
  109.8 1.1 collective-permute-start.17
  110.9 3.6 %collective-permute-start.18 = (f32[2,64]{1,0:T(2,128)S(1)}, f32[2,64]{1,0:T(2,128)S(1)}, u32[]{:S(2)}, u32[]{:S(2)}) collective-permute-start(f32[2,64]{1,0:T(2,128)S(1)} %add.93), channel_id=1, source_target_pairs={{0,8},{4,12},{8,0},{12,4},{16,24},{20,28},{24,16},{28,20},{1,9},{5... | collective-permute-start | bytes 1544 | tf_op jit(solution)/shard_map/ppermute | solution.py:16
  114.5 3.6 %collective-permute-start.19 = (f32[2,64]{1,0:T(2,128)S(1)}, f32[2,64]{1,0:T(2,128)S(1)}, u32[]{:S(2)}, u32[]{:S(2)}) collective-permute-start(f32[2,64]{1,0:T(2,128)S(1)} %add.94), channel_id=1, source_target_pairs={{0,16},{4,20},{8,24},{12,28},{16,0},{20,4},{24,8},{28,12},{1,17},{... | collective-permute-start | bytes 1544 | tf_op jit(solution)/shard_map/ppermute | solution.py:16

commit v6 on v5

--- a/solution.py
+++ b/solution.py
@@ -25,6 +25,20 @@
         x = jnp.where(first, jnp.concatenate([x, other], dim), jnp.concatenate([other, x], dim))
         b *= 2
     return x
+
+
+def _gather_far_first(x, axis, n):
+    me = lax.axis_index(axis)
+    y = x[None]
+    b = n // 2
+    while b >= 1:
+        other = _swap(y, axis, n, b)
+        first = (me // b) % 2 == 0
+        lo = jnp.where(first, y, other)
+        hi = jnp.where(first, other, y)
+        y = jnp.stack([lo, hi], axis=1).reshape((2 * y.shape[0],) + x.shape)
+        b //= 2
+    return y.reshape((n * x.shape[0],) + x.shape[1:])
 
 
 def _allreduce_bf16(x, axis, n, dim, works=()):
@@ -114,7 +128,7 @@
 
 def local(out_grads, in_acts, out_basis, in_basis, eigenvalues, queries, *, nr, nc, nl, ng):
     acts_all = _gather(in_acts, "row", nr, 0)
-    grads_all = _gather(out_grads, "col", nc, 0)
+    grads_all = _gather_far_first(out_grads, "col", nc)
     act_part = jnp.dot(acts_all, in_basis, preferred_element_type=F32)
     nb = out_basis.shape[1] // 128
     cuts = [128 * round(i * nb / ng) for i in range(ng + 1)]
@@ -127,7 +141,11 @@
     kk = queries.shape[1]
     tk = next(c for c in (512, 256, 128, kk) if kk % c == 0)
     nt = kk // tk
-    bounds = [round(i * nt / nl) for i in range(nl + 1)]
+    weights = [2, 4, 2, 2, 2, 2] if nl == 6 else [1] * nl
+    acc = [0]
+    for w in weights:
+        acc.append(acc[-1] + w)
+    bounds = [round(a * nt / acc[-1]) for a in acc]
     spans = [(t0, t1) for t0, t1 in zip(bounds[:-1], bounds[1:]) if t1 > t0]
     works = [
         (functools.partial(lambda a, t0, t1: _lifted(a, eigenvalues, queries, t0, t1, tk), t0=t0, t1=t1), act_rot)

time: 119 us -> 117 us (0.983)
  transfers between devices with their start and end apart: 20 -> 20, of which waited for: 12 -> 12; matrix products, arithmetic and copies ran while one was open for 23% -> 23% of each run, Pallas kernels for 30% -> 31%
where the time goes in v6:
time: 117 us
  Pallas kernels  35.6 us (30%)
  matrix products  26.1 us (22%)
  starting transfers between devices  24.9 us (21%)
  waiting for transfers between devices  24.4 us (21%)
  other arithmetic  5.37 us (5%)
    pallas_call x6, Pallas kernels, _lifted(): pl.pallas_call(_lifted_kernel, grid=(t1 - t0,), in_specs=[pl.BlockSpec((t...  35.6 us
    ppermute x20, starting transfers between devices, _swap(): return lax.ppermute(x, axis, [(i, i ^ b) for i in range(n)])  24.9 us
    ppermute x20, waiting for transfers between devices, _swap(): return lax.ppermute(x, axis, [(i, i ^ b) for i in range(n)])  24.4 us
    dot_general x3, matrix products, local(): jnp.dot(g, out_basis[:, c0:c1], preferred_element_type=F32)  23.1 us
    dot_general x1, matrix products, local(): act_part = jnp.dot(acts_all, in_basis, preferred_element_type=F32)  3.04 us
  transfers between devices with their start and end apart: 20, of which 12 were waited for; matrix products, arithmetic and copies ran while one was open for 23% of the time, Pallas kernels for 31%

profile of v6, /device:TPU:0, one launch (start us, length us, event | category | flops | bytes accessed | tf_op | source)
XLA Modules:
  0.0 116.7 jit_solution(17480442977513130324)
XLA Ops:
  0.5 1.1 collective-permute-done
  2.4 2.9 %collective-permute-start.1 = (bf16[16,2048]{1,0:T(8,128)(2,1)S(1)}, bf16[16,2048]{1,0:T(8,128)(2,1)S(1)}, u32[]{:S(2)}, u32[]{:S(2)}) collective-permute-start(bf16[16,2048]{1,0:T(8,128)(2,1)S(1)} %maximum_select_fusion.7), channel_id=1, source_target_pairs={{0,8},{4,12},{8,0},{12,4},{16,24},{20,28},{24,16},{28,20},{1,9},{5... | collective-permute-start | bytes 196616 | tf_op jit(solution)/shard_map/ppermute | solution.py:16
  5.3 2.6 %collective-permute-start.4 = (bf16[1,16,3584]{2,1,0:T(8,128)(2,1)}, bf16[1,16,3584]{2,1,0:T(8,128)(2,1)S(1)}, u32[]{:S(2)}, u32[]{:S(2)}) collective-permute-start(bf16[1,16,3584]{2,1,0:T(8,128)(2,1)} %bitcast.27), channel_id=1, source_target_pairs={{0,2},{1,3},{2,0},{3,1},{4,6},{5,7},{6,4},{7,5},{8,10},{9,11},{10,... | collective-permute-start | bytes 344072 | tf_op jit(solution)/shard_map/ppermute | solution.py:16
  7.9 1.8 %collective-permute-start.2 = (bf16[32,2048]{1,0:T(8,128)(2,1)S(1)}, bf16[32,2048]{1,0:T(8,128)(2,1)S(1)}, u32[]{:S(2)}, u32[]{:S(2)}) collective-permute-start(bf16[32,2048]{1,0:T(8,128)(2,1)S(1)} %maximum_select_fusion.5), channel_id=1, source_target_pairs={{0,16},{4,20},{8,24},{12,28},{16,0},{20,4},{24,8},{28,12},{1,17},{... | collective-permute-start | bytes 393224 | tf_op jit(solution)/shard_map/ppermute | solution.py:16
  9.7 4.1 %collective-permute-done.4 = bf16[1,16,3584]{2,1,0:T(8,128)(2,1)S(1)} collective-permute-done((bf16[1,16,3584]{2,1,0:T(8,128)(2,1)}, bf16[1,16,3584]{2,1,0:T(8,128)(2,1)S(1)}, u32[]{:S(2)}, u32[]{:S(2)}) %collective-permute-start.4) | collective-permute-done | bytes 114720 | tf_op jit(solution)/shard_map/ppermute | solution.py:16
  13.8 0.9 select_bitcast_fusion.3
  15.6 3.0 %fusion.7 = f32[64,1024]{1,0:T(8,128)S(1)} fusion(bf16[2048,1024]{1,0:T(8,128)(2,1)} %param.9, bf16[32,2048]{1,0:T(8,128)(2,1)S(1)} %collective-permute-done.2, bf16[32,2048]{1,0:T(8,128)(2,1)S(1)} %maximum_select_fusion.5, pred[]{:T(512)S(6)} %eq.54), kind=kOutput, calls=%fused_computation.23 | convolution fusion | flops 269615104 | bytes 4718593 | tf_op jit(solution)/shard_map/dot_general | solution.py:132
  18.6 1.3 %collective-permute-start.3 = (f32[64,512]{1,0:T(8,128)S(1)}, f32[64,512]{1,0:T(8,128)S(1)}, u32[]{:S(2)}, u32[]{:S(2)}) collective-permute-start(f32[64,512]{1,0:T(8,128)S(1)} %slice_select_fusion.2), channel_id=1, source_target_pairs={{0,1},{1,0},{2,3},{3,2},{4,5},{5,4},{6,7},{7,6},{8,9},{9,8},{10,11... | collective-permute-start | bytes 393224 | tf_op jit(solution)/shard_map/ppermute | solution.py:16
  20.0 1.6 %collective-permute-done.5 = bf16[2,16,3584]{2,1,0:T(8,128)(2,1)S(1)} collective-permute-done((bf16[2,16,3584]{2,1,0:T(8,128)(2,1)S(1)}, bf16[2,16,3584]{2,1,0:T(8,128)(2,1)S(1)}, u32[]{:S(2)}, u32[]{:S(2)}) %collective-permute-start.5) | collective-permute-done | bytes 229408 | tf_op jit(solution)/shard_map/ppermute | solution.py:16
  21.7 2.5 %collective-permute-done.3 = f32[64,512]{1,0:T(8,128)S(1)} collective-permute-done((f32[64,512]{1,0:T(8,128)S(1)}, f32[64,512]{1,0:T(8,128)S(1)}, u32[]{:S(2)}, u32[]{:S(2)}) %collective-permute-start.3) | collective-permute-done | bytes 131104 | tf_op jit(solution)/shard_map/ppermute | solution.py:16
  24.2 3.3 %collective-permute-start.6 = (f32[64,256]{1,0:T(8,128)S(1)}, f32[64,256]{1,0:T(8,128)S(1)}, u32[]{:S(2)}, u32[]{:S(2)}) collective-permute-start(f32[64,256]{1,0:T(8,128)S(1)} %slice_select_fusion.3), channel_id=1, source_target_pairs={{0,2},{1,3},{2,0},{3,1},{4,6},{5,7},{6,4},{7,5},{8,10},{9,11},{10,... | collective-permute-start | bytes 196616 | tf_op jit(solution)/shard_map/ppermute | solution.py:16
  27.6 8.0 %fusion.2 = f32[64,2432]{1,0:T(8,128)S(1)} fusion(bf16[64,3584]{1,0:T(8,128)(2,1)S(1)} %bitcast.24, bf16[3584,7168]{1,0:T(8,128)(2,1)} %param.8), kind=kOutput, calls=%fused_computation.2 | convolution fusion | flops 1115684864 | bytes 18513920 | tf_op jit(solution)/shard_map/dot_general | solution.py:136
  35.6 7.3 %fusion.4 = f32[64,2304]{1,0:T(8,128)S(1)} fusion(bf16[64,3584]{1,0:T(8,128)(2,1)S(1)} %bitcast.25, bf16[3584,7168]{1,0:T(8,128)(2,1)} %param.8), kind=kOutput, calls=%fused_computation.4 | convolution fusion | flops 1056964608 | bytes 17563648 | tf_op jit(solution)/shard_map/dot_general | solution.py:136
  43.0 1.8 %collective-permute-start.8 = (bf16[64,512]{1,0:T(8,128)(2,1)S(1)}, bf16[64,512]{1,0:T(8,128)(2,1)S(1)}, u32[]{:S(2)}, u32[]{:S(2)}) collective-permute-start(bf16[64,512]{1,0:T(8,128)(2,1)S(1)} %maximum_select_fusion.8), channel_id=1, source_target_pairs={{0,1},{1,0},{2,3},{3,2},{4,5},{5,4},{6,7},{7,6},{8,9},{9,8},{10,11... | collective-permute-start | bytes 196616 | tf_op jit(solution)/shard_map/ppermute | solution.py:16
  44.8 7.8 %fusion = f32[64,2432]{1,0:T(8,128)S(1)} fusion(bf16[64,3584]{1,0:T(8,128)(2,1)S(1)} %bitcast.26, bf16[3584,7168]{1,0:T(8,128)(2,1)} %param.8), kind=kOutput, calls=%fused_computation | convolution fusion | flops 1115684864 | bytes 18513920 | tf_op jit(solution)/shard_map/dot_general | solution.py:136
  52.9 5.3 %shard_map.64 = f32[2,64,1024]{2,1,0:T(8,128)S(1)} custom-call(bf16[64,1024]{1,0:T(8,128)(2,1)S(1)} %maximum_select_fusion.6.a_ref, bf16[7168,1024]{1,0:T(8,128)(2,1)} %e_ref.11, bf16[2,7168,1024]{2,1,0:T(8,128)(2,1)} %q_ref.11), custom_call_target="tpu_custom_call" | custom-call | flops 536870912 | bytes 6815744 | tf_op jit(solution)/shard_map/pallas_call | solution.py:108
  58.2 1.3 %select_add_fusion = f32[64,3584]{1,0:T(8,128)S(1)} fusion(f32[64,3584]{1,0:T(8,128)} %collective-permute-done.9, f32[64,2304]{1,0:T(8,128)S(1)} %fusion.4, f32[64,2432]{1,0:T(8,128)S(1)} %fusion.2, f32[64,2432]{1,0:T(8,128)S(1)} %fusion, pred[]{:T(512)S(6)} %eq.51), kind=kLoop, calls=%fused_computation.10 | loop fusion | flops 917504 | bytes 3670017 | tf_op jit(solution)/shard_map/add | solution.py:70
  60.2 8.9 %shard_map.65 = f32[2,64,2048]{2,1,0:T(8,128)S(1)} custom-call(bf16[64,1024]{1,0:T(8,128)(2,1)S(1)} %maximum_select_fusion.6.a_ref, bf16[7168,1024]{1,0:T(8,128)(2,1)} %e_ref.11, bf16[2,7168,1024]{2,1,0:T(8,128)(2,1)} %q_ref.11), custom_call_target="tpu_custom_call" | custom-call | flops 1073741824 | bytes 13631488 | tf_op jit(solution)/shard_map/pallas_call | solution.py:108
  69.1 3.4 %collective-permute-done.10 = f32[64,1792]{1,0:T(8,128)S(1)} collective-permute-done((f32[64,1792]{1,0:T(8,128)S(1)}, f32[64,1792]{1,0:T(8,128)S(1)}, u32[]{:S(2)}, u32[]{:S(2)}) %collective-permute-start.10) | collective-permute-done | bytes 458784 | tf_op jit(solution)/shard_map/ppermute | solution.py:16
  72.7 1.6 %collective-permute-start.11 = (f32[64,896]{1,0:T(8,128)S(1)}, f32[64,896]{1,0:T(8,128)S(1)}, u32[]{:S(2)}, u32[]{:S(2)}) collective-permute-start(f32[64,896]{1,0:T(8,128)S(1)} %slice_select_fusion.1), channel_id=1, source_target_pairs={{0,16},{4,20},{8,24},{12,28},{16,0},{20,4},{24,8},{28,12},{1,17},{... | collective-permute-start | bytes 688136 | tf_op jit(solution)/shard_map/ppermute | solution.py:16
  74.2 5.3 %shard_map.66 = f32[2,64,1024]{2,1,0:T(8,128)S(1)} custom-call(bf16[64,1024]{1,0:T(8,128)(2,1)S(1)} %maximum_select_fusion.6.a_ref, bf16[7168,1024]{1,0:T(8,128)(2,1)} %e_ref.11, bf16[2,7168,1024]{2,1,0:T(8,128)(2,1)} %q_ref.11), custom_call_target="tpu_custom_call" | custom-call | flops 536870912 | bytes 6815744 | tf_op jit(solution)/shard_map/pallas_call | solution.py:108
  80.0 1.6 %collective-permute-start.12 = (bf16[64,896]{1,0:T(8,128)(2,1)S(1)}, bf16[64,896]{1,0:T(8,128)(2,1)S(1)}, u32[]{:S(2)}, u32[]{:S(2)}) collective-permute-start(bf16[64,896]{1,0:T(8,128)(2,1)S(1)} %add_convert_fusion), channel_id=1, source_target_pairs={{0,16},{4,20},{8,24},{12,28},{16,0},{20,4},{24,8},{28,12},{1,17},{... | collective-permute-start | bytes 344072 | tf_op jit(solution)/shard_map/ppermute | solution.py:16
  81.5 5.3 %shard_map.67 = f32[2,64,1024]{2,1,0:T(8,128)S(1)} custom-call(bf16[64,1024]{1,0:T(8,128)(2,1)S(1)} %maximum_select_fusion.6.a_ref, bf16[7168,1024]{1,0:T(8,128)(2,1)} %e_ref.11, bf16[2,7168,1024]{2,1,0:T(8,128)(2,1)} %q_ref.11), custom_call_target="tpu_custom_call" | custom-call | flops 536870912 | bytes 6815744 | tf_op jit(solution)/shard_map/pallas_call | solution.py:108
  87.5 5.3 %shard_map.68 = f32[2,64,1024]{2,1,0:T(8,128)S(1)} custom-call(bf16[64,1024]{1,0:T(8,128)(2,1)S(1)} %maximum_select_fusion.6.a_ref, bf16[7168,1024]{1,0:T(8,128)(2,1)} %e_ref.11, bf16[2,7168,1024]{2,1,0:T(8,128)(2,1)} %q_ref.11), custom_call_target="tpu_custom_call" | custom-call | flops 536870912 | bytes 6815744 | tf_op jit(solution)/shard_map/pallas_call | solution.py:108
  93.2 5.5 %shard_map.69 = f32[2,64,1024]{2,1,0:T(8,128)S(1)} custom-call(bf16[64,1024]{1,0:T(8,128)(2,1)S(1)} %maximum_select_fusion.6.a_ref, bf16[7168,1024]{1,0:T(8,128)(2,1)} %e_ref.11, bf16[2,7168,1024]{2,1,0:T(8,128)(2,1)} %q_ref.11), custom_call_target="tpu_custom_call" | custom-call | flops 536870912 | bytes 6815744 | tf_op jit(solution)/shard_map/pallas_call | solution.py:108
  100.1 3.3 %collective-permute-done.15 = f32[2,64]{1,0:T(2,128)S(1)} collective-permute-done((f32[2,64]{1,0:T(2,128)S(1)}, f32[2,64]{1,0:T(2,128)S(1)}, u32[]{:S(2)}, u32[]{:S(2)}) %collective-permute-start.15) | collective-permute-done | bytes 544 | tf_op jit(solution)/shard_map/ppermute | solution.py:16
  103.4 2.9 %collective-permute-start.16 = (f32[2,64]{1,0:T(2,128)S(1)}, f32[2,64]{1,0:T(2,128)S(1)}, u32[]{:S(2)}, u32[]{:S(2)}) collective-permute-start(f32[2,64]{1,0:T(2,128)S(1)} %add.91), channel_id=1, source_target_pairs={{0,2},{1,3},{2,0},{3,1},{4,6},{5,7},{6,4},{7,5},{8,10},{9,11},{10,... | collective-permute-start | bytes 1544 | tf_op jit(solution)/shard_map/ppermute | solution.py:16
  106.3 1.6 %collective-permute-done.16 = f32[2,64]{1,0:T(2,128)S(1)} collective-permute-done((f32[2,64]{1,0:T(2,128)S(1)}, f32[2,64]{1,0:T(2,128)S(1)}, u32[]{:S(2)}, u32[]{:S(2)}) %collective-permute-start.16) | collective-permute-done | bytes 544 | tf_op jit(solution)/shard_map/ppermute | solution.py:16
  107.9 1.1 collective-permute-done.17
  109.0 1.3 %collective-permute-start.18 = (f32[2,64]{1,0:T(2,128)S(1)}, f32[2,64]{1,0:T(2,128)S(1)}, u32[]{:S(2)}, u32[]{:S(2)}) collective-permute-start(f32[2,64]{1,0:T(2,128)S(1)} %add.93), channel_id=1, source_target_pairs={{0,8},{4,12},{8,0},{12,4},{16,24},{20,28},{24,16},{28,20},{1,9},{5... | collective-permute-start | bytes 1544 | tf_op jit(solution)/shard_map/ppermute | solution.py:16
  110.3 2.3 %collective-permute-done.18 = f32[2,64]{1,0:T(2,128)S(1)} collective-permute-done((f32[2,64]{1,0:T(2,128)S(1)}, f32[2,64]{1,0:T(2,128)S(1)}, u32[]{:S(2)}, u32[]{:S(2)}) %collective-permute-start.18) | collective-permute-done | bytes 544 | tf_op jit(solution)/shard_map/ppermute | solution.py:16
  113.4 2.8 %collective-permute-done.19 = f32[2,64]{1,0:T(2,128)S(1)} collective-permute-done((f32[2,64]{1,0:T(2,128)S(1)}, f32[2,64]{1,0:T(2,128)S(1)}, u32[]{:S(2)}, u32[]{:S(2)}) %collective-permute-start.19) | collective-permute-done | bytes 544 | tf_op jit(solution)/shard_map/ppermute | solution.py:16
  (51 shorter events, 7.6 us)
Async XLA Ops:
  0.0 1.5 %collective-permute-start = (bf16[8,2048]{1,0:T(8,128)(2,1)}, bf16[8,2048]{1,0:T(8,128)(2,1)S(1)}, u32[]{:S(2)}, u32[]{:S(2)}) collective-permute-start(bf16[8,2048]{1,0:T(8,128)(2,1)} %param.7), channel_id=1, source_target_pairs={{0,4},{4,0},{8,12},{12,8},{16,20},{20,16},{24,28},{28,24},{1,5},{5... | collective-permute-start | bytes 98312 | tf_op jit(solution)/shard_map/ppermute | solution.py:16
  2.4 5.5 %collective-permute-start.1 = (bf16[16,2048]{1,0:T(8,128)(2,1)S(1)}, bf16[16,2048]{1,0:T(8,128)(2,1)S(1)}, u32[]{:S(2)}, u32[]{:S(2)}) collective-permute-start(bf16[16,2048]{1,0:T(8,128)(2,1)S(1)} %maximum_select_fusion.7), channel_id=1, source_target_pairs={{0,8},{4,12},{8,0},{12,4},{16,24},{20,28},{24,16},{28,20},{1,9},{5... | collective-permute-start | bytes 196616 | tf_op jit(solution)/shard_map/ppermute | solution.py:16
  5.3 8.5 %collective-permute-start.4 = (bf16[1,16,3584]{2,1,0:T(8,128)(2,1)}, bf16[1,16,3584]{2,1,0:T(8,128)(2,1)S(1)}, u32[]{:S(2)}, u32[]{:S(2)}) collective-permute-start(bf16[1,16,3584]{2,1,0:T(8,128)(2,1)} %bitcast.27), channel_id=1, source_target_pairs={{0,2},{1,3},{2,0},{3,1},{4,6},{5,7},{6,4},{7,5},{8,10},{9,11},{10,... | collective-permute-start | bytes 344072 | tf_op jit(solution)/shard_map/ppermute | solution.py:16
  7.9 7.7 %collective-permute-start.2 = (bf16[32,2048]{1,0:T(8,128)(2,1)S(1)}, bf16[32,2048]{1,0:T(8,128)(2,1)S(1)}, u32[]{:S(2)}, u32[]{:S(2)}) collective-permute-start(bf16[32,2048]{1,0:T(8,128)(2,1)S(1)} %maximum_select_fusion.5), channel_id=1, source_target_pairs={{0,16},{4,20},{8,24},{12,28},{16,0},{20,4},{24,8},{28,12},{1,17},{... | collective-permute-start | bytes 393224 | tf_op jit(solution)/shard_map/ppermute | solution.py:16
  14.7 6.9 %collective-permute-start.5 = (bf16[2,16,3584]{2,1,0:T(8,128)(2,1)S(1)}, bf16[2,16,3584]{2,1,0:T(8,128)(2,1)S(1)}, u32[]{:S(2)}, u32[]{:S(2)}) collective-permute-start(bf16[2,16,3584]{2,1,0:T(8,128)(2,1)S(1)} %maximum_bitcast_fusion), channel_id=1, source_target_pairs={{0,1},{1,0},{2,3},{3,2},{4,5},{5,4},{6,7},{7,6},{8,9},{9,8},{10,11... | collective-permute-start | bytes 688136 | tf_op jit(solution)/shard_map/ppermute | solution.py:16
  18.6 5.5 %collective-permute-start.3 = (f32[64,512]{1,0:T(8,128)S(1)}, f32[64,512]{1,0:T(8,128)S(1)}, u32[]{:S(2)}, u32[]{:S(2)}) collective-permute-start(f32[64,512]{1,0:T(8,128)S(1)} %slice_select_fusion.2), channel_id=1, source_target_pairs={{0,1},{1,0},{2,3},{3,2},{4,5},{5,4},{6,7},{7,6},{8,9},{9,8},{10,11... | collective-permute-start | bytes 393224 | tf_op jit(solution)/shard_map/ppermute | solution.py:16
  24.2 11.3 %collective-permute-start.6 = (f32[64,256]{1,0:T(8,128)S(1)}, f32[64,256]{1,0:T(8,128)S(1)}, u32[]{:S(2)}, u32[]{:S(2)}) collective-permute-start(f32[64,256]{1,0:T(8,128)S(1)} %slice_select_fusion.3), channel_id=1, source_target_pairs={{0,2},{1,3},{2,0},{3,1},{4,6},{5,7},{6,4},{7,5},{8,10},{9,11},{10,... | collective-permute-start | bytes 196616 | tf_op jit(solution)/shard_map/ppermute | solution.py:16
  35.6 7.4 %collective-permute-start.7 = (bf16[64,256]{1,0:T(8,128)(2,1)S(1)}, bf16[64,256]{1,0:T(8,128)(2,1)S(1)}, u32[]{:S(2)}, u32[]{:S(2)}) collective-permute-start(bf16[64,256]{1,0:T(8,128)(2,1)S(1)} %add_convert_fusion.1), channel_id=1, source_target_pairs={{0,2},{1,3},{2,0},{3,1},{4,6},{5,7},{6,4},{7,5},{8,10},{9,11},{10,... | collective-permute-start | bytes 98312 | tf_op jit(solution)/shard_map/ppermute | solution.py:16
  43.0 9.6 %collective-permute-start.8 = (bf16[64,512]{1,0:T(8,128)(2,1)S(1)}, bf16[64,512]{1,0:T(8,128)(2,1)S(1)}, u32[]{:S(2)}, u32[]{:S(2)}) collective-permute-start(bf16[64,512]{1,0:T(8,128)(2,1)S(1)} %maximum_select_fusion.8), channel_id=1, source_target_pairs={{0,1},{1,0},{2,3},{3,2},{4,5},{5,4},{6,7},{7,6},{8,9},{9,8},{10,11... | collective-permute-start | bytes 196616 | tf_op jit(solution)/shard_map/ppermute | solution.py:16
  52.8 5.4 %collective-permute-start.9 = (f32[64,3584]{1,0:T(8,128)S(1)}, f32[64,3584]{1,0:T(8,128)}, u32[]{:S(2)}, u32[]{:S(2)}) collective-permute-start(f32[64,3584]{1,0:T(8,128)S(1)} %fusion.6), channel_id=1, source_target_pairs={{0,4},{4,0},{8,12},{12,8},{16,20},{20,16},{24,28},{28,24},{1,5},{5... | collective-permute-start | bytes 2752520 | tf_op jit(solution)/shard_map/ppermute | solution.py:16
  59.6 13.0 %collective-permute-start.10 = (f32[64,1792]{1,0:T(8,128)S(1)}, f32[64,1792]{1,0:T(8,128)S(1)}, u32[]{:S(2)}, u32[]{:S(2)}) collective-permute-start(f32[64,1792]{1,0:T(8,128)S(1)} %slice_select_fusion), channel_id=1, source_target_pairs={{0,8},{4,12},{8,0},{12,4},{16,24},{20,28},{24,16},{28,20},{1,9},{5... | collective-permute-start | bytes 1376264 | tf_op jit(solution)/shard_map/ppermute | solution.py:16
  72.7 7.3 %collective-permute-start.11 = (f32[64,896]{1,0:T(8,128)S(1)}, f32[64,896]{1,0:T(8,128)S(1)}, u32[]{:S(2)}, u32[]{:S(2)}) collective-permute-start(f32[64,896]{1,0:T(8,128)S(1)} %slice_select_fusion.1), channel_id=1, source_target_pairs={{0,16},{4,20},{8,24},{12,28},{16,0},{20,4},{24,8},{28,12},{1,17},{... | collective-permute-start | bytes 688136 | tf_op jit(solution)/shard_map/ppermute | solution.py:16
  80.0 6.9 %collective-permute-start.12 = (bf16[64,896]{1,0:T(8,128)(2,1)S(1)}, bf16[64,896]{1,0:T(8,128)(2,1)S(1)}, u32[]{:S(2)}, u32[]{:S(2)}) collective-permute-start(bf16[64,896]{1,0:T(8,128)(2,1)S(1)} %add_convert_fusion), channel_id=1, source_target_pairs={{0,16},{4,20},{8,24},{12,28},{16,0},{20,4},{24,8},{28,12},{1,17},{... | collective-permute-start | bytes 344072 | tf_op jit(solution)/shard_map/ppermute | solution.py:16
  86.9 6.1 %collective-permute-start.13 = (bf16[64,1792]{1,0:T(8,128)(2,1)S(1)}, bf16[64,1792]{1,0:T(8,128)(2,1)S(1)}, u32[]{:S(2)}, u32[]{:S(2)}) collective-permute-start(bf16[64,1792]{1,0:T(8,128)(2,1)S(1)} %maximum_select_fusion.4), channel_id=1, source_target_pairs={{0,8},{4,12},{8,0},{12,4},{16,24},{20,28},{24,16},{28,20},{1,9},{5... | collective-permute-start | bytes 688136 | tf_op jit(solution)/shard_map/ppermute | solution.py:16
  93.1 5.6 %collective-permute-start.14 = (bf16[64,3584]{1,0:T(8,128)(2,1)S(1)}, bf16[64,3584]{1,0:T(8,128)(2,1)S(1)}, u32[]{:S(2)}, u32[]{:S(2)}) collective-permute-start(bf16[64,3584]{1,0:T(8,128)(2,1)S(1)} %maximum_select_fusion.1), channel_id=1, source_target_pairs={{0,4},{4,0},{8,12},{12,8},{16,20},{20,16},{24,28},{28,24},{1,5},{5... | collective-permute-start | bytes 1376264 | tf_op jit(solution)/shard_map/ppermute | solution.py:16
  99.8 3.6 %collective-permute-start.15 = (f32[2,64]{1,0:T(2,128)S(1)}, f32[2,64]{1,0:T(2,128)S(1)}, u32[]{:S(2)}, u32[]{:S(2)}) collective-permute-start(f32[2,64]{1,0:T(2,128)S(1)} %add_add_fusion), channel_id=1, source_target_pairs={{0,1},{1,0},{2,3},{3,2},{4,5},{5,4},{6,7},{7,6},{8,9},{9,8},{10,11... | collective-permute-start | bytes 1544 | tf_op jit(solution)/shard_map/ppermute | solution.py:16
  103.4 4.5 %collective-permute-start.16 = (f32[2,64]{1,0:T(2,128)S(1)}, f32[2,64]{1,0:T(2,128)S(1)}, u32[]{:S(2)}, u32[]{:S(2)}) collective-permute-start(f32[2,64]{1,0:T(2,128)S(1)} %add.91), channel_id=1, source_target_pairs={{0,2},{1,3},{2,0},{3,1},{4,6},{5,7},{6,4},{7,5},{8,10},{9,11},{10,... | collective-permute-start | bytes 1544 | tf_op jit(solution)/shard_map/ppermute | solution.py:16
  107.9 1.1 collective-permute-start.17
  109.0 3.6 %collective-permute-start.18 = (f32[2,64]{1,0:T(2,128)S(1)}, f32[2,64]{1,0:T(2,128)S(1)}, u32[]{:S(2)}, u32[]{:S(2)}) collective-permute-start(f32[2,64]{1,0:T(2,128)S(1)} %add.93), channel_id=1, source_target_pairs={{0,8},{4,12},{8,0},{12,4},{16,24},{20,28},{24,16},{28,20},{1,9},{5... | collective-permute-start | bytes 1544 | tf_op jit(solution)/shard_map/ppermute | solution.py:16
  112.6 3.6 %collective-permute-start.19 = (f32[2,64]{1,0:T(2,128)S(1)}, f32[2,64]{1,0:T(2,128)S(1)}, u32[]{:S(2)}, u32[]{:S(2)}) collective-permute-start(f32[2,64]{1,0:T(2,128)S(1)} %add.94), channel_id=1, source_target_pairs={{0,16},{4,20},{8,24},{12,28},{16,0},{20,4},{24,8},{28,12},{1,17},{... | collective-permute-start | bytes 1544 | tf_op jit(solution)/shard_map/ppermute | solution.py:16

commit v7 on v6

--- a/solution.py
+++ b/solution.py
@@ -93,12 +93,8 @@
     a = a_ref[...]
     dims = (((1,), (1,)), ((), ()))
     for qi in range(q_ref.shape[0]):
-        s = q_ref[qi].astype(F32) * recip
-        hi = s.astype(BF16)
-        lo = (s - hi.astype(F32)).astype(BF16)
-        o_ref[qi] = lax.dot_general(a, hi, dims, preferred_element_type=F32) + lax.dot_general(
-            a, lo, dims, preferred_element_type=F32
-        )
+        s = (q_ref[qi].astype(F32) * recip).astype(BF16)
+        o_ref[qi] = lax.dot_general(a, s, dims, preferred_element_type=F32)
 
 
 def _lifted(act_rot, eigenvalues, queries, t0, t1, tk):
@@ -119,7 +115,7 @@
             dimension_semantics=("arbitrary",), vmem_limit_bytes=48 * 1024 * 1024
         ),
         cost_estimate=pl.CostEstimate(
-            flops=4 * nq * kc * jj * tt,
+            flops=2 * nq * kc * jj * tt,
             bytes_accessed=(nq + 1) * kc * jj * 2 + nq * tt * kc * 4,
             transcendentals=0,
         ),
@@ -141,7 +137,7 @@
     kk = queries.shape[1]
     tk = next(c for c in (512, 256, 128, kk) if kk % c == 0)
     nt = kk // tk
-    weights = [2, 4, 2, 2, 2, 2] if nl == 6 else [1] * nl
+    weights = [2, 5, 2, 2, 2, 1] if nl == 6 else [1] * nl
     acc = [0]
     for w in weights:
         acc.append(acc[-1] + w)

time: 117 us -> 111 us (0.949)
  Pallas kernels: 35.6 us -> 26.3 us
  waiting for transfers between devices: 24.4 us -> 28.4 us
    pallas_call x6, Pallas kernels: 35.6 us -> 26.3 us  [_lifted(): pl.pallas_call(_lifted_kernel, grid=(t1 - t0,), in_specs=[pl.BlockSpec((t...]
    ppermute x20, waiting for transfers between devices: 24.4 us -> 28.4 us  [_swap(): return lax.ppermute(x, axis, [(i, i ^ b) for i in range(n)])]
  transfers between devices with their start and end apart: 20 -> 20, of which waited for: 12 -> 12; matrix products, arithmetic and copies ran while one was open for 23% -> 25% of each run, Pallas kernels for 31% -> 24%
where the time goes in v7:
time: 111 us
  waiting for transfers between devices  28.4 us (26%)
  Pallas kernels  26.3 us (24%)
  matrix products  26.1 us (24%)
  starting transfers between devices  24.4 us (22%)
  other arithmetic  5.39 us (5%)
    ppermute x20, waiting for transfers between devices, _swap(): return lax.ppermute(x, axis, [(i, i ^ b) for i in range(n)])  28.4 us
    pallas_call x6, Pallas kernels, _lifted(): pl.pallas_call(_lifted_kernel, grid=(t1 - t0,), in_specs=[pl.BlockSpec((t...  26.3 us
    ppermute x20, starting transfers between devices, _swap(): return lax.ppermute(x, axis, [(i, i ^ b) for i in range(n)])  24.4 us
    dot_general x3, matrix products, local(): jnp.dot(g, out_basis[:, c0:c1], preferred_element_type=F32)  23.1 us
    dot_general x1, matrix products, local(): act_part = jnp.dot(acts_all, in_basis, preferred_element_type=F32)  3.03 us
  transfers between devices with their start and end apart: 20, of which 12 were waited for; matrix products, arithmetic and copies ran while one was open for 25% of the time, Pallas kernels for 24%

profile of v7, /device:TPU:0, one launch (start us, length us, event | category | flops | bytes accessed | tf_op | source)
XLA Modules:
  0.0 111.0 jit_solution(5104208043204100532)
XLA Ops:
  0.5 1.1 collective-permute-done
  2.4 2.9 %collective-permute-start.1 = (bf16[16,2048]{1,0:T(8,128)(2,1)S(1)}, bf16[16,2048]{1,0:T(8,128)(2,1)S(1)}, u32[]{:S(2)}, u32[]{:S(2)}) collective-permute-start(bf16[16,2048]{1,0:T(8,128)(2,1)S(1)} %maximum_select_fusion.7), channel_id=1, source_target_pairs={{0,8},{4,12},{8,0},{12,4},{16,24},{20,28},{24,16},{28,20},{1,9},{5... | collective-permute-start | bytes 196616 | tf_op jit(solution)/shard_map/ppermute | solution.py:16
  5.3 2.6 %collective-permute-start.4 = (bf16[1,16,3584]{2,1,0:T(8,128)(2,1)}, bf16[1,16,3584]{2,1,0:T(8,128)(2,1)S(1)}, u32[]{:S(2)}, u32[]{:S(2)}) collective-permute-start(bf16[1,16,3584]{2,1,0:T(8,128)(2,1)} %bitcast.27), channel_id=1, source_target_pairs={{0,2},{1,3},{2,0},{3,1},{4,6},{5,7},{6,4},{7,5},{8,10},{9,11},{10,... | collective-permute-start | bytes 344072 | tf_op jit(solution)/shard_map/ppermute | solution.py:16
  7.9 1.8 %collective-permute-start.2 = (bf16[32,2048]{1,0:T(8,128)(2,1)S(1)}, bf16[32,2048]{1,0:T(8,128)(2,1)S(1)}, u32[]{:S(2)}, u32[]{:S(2)}) collective-permute-start(bf16[32,2048]{1,0:T(8,128)(2,1)S(1)} %maximum_select_fusion.5), channel_id=1, source_target_pairs={{0,16},{4,20},{8,24},{12,28},{16,0},{20,4},{24,8},{28,12},{1,17},{... | collective-permute-start | bytes 393224 | tf_op jit(solution)/shard_map/ppermute | solution.py:16
  9.7 4.1 %collective-permute-done.4 = bf16[1,16,3584]{2,1,0:T(8,128)(2,1)S(1)} collective-permute-done((bf16[1,16,3584]{2,1,0:T(8,128)(2,1)}, bf16[1,16,3584]{2,1,0:T(8,128)(2,1)S(1)}, u32[]{:S(2)}, u32[]{:S(2)}) %collective-permute-start.4) | collective-permute-done | bytes 114720 | tf_op jit(solution)/shard_map/ppermute | solution.py:16
  15.6 3.0 %fusion.7 = f32[64,1024]{1,0:T(8,128)S(1)} fusion(bf16[2048,1024]{1,0:T(8,128)(2,1)} %param.9, bf16[32,2048]{1,0:T(8,128)(2,1)S(1)} %collective-permute-done.2, bf16[32,2048]{1,0:T(8,128)(2,1)S(1)} %maximum_select_fusion.5, pred[]{:T(512)S(6)} %eq.54), kind=kOutput, calls=%fused_computation.22 | convolution fusion | flops 269615104 | bytes 4718593 | tf_op jit(solution)/shard_map/dot_general | solution.py:128
  18.6 1.3 %collective-permute-start.3 = (f32[64,512]{1,0:T(8,128)S(1)}, f32[64,512]{1,0:T(8,128)S(1)}, u32[]{:S(2)}, u32[]{:S(2)}) collective-permute-start(f32[64,512]{1,0:T(8,128)S(1)} %slice_select_fusion.2), channel_id=1, source_target_pairs={{0,1},{1,0},{2,3},{3,2},{4,5},{5,4},{6,7},{7,6},{8,9},{9,8},{10,11... | collective-permute-start | bytes 393224 | tf_op jit(solution)/shard_map/ppermute | solution.py:16
  20.0 1.6 %collective-permute-done.5 = bf16[2,16,3584]{2,1,0:T(8,128)(2,1)S(1)} collective-permute-done((bf16[2,16,3584]{2,1,0:T(8,128)(2,1)S(1)}, bf16[2,16,3584]{2,1,0:T(8,128)(2,1)S(1)}, u32[]{:S(2)}, u32[]{:S(2)}) %collective-permute-start.5) | collective-permute-done | bytes 229408 | tf_op jit(solution)/shard_map/ppermute | solution.py:16
  21.7 2.5 %collective-permute-done.3 = f32[64,512]{1,0:T(8,128)S(1)} collective-permute-done((f32[64,512]{1,0:T(8,128)S(1)}, f32[64,512]{1,0:T(8,128)S(1)}, u32[]{:S(2)}, u32[]{:S(2)}) %collective-permute-start.3) | collective-permute-done | bytes 131104 | tf_op jit(solution)/shard_map/ppermute | solution.py:16
  24.2 3.3 %collective-permute-start.6 = (f32[64,256]{1,0:T(8,128)S(1)}, f32[64,256]{1,0:T(8,128)S(1)}, u32[]{:S(2)}, u32[]{:S(2)}) collective-permute-start(f32[64,256]{1,0:T(8,128)S(1)} %slice_select_fusion.3), channel_id=1, source_target_pairs={{0,2},{1,3},{2,0},{3,1},{4,6},{5,7},{6,4},{7,5},{8,10},{9,11},{10,... | collective-permute-start | bytes 196616 | tf_op jit(solution)/shard_map/ppermute | solution.py:16
  27.6 8.0 %fusion.2 = f32[64,2432]{1,0:T(8,128)S(1)} fusion(bf16[64,3584]{1,0:T(8,128)(2,1)S(1)} %bitcast.24, bf16[3584,7168]{1,0:T(8,128)(2,1)} %param.8), kind=kOutput, calls=%fused_computation.2 | convolution fusion | flops 1115684864 | bytes 18513920 | tf_op jit(solution)/shard_map/dot_general | solution.py:132
  35.7 7.3 %fusion.4 = f32[64,2304]{1,0:T(8,128)S(1)} fusion(bf16[64,3584]{1,0:T(8,128)(2,1)S(1)} %bitcast.25, bf16[3584,7168]{1,0:T(8,128)(2,1)} %param.8), kind=kOutput, calls=%fused_computation.4 | convolution fusion | flops 1056964608 | bytes 17563648 | tf_op jit(solution)/shard_map/dot_general | solution.py:132
  43.0 1.8 %collective-permute-start.8 = (bf16[64,512]{1,0:T(8,128)(2,1)S(1)}, bf16[64,512]{1,0:T(8,128)(2,1)S(1)}, u32[]{:S(2)}, u32[]{:S(2)}) collective-permute-start(bf16[64,512]{1,0:T(8,128)(2,1)S(1)} %maximum_select_fusion.8), channel_id=1, source_target_pairs={{0,1},{1,0},{2,3},{3,2},{4,5},{5,4},{6,7},{7,6},{8,9},{9,8},{10,11... | collective-permute-start | bytes 196616 | tf_op jit(solution)/shard_map/ppermute | solution.py:16
  44.8 7.8 %fusion = f32[64,2432]{1,0:T(8,128)S(1)} fusion(bf16[64,3584]{1,0:T(8,128)(2,1)S(1)} %bitcast.26, bf16[3584,7168]{1,0:T(8,128)(2,1)} %param.8), kind=kOutput, calls=%fused_computation | convolution fusion | flops 1115684864 | bytes 18513920 | tf_op jit(solution)/shard_map/dot_general | solution.py:132
  52.9 3.8 %shard_map.64 = f32[2,64,1024]{2,1,0:T(8,128)S(1)} custom-call(bf16[64,1024]{1,0:T(8,128)(2,1)S(1)} %maximum_select_fusion.6.a_ref, bf16[7168,1024]{1,0:T(8,128)(2,1)} %e_ref.11, bf16[2,7168,1024]{2,1,0:T(8,128)(2,1)} %q_ref.11), custom_call_target="tpu_custom_call" | custom-call | flops 268435456 | bytes 6815744 | tf_op jit(solution)/shard_map/pallas_call | solution.py:104
  56.7 1.3 %select_add_fusion = f32[64,3584]{1,0:T(8,128)S(1)} fusion(f32[64,3584]{1,0:T(8,128)} %collective-permute-done.9, f32[64,2304]{1,0:T(8,128)S(1)} %fusion.4, f32[64,2432]{1,0:T(8,128)S(1)} %fusion.2, f32[64,2432]{1,0:T(8,128)S(1)} %fusion, pred[]{:T(512)S(6)} %eq.51), kind=kLoop, calls=%fused_computation.10 | loop fusion | flops 917504 | bytes 3670017 | tf_op jit(solution)/shard_map/add | solution.py:70
  58.7 8.5 %shard_map.65 = f32[2,64,2560]{2,1,0:T(8,128)S(1)} custom-call(bf16[64,1024]{1,0:T(8,128)(2,1)S(1)} %maximum_select_fusion.6.a_ref, bf16[7168,1024]{1,0:T(8,128)(2,1)} %e_ref.11, bf16[2,7168,1024]{2,1,0:T(8,128)(2,1)} %q_ref.11), custom_call_target="tpu_custom_call" | custom-call | flops 671088640 | bytes 17039360 | tf_op jit(solution)/shard_map/pallas_call | solution.py:104
  67.1 3.9 %collective-permute-done.10 = f32[64,1792]{1,0:T(8,128)S(1)} collective-permute-done((f32[64,1792]{1,0:T(8,128)S(1)}, f32[64,1792]{1,0:T(8,128)S(1)}, u32[]{:S(2)}, u32[]{:S(2)}) %collective-permute-start.10) | collective-permute-done | bytes 458784 | tf_op jit(solution)/shard_map/ppermute | solution.py:16
  71.1 1.6 %collective-permute-start.11 = (f32[64,896]{1,0:T(8,128)S(1)}, f32[64,896]{1,0:T(8,128)S(1)}, u32[]{:S(2)}, u32[]{:S(2)}) collective-permute-start(f32[64,896]{1,0:T(8,128)S(1)} %slice_select_fusion.1), channel_id=1, source_target_pairs={{0,16},{4,20},{8,24},{12,28},{16,0},{20,4},{24,8},{28,12},{1,17},{... | collective-permute-start | bytes 688136 | tf_op jit(solution)/shard_map/ppermute | solution.py:16
  72.7 3.8 %shard_map.66 = f32[2,64,1024]{2,1,0:T(8,128)S(1)} custom-call(bf16[64,1024]{1,0:T(8,128)(2,1)S(1)} %maximum_select_fusion.6.a_ref, bf16[7168,1024]{1,0:T(8,128)(2,1)} %e_ref.11, bf16[2,7168,1024]{2,1,0:T(8,128)(2,1)} %q_ref.11), custom_call_target="tpu_custom_call" | custom-call | flops 268435456 | bytes 6815744 | tf_op jit(solution)/shard_map/pallas_call | solution.py:104
  76.5 1.9 %collective-permute-done.11 = f32[64,896]{1,0:T(8,128)S(1)} collective-permute-done((f32[64,896]{1,0:T(8,128)S(1)}, f32[64,896]{1,0:T(8,128)S(1)}, u32[]{:S(2)}, u32[]{:S(2)}) %collective-permute-start.11) | collective-permute-done | bytes 229408 | tf_op jit(solution)/shard_map/ppermute | solution.py:16
  78.4 1.6 %collective-permute-start.12 = (bf16[64,896]{1,0:T(8,128)(2,1)S(1)}, bf16[64,896]{1,0:T(8,128)(2,1)S(1)}, u32[]{:S(2)}, u32[]{:S(2)}) collective-permute-start(bf16[64,896]{1,0:T(8,128)(2,1)S(1)} %add_convert_fusion), channel_id=1, source_target_pairs={{0,16},{4,20},{8,24},{12,28},{16,0},{20,4},{24,8},{28,12},{1,17},{... | collective-permute-start | bytes 344072 | tf_op jit(solution)/shard_map/ppermute | solution.py:16
  80.0 3.8 %shard_map.67 = f32[2,64,1024]{2,1,0:T(8,128)S(1)} custom-call(bf16[64,1024]{1,0:T(8,128)(2,1)S(1)} %maximum_select_fusion.6.a_ref, bf16[7168,1024]{1,0:T(8,128)(2,1)} %e_ref.11, bf16[2,7168,1024]{2,1,0:T(8,128)(2,1)} %q_ref.11), custom_call_target="tpu_custom_call" | custom-call | flops 268435456 | bytes 6815744 | tf_op jit(solution)/shard_map/pallas_call | solution.py:104
  84.5 3.8 %shard_map.68 = f32[2,64,1024]{2,1,0:T(8,128)S(1)} custom-call(bf16[64,1024]{1,0:T(8,128)(2,1)S(1)} %maximum_select_fusion.6.a_ref, bf16[7168,1024]{1,0:T(8,128)(2,1)} %e_ref.11, bf16[2,7168,1024]{2,1,0:T(8,128)(2,1)} %q_ref.11), custom_call_target="tpu_custom_call" | custom-call | flops 268435456 | bytes 6815744 | tf_op jit(solution)/shard_map/pallas_call | solution.py:104
  88.2 1.7 %collective-permute-done.13 = bf16[64,1792]{1,0:T(8,128)(2,1)S(1)} collective-permute-done((bf16[64,1792]{1,0:T(8,128)(2,1)S(1)}, bf16[64,1792]{1,0:T(8,128)(2,1)S(1)}, u32[]{:S(2)}, u32[]{:S(2)}) %collective-permute-start.13) | collective-permute-done | bytes 229408 | tf_op jit(solution)/shard_map/ppermute | solution.py:16
  90.1 2.8 %shard_map.69 = f32[2,64,512]{2,1,0:T(8,128)S(1)} custom-call(bf16[64,1024]{1,0:T(8,128)(2,1)S(1)} %maximum_select_fusion.6.a_ref, bf16[7168,1024]{1,0:T(8,128)(2,1)} %e_ref.11, bf16[2,7168,1024]{2,1,0:T(8,128)(2,1)} %q_ref.11), custom_call_target="tpu_custom_call" | custom-call | flops 134217728 | bytes 3407872 | tf_op jit(solution)/shard_map/pallas_call | solution.py:104
  94.4 3.3 %collective-permute-done.15 = f32[2,64]{1,0:T(2,128)S(1)} collective-permute-done((f32[2,64]{1,0:T(2,128)S(1)}, f32[2,64]{1,0:T(2,128)S(1)}, u32[]{:S(2)}, u32[]{:S(2)}) %collective-permute-start.15) | collective-permute-done | bytes 544 | tf_op jit(solution)/shard_map/ppermute | solution.py:16
  97.7 2.9 %collective-permute-start.16 = (f32[2,64]{1,0:T(2,128)S(1)}, f32[2,64]{1,0:T(2,128)S(1)}, u32[]{:S(2)}, u32[]{:S(2)}) collective-permute-start(f32[2,64]{1,0:T(2,128)S(1)} %add.91), channel_id=1, source_target_pairs={{0,2},{1,3},{2,0},{3,1},{4,6},{5,7},{6,4},{7,5},{8,10},{9,11},{10,... | collective-permute-start | bytes 1544 | tf_op jit(solution)/shard_map/ppermute | solution.py:16
  100.6 1.6 %collective-permute-done.16 = f32[2,64]{1,0:T(2,128)S(1)} collective-permute-done((f32[2,64]{1,0:T(2,128)S(1)}, f32[2,64]{1,0:T(2,128)S(1)}, u32[]{:S(2)}, u32[]{:S(2)}) %collective-permute-start.16) | collective-permute-done | bytes 544 | tf_op jit(solution)/shard_map/ppermute | solution.py:16
  102.1 1.1 %collective-permute-done.17 = f32[2,64]{1,0:T(2,128)S(1)} collective-permute-done((f32[2,64]{1,0:T(2,128)S(1)}, f32[2,64]{1,0:T(2,128)S(1)}, u32[]{:S(2)}, u32[]{:S(2)}) %collective-permute-start.17) | collective-permute-done | bytes 544 | tf_op jit(solution)/shard_map/ppermute | solution.py:16
  103.8 3.0 %collective-permute-done.18 = f32[2,64]{1,0:T(2,128)S(1)} collective-permute-done((f32[2,64]{1,0:T(2,128)S(1)}, f32[2,64]{1,0:T(2,128)S(1)}, u32[]{:S(2)}, u32[]{:S(2)}) %collective-permute-start.18) | collective-permute-done | bytes 544 | tf_op jit(solution)/shard_map/ppermute | solution.py:16
  107.9 2.6 %collective-permute-done.19 = f32[2,64]{1,0:T(2,128)S(1)} collective-permute-done((f32[2,64]{1,0:T(2,128)S(1)}, f32[2,64]{1,0:T(2,128)S(1)}, u32[]{:S(2)}, u32[]{:S(2)}) %collective-permute-start.19) | collective-permute-done | bytes 544 | tf_op jit(solution)/shard_map/ppermute | solution.py:16
  (52 shorter events, 8.7 us)
Async XLA Ops:
  0.0 1.5 %collective-permute-start = (bf16[8,2048]{1,0:T(8,128)(2,1)}, bf16[8,2048]{1,0:T(8,128)(2,1)S(1)}, u32[]{:S(2)}, u32[]{:S(2)}) collective-permute-start(bf16[8,2048]{1,0:T(8,128)(2,1)} %param.7), channel_id=1, source_target_pairs={{0,4},{4,0},{8,12},{12,8},{16,20},{20,16},{24,28},{28,24},{1,5},{5... | collective-permute-start | bytes 98312 | tf_op jit(solution)/shard_map/ppermute | solution.py:16
  2.4 5.5 %collective-permute-start.1 = (bf16[16,2048]{1,0:T(8,128)(2,1)S(1)}, bf16[16,2048]{1,0:T(8,128)(2,1)S(1)}, u32[]{:S(2)}, u32[]{:S(2)}) collective-permute-start(bf16[16,2048]{1,0:T(8,128)(2,1)S(1)} %maximum_select_fusion.7), channel_id=1, source_target_pairs={{0,8},{4,12},{8,0},{12,4},{16,24},{20,28},{24,16},{28,20},{1,9},{5... | collective-permute-start | bytes 196616 | tf_op jit(solution)/shard_map/ppermute | solution.py:16
  5.3 8.5 %collective-permute-start.4 = (bf16[1,16,3584]{2,1,0:T(8,128)(2,1)}, bf16[1,16,3584]{2,1,0:T(8,128)(2,1)S(1)}, u32[]{:S(2)}, u32[]{:S(2)}) collective-permute-start(bf16[1,16,3584]{2,1,0:T(8,128)(2,1)} %bitcast.27), channel_id=1, source_target_pairs={{0,2},{1,3},{2,0},{3,1},{4,6},{5,7},{6,4},{7,5},{8,10},{9,11},{10,... | collective-permute-start | bytes 344072 | tf_op jit(solution)/shard_map/ppermute | solution.py:16
  7.9 7.7 %collective-permute-start.2 = (bf16[32,2048]{1,0:T(8,128)(2,1)S(1)}, bf16[32,2048]{1,0:T(8,128)(2,1)S(1)}, u32[]{:S(2)}, u32[]{:S(2)}) collective-permute-start(bf16[32,2048]{1,0:T(8,128)(2,1)S(1)} %maximum_select_fusion.5), channel_id=1, source_target_pairs={{0,16},{4,20},{8,24},{12,28},{16,0},{20,4},{24,8},{28,12},{1,17},{... | collective-permute-start | bytes 393224 | tf_op jit(solution)/shard_map/ppermute | solution.py:16
  14.7 6.9 %collective-permute-start.5 = (bf16[2,16,3584]{2,1,0:T(8,128)(2,1)S(1)}, bf16[2,16,3584]{2,1,0:T(8,128)(2,1)S(1)}, u32[]{:S(2)}, u32[]{:S(2)}) collective-permute-start(bf16[2,16,3584]{2,1,0:T(8,128)(2,1)S(1)} %maximum_bitcast_fusion), channel_id=1, source_target_pairs={{0,1},{1,0},{2,3},{3,2},{4,5},{5,4},{6,7},{7,6},{8,9},{9,8},{10,11... | collective-permute-start | bytes 688136 | tf_op jit(solution)/shard_map/ppermute | solution.py:16
  18.6 5.5 %collective-permute-start.3 = (f32[64,512]{1,0:T(8,128)S(1)}, f32[64,512]{1,0:T(8,128)S(1)}, u32[]{:S(2)}, u32[]{:S(2)}) collective-permute-start(f32[64,512]{1,0:T(8,128)S(1)} %slice_select_fusion.2), channel_id=1, source_target_pairs={{0,1},{1,0},{2,3},{3,2},{4,5},{5,4},{6,7},{7,6},{8,9},{9,8},{10,11... | collective-permute-start | bytes 393224 | tf_op jit(solution)/shard_map/ppermute | solution.py:16
  24.2 11.3 %collective-permute-start.6 = (f32[64,256]{1,0:T(8,128)S(1)}, f32[64,256]{1,0:T(8,128)S(1)}, u32[]{:S(2)}, u32[]{:S(2)}) collective-permute-start(f32[64,256]{1,0:T(8,128)S(1)} %slice_select_fusion.3), channel_id=1, source_target_pairs={{0,2},{1,3},{2,0},{3,1},{4,6},{5,7},{6,4},{7,5},{8,10},{9,11},{10,... | collective-permute-start | bytes 196616 | tf_op jit(solution)/shard_map/ppermute | solution.py:16
  35.6 7.4 %collective-permute-start.7 = (bf16[64,256]{1,0:T(8,128)(2,1)S(1)}, bf16[64,256]{1,0:T(8,128)(2,1)S(1)}, u32[]{:S(2)}, u32[]{:S(2)}) collective-permute-start(bf16[64,256]{1,0:T(8,128)(2,1)S(1)} %add_convert_fusion.1), channel_id=1, source_target_pairs={{0,2},{1,3},{2,0},{3,1},{4,6},{5,7},{6,4},{7,5},{8,10},{9,11},{10,... | collective-permute-start | bytes 98312 | tf_op jit(solution)/shard_map/ppermute | solution.py:16
  43.0 9.6 %collective-permute-start.8 = (bf16[64,512]{1,0:T(8,128)(2,1)S(1)}, bf16[64,512]{1,0:T(8,128)(2,1)S(1)}, u32[]{:S(2)}, u32[]{:S(2)}) collective-permute-start(bf16[64,512]{1,0:T(8,128)(2,1)S(1)} %maximum_select_fusion.8), channel_id=1, source_target_pairs={{0,1},{1,0},{2,3},{3,2},{4,5},{5,4},{6,7},{7,6},{8,9},{9,8},{10,11... | collective-permute-start | bytes 196616 | tf_op jit(solution)/shard_map/ppermute | solution.py:16
  52.8 3.9 %collective-permute-start.9 = (f32[64,3584]{1,0:T(8,128)S(1)}, f32[64,3584]{1,0:T(8,128)}, u32[]{:S(2)}, u32[]{:S(2)}) collective-permute-start(f32[64,3584]{1,0:T(8,128)S(1)} %fusion.6), channel_id=1, source_target_pairs={{0,4},{4,0},{8,12},{12,8},{16,20},{20,16},{24,28},{28,24},{1,5},{5... | collective-permute-start | bytes 2752520 | tf_op jit(solution)/shard_map/ppermute | solution.py:16
  58.1 13.0 %collective-permute-start.10 = (f32[64,1792]{1,0:T(8,128)S(1)}, f32[64,1792]{1,0:T(8,128)S(1)}, u32[]{:S(2)}, u32[]{:S(2)}) collective-permute-start(f32[64,1792]{1,0:T(8,128)S(1)} %slice_select_fusion), channel_id=1, source_target_pairs={{0,8},{4,12},{8,0},{12,4},{16,24},{20,28},{24,16},{28,20},{1,9},{5... | collective-permute-start | bytes 1376264 | tf_op jit(solution)/shard_map/ppermute | solution.py:16
  71.1 7.3 %collective-permute-start.11 = (f32[64,896]{1,0:T(8,128)S(1)}, f32[64,896]{1,0:T(8,128)S(1)}, u32[]{:S(2)}, u32[]{:S(2)}) collective-permute-start(f32[64,896]{1,0:T(8,128)S(1)} %slice_select_fusion.1), channel_id=1, source_target_pairs={{0,16},{4,20},{8,24},{12,28},{16,0},{20,4},{24,8},{28,12},{1,17},{... | collective-permute-start | bytes 688136 | tf_op jit(solution)/shard_map/ppermute | solution.py:16
  78.4 5.4 %collective-permute-start.12 = (bf16[64,896]{1,0:T(8,128)(2,1)S(1)}, bf16[64,896]{1,0:T(8,128)(2,1)S(1)}, u32[]{:S(2)}, u32[]{:S(2)}) collective-permute-start(bf16[64,896]{1,0:T(8,128)(2,1)S(1)} %add_convert_fusion), channel_id=1, source_target_pairs={{0,16},{4,20},{8,24},{12,28},{16,0},{20,4},{24,8},{28,12},{1,17},{... | collective-permute-start | bytes 344072 | tf_op jit(solution)/shard_map/ppermute | solution.py:16
  83.9 6.1 %collective-permute-start.13 = (bf16[64,1792]{1,0:T(8,128)(2,1)S(1)}, bf16[64,1792]{1,0:T(8,128)(2,1)S(1)}, u32[]{:S(2)}, u32[]{:S(2)}) collective-permute-start(bf16[64,1792]{1,0:T(8,128)(2,1)S(1)} %maximum_select_fusion.4), channel_id=1, source_target_pairs={{0,8},{4,12},{8,0},{12,4},{16,24},{20,28},{24,16},{28,20},{1,9},{5... | collective-permute-start | bytes 688136 | tf_op jit(solution)/shard_map/ppermute | solution.py:16
  90.1 2.9 %collective-permute-start.14 = (bf16[64,3584]{1,0:T(8,128)(2,1)S(1)}, bf16[64,3584]{1,0:T(8,128)(2,1)S(1)}, u32[]{:S(2)}, u32[]{:S(2)}) collective-permute-start(bf16[64,3584]{1,0:T(8,128)(2,1)S(1)} %maximum_select_fusion.1), channel_id=1, source_target_pairs={{0,4},{4,0},{8,12},{12,8},{16,20},{20,16},{24,28},{28,24},{1,5},{5... | collective-permute-start | bytes 1376264 | tf_op jit(solution)/shard_map/ppermute | solution.py:16
  94.0 3.6 %collective-permute-start.15 = (f32[2,64]{1,0:T(2,128)S(1)}, f32[2,64]{1,0:T(2,128)S(1)}, u32[]{:S(2)}, u32[]{:S(2)}) collective-permute-start(f32[2,64]{1,0:T(2,128)S(1)} %add_add_fusion), channel_id=1, source_target_pairs={{0,1},{1,0},{2,3},{3,2},{4,5},{5,4},{6,7},{7,6},{8,9},{9,8},{10,11... | collective-permute-start | bytes 1544 | tf_op jit(solution)/shard_map/ppermute | solution.py:16
  97.7 4.5 %collective-permute-start.16 = (f32[2,64]{1,0:T(2,128)S(1)}, f32[2,64]{1,0:T(2,128)S(1)}, u32[]{:S(2)}, u32[]{:S(2)}) collective-permute-start(f32[2,64]{1,0:T(2,128)S(1)} %add.91), channel_id=1, source_target_pairs={{0,2},{1,3},{2,0},{3,1},{4,6},{5,7},{6,4},{7,5},{8,10},{9,11},{10,... | collective-permute-start | bytes 1544 | tf_op jit(solution)/shard_map/ppermute | solution.py:16
  102.1 1.1 %collective-permute-start.17 = (f32[2,64]{1,0:T(2,128)S(1)}, f32[2,64]{1,0:T(2,128)S(1)}, u32[]{:S(2)}, u32[]{:S(2)}) collective-permute-start(f32[2,64]{1,0:T(2,128)S(1)} %add.92), channel_id=1, source_target_pairs={{0,4},{4,0},{8,12},{12,8},{16,20},{20,16},{24,28},{28,24},{1,5},{5... | collective-permute-start | bytes 1544 | tf_op jit(solution)/shard_map/ppermute | solution.py:16
  103.3 3.6 %collective-permute-start.18 = (f32[2,64]{1,0:T(2,128)S(1)}, f32[2,64]{1,0:T(2,128)S(1)}, u32[]{:S(2)}, u32[]{:S(2)}) collective-permute-start(f32[2,64]{1,0:T(2,128)S(1)} %add.93), channel_id=1, source_target_pairs={{0,8},{4,12},{8,0},{12,4},{16,24},{20,28},{24,16},{28,20},{1,9},{5... | collective-permute-start | bytes 1544 | tf_op jit(solution)/shard_map/ppermute | solution.py:16
  106.9 3.6 %collective-permute-start.19 = (f32[2,64]{1,0:T(2,128)S(1)}, f32[2,64]{1,0:T(2,128)S(1)}, u32[]{:S(2)}, u32[]{:S(2)}) collective-permute-start(f32[2,64]{1,0:T(2,128)S(1)} %add.94), channel_id=1, source_target_pairs={{0,16},{4,20},{8,24},{12,28},{16,0},{20,4},{24,8},{28,12},{1,17},{... | collective-permute-start | bytes 1544 | tf_op jit(solution)/shard_map/ppermute | solution.py:16

commit v8 on v7

--- a/solution.py
+++ b/solution.py
@@ -41,43 +41,52 @@
     return y.reshape((n * x.shape[0],) + x.shape[1:])
 
 
-def _allreduce_bf16(x, axis, n, dim, works=()):
+def _allreduce_bf16(x, axis, n, dim, works=(), paths=1):
     me = lax.axis_index(axis)
+    bits = []
+    b = 1
+    while b < n:
+        bits.append(b)
+        b *= 2
+    orders = [bits, bits[:1] + bits[:0:-1]][:paths]
     works = list(works)
     done = []
 
-    def swap(v, b):
-        if not works:
-            return _swap(v, axis, n, b)
-        work, arg = works.pop(0)
+    def swap(vs, bs):
+        work, arg = works.pop(0) if works else (None, None)
         if work is None:
-            return _swap(v, axis, n, b)
-        v, arg = lax.optimization_barrier((v, arg))
+            return [_swap(v, axis, n, b) for v, b in zip(vs, bs)]
+        *vs, arg = lax.optimization_barrier((*vs, arg))
         result = work(arg)
-        other = _swap(v, axis, n, b)
-        other, result = lax.optimization_barrier((other, result))
+        others = [_swap(v, axis, n, b) for v, b in zip(vs, bs)]
+        *others, result = lax.optimization_barrier((*others, result))
         done.append(result)
-        return other
+        return others
 
-    b = 1
-    while b < n:
-        half = x.shape[dim] // 2
-        upper = (me // b) % 2 == 1
-        lo = lax.slice_in_dim(x, 0, half, axis=dim)
-        hi = lax.slice_in_dim(x, half, 2 * half, axis=dim)
-        keep = jnp.where(upper, hi, lo)
-        send = jnp.where(upper, lo, hi)
-        x = keep + swap(send, b)
-        b *= 2
-    x = x.astype(BF16)
-    b = n // 2
-    while b >= 1:
-        other = swap(x, b)
-        first = (me // b) % 2 == 0
-        x = jnp.where(first, jnp.concatenate([x, other], dim), jnp.concatenate([other, x], dim))
-        b //= 2
+    w = x.shape[dim] // len(orders)
+    xs = [lax.slice_in_dim(x, p * w, (p + 1) * w, axis=dim) for p in range(len(orders))]
+    for r in range(len(bits)):
+        keeps, sends = [], []
+        for p, v in enumerate(xs):
+            b = orders[p][r]
+            half = v.shape[dim] // 2
+            upper = (me // b) % 2 == 1
+            lo = lax.slice_in_dim(v, 0, half, axis=dim)
+            hi = lax.slice_in_dim(v, half, 2 * half, axis=dim)
+            keeps.append(jnp.where(upper, hi, lo))
+            sends.append(jnp.where(upper, lo, hi))
+        others = swap(sends, [o[r] for o in orders])
+        xs = [k + o for k, o in zip(keeps, others)]
+    xs = [v.astype(BF16) for v in xs]
+    for r in reversed(range(len(bits))):
+        others = swap(xs, [o[r] for o in orders])
+        new = []
+        for p, (v, other) in enumerate(zip(xs, others)):
+            first = (me // orders[p][r]) % 2 == 0
+            new.append(jnp.where(first, jnp.concatenate([v, other], dim), jnp.concatenate([other, v], dim)))
+        xs = new
     done += [work(arg) for work, arg in works if work is not None]
-    return x, done
+    return jnp.concatenate(xs, dim) if len(xs) > 1 else xs[0], done
 
 
 def _allreduce_small(x, axis, n):
@@ -147,7 +156,7 @@
         (functools.partial(lambda a, t0, t1: _lifted(a, eigenvalues, queries, t0, t1, tk), t0=t0, t1=t1), act_rot)
         for t0, t1 in spans
     ]
-    grad_rot, lifted = _allreduce_bf16(grad_part, "row", nr, 1, works)
+    grad_rot, lifted = _allreduce_bf16(grad_part, "row", nr, 1, works, paths=2)
     partial = None
     for (t0, t1), piece in zip(spans, lifted):
         g = grad_rot[:, t0 * tk : t1 * tk].astype(F32)

time: 111 us -> 109 us (0.982)
  waiting for transfers between devices: 28.4 us -> 20.8 us
  starting transfers between devices: 24.4 us -> 30 us
    ppermute x20 -> x26, waiting for transfers between devices: 28.4 us -> 20.8 us  [_swap(): return lax.ppermute(x, axis, [(i, i ^ b) for i in range(n)])]
    ppermute x20 -> x26, starting transfers between devices: 24.4 us -> 30 us  [_swap(): return lax.ppermute(x, axis, [(i, i ^ b) for i in range(n)])]
    add x3 -> x4, other arithmetic: 1.4 us -> 0.23 us  [_allreduce_bf16(): xs = [k + o for k, o in zip(keeps, others)]]
  transfers between devices with their start and end apart: 20 -> 26, of which waited for: 12 -> 10; matrix products, arithmetic and copies ran while one was open for 25% -> 25% of each run, Pallas kernels for 24% -> 24%
where the time goes in v8:
time: 109 us
  starting transfers between devices  30 us (28%)
  Pallas kernels  26.3 us (24%)
  matrix products  26.1 us (24%)
  waiting for transfers between devices  20.8 us (19%)
  other arithmetic  5.59 us (5%)
    ppermute x26, starting transfers between devices, _swap(): return lax.ppermute(x, axis, [(i, i ^ b) for i in range(n)])  30 us
    pallas_call x6, Pallas kernels, _lifted(): pl.pallas_call(_lifted_kernel, grid=(t1 - t0,), in_specs=[pl.BlockSpec((t...  26.3 us
    dot_general x3, matrix products, local(): jnp.dot(g, out_basis[:, c0:c1], preferred_element_type=F32)  23.1 us
    ppermute x26, waiting for transfers between devices, _swap(): return lax.ppermute(x, axis, [(i, i ^ b) for i in range(n)])  20.8 us
    dot_general x1, matrix products, local(): act_part = jnp.dot(acts_all, in_basis, preferred_element_type=F32)  3.03 us
  transfers between devices with their start and end apart: 26, of which 10 were waited for; matrix products, arithmetic and copies ran while one was open for 25% of the time, Pallas kernels for 24%

profile of v8, /device:TPU:0, one launch (start us, length us, event | category | flops | bytes accessed | tf_op | source)
XLA Modules:
  0.0 109.2 jit_solution(8774099664768114925)
XLA Ops:
  0.5 1.1 collective-permute-done
  2.4 2.9 %collective-permute-start.1 = (bf16[16,2048]{1,0:T(8,128)(2,1)S(1)}, bf16[16,2048]{1,0:T(8,128)(2,1)S(1)}, u32[]{:S(2)}, u32[]{:S(2)}) collective-permute-start(bf16[16,2048]{1,0:T(8,128)(2,1)S(1)} %maximum_select_fusion.10), channel_id=1, source_target_pairs={{0,8},{4,12},{8,0},{12,4},{16,24},{20,28},{24,16},{28,20},{1,9},{5... | collective-permute-start | bytes 196616 | tf_op jit(solution)/shard_map/ppermute | solution.py:16
  5.3 2.6 %collective-permute-start.4 = (bf16[1,16,3584]{2,1,0:T(8,128)(2,1)}, bf16[1,16,3584]{2,1,0:T(8,128)(2,1)S(1)}, u32[]{:S(2)}, u32[]{:S(2)}) collective-permute-start(bf16[1,16,3584]{2,1,0:T(8,128)(2,1)} %bitcast.27), channel_id=1, source_target_pairs={{0,2},{1,3},{2,0},{3,1},{4,6},{5,7},{6,4},{7,5},{8,10},{9,11},{10,... | collective-permute-start | bytes 344072 | tf_op jit(solution)/shard_map/ppermute | solution.py:16
  7.9 1.8 %collective-permute-start.2 = (bf16[32,2048]{1,0:T(8,128)(2,1)S(1)}, bf16[32,2048]{1,0:T(8,128)(2,1)S(1)}, u32[]{:S(2)}, u32[]{:S(2)}) collective-permute-start(bf16[32,2048]{1,0:T(8,128)(2,1)S(1)} %maximum_select_fusion.6), channel_id=1, source_target_pairs={{0,16},{4,20},{8,24},{12,28},{16,0},{20,4},{24,8},{28,12},{1,17},{... | collective-permute-start | bytes 393224 | tf_op jit(solution)/shard_map/ppermute | solution.py:16
  9.7 4.1 %collective-permute-done.4 = bf16[1,16,3584]{2,1,0:T(8,128)(2,1)S(1)} collective-permute-done((bf16[1,16,3584]{2,1,0:T(8,128)(2,1)}, bf16[1,16,3584]{2,1,0:T(8,128)(2,1)S(1)}, u32[]{:S(2)}, u32[]{:S(2)}) %collective-permute-start.4) | collective-permute-done | bytes 114720 | tf_op jit(solution)/shard_map/ppermute | solution.py:16
  15.6 3.0 %fusion.6 = f32[64,1024]{1,0:T(8,128)S(1)} fusion(bf16[2048,1024]{1,0:T(8,128)(2,1)} %param.9, bf16[32,2048]{1,0:T(8,128)(2,1)S(1)} %collective-permute-done.2, bf16[32,2048]{1,0:T(8,128)(2,1)S(1)} %maximum_select_fusion.6, pred[]{:T(512)S(6)} %eq.66), kind=kOutput, calls=%fused_computation.22 | convolution fusion | flops 269615104 | bytes 4718593 | tf_op jit(solution)/shard_map/dot_general | solution.py:137
  18.6 1.3 %collective-permute-start.3 = (f32[64,512]{1,0:T(8,128)S(1)}, f32[64,512]{1,0:T(8,128)S(1)}, u32[]{:S(2)}, u32[]{:S(2)}) collective-permute-start(f32[64,512]{1,0:T(8,128)S(1)} %slice_select_fusion.6), channel_id=1, source_target_pairs={{0,1},{1,0},{2,3},{3,2},{4,5},{5,4},{6,7},{7,6},{8,9},{9,8},{10,11... | collective-permute-start | bytes 393224 | tf_op jit(solution)/shard_map/ppermute | solution.py:16
  20.0 1.6 %collective-permute-done.5 = bf16[2,16,3584]{2,1,0:T(8,128)(2,1)S(1)} collective-permute-done((bf16[2,16,3584]{2,1,0:T(8,128)(2,1)S(1)}, bf16[2,16,3584]{2,1,0:T(8,128)(2,1)S(1)}, u32[]{:S(2)}, u32[]{:S(2)}) %collective-permute-start.5) | collective-permute-done | bytes 229408 | tf_op jit(solution)/shard_map/ppermute | solution.py:16
  21.7 2.5 %collective-permute-done.3 = f32[64,512]{1,0:T(8,128)S(1)} collective-permute-done((f32[64,512]{1,0:T(8,128)S(1)}, f32[64,512]{1,0:T(8,128)S(1)}, u32[]{:S(2)}, u32[]{:S(2)}) %collective-permute-start.3) | collective-permute-done | bytes 131104 | tf_op jit(solution)/shard_map/ppermute | solution.py:16
  24.2 3.3 %collective-permute-start.6 = (f32[64,256]{1,0:T(8,128)S(1)}, f32[64,256]{1,0:T(8,128)S(1)}, u32[]{:S(2)}, u32[]{:S(2)}) collective-permute-start(f32[64,256]{1,0:T(8,128)S(1)} %slice_select_fusion.7), channel_id=1, source_target_pairs={{0,2},{1,3},{2,0},{3,1},{4,6},{5,7},{6,4},{7,5},{8,10},{9,11},{10,... | collective-permute-start | bytes 196616 | tf_op jit(solution)/shard_map/ppermute | solution.py:16
  27.6 8.0 %fusion.2 = f32[64,2432]{1,0:T(8,128)S(1)} fusion(bf16[64,3584]{1,0:T(8,128)(2,1)S(1)} %bitcast.24, bf16[3584,7168]{1,0:T(8,128)(2,1)} %param.8), kind=kOutput, calls=%fused_computation.2 | convolution fusion | flops 1115684864 | bytes 18513920 | tf_op jit(solution)/shard_map/dot_general | solution.py:141
  35.7 7.3 %fusion.4 = f32[64,2304]{1,0:T(8,128)S(1)} fusion(bf16[64,3584]{1,0:T(8,128)(2,1)S(1)} %bitcast.25, bf16[3584,7168]{1,0:T(8,128)(2,1)} %param.8), kind=kOutput, calls=%fused_computation.4 | convolution fusion | flops 1056964608 | bytes 17563648 | tf_op jit(solution)/shard_map/dot_general | solution.py:141
  43.0 1.8 %collective-permute-start.8 = (bf16[64,512]{1,0:T(8,128)(2,1)S(1)}, bf16[64,512]{1,0:T(8,128)(2,1)S(1)}, u32[]{:S(2)}, u32[]{:S(2)}) collective-permute-start(bf16[64,512]{1,0:T(8,128)(2,1)S(1)} %maximum_select_fusion.11), channel_id=1, source_target_pairs={{0,1},{1,0},{2,3},{3,2},{4,5},{5,4},{6,7},{7,6},{8,9},{9,8},{10,11... | collective-permute-start | bytes 196616 | tf_op jit(solution)/shard_map/ppermute | solution.py:16
  44.8 7.8 %fusion = f32[64,2432]{1,0:T(8,128)S(1)} fusion(bf16[64,3584]{1,0:T(8,128)(2,1)S(1)} %bitcast.26, bf16[3584,7168]{1,0:T(8,128)(2,1)} %param.8), kind=kOutput, calls=%fused_computation | convolution fusion | flops 1115684864 | bytes 18513920 | tf_op jit(solution)/shard_map/dot_general | solution.py:141
  54.1 3.8 %shard_map.64 = f32[2,64,1024]{2,1,0:T(8,128)S(1)} custom-call(bf16[64,1024]{1,0:T(8,128)(2,1)S(1)} %maximum_select_fusion.7.a_ref, bf16[7168,1024]{1,0:T(8,128)(2,1)} %e_ref.11, bf16[2,7168,1024]{2,1,0:T(8,128)(2,1)} %q_ref.11), custom_call_target="tpu_custom_call" | custom-call | flops 268435456 | bytes 6815744 | tf_op jit(solution)/shard_map/pallas_call | solution.py:113
  58.7 1.5 %collective-permute-start.12 = (f32[64,896]{1,0:T(8,128)S(1)}, f32[64,896]{1,0:T(8,128)S(1)}, u32[]{:S(2)}, u32[]{:S(2)}) collective-permute-start(f32[64,896]{1,0:T(8,128)S(1)} %slice_select_fusion.2), channel_id=1, source_target_pairs={{0,16},{4,20},{8,24},{12,28},{16,0},{20,4},{24,8},{28,12},{1,17},{... | collective-permute-start | bytes 688136 | tf_op jit(solution)/shard_map/ppermute | solution.py:16
  60.2 8.5 %shard_map.65 = f32[2,64,2560]{2,1,0:T(8,128)S(1)} custom-call(bf16[64,1024]{1,0:T(8,128)(2,1)S(1)} %maximum_select_fusion.7.a_ref, bf16[7168,1024]{1,0:T(8,128)(2,1)} %e_ref.11, bf16[2,7168,1024]{2,1,0:T(8,128)(2,1)} %q_ref.11), custom_call_target="tpu_custom_call" | custom-call | flops 671088640 | bytes 17039360 | tf_op jit(solution)/shard_map/pallas_call | solution.py:113
  69.6 1.5 %collective-permute-start.14 = (f32[64,448]{1,0:T(8,128)S(1)}, f32[64,448]{1,0:T(8,128)S(1)}, u32[]{:S(2)}, u32[]{:S(2)}) collective-permute-start(f32[64,448]{1,0:T(8,128)S(1)} %slice_select_fusion.4), channel_id=1, source_target_pairs={{0,8},{4,12},{8,0},{12,4},{16,24},{20,28},{24,16},{28,20},{1,9},{5... | collective-permute-start | bytes 344072 | tf_op jit(solution)/shard_map/ppermute | solution.py:16
  71.1 3.8 %shard_map.66 = f32[2,64,1024]{2,1,0:T(8,128)S(1)} custom-call(bf16[64,1024]{1,0:T(8,128)(2,1)S(1)} %maximum_select_fusion.7.a_ref, bf16[7168,1024]{1,0:T(8,128)(2,1)} %e_ref.11, bf16[2,7168,1024]{2,1,0:T(8,128)(2,1)} %q_ref.11), custom_call_target="tpu_custom_call" | custom-call | flops 268435456 | bytes 6815744 | tf_op jit(solution)/shard_map/pallas_call | solution.py:113
  75.1 1.6 %collective-permute-start.15 = (bf16[64,448]{1,0:T(8,128)(2,1)S(1)}, bf16[64,448]{1,0:T(8,128)(2,1)S(1)}, u32[]{:S(2)}, u32[]{:S(2)}) collective-permute-start(bf16[64,448]{1,0:T(8,128)(2,1)S(1)} %add_convert_fusion.1), channel_id=1, source_target_pairs={{0,16},{4,20},{8,24},{12,28},{16,0},{20,4},{24,8},{28,12},{1,17},{... | collective-permute-start | bytes 172040 | tf_op jit(solution)/shard_map/ppermute | solution.py:16
  76.7 1.2 %collective-permute-start.16 = (bf16[64,448]{1,0:T(8,128)(2,1)S(1)}, bf16[64,448]{1,0:T(8,128)(2,1)S(1)}, u32[]{:S(2)}, u32[]{:S(2)}) collective-permute-start(bf16[64,448]{1,0:T(8,128)(2,1)S(1)} %add_convert_fusion), channel_id=1, source_target_pairs={{0,8},{4,12},{8,0},{12,4},{16,24},{20,28},{24,16},{28,20},{1,9},{5... | collective-permute-start | bytes 172040 | tf_op jit(solution)/shard_map/ppermute | solution.py:16
  77.8 3.8 %shard_map.67 = f32[2,64,1024]{2,1,0:T(8,128)S(1)} custom-call(bf16[64,1024]{1,0:T(8,128)(2,1)S(1)} %maximum_select_fusion.7.a_ref, bf16[7168,1024]{1,0:T(8,128)(2,1)} %e_ref.11, bf16[2,7168,1024]{2,1,0:T(8,128)(2,1)} %q_ref.11), custom_call_target="tpu_custom_call" | custom-call | flops 268435456 | bytes 6815744 | tf_op jit(solution)/shard_map/pallas_call | solution.py:113
  83.3 3.8 %shard_map.68 = f32[2,64,1024]{2,1,0:T(8,128)S(1)} custom-call(bf16[64,1024]{1,0:T(8,128)(2,1)S(1)} %maximum_select_fusion.7.a_ref, bf16[7168,1024]{1,0:T(8,128)(2,1)} %e_ref.11, bf16[2,7168,1024]{2,1,0:T(8,128)(2,1)} %q_ref.11), custom_call_target="tpu_custom_call" | custom-call | flops 268435456 | bytes 6815744 | tf_op jit(solution)/shard_map/pallas_call | solution.py:113
  88.3 2.8 %shard_map.69 = f32[2,64,512]{2,1,0:T(8,128)S(1)} custom-call(bf16[64,1024]{1,0:T(8,128)(2,1)S(1)} %maximum_select_fusion.7.a_ref, bf16[7168,1024]{1,0:T(8,128)(2,1)} %e_ref.11, bf16[2,7168,1024]{2,1,0:T(8,128)(2,1)} %q_ref.11), custom_call_target="tpu_custom_call" | custom-call | flops 134217728 | bytes 3407872 | tf_op jit(solution)/shard_map/pallas_call | solution.py:113
  92.6 3.3 %collective-permute-done.21 = f32[2,64]{1,0:T(2,128)S(1)} collective-permute-done((f32[2,64]{1,0:T(2,128)S(1)}, f32[2,64]{1,0:T(2,128)S(1)}, u32[]{:S(2)}, u32[]{:S(2)}) %collective-permute-start.21) | collective-permute-done | bytes 544 | tf_op jit(solution)/shard_map/ppermute | solution.py:16
  95.9 2.9 %collective-permute-start.22 = (f32[2,64]{1,0:T(2,128)S(1)}, f32[2,64]{1,0:T(2,128)S(1)}, u32[]{:S(2)}, u32[]{:S(2)}) collective-permute-start(f32[2,64]{1,0:T(2,128)S(1)} %add.109), channel_id=1, source_target_pairs={{0,2},{1,3},{2,0},{3,1},{4,6},{5,7},{6,4},{7,5},{8,10},{9,11},{10,... | collective-permute-start | bytes 1544 | tf_op jit(solution)/shard_map/ppermute | solution.py:16
  98.8 1.6 %collective-permute-done.22 = f32[2,64]{1,0:T(2,128)S(1)} collective-permute-done((f32[2,64]{1,0:T(2,128)S(1)}, f32[2,64]{1,0:T(2,128)S(1)}, u32[]{:S(2)}, u32[]{:S(2)}) %collective-permute-start.22) | collective-permute-done | bytes 544 | tf_op jit(solution)/shard_map/ppermute | solution.py:16
  100.4 1.1 %collective-permute-done.23 = f32[2,64]{1,0:T(2,128)S(1)} collective-permute-done((f32[2,64]{1,0:T(2,128)S(1)}, f32[2,64]{1,0:T(2,128)S(1)}, u32[]{:S(2)}, u32[]{:S(2)}) %collective-permute-start.23) | collective-permute-done | bytes 544 | tf_op jit(solution)/shard_map/ppermute | solution.py:16
  101.5 1.2 %collective-permute-start.24 = (f32[2,64]{1,0:T(2,128)S(1)}, f32[2,64]{1,0:T(2,128)S(1)}, u32[]{:S(2)}, u32[]{:S(2)}) collective-permute-start(f32[2,64]{1,0:T(2,128)S(1)} %add.111), channel_id=1, source_target_pairs={{0,8},{4,12},{8,0},{12,4},{16,24},{20,28},{24,16},{28,20},{1,9},{5... | collective-permute-start | bytes 1544 | tf_op jit(solution)/shard_map/ppermute | solution.py:16
  102.7 2.4 %collective-permute-done.24 = f32[2,64]{1,0:T(2,128)S(1)} collective-permute-done((f32[2,64]{1,0:T(2,128)S(1)}, f32[2,64]{1,0:T(2,128)S(1)}, u32[]{:S(2)}, u32[]{:S(2)}) %collective-permute-start.24) | collective-permute-done | bytes 544 | tf_op jit(solution)/shard_map/ppermute | solution.py:16
  105.1 1.0 collective-permute-start.25
  106.1 2.5 %collective-permute-done.25 = f32[2,64]{1,0:T(2,128)S(1)} collective-permute-done((f32[2,64]{1,0:T(2,128)S(1)}, f32[2,64]{1,0:T(2,128)S(1)}, u32[]{:S(2)}, u32[]{:S(2)}) %collective-permute-start.25) | collective-permute-done | bytes 544 | tf_op jit(solution)/shard_map/ppermute | solution.py:16
  (73 shorter events, 11.6 us)
Async XLA Ops:
  0.0 1.5 %collective-permute-start = (bf16[8,2048]{1,0:T(8,128)(2,1)}, bf16[8,2048]{1,0:T(8,128)(2,1)S(1)}, u32[]{:S(2)}, u32[]{:S(2)}) collective-permute-start(bf16[8,2048]{1,0:T(8,128)(2,1)} %param.7), channel_id=1, source_target_pairs={{0,4},{4,0},{8,12},{12,8},{16,20},{20,16},{24,28},{28,24},{1,5},{5... | collective-permute-start | bytes 98312 | tf_op jit(solution)/shard_map/ppermute | solution.py:16
  2.4 5.5 %collective-permute-start.1 = (bf16[16,2048]{1,0:T(8,128)(2,1)S(1)}, bf16[16,2048]{1,0:T(8,128)(2,1)S(1)}, u32[]{:S(2)}, u32[]{:S(2)}) collective-permute-start(bf16[16,2048]{1,0:T(8,128)(2,1)S(1)} %maximum_select_fusion.10), channel_id=1, source_target_pairs={{0,8},{4,12},{8,0},{12,4},{16,24},{20,28},{24,16},{28,20},{1,9},{5... | collective-permute-start | bytes 196616 | tf_op jit(solution)/shard_map/ppermute | solution.py:16
  5.3 8.5 %collective-permute-start.4 = (bf16[1,16,3584]{2,1,0:T(8,128)(2,1)}, bf16[1,16,3584]{2,1,0:T(8,128)(2,1)S(1)}, u32[]{:S(2)}, u32[]{:S(2)}) collective-permute-start(bf16[1,16,3584]{2,1,0:T(8,128)(2,1)} %bitcast.27), channel_id=1, source_target_pairs={{0,2},{1,3},{2,0},{3,1},{4,6},{5,7},{6,4},{7,5},{8,10},{9,11},{10,... | collective-permute-start | bytes 344072 | tf_op jit(solution)/shard_map/ppermute | solution.py:16
  7.9 7.7 %collective-permute-start.2 = (bf16[32,2048]{1,0:T(8,128)(2,1)S(1)}, bf16[32,2048]{1,0:T(8,128)(2,1)S(1)}, u32[]{:S(2)}, u32[]{:S(2)}) collective-permute-start(bf16[32,2048]{1,0:T(8,128)(2,1)S(1)} %maximum_select_fusion.6), channel_id=1, source_target_pairs={{0,16},{4,20},{8,24},{12,28},{16,0},{20,4},{24,8},{28,12},{1,17},{... | collective-permute-start | bytes 393224 | tf_op jit(solution)/shard_map/ppermute | solution.py:16
  14.7 6.9 %collective-permute-start.5 = (bf16[2,16,3584]{2,1,0:T(8,128)(2,1)S(1)}, bf16[2,16,3584]{2,1,0:T(8,128)(2,1)S(1)}, u32[]{:S(2)}, u32[]{:S(2)}) collective-permute-start(bf16[2,16,3584]{2,1,0:T(8,128)(2,1)S(1)} %maximum_bitcast_fusion), channel_id=1, source_target_pairs={{0,1},{1,0},{2,3},{3,2},{4,5},{5,4},{6,7},{7,6},{8,9},{9,8},{10,11... | collective-permute-start | bytes 688136 | tf_op jit(solution)/shard_map/ppermute | solution.py:16
  18.6 5.5 %collective-permute-start.3 = (f32[64,512]{1,0:T(8,128)S(1)}, f32[64,512]{1,0:T(8,128)S(1)}, u32[]{:S(2)}, u32[]{:S(2)}) collective-permute-start(f32[64,512]{1,0:T(8,128)S(1)} %slice_select_fusion.6), channel_id=1, source_target_pairs={{0,1},{1,0},{2,3},{3,2},{4,5},{5,4},{6,7},{7,6},{8,9},{9,8},{10,11... | collective-permute-start | bytes 393224 | tf_op jit(solution)/shard_map/ppermute | solution.py:16
  24.2 11.3 %collective-permute-start.6 = (f32[64,256]{1,0:T(8,128)S(1)}, f32[64,256]{1,0:T(8,128)S(1)}, u32[]{:S(2)}, u32[]{:S(2)}) collective-permute-start(f32[64,256]{1,0:T(8,128)S(1)} %slice_select_fusion.7), channel_id=1, source_target_pairs={{0,2},{1,3},{2,0},{3,1},{4,6},{5,7},{6,4},{7,5},{8,10},{9,11},{10,... | collective-permute-start | bytes 196616 | tf_op jit(solution)/shard_map/ppermute | solution.py:16
  35.6 7.4 %collective-permute-start.7 = (bf16[64,256]{1,0:T(8,128)(2,1)S(1)}, bf16[64,256]{1,0:T(8,128)(2,1)S(1)}, u32[]{:S(2)}, u32[]{:S(2)}) collective-permute-start(bf16[64,256]{1,0:T(8,128)(2,1)S(1)} %add_convert_fusion.2), channel_id=1, source_target_pairs={{0,2},{1,3},{2,0},{3,1},{4,6},{5,7},{6,4},{7,5},{8,10},{9,11},{10,... | collective-permute-start | bytes 98312 | tf_op jit(solution)/shard_map/ppermute | solution.py:16
  43.0 9.6 %collective-permute-start.8 = (bf16[64,512]{1,0:T(8,128)(2,1)S(1)}, bf16[64,512]{1,0:T(8,128)(2,1)S(1)}, u32[]{:S(2)}, u32[]{:S(2)}) collective-permute-start(bf16[64,512]{1,0:T(8,128)(2,1)S(1)} %maximum_select_fusion.11), channel_id=1, source_target_pairs={{0,1},{1,0},{2,3},{3,2},{4,5},{5,4},{6,7},{7,6},{8,9},{9,8},{10,11... | collective-permute-start | bytes 196616 | tf_op jit(solution)/shard_map/ppermute | solution.py:16
  53.6 4.3 %collective-permute-start.9 = (f32[64,1792]{1,0:T(8,128)}, f32[64,1792]{1,0:T(8,128)S(1)}, u32[]{:S(2)}, u32[]{:S(2)}) collective-permute-start(f32[64,1792]{1,0:T(8,128)} %get-tuple-element.65), channel_id=1, source_target_pairs={{0,4},{4,0},{8,12},{12,8},{16,20},{20,16},{24,28},{28,24},{1,5},{5... | collective-permute-start | bytes 1376264 | tf_op jit(solution)/shard_map/ppermute | solution.py:16
  53.6 4.3 %collective-permute-start.10 = (f32[64,1792]{1,0:T(8,128)S(1)}, f32[64,1792]{1,0:T(8,128)S(1)}, u32[]{:S(2)}, u32[]{:S(2)}) collective-permute-start(f32[64,1792]{1,0:T(8,128)S(1)} %get-tuple-element.66), channel_id=1, source_target_pairs={{0,4},{4,0},{8,12},{12,8},{16,20},{20,16},{24,28},{28,24},{1,5},{5... | collective-permute-start | bytes 1376264 | tf_op jit(solution)/shard_map/ppermute | solution.py:16
  58.1 10.6 %collective-permute-start.11 = (f32[64,896]{1,0:T(8,128)S(1)}, f32[64,896]{1,0:T(8,128)S(1)}, u32[]{:S(2)}, u32[]{:S(2)}) collective-permute-start(f32[64,896]{1,0:T(8,128)S(1)} %slice_select_fusion.3), channel_id=1, source_target_pairs={{0,8},{4,12},{8,0},{12,4},{16,24},{20,28},{24,16},{28,20},{1,9},{5... | collective-permute-start | bytes 688136 | tf_op jit(solution)/shard_map/ppermute | solution.py:16
  58.7 10.0 %collective-permute-start.12 = (f32[64,896]{1,0:T(8,128)S(1)}, f32[64,896]{1,0:T(8,128)S(1)}, u32[]{:S(2)}, u32[]{:S(2)}) collective-permute-start(f32[64,896]{1,0:T(8,128)S(1)} %slice_select_fusion.2), channel_id=1, source_target_pairs={{0,16},{4,20},{8,24},{12,28},{16,0},{20,4},{24,8},{28,12},{1,17},{... | collective-permute-start | bytes 688136 | tf_op jit(solution)/shard_map/ppermute | solution.py:16
  69.0 5.8 %collective-permute-start.13 = (f32[64,448]{1,0:T(8,128)S(1)}, f32[64,448]{1,0:T(8,128)S(1)}, u32[]{:S(2)}, u32[]{:S(2)}) collective-permute-start(f32[64,448]{1,0:T(8,128)S(1)} %slice_select_fusion.5), channel_id=1, source_target_pairs={{0,16},{4,20},{8,24},{12,28},{16,0},{20,4},{24,8},{28,12},{1,17},{... | collective-permute-start | bytes 344072 | tf_op jit(solution)/shard_map/ppermute | solution.py:16
  69.6 5.3 %collective-permute-start.14 = (f32[64,448]{1,0:T(8,128)S(1)}, f32[64,448]{1,0:T(8,128)S(1)}, u32[]{:S(2)}, u32[]{:S(2)}) collective-permute-start(f32[64,448]{1,0:T(8,128)S(1)} %slice_select_fusion.4), channel_id=1, source_target_pairs={{0,8},{4,12},{8,0},{12,4},{16,24},{20,28},{24,16},{28,20},{1,9},{5... | collective-permute-start | bytes 344072 | tf_op jit(solution)/shard_map/ppermute | solution.py:16
  75.1 6.5 %collective-permute-start.15 = (bf16[64,448]{1,0:T(8,128)(2,1)S(1)}, bf16[64,448]{1,0:T(8,128)(2,1)S(1)}, u32[]{:S(2)}, u32[]{:S(2)}) collective-permute-start(bf16[64,448]{1,0:T(8,128)(2,1)S(1)} %add_convert_fusion.1), channel_id=1, source_target_pairs={{0,16},{4,20},{8,24},{12,28},{16,0},{20,4},{24,8},{28,12},{1,17},{... | collective-permute-start | bytes 172040 | tf_op jit(solution)/shard_map/ppermute | solution.py:16
  76.7 5.0 %collective-permute-start.16 = (bf16[64,448]{1,0:T(8,128)(2,1)S(1)}, bf16[64,448]{1,0:T(8,128)(2,1)S(1)}, u32[]{:S(2)}, u32[]{:S(2)}) collective-permute-start(bf16[64,448]{1,0:T(8,128)(2,1)S(1)} %add_convert_fusion), channel_id=1, source_target_pairs={{0,8},{4,12},{8,0},{12,4},{16,24},{20,28},{24,16},{28,20},{1,9},{5... | collective-permute-start | bytes 172040 | tf_op jit(solution)/shard_map/ppermute | solution.py:16
  81.8 5.2 %collective-permute-start.17 = (bf16[64,896]{1,0:T(8,128)(2,1)S(1)}, bf16[64,896]{1,0:T(8,128)(2,1)S(1)}, u32[]{:S(2)}, u32[]{:S(2)}) collective-permute-start(bf16[64,896]{1,0:T(8,128)(2,1)S(1)} %maximum_select_fusion.8), channel_id=1, source_target_pairs={{0,8},{4,12},{8,0},{12,4},{16,24},{20,28},{24,16},{28,20},{1,9},{5... | collective-permute-start | bytes 344072 | tf_op jit(solution)/shard_map/ppermute | solution.py:16
  82.8 4.8 %collective-permute-start.18 = (bf16[64,896]{1,0:T(8,128)(2,1)S(1)}, bf16[64,896]{1,0:T(8,128)(2,1)S(1)}, u32[]{:S(2)}, u32[]{:S(2)}) collective-permute-start(bf16[64,896]{1,0:T(8,128)(2,1)S(1)} %maximum_select_fusion.9), channel_id=1, source_target_pairs={{0,16},{4,20},{8,24},{12,28},{16,0},{20,4},{24,8},{28,12},{1,17},{... | collective-permute-start | bytes 344072 | tf_op jit(solution)/shard_map/ppermute | solution.py:16
  87.7 3.4 %collective-permute-start.19 = (bf16[64,1792]{1,0:T(8,128)(2,1)S(1)}, bf16[64,1792]{1,0:T(8,128)(2,1)S(1)}, u32[]{:S(2)}, u32[]{:S(2)}) collective-permute-start(bf16[64,1792]{1,0:T(8,128)(2,1)S(1)} %maximum_select_fusion.4), channel_id=1, source_target_pairs={{0,4},{4,0},{8,12},{12,8},{16,20},{20,16},{24,28},{28,24},{1,5},{5... | collective-permute-start | bytes 688136 | tf_op jit(solution)/shard_map/ppermute | solution.py:16
  87.8 3.3 %collective-permute-start.20 = (bf16[64,1792]{1,0:T(8,128)(2,1)S(1)}, bf16[64,1792]{1,0:T(8,128)(2,1)S(1)}, u32[]{:S(2)}, u32[]{:S(2)}) collective-permute-start(bf16[64,1792]{1,0:T(8,128)(2,1)S(1)} %maximum_select_fusion.5), channel_id=1, source_target_pairs={{0,4},{4,0},{8,12},{12,8},{16,20},{20,16},{24,28},{28,24},{1,5},{5... | collective-permute-start | bytes 688136 | tf_op jit(solution)/shard_map/ppermute | solution.py:16
  92.3 3.6 %collective-permute-start.21 = (f32[2,64]{1,0:T(2,128)S(1)}, f32[2,64]{1,0:T(2,128)S(1)}, u32[]{:S(2)}, u32[]{:S(2)}) collective-permute-start(f32[2,64]{1,0:T(2,128)S(1)} %add_add_fusion), channel_id=1, source_target_pairs={{0,1},{1,0},{2,3},{3,2},{4,5},{5,4},{6,7},{7,6},{8,9},{9,8},{10,11... | collective-permute-start | bytes 1544 | tf_op jit(solution)/shard_map/ppermute | solution.py:16
  95.9 4.5 %collective-permute-start.22 = (f32[2,64]{1,0:T(2,128)S(1)}, f32[2,64]{1,0:T(2,128)S(1)}, u32[]{:S(2)}, u32[]{:S(2)}) collective-permute-start(f32[2,64]{1,0:T(2,128)S(1)} %add.109), channel_id=1, source_target_pairs={{0,2},{1,3},{2,0},{3,1},{4,6},{5,7},{6,4},{7,5},{8,10},{9,11},{10,... | collective-permute-start | bytes 1544 | tf_op jit(solution)/shard_map/ppermute | solution.py:16
  100.4 1.1 %collective-permute-start.23 = (f32[2,64]{1,0:T(2,128)S(1)}, f32[2,64]{1,0:T(2,128)S(1)}, u32[]{:S(2)}, u32[]{:S(2)}) collective-permute-start(f32[2,64]{1,0:T(2,128)S(1)} %add.110), channel_id=1, source_target_pairs={{0,4},{4,0},{8,12},{12,8},{16,20},{20,16},{24,28},{28,24},{1,5},{5... | collective-permute-start | bytes 1544 | tf_op jit(solution)/shard_map/ppermute | solution.py:16
  101.5 3.6 %collective-permute-start.24 = (f32[2,64]{1,0:T(2,128)S(1)}, f32[2,64]{1,0:T(2,128)S(1)}, u32[]{:S(2)}, u32[]{:S(2)}) collective-permute-start(f32[2,64]{1,0:T(2,128)S(1)} %add.111), channel_id=1, source_target_pairs={{0,8},{4,12},{8,0},{12,4},{16,24},{20,28},{24,16},{28,20},{1,9},{5... | collective-permute-start | bytes 1544 | tf_op jit(solution)/shard_map/ppermute | solution.py:16
  105.1 3.6 %collective-permute-start.25 = (f32[2,64]{1,0:T(2,128)S(1)}, f32[2,64]{1,0:T(2,128)S(1)}, u32[]{:S(2)}, u32[]{:S(2)}) collective-permute-start(f32[2,64]{1,0:T(2,128)S(1)} %add.112), channel_id=1, source_target_pairs={{0,16},{4,20},{8,24},{12,28},{16,0},{20,4},{24,8},{28,12},{1,17},{... | collective-permute-start | bytes 1544 | tf_op jit(solution)/shard_map/ppermute | solution.py:16

commit v9 on v8

--- a/solution.py
+++ b/solution.py
@@ -53,10 +53,11 @@
     done = []
 
     def swap(vs, bs):
-        work, arg = works.pop(0) if works else (None, None)
+        work, arg, *free = works.pop(0) if works else (None, None)
         if work is None:
             return [_swap(v, axis, n, b) for v, b in zip(vs, bs)]
-        *vs, arg = lax.optimization_barrier((*vs, arg))
+        if not free:
+            *vs, arg = lax.optimization_barrier((*vs, arg))
         result = work(arg)
         others = [_swap(v, axis, n, b) for v, b in zip(vs, bs)]
         *others, result = lax.optimization_barrier((*others, result))
@@ -85,7 +86,7 @@
             first = (me // orders[p][r]) % 2 == 0
             new.append(jnp.where(first, jnp.concatenate([v, other], dim), jnp.concatenate([other, v], dim)))
         xs = new
-    done += [work(arg) for work, arg in works if work is not None]
+    done += [w[0](w[1]) for w in works if w[0] is not None]
     return jnp.concatenate(xs, dim) if len(xs) > 1 else xs[0], done
 
 
@@ -137,10 +138,11 @@
     act_part = jnp.dot(acts_all, in_basis, preferred_element_type=F32)
     nb = out_basis.shape[1] // 128
     cuts = [128 * round(i * nb / ng) for i in range(ng + 1)]
-    grad_works = [(None, None)] + [
+    grad_works = [
         (functools.partial(lambda g, c0, c1: jnp.dot(g, out_basis[:, c0:c1], preferred_element_type=F32), c0=c0, c1=c1), grads_all)
         for c0, c1 in zip(cuts[:-1], cuts[1:])
     ]
+    grad_works[0] = grad_works[0] + (True,)
     act_rot, grad_parts = _allreduce_bf16(act_part, "col", nc, 1, grad_works)
     grad_part = jnp.concatenate(grad_parts, axis=1)
     kk = queries.shape[1]
@@ -174,5 +176,5 @@
         P("col", "row"),
         P(None, "col", "row"),
     )
-    fn = functools.partial(local, nr=mesh.shape["row"], nc=mesh.shape["col"], nl=6, ng=3)
+    fn = functools.partial(local, nr=mesh.shape["row"], nc=mesh.shape["col"], nl=6, ng=4)
     return jax.shard_map(fn, mesh=mesh, in_specs=in_specs, out_specs=P(), check_vma=False)

time: 109 us -> 109 us (level)
  waiting for transfers between devices: 20.8 us -> 18.6 us
    ppermute x26, waiting for transfers between devices: 20.8 us -> 18.6 us  [_swap(): return lax.ppermute(x, axis, [(i, i ^ b) for i in range(n)])]
    dot_general x3 -> x4, matrix products: 23.1 us -> 23.9 us  [local(): jnp.dot(g, out_basis[:, c0:c1], preferred_element_type=F32)]
  transfers between devices with their start and end apart: 26 -> 26, of which waited for: 10 -> 9; matrix products, arithmetic and copies ran while one was open for 25% -> 26% of each run, Pallas kernels for 24% -> 24%
where the time goes in v9:
time: 109 us
  starting transfers between devices  30.5 us (28%)
  matrix products  26.9 us (25%)
  Pallas kernels  26.3 us (24%)
  waiting for transfers between devices  18.6 us (17%)
  other arithmetic  5.85 us (5%)
    ppermute x26, starting transfers between devices, _swap(): return lax.ppermute(x, axis, [(i, i ^ b) for i in range(n)])  30.5 us
    pallas_call x6, Pallas kernels, _lifted(): pl.pallas_call(_lifted_kernel, grid=(t1 - t0,), in_specs=[pl.BlockSpec((t...  26.3 us
    dot_general x4, matrix products, local(): jnp.dot(g, out_basis[:, c0:c1], preferred_element_type=F32)  23.9 us
    ppermute x26, waiting for transfers between devices, _swap(): return lax.ppermute(x, axis, [(i, i ^ b) for i in range(n)])  18.6 us
    dot_general x1, matrix products, local(): act_part = jnp.dot(acts_all, in_basis, preferred_element_type=F32)  3.03 us
  transfers between devices with their start and end apart: 26, of which 9 were waited for; matrix products, arithmetic and copies ran while one was open for 26% of the time, Pallas kernels for 24%

profile of v9, /device:TPU:0, one launch (start us, length us, event | category | flops | bytes accessed | tf_op | source)
XLA Modules:
  0.0 108.6 jit_solution(13705207828909758551)
XLA Ops:
  0.5 1.1 collective-permute-done
  2.4 2.9 %collective-permute-start.1 = (bf16[16,2048]{1,0:T(8,128)(2,1)S(1)}, bf16[16,2048]{1,0:T(8,128)(2,1)S(1)}, u32[]{:S(2)}, u32[]{:S(2)}) collective-permute-start(bf16[16,2048]{1,0:T(8,128)(2,1)S(1)} %maximum_select_fusion.10), channel_id=1, source_target_pairs={{0,8},{4,12},{8,0},{12,4},{16,24},{20,28},{24,16},{28,20},{1,9},{5... | collective-permute-start | bytes 196616 | tf_op jit(solution)/shard_map/ppermute | solution.py:16
  5.3 2.6 %collective-permute-start.4 = (bf16[1,16,3584]{2,1,0:T(8,128)(2,1)}, bf16[1,16,3584]{2,1,0:T(8,128)(2,1)S(1)}, u32[]{:S(2)}, u32[]{:S(2)}) collective-permute-start(bf16[1,16,3584]{2,1,0:T(8,128)(2,1)} %bitcast.29), channel_id=1, source_target_pairs={{0,2},{1,3},{2,0},{3,1},{4,6},{5,7},{6,4},{7,5},{8,10},{9,11},{10,... | collective-permute-start | bytes 344072 | tf_op jit(solution)/shard_map/ppermute | solution.py:16
  7.9 1.8 %collective-permute-start.2 = (bf16[32,2048]{1,0:T(8,128)(2,1)S(1)}, bf16[32,2048]{1,0:T(8,128)(2,1)S(1)}, u32[]{:S(2)}, u32[]{:S(2)}) collective-permute-start(bf16[32,2048]{1,0:T(8,128)(2,1)S(1)} %maximum_select_fusion.6), channel_id=1, source_target_pairs={{0,16},{4,20},{8,24},{12,28},{16,0},{20,4},{24,8},{28,12},{1,17},{... | collective-permute-start | bytes 393224 | tf_op jit(solution)/shard_map/ppermute | solution.py:16
  9.7 4.1 %collective-permute-done.4 = bf16[1,16,3584]{2,1,0:T(8,128)(2,1)S(1)} collective-permute-done((bf16[1,16,3584]{2,1,0:T(8,128)(2,1)}, bf16[1,16,3584]{2,1,0:T(8,128)(2,1)S(1)}, u32[]{:S(2)}, u32[]{:S(2)}) %collective-permute-start.4) | collective-permute-done | bytes 114720 | tf_op jit(solution)/shard_map/ppermute | solution.py:16
  15.6 3.0 %fusion.8 = f32[64,1024]{1,0:T(8,128)S(1)} fusion(bf16[2048,1024]{1,0:T(8,128)(2,1)} %param.9, bf16[32,2048]{1,0:T(8,128)(2,1)S(1)} %collective-permute-done.2, bf16[32,2048]{1,0:T(8,128)(2,1)S(1)} %maximum_select_fusion.6, pred[]{:T(512)S(6)} %eq.65), kind=kOutput, calls=%fused_computation.20 | convolution fusion | flops 269615104 | bytes 4718593 | tf_op jit(solution)/shard_map/dot_general | solution.py:138
  18.6 1.3 %collective-permute-start.3 = (f32[64,512]{1,0:T(8,128)S(1)}, f32[64,512]{1,0:T(8,128)S(1)}, u32[]{:S(2)}, u32[]{:S(2)}) collective-permute-start(f32[64,512]{1,0:T(8,128)S(1)} %slice_select_fusion.4), channel_id=1, source_target_pairs={{0,1},{1,0},{2,3},{3,2},{4,5},{5,4},{6,7},{7,6},{8,9},{9,8},{10,11... | collective-permute-start | bytes 393224 | tf_op jit(solution)/shard_map/ppermute | solution.py:16
  20.0 1.6 %collective-permute-done.5 = bf16[2,16,3584]{2,1,0:T(8,128)(2,1)S(1)} collective-permute-done((bf16[2,16,3584]{2,1,0:T(8,128)(2,1)S(1)}, bf16[2,16,3584]{2,1,0:T(8,128)(2,1)S(1)}, u32[]{:S(2)}, u32[]{:S(2)}) %collective-permute-start.5) | collective-permute-done | bytes 229408 | tf_op jit(solution)/shard_map/ppermute | solution.py:16
  21.7 6.0 %fusion.6 = f32[64,1792]{1,0:T(8,128)S(1)} fusion(bf16[64,3584]{1,0:T(8,128)(2,1)S(1)} %bitcast.25, bf16[3584,7168]{1,0:T(8,128)(2,1)} %param.8), kind=kOutput, calls=%fused_computation.6 | convolution fusion | flops 822083584 | bytes 13762560 | tf_op jit(solution)/shard_map/dot_general | solution.py:142
  27.7 3.3 %collective-permute-start.6 = (f32[64,256]{1,0:T(8,128)S(1)}, f32[64,256]{1,0:T(8,128)S(1)}, u32[]{:S(2)}, u32[]{:S(2)}) collective-permute-start(f32[64,256]{1,0:T(8,128)S(1)} %slice_select_fusion.5), channel_id=1, source_target_pairs={{0,2},{1,3},{2,0},{3,1},{4,6},{5,7},{6,4},{7,5},{8,10},{9,11},{10,... | collective-permute-start | bytes 196616 | tf_op jit(solution)/shard_map/ppermute | solution.py:16
  31.1 6.0 %fusion.4 = f32[64,1792]{1,0:T(8,128)S(1)} fusion(bf16[64,3584]{1,0:T(8,128)(2,1)S(1)} %bitcast.26, bf16[3584,7168]{1,0:T(8,128)(2,1)} %param.8), kind=kOutput, calls=%fused_computation.4 | convolution fusion | flops 822083584 | bytes 13762560 | tf_op jit(solution)/shard_map/dot_general | solution.py:142
  37.2 6.0 %fusion.2 = f32[64,1792]{1,0:T(8,128)S(1)} fusion(bf16[64,3584]{1,0:T(8,128)(2,1)S(1)} %bitcast.27, bf16[3584,7168]{1,0:T(8,128)(2,1)} %param.8), kind=kOutput, calls=%fused_computation.2 | convolution fusion | flops 822083584 | bytes 13762560 | tf_op jit(solution)/shard_map/dot_general | solution.py:142
  43.3 2.5 %collective-permute-start.8 = (bf16[64,512]{1,0:T(8,128)(2,1)S(1)}, bf16[64,512]{1,0:T(8,128)(2,1)S(1)}, u32[]{:S(2)}, u32[]{:S(2)}) collective-permute-start(bf16[64,512]{1,0:T(8,128)(2,1)S(1)} %maximum_select_fusion.11), channel_id=1, source_target_pairs={{0,1},{1,0},{2,3},{3,2},{4,5},{5,4},{6,7},{7,6},{8,9},{9,8},{10,11... | collective-permute-start | bytes 196616 | tf_op jit(solution)/shard_map/ppermute | solution.py:16
  45.8 6.0 %fusion = f32[64,1792]{1,0:T(8,128)S(1)} fusion(bf16[64,3584]{1,0:T(8,128)(2,1)S(1)} %bitcast.28, bf16[3584,7168]{1,0:T(8,128)(2,1)} %param.8), kind=kOutput, calls=%fused_computation | convolution fusion | flops 822083584 | bytes 13762560 | tf_op jit(solution)/shard_map/dot_general | solution.py:142
  52.4 3.8 %shard_map.64 = f32[2,64,1024]{2,1,0:T(8,128)S(1)} custom-call(bf16[64,1024]{1,0:T(8,128)(2,1)S(1)} %maximum_select_fusion.7.a_ref, bf16[7168,1024]{1,0:T(8,128)(2,1)} %e_ref.11, bf16[2,7168,1024]{2,1,0:T(8,128)(2,1)} %q_ref.11), custom_call_target="tpu_custom_call" | custom-call | flops 268435456 | bytes 6815744 | tf_op jit(solution)/shard_map/pallas_call | solution.py:114
  56.2 1.1 %select_add_fusion = f32[64,1792]{1,0:T(8,128)S(1)} fusion(f32[64,1792]{1,0:T(8,128)} %collective-permute-done.10, f32[64,1792]{1,0:T(8,128)S(1)} %fusion, f32[64,1792]{1,0:T(8,128)S(1)} %fusion.2, pred[]{:T(512)S(6)} %eq.63), kind=kLoop, calls=%fused_computation.16 | loop fusion | flops 229376 | bytes 1835009 | tf_op jit(solution)/shard_map/add | solution.py:80
  58.0 1.5 %collective-permute-start.12 = (f32[64,896]{1,0:T(8,128)S(1)}, f32[64,896]{1,0:T(8,128)S(1)}, u32[]{:S(2)}, u32[]{:S(2)}) collective-permute-start(f32[64,896]{1,0:T(8,128)S(1)} %slice_select_fusion), channel_id=1, source_target_pairs={{0,16},{4,20},{8,24},{12,28},{16,0},{20,4},{24,8},{28,12},{1,17},{... | collective-permute-start | bytes 688136 | tf_op jit(solution)/shard_map/ppermute | solution.py:16
  59.6 8.5 %shard_map.65 = f32[2,64,2560]{2,1,0:T(8,128)S(1)} custom-call(bf16[64,1024]{1,0:T(8,128)(2,1)S(1)} %maximum_select_fusion.7.a_ref, bf16[7168,1024]{1,0:T(8,128)(2,1)} %e_ref.11, bf16[2,7168,1024]{2,1,0:T(8,128)(2,1)} %q_ref.11), custom_call_target="tpu_custom_call" | custom-call | flops 671088640 | bytes 17039360 | tf_op jit(solution)/shard_map/pallas_call | solution.py:114
  68.9 1.5 %collective-permute-start.14 = (f32[64,448]{1,0:T(8,128)S(1)}, f32[64,448]{1,0:T(8,128)S(1)}, u32[]{:S(2)}, u32[]{:S(2)}) collective-permute-start(f32[64,448]{1,0:T(8,128)S(1)} %slice_select_fusion.2), channel_id=1, source_target_pairs={{0,8},{4,12},{8,0},{12,4},{16,24},{20,28},{24,16},{28,20},{1,9},{5... | collective-permute-start | bytes 344072 | tf_op jit(solution)/shard_map/ppermute | solution.py:16
  70.4 3.8 %shard_map.66 = f32[2,64,1024]{2,1,0:T(8,128)S(1)} custom-call(bf16[64,1024]{1,0:T(8,128)(2,1)S(1)} %maximum_select_fusion.7.a_ref, bf16[7168,1024]{1,0:T(8,128)(2,1)} %e_ref.11, bf16[2,7168,1024]{2,1,0:T(8,128)(2,1)} %q_ref.11), custom_call_target="tpu_custom_call" | custom-call | flops 268435456 | bytes 6815744 | tf_op jit(solution)/shard_map/pallas_call | solution.py:114
  74.4 1.6 %collective-permute-start.15 = (bf16[64,448]{1,0:T(8,128)(2,1)S(1)}, bf16[64,448]{1,0:T(8,128)(2,1)S(1)}, u32[]{:S(2)}, u32[]{:S(2)}) collective-permute-start(bf16[64,448]{1,0:T(8,128)(2,1)S(1)} %add_convert_fusion.1), channel_id=1, source_target_pairs={{0,16},{4,20},{8,24},{12,28},{16,0},{20,4},{24,8},{28,12},{1,17},{... | collective-permute-start | bytes 172040 | tf_op jit(solution)/shard_map/ppermute | solution.py:16
  76.0 1.2 %collective-permute-start.16 = (bf16[64,448]{1,0:T(8,128)(2,1)S(1)}, bf16[64,448]{1,0:T(8,128)(2,1)S(1)}, u32[]{:S(2)}, u32[]{:S(2)}) collective-permute-start(bf16[64,448]{1,0:T(8,128)(2,1)S(1)} %add_convert_fusion), channel_id=1, source_target_pairs={{0,8},{4,12},{8,0},{12,4},{16,24},{20,28},{24,16},{28,20},{1,9},{5... | collective-permute-start | bytes 172040 | tf_op jit(solution)/shard_map/ppermute | solution.py:16
  77.2 3.8 %shard_map.67 = f32[2,64,1024]{2,1,0:T(8,128)S(1)} custom-call(bf16[64,1024]{1,0:T(8,128)(2,1)S(1)} %maximum_select_fusion.7.a_ref, bf16[7168,1024]{1,0:T(8,128)(2,1)} %e_ref.11, bf16[2,7168,1024]{2,1,0:T(8,128)(2,1)} %q_ref.11), custom_call_target="tpu_custom_call" | custom-call | flops 268435456 | bytes 6815744 | tf_op jit(solution)/shard_map/pallas_call | solution.py:114
  82.6 3.8 %shard_map.68 = f32[2,64,1024]{2,1,0:T(8,128)S(1)} custom-call(bf16[64,1024]{1,0:T(8,128)(2,1)S(1)} %maximum_select_fusion.7.a_ref, bf16[7168,1024]{1,0:T(8,128)(2,1)} %e_ref.11, bf16[2,7168,1024]{2,1,0:T(8,128)(2,1)} %q_ref.11), custom_call_target="tpu_custom_call" | custom-call | flops 268435456 | bytes 6815744 | tf_op jit(solution)/shard_map/pallas_call | solution.py:114
  87.6 2.8 %shard_map.69 = f32[2,64,512]{2,1,0:T(8,128)S(1)} custom-call(bf16[64,1024]{1,0:T(8,128)(2,1)S(1)} %maximum_select_fusion.7.a_ref, bf16[7168,1024]{1,0:T(8,128)(2,1)} %e_ref.11, bf16[2,7168,1024]{2,1,0:T(8,128)(2,1)} %q_ref.11), custom_call_target="tpu_custom_call" | custom-call | flops 134217728 | bytes 3407872 | tf_op jit(solution)/shard_map/pallas_call | solution.py:114
  91.7 3.5 %collective-permute-done.21 = f32[2,64]{1,0:T(2,128)S(1)} collective-permute-done((f32[2,64]{1,0:T(2,128)S(1)}, f32[2,64]{1,0:T(2,128)S(1)}, u32[]{:S(2)}, u32[]{:S(2)}) %collective-permute-start.21) | collective-permute-done | bytes 544 | tf_op jit(solution)/shard_map/ppermute | solution.py:16
  95.3 2.9 %collective-permute-start.22 = (f32[2,64]{1,0:T(2,128)S(1)}, f32[2,64]{1,0:T(2,128)S(1)}, u32[]{:S(2)}, u32[]{:S(2)}) collective-permute-start(f32[2,64]{1,0:T(2,128)S(1)} %add.109), channel_id=1, source_target_pairs={{0,2},{1,3},{2,0},{3,1},{4,6},{5,7},{6,4},{7,5},{8,10},{9,11},{10,... | collective-permute-start | bytes 1544 | tf_op jit(solution)/shard_map/ppermute | solution.py:16
  98.2 1.6 %collective-permute-done.22 = f32[2,64]{1,0:T(2,128)S(1)} collective-permute-done((f32[2,64]{1,0:T(2,128)S(1)}, f32[2,64]{1,0:T(2,128)S(1)}, u32[]{:S(2)}, u32[]{:S(2)}) %collective-permute-start.22) | collective-permute-done | bytes 544 | tf_op jit(solution)/shard_map/ppermute | solution.py:16
  99.7 1.1 %collective-permute-done.23 = f32[2,64]{1,0:T(2,128)S(1)} collective-permute-done((f32[2,64]{1,0:T(2,128)S(1)}, f32[2,64]{1,0:T(2,128)S(1)}, u32[]{:S(2)}, u32[]{:S(2)}) %collective-permute-start.23) | collective-permute-done | bytes 544 | tf_op jit(solution)/shard_map/ppermute | solution.py:16
  100.9 1.2 %collective-permute-start.24 = (f32[2,64]{1,0:T(2,128)S(1)}, f32[2,64]{1,0:T(2,128)S(1)}, u32[]{:S(2)}, u32[]{:S(2)}) collective-permute-start(f32[2,64]{1,0:T(2,128)S(1)} %add.111), channel_id=1, source_target_pairs={{0,8},{4,12},{8,0},{12,4},{16,24},{20,28},{24,16},{28,20},{1,9},{5... | collective-permute-start | bytes 1544 | tf_op jit(solution)/shard_map/ppermute | solution.py:16
  102.1 2.4 %collective-permute-done.24 = f32[2,64]{1,0:T(2,128)S(1)} collective-permute-done((f32[2,64]{1,0:T(2,128)S(1)}, f32[2,64]{1,0:T(2,128)S(1)}, u32[]{:S(2)}, u32[]{:S(2)}) %collective-permute-start.24) | collective-permute-done | bytes 544 | tf_op jit(solution)/shard_map/ppermute | solution.py:16
  105.5 2.5 %collective-permute-done.25 = f32[2,64]{1,0:T(2,128)S(1)} collective-permute-done((f32[2,64]{1,0:T(2,128)S(1)}, f32[2,64]{1,0:T(2,128)S(1)}, u32[]{:S(2)}, u32[]{:S(2)}) %collective-permute-start.25) | collective-permute-done | bytes 544 | tf_op jit(solution)/shard_map/ppermute | solution.py:16
  (76 shorter events, 11.6 us)
Async XLA Ops:
  0.0 1.5 %collective-permute-start = (bf16[8,2048]{1,0:T(8,128)(2,1)}, bf16[8,2048]{1,0:T(8,128)(2,1)S(1)}, u32[]{:S(2)}, u32[]{:S(2)}) collective-permute-start(bf16[8,2048]{1,0:T(8,128)(2,1)} %param.7), channel_id=1, source_target_pairs={{0,4},{4,0},{8,12},{12,8},{16,20},{20,16},{24,28},{28,24},{1,5},{5... | collective-permute-start | bytes 98312 | tf_op jit(solution)/shard_map/ppermute | solution.py:16
  2.4 5.5 %collective-permute-start.1 = (bf16[16,2048]{1,0:T(8,128)(2,1)S(1)}, bf16[16,2048]{1,0:T(8,128)(2,1)S(1)}, u32[]{:S(2)}, u32[]{:S(2)}) collective-permute-start(bf16[16,2048]{1,0:T(8,128)(2,1)S(1)} %maximum_select_fusion.10), channel_id=1, source_target_pairs={{0,8},{4,12},{8,0},{12,4},{16,24},{20,28},{24,16},{28,20},{1,9},{5... | collective-permute-start | bytes 196616 | tf_op jit(solution)/shard_map/ppermute | solution.py:16
  5.3 8.5 %collective-permute-start.4 = (bf16[1,16,3584]{2,1,0:T(8,128)(2,1)}, bf16[1,16,3584]{2,1,0:T(8,128)(2,1)S(1)}, u32[]{:S(2)}, u32[]{:S(2)}) collective-permute-start(bf16[1,16,3584]{2,1,0:T(8,128)(2,1)} %bitcast.29), channel_id=1, source_target_pairs={{0,2},{1,3},{2,0},{3,1},{4,6},{5,7},{6,4},{7,5},{8,10},{9,11},{10,... | collective-permute-start | bytes 344072 | tf_op jit(solution)/shard_map/ppermute | solution.py:16
  7.9 7.7 %collective-permute-start.2 = (bf16[32,2048]{1,0:T(8,128)(2,1)S(1)}, bf16[32,2048]{1,0:T(8,128)(2,1)S(1)}, u32[]{:S(2)}, u32[]{:S(2)}) collective-permute-start(bf16[32,2048]{1,0:T(8,128)(2,1)S(1)} %maximum_select_fusion.6), channel_id=1, source_target_pairs={{0,16},{4,20},{8,24},{12,28},{16,0},{20,4},{24,8},{28,12},{1,17},{... | collective-permute-start | bytes 393224 | tf_op jit(solution)/shard_map/ppermute | solution.py:16
  14.7 6.9 %collective-permute-start.5 = (bf16[2,16,3584]{2,1,0:T(8,128)(2,1)S(1)}, bf16[2,16,3584]{2,1,0:T(8,128)(2,1)S(1)}, u32[]{:S(2)}, u32[]{:S(2)}) collective-permute-start(bf16[2,16,3584]{2,1,0:T(8,128)(2,1)S(1)} %maximum_bitcast_fusion), channel_id=1, source_target_pairs={{0,1},{1,0},{2,3},{3,2},{4,5},{5,4},{6,7},{7,6},{8,9},{9,8},{10,11... | collective-permute-start | bytes 688136 | tf_op jit(solution)/shard_map/ppermute | solution.py:16
  18.6 9.0 %collective-permute-start.3 = (f32[64,512]{1,0:T(8,128)S(1)}, f32[64,512]{1,0:T(8,128)S(1)}, u32[]{:S(2)}, u32[]{:S(2)}) collective-permute-start(f32[64,512]{1,0:T(8,128)S(1)} %slice_select_fusion.4), channel_id=1, source_target_pairs={{0,1},{1,0},{2,3},{3,2},{4,5},{5,4},{6,7},{7,6},{8,9},{9,8},{10,11... | collective-permute-start | bytes 393224 | tf_op jit(solution)/shard_map/ppermute | solution.py:16
  27.7 9.3 %collective-permute-start.6 = (f32[64,256]{1,0:T(8,128)S(1)}, f32[64,256]{1,0:T(8,128)S(1)}, u32[]{:S(2)}, u32[]{:S(2)}) collective-permute-start(f32[64,256]{1,0:T(8,128)S(1)} %slice_select_fusion.5), channel_id=1, source_target_pairs={{0,2},{1,3},{2,0},{3,1},{4,6},{5,7},{6,4},{7,5},{8,10},{9,11},{10,... | collective-permute-start | bytes 196616 | tf_op jit(solution)/shard_map/ppermute | solution.py:16
  37.1 6.2 %collective-permute-start.7 = (bf16[64,256]{1,0:T(8,128)(2,1)S(1)}, bf16[64,256]{1,0:T(8,128)(2,1)S(1)}, u32[]{:S(2)}, u32[]{:S(2)}) collective-permute-start(bf16[64,256]{1,0:T(8,128)(2,1)S(1)} %add_convert_fusion.2), channel_id=1, source_target_pairs={{0,2},{1,3},{2,0},{3,1},{4,6},{5,7},{6,4},{7,5},{8,10},{9,11},{10,... | collective-permute-start | bytes 98312 | tf_op jit(solution)/shard_map/ppermute | solution.py:16
  43.3 8.5 %collective-permute-start.8 = (bf16[64,512]{1,0:T(8,128)(2,1)S(1)}, bf16[64,512]{1,0:T(8,128)(2,1)S(1)}, u32[]{:S(2)}, u32[]{:S(2)}) collective-permute-start(bf16[64,512]{1,0:T(8,128)(2,1)S(1)} %maximum_select_fusion.11), channel_id=1, source_target_pairs={{0,1},{1,0},{2,3},{3,2},{4,5},{5,4},{6,7},{7,6},{8,9},{9,8},{10,11... | collective-permute-start | bytes 196616 | tf_op jit(solution)/shard_map/ppermute | solution.py:16
  51.8 4.3 %collective-permute-start.9 = (f32[64,1792]{1,0:T(8,128)S(1)}, f32[64,1792]{1,0:T(8,128)S(1)}, u32[]{:S(2)}, u32[]{:S(2)}) collective-permute-start(f32[64,1792]{1,0:T(8,128)S(1)} %broadcast_select_fusion.1), channel_id=1, source_target_pairs={{0,4},{4,0},{8,12},{12,8},{16,20},{20,16},{24,28},{28,24},{1,5},{5... | collective-permute-start | bytes 1376264 | tf_op jit(solution)/shard_map/ppermute | solution.py:16
  51.9 4.3 %collective-permute-start.10 = (f32[64,1792]{1,0:T(8,128)S(1)}, f32[64,1792]{1,0:T(8,128)}, u32[]{:S(2)}, u32[]{:S(2)}) collective-permute-start(f32[64,1792]{1,0:T(8,128)S(1)} %broadcast_select_fusion), channel_id=1, source_target_pairs={{0,4},{4,0},{8,12},{12,8},{16,20},{20,16},{24,28},{28,24},{1,5},{5... | collective-permute-start | bytes 1376264 | tf_op jit(solution)/shard_map/ppermute | solution.py:16
  57.4 10.6 %collective-permute-start.11 = (f32[64,896]{1,0:T(8,128)S(1)}, f32[64,896]{1,0:T(8,128)S(1)}, u32[]{:S(2)}, u32[]{:S(2)}) collective-permute-start(f32[64,896]{1,0:T(8,128)S(1)} %slice_select_fusion.1), channel_id=1, source_target_pairs={{0,8},{4,12},{8,0},{12,4},{16,24},{20,28},{24,16},{28,20},{1,9},{5... | collective-permute-start | bytes 688136 | tf_op jit(solution)/shard_map/ppermute | solution.py:16
  58.0 10.0 %collective-permute-start.12 = (f32[64,896]{1,0:T(8,128)S(1)}, f32[64,896]{1,0:T(8,128)S(1)}, u32[]{:S(2)}, u32[]{:S(2)}) collective-permute-start(f32[64,896]{1,0:T(8,128)S(1)} %slice_select_fusion), channel_id=1, source_target_pairs={{0,16},{4,20},{8,24},{12,28},{16,0},{20,4},{24,8},{28,12},{1,17},{... | collective-permute-start | bytes 688136 | tf_op jit(solution)/shard_map/ppermute | solution.py:16
  68.4 5.8 %collective-permute-start.13 = (f32[64,448]{1,0:T(8,128)S(1)}, f32[64,448]{1,0:T(8,128)S(1)}, u32[]{:S(2)}, u32[]{:S(2)}) collective-permute-start(f32[64,448]{1,0:T(8,128)S(1)} %slice_select_fusion.3), channel_id=1, source_target_pairs={{0,16},{4,20},{8,24},{12,28},{16,0},{20,4},{24,8},{28,12},{1,17},{... | collective-permute-start | bytes 344072 | tf_op jit(solution)/shard_map/ppermute | solution.py:16
  68.9 5.3 %collective-permute-start.14 = (f32[64,448]{1,0:T(8,128)S(1)}, f32[64,448]{1,0:T(8,128)S(1)}, u32[]{:S(2)}, u32[]{:S(2)}) collective-permute-start(f32[64,448]{1,0:T(8,128)S(1)} %slice_select_fusion.2), channel_id=1, source_target_pairs={{0,8},{4,12},{8,0},{12,4},{16,24},{20,28},{24,16},{28,20},{1,9},{5... | collective-permute-start | bytes 344072 | tf_op jit(solution)/shard_map/ppermute | solution.py:16
  74.4 6.5 %collective-permute-start.15 = (bf16[64,448]{1,0:T(8,128)(2,1)S(1)}, bf16[64,448]{1,0:T(8,128)(2,1)S(1)}, u32[]{:S(2)}, u32[]{:S(2)}) collective-permute-start(bf16[64,448]{1,0:T(8,128)(2,1)S(1)} %add_convert_fusion.1), channel_id=1, source_target_pairs={{0,16},{4,20},{8,24},{12,28},{16,0},{20,4},{24,8},{28,12},{1,17},{... | collective-permute-start | bytes 172040 | tf_op jit(solution)/shard_map/ppermute | solution.py:16
  76.0 5.0 %collective-permute-start.16 = (bf16[64,448]{1,0:T(8,128)(2,1)S(1)}, bf16[64,448]{1,0:T(8,128)(2,1)S(1)}, u32[]{:S(2)}, u32[]{:S(2)}) collective-permute-start(bf16[64,448]{1,0:T(8,128)(2,1)S(1)} %add_convert_fusion), channel_id=1, source_target_pairs={{0,8},{4,12},{8,0},{12,4},{16,24},{20,28},{24,16},{28,20},{1,9},{5... | collective-permute-start | bytes 172040 | tf_op jit(solution)/shard_map/ppermute | solution.py:16
  81.2 5.2 %collective-permute-start.17 = (bf16[64,896]{1,0:T(8,128)(2,1)S(1)}, bf16[64,896]{1,0:T(8,128)(2,1)S(1)}, u32[]{:S(2)}, u32[]{:S(2)}) collective-permute-start(bf16[64,896]{1,0:T(8,128)(2,1)S(1)} %maximum_select_fusion.8), channel_id=1, source_target_pairs={{0,8},{4,12},{8,0},{12,4},{16,24},{20,28},{24,16},{28,20},{1,9},{5... | collective-permute-start | bytes 344072 | tf_op jit(solution)/shard_map/ppermute | solution.py:16
  82.1 4.8 %collective-permute-start.18 = (bf16[64,896]{1,0:T(8,128)(2,1)S(1)}, bf16[64,896]{1,0:T(8,128)(2,1)S(1)}, u32[]{:S(2)}, u32[]{:S(2)}) collective-permute-start(bf16[64,896]{1,0:T(8,128)(2,1)S(1)} %maximum_select_fusion.9), channel_id=1, source_target_pairs={{0,16},{4,20},{8,24},{12,28},{16,0},{20,4},{24,8},{28,12},{1,17},{... | collective-permute-start | bytes 344072 | tf_op jit(solution)/shard_map/ppermute | solution.py:16
  87.0 3.4 %collective-permute-start.19 = (bf16[64,1792]{1,0:T(8,128)(2,1)S(1)}, bf16[64,1792]{1,0:T(8,128)(2,1)S(1)}, u32[]{:S(2)}, u32[]{:S(2)}) collective-permute-start(bf16[64,1792]{1,0:T(8,128)(2,1)S(1)} %maximum_select_fusion.4), channel_id=1, source_target_pairs={{0,4},{4,0},{8,12},{12,8},{16,20},{20,16},{24,28},{28,24},{1,5},{5... | collective-permute-start | bytes 688136 | tf_op jit(solution)/shard_map/ppermute | solution.py:16
  87.1 3.3 %collective-permute-start.20 = (bf16[64,1792]{1,0:T(8,128)(2,1)S(1)}, bf16[64,1792]{1,0:T(8,128)(2,1)S(1)}, u32[]{:S(2)}, u32[]{:S(2)}) collective-permute-start(bf16[64,1792]{1,0:T(8,128)(2,1)S(1)} %maximum_select_fusion.5), channel_id=1, source_target_pairs={{0,4},{4,0},{8,12},{12,8},{16,20},{20,16},{24,28},{28,24},{1,5},{5... | collective-permute-start | bytes 688136 | tf_op jit(solution)/shard_map/ppermute | solution.py:16
  91.6 3.6 %collective-permute-start.21 = (f32[2,64]{1,0:T(2,128)S(1)}, f32[2,64]{1,0:T(2,128)S(1)}, u32[]{:S(2)}, u32[]{:S(2)}) collective-permute-start(f32[2,64]{1,0:T(2,128)S(1)} %add_add_fusion), channel_id=1, source_target_pairs={{0,1},{1,0},{2,3},{3,2},{4,5},{5,4},{6,7},{7,6},{8,9},{9,8},{10,11... | collective-permute-start | bytes 1544 | tf_op jit(solution)/shard_map/ppermute | solution.py:16
  95.3 4.5 %collective-permute-start.22 = (f32[2,64]{1,0:T(2,128)S(1)}, f32[2,64]{1,0:T(2,128)S(1)}, u32[]{:S(2)}, u32[]{:S(2)}) collective-permute-start(f32[2,64]{1,0:T(2,128)S(1)} %add.109), channel_id=1, source_target_pairs={{0,2},{1,3},{2,0},{3,1},{4,6},{5,7},{6,4},{7,5},{8,10},{9,11},{10,... | collective-permute-start | bytes 1544 | tf_op jit(solution)/shard_map/ppermute | solution.py:16
  99.7 1.1 %collective-permute-start.23 = (f32[2,64]{1,0:T(2,128)S(1)}, f32[2,64]{1,0:T(2,128)S(1)}, u32[]{:S(2)}, u32[]{:S(2)}) collective-permute-start(f32[2,64]{1,0:T(2,128)S(1)} %add.110), channel_id=1, source_target_pairs={{0,4},{4,0},{8,12},{12,8},{16,20},{20,16},{24,28},{28,24},{1,5},{5... | collective-permute-start | bytes 1544 | tf_op jit(solution)/shard_map/ppermute | solution.py:16
  100.9 3.6 %collective-permute-start.24 = (f32[2,64]{1,0:T(2,128)S(1)}, f32[2,64]{1,0:T(2,128)S(1)}, u32[]{:S(2)}, u32[]{:S(2)}) collective-permute-start(f32[2,64]{1,0:T(2,128)S(1)} %add.111), channel_id=1, source_target_pairs={{0,8},{4,12},{8,0},{12,4},{16,24},{20,28},{24,16},{28,20},{1,9},{5... | collective-permute-start | bytes 1544 | tf_op jit(solution)/shard_map/ppermute | solution.py:16
  104.5 3.6 %collective-permute-start.25 = (f32[2,64]{1,0:T(2,128)S(1)}, f32[2,64]{1,0:T(2,128)S(1)}, u32[]{:S(2)}, u32[]{:S(2)}) collective-permute-start(f32[2,64]{1,0:T(2,128)S(1)} %add.112), channel_id=1, source_target_pairs={{0,16},{4,20},{8,24},{12,28},{16,0},{20,4},{24,8},{28,12},{1,17},{... | collective-permute-start | bytes 1544 | tf_op jit(solution)/shard_map/ppermute | solution.py:16

commit v10 on v9

--- a/solution.py
+++ b/solution.py
@@ -48,7 +48,7 @@
     while b < n:
         bits.append(b)
         b *= 2
-    orders = [bits, bits[:1] + bits[:0:-1]][:paths]
+    orders = [bits, bits[:1] + bits[:0:-1]][: max(paths, 1)]
     works = list(works)
     done = []
 
@@ -64,6 +64,11 @@
         done.append(result)
         return others
 
+    if paths == 0:
+        for b in bits:
+            x = x + swap([x], [b])[0]
+        done += [w[0](w[1]) for w in works if w[0] is not None]
+        return x.astype(BF16), done
     w = x.shape[dim] // len(orders)
     xs = [lax.slice_in_dim(x, p * w, (p + 1) * w, axis=dim) for p in range(len(orders))]
     for r in range(len(bits)):
@@ -143,7 +148,7 @@
         for c0, c1 in zip(cuts[:-1], cuts[1:])
     ]
     grad_works[0] = grad_works[0] + (True,)
-    act_rot, grad_parts = _allreduce_bf16(act_part, "col", nc, 1, grad_works)
+    act_rot, grad_parts = _allreduce_bf16(act_part, "col", nc, 1, grad_works, paths=0)
     grad_part = jnp.concatenate(grad_parts, axis=1)
     kk = queries.shape[1]
     tk = next(c for c in (512, 256, 128, kk) if kk % c == 0)

time: 109 us -> 112 us (1.028)
  waiting for transfers between devices: 18.6 us -> 24.1 us
  starting transfers between devices: 30.5 us -> 27.7 us
  matrix products: 26.9 us -> 28.8 us
    ppermute x26 -> x24, waiting for transfers between devices: 18.6 us -> 24.1 us  [_swap(): return lax.ppermute(x, axis, [(i, i ^ b) for i in range(n)])]
    ppermute x26 -> x24, starting transfers between devices: 30.5 us -> 27.7 us  [_swap(): return lax.ppermute(x, axis, [(i, i ^ b) for i in range(n)])]
    dot_general x4, matrix products: 23.9 us -> 25.7 us  [local(): jnp.dot(g, out_basis[:, c0:c1], preferred_element_type=F32)]
  transfers between devices with their start and end apart: 26 -> 24, of which waited for: 9 -> 10; matrix products, arithmetic and copies ran while one was open for 26% -> 27% of each run, Pallas kernels for 24% -> 23%
where the time goes in v10:
time: 112 us
  matrix products  28.8 us (26%)
  starting transfers between devices  27.7 us (25%)
  Pallas kernels  26.3 us (23%)
  waiting for transfers between devices  24.1 us (22%)
  other arithmetic  4.73 us (4%)
    ppermute x24, starting transfers between devices, _swap(): return lax.ppermute(x, axis, [(i, i ^ b) for i in range(n)])  27.7 us
    pallas_call x6, Pallas kernels, _lifted(): pl.pallas_call(_lifted_kernel, grid=(t1 - t0,), in_specs=[pl.BlockSpec((t...  26.3 us
    dot_general x4, matrix products, local(): jnp.dot(g, out_basis[:, c0:c1], preferred_element_type=F32)  25.7 us
    ppermute x24, waiting for transfers between devices, _swap(): return lax.ppermute(x, axis, [(i, i ^ b) for i in range(n)])  24.1 us
    dot_general x1, matrix products, local(): act_part = jnp.dot(acts_all, in_basis, preferred_element_type=F32)  3.03 us
  transfers between devices with their start and end apart: 24, of which 10 were waited for; matrix products, arithmetic and copies ran while one was open for 27% of the time, Pallas kernels for 23%

profile of v10, /device:TPU:0, one launch (start us, length us, event | category | flops | bytes accessed | tf_op | source)
XLA Modules:
  0.0 112.0 jit_solution(13654442434755493908)
XLA Ops:
  0.5 1.1 collective-permute-done
  2.4 2.9 %collective-permute-start.1 = (bf16[16,2048]{1,0:T(8,128)(2,1)S(1)}, bf16[16,2048]{1,0:T(8,128)(2,1)S(1)}, u32[]{:S(2)}, u32[]{:S(2)}) collective-permute-start(bf16[16,2048]{1,0:T(8,128)(2,1)S(1)} %maximum_select_fusion.9), channel_id=1, source_target_pairs={{0,8},{4,12},{8,0},{12,4},{16,24},{20,28},{24,16},{28,20},{1,9},{5... | collective-permute-start | bytes 196616 | tf_op jit(solution)/shard_map/ppermute | solution.py:16
  5.3 2.6 %collective-permute-start.4 = (bf16[1,16,3584]{2,1,0:T(8,128)(2,1)}, bf16[1,16,3584]{2,1,0:T(8,128)(2,1)S(1)}, u32[]{:S(2)}, u32[]{:S(2)}) collective-permute-start(bf16[1,16,3584]{2,1,0:T(8,128)(2,1)} %bitcast.29), channel_id=1, source_target_pairs={{0,2},{1,3},{2,0},{3,1},{4,6},{5,7},{6,4},{7,5},{8,10},{9,11},{10,... | collective-permute-start | bytes 344072 | tf_op jit(solution)/shard_map/ppermute | solution.py:16
  7.9 1.8 %collective-permute-start.2 = (bf16[32,2048]{1,0:T(8,128)(2,1)S(1)}, bf16[32,2048]{1,0:T(8,128)(2,1)S(1)}, u32[]{:S(2)}, u32[]{:S(2)}) collective-permute-start(bf16[32,2048]{1,0:T(8,128)(2,1)S(1)} %maximum_select_fusion.6), channel_id=1, source_target_pairs={{0,16},{4,20},{8,24},{12,28},{16,0},{20,4},{24,8},{28,12},{1,17},{... | collective-permute-start | bytes 393224 | tf_op jit(solution)/shard_map/ppermute | solution.py:16
  9.7 4.1 %collective-permute-done.4 = bf16[1,16,3584]{2,1,0:T(8,128)(2,1)S(1)} collective-permute-done((bf16[1,16,3584]{2,1,0:T(8,128)(2,1)}, bf16[1,16,3584]{2,1,0:T(8,128)(2,1)S(1)}, u32[]{:S(2)}, u32[]{:S(2)}) %collective-permute-start.4) | collective-permute-done | bytes 114720 | tf_op jit(solution)/shard_map/ppermute | solution.py:16
  15.6 3.0 %fusion.8 = f32[64,1024]{1,0:T(8,128)S(1)} fusion(bf16[2048,1024]{1,0:T(8,128)(2,1)} %param.9, bf16[32,2048]{1,0:T(8,128)(2,1)S(1)} %collective-permute-done.2, bf16[32,2048]{1,0:T(8,128)(2,1)S(1)} %maximum_select_fusion.6, pred[]{:T(512)S(6)} %eq.52), kind=kOutput, calls=%fused_computation.20 | convolution fusion | flops 269615104 | bytes 4718593 | tf_op jit(solution)/shard_map/dot_general | solution.py:143
  18.6 1.3 %collective-permute-start.3 = (f32[64,1024]{1,0:T(8,128)S(1)}, f32[64,1024]{1,0:T(8,128)S(1)}, u32[]{:S(2)}, u32[]{:S(2)}) collective-permute-start(f32[64,1024]{1,0:T(8,128)S(1)} %fusion.8), channel_id=1, source_target_pairs={{0,1},{1,0},{2,3},{3,2},{4,5},{5,4},{6,7},{7,6},{8,9},{9,8},{10,11... | collective-permute-start | bytes 786440 | tf_op jit(solution)/shard_map/ppermute | solution.py:16
  19.9 1.7 %collective-permute-done.5 = bf16[2,16,3584]{2,1,0:T(8,128)(2,1)S(1)} collective-permute-done((bf16[2,16,3584]{2,1,0:T(8,128)(2,1)S(1)}, bf16[2,16,3584]{2,1,0:T(8,128)(2,1)S(1)}, u32[]{:S(2)}, u32[]{:S(2)}) %collective-permute-start.5) | collective-permute-done | bytes 229408 | tf_op jit(solution)/shard_map/ppermute | solution.py:16
  21.7 6.0 %fusion = f32[64,1792]{1,0:T(8,128)S(1)} fusion(bf16[64,3584]{1,0:T(8,128)(2,1)S(1)} %bitcast.25, bf16[3584,7168]{1,0:T(8,128)(2,1)} %param.8), kind=kOutput, calls=%fused_computation | convolution fusion | flops 822083584 | bytes 13762560 | tf_op jit(solution)/shard_map/dot_general | solution.py:147
  27.7 7.8 %broadcast_select_fusion = (f32[64,1792]{1,0:T(8,128)}, f32[64,1792]{1,0:T(8,128)S(1)}) fusion(f32[64,1792]{1,0:T(8,128)S(1)} %fusion, pred[]{:T(512)S(6)} %eq.51, bf16[64,3584]{1,0:T(8,128)(2,1)S(1)} %bitcast.26, bf16[3584,7168]{1,0:T(8,128)(2,1)} %param.8), kind=kOutput, calls=%fused_computation.36 | convolution fusion | flops 822198272 | bytes 14680065 | tf_op jit(solution)/shard_map/dot_general | solution.py:147
  35.5 6.0 %fusion.6 = f32[64,1792]{1,0:T(8,128)S(1)} fusion(bf16[64,3584]{1,0:T(8,128)(2,1)S(1)} %bitcast.27, bf16[3584,7168]{1,0:T(8,128)(2,1)} %param.8), kind=kOutput, calls=%fused_computation.6 | convolution fusion | flops 822083584 | bytes 13762560 | tf_op jit(solution)/shard_map/dot_general | solution.py:147
  41.6 3.3 %collective-permute-start.6 = (f32[64,1024]{1,0:T(8,128)S(1)}, f32[64,1024]{1,0:T(8,128)S(1)}, u32[]{:S(2)}, u32[]{:S(2)}) collective-permute-start(f32[64,1024]{1,0:T(8,128)S(1)} %add.92), channel_id=1, source_target_pairs={{0,2},{1,3},{2,0},{3,1},{4,6},{5,7},{6,4},{7,5},{8,10},{9,11},{10,... | collective-permute-start | bytes 786440 | tf_op jit(solution)/shard_map/ppermute | solution.py:16
  44.9 6.0 %fusion.4 = f32[64,1792]{1,0:T(8,128)S(1)} fusion(bf16[64,3584]{1,0:T(8,128)(2,1)S(1)} %bitcast.28, bf16[3584,7168]{1,0:T(8,128)(2,1)} %param.8), kind=kOutput, calls=%fused_computation.4 | convolution fusion | flops 822083584 | bytes 13762560 | tf_op jit(solution)/shard_map/dot_general | solution.py:147
  50.9 5.3 %collective-permute-done.6 = f32[64,1024]{1,0:T(8,128)S(1)} collective-permute-done((f32[64,1024]{1,0:T(8,128)S(1)}, f32[64,1024]{1,0:T(8,128)S(1)}, u32[]{:S(2)}, u32[]{:S(2)}) %collective-permute-start.6) | collective-permute-done | bytes 262176 | tf_op jit(solution)/shard_map/ppermute | solution.py:16
  56.9 3.8 %shard_map.64 = f32[2,64,1024]{2,1,0:T(8,128)S(1)} custom-call(bf16[64,1024]{1,0:T(8,128)(2,1)S(1)} %add_convert_fusion.a_ref, bf16[7168,1024]{1,0:T(8,128)(2,1)} %e_ref.11, bf16[2,7168,1024]{2,1,0:T(8,128)(2,1)} %q_ref.11), custom_call_target="tpu_custom_call" | custom-call | flops 268435456 | bytes 6815744 | tf_op jit(solution)/shard_map/pallas_call | solution.py:119
  61.5 1.5 %collective-permute-start.10 = (f32[64,896]{1,0:T(8,128)S(1)}, f32[64,896]{1,0:T(8,128)S(1)}, u32[]{:S(2)}, u32[]{:S(2)}) collective-permute-start(f32[64,896]{1,0:T(8,128)S(1)} %slice_select_fusion), channel_id=1, source_target_pairs={{0,16},{4,20},{8,24},{12,28},{16,0},{20,4},{24,8},{28,12},{1,17},{... | collective-permute-start | bytes 688136 | tf_op jit(solution)/shard_map/ppermute | solution.py:16
  63.0 8.5 %shard_map.65 = f32[2,64,2560]{2,1,0:T(8,128)S(1)} custom-call(bf16[64,1024]{1,0:T(8,128)(2,1)S(1)} %add_convert_fusion.a_ref, bf16[7168,1024]{1,0:T(8,128)(2,1)} %e_ref.11, bf16[2,7168,1024]{2,1,0:T(8,128)(2,1)} %q_ref.11), custom_call_target="tpu_custom_call" | custom-call | flops 671088640 | bytes 17039360 | tf_op jit(solution)/shard_map/pallas_call | solution.py:119
  72.4 1.5 %collective-permute-start.12 = (f32[64,448]{1,0:T(8,128)S(1)}, f32[64,448]{1,0:T(8,128)S(1)}, u32[]{:S(2)}, u32[]{:S(2)}) collective-permute-start(f32[64,448]{1,0:T(8,128)S(1)} %slice_select_fusion.2), channel_id=1, source_target_pairs={{0,8},{4,12},{8,0},{12,4},{16,24},{20,28},{24,16},{28,20},{1,9},{5... | collective-permute-start | bytes 344072 | tf_op jit(solution)/shard_map/ppermute | solution.py:16
  73.9 3.8 %shard_map.66 = f32[2,64,1024]{2,1,0:T(8,128)S(1)} custom-call(bf16[64,1024]{1,0:T(8,128)(2,1)S(1)} %add_convert_fusion.a_ref, bf16[7168,1024]{1,0:T(8,128)(2,1)} %e_ref.11, bf16[2,7168,1024]{2,1,0:T(8,128)(2,1)} %q_ref.11), custom_call_target="tpu_custom_call" | custom-call | flops 268435456 | bytes 6815744 | tf_op jit(solution)/shard_map/pallas_call | solution.py:119
  77.9 1.6 %collective-permute-start.13 = (bf16[64,448]{1,0:T(8,128)(2,1)S(1)}, bf16[64,448]{1,0:T(8,128)(2,1)S(1)}, u32[]{:S(2)}, u32[]{:S(2)}) collective-permute-start(bf16[64,448]{1,0:T(8,128)(2,1)S(1)} %add_convert_fusion.2), channel_id=1, source_target_pairs={{0,16},{4,20},{8,24},{12,28},{16,0},{20,4},{24,8},{28,12},{1,17},{... | collective-permute-start | bytes 172040 | tf_op jit(solution)/shard_map/ppermute | solution.py:16
  79.5 1.2 %collective-permute-start.14 = (bf16[64,448]{1,0:T(8,128)(2,1)S(1)}, bf16[64,448]{1,0:T(8,128)(2,1)S(1)}, u32[]{:S(2)}, u32[]{:S(2)}) collective-permute-start(bf16[64,448]{1,0:T(8,128)(2,1)S(1)} %add_convert_fusion.1), channel_id=1, source_target_pairs={{0,8},{4,12},{8,0},{12,4},{16,24},{20,28},{24,16},{28,20},{1,9},{5... | collective-permute-start | bytes 172040 | tf_op jit(solution)/shard_map/ppermute | solution.py:16
  80.6 3.8 %shard_map.67 = f32[2,64,1024]{2,1,0:T(8,128)S(1)} custom-call(bf16[64,1024]{1,0:T(8,128)(2,1)S(1)} %add_convert_fusion.a_ref, bf16[7168,1024]{1,0:T(8,128)(2,1)} %e_ref.11, bf16[2,7168,1024]{2,1,0:T(8,128)(2,1)} %q_ref.11), custom_call_target="tpu_custom_call" | custom-call | flops 268435456 | bytes 6815744 | tf_op jit(solution)/shard_map/pallas_call | solution.py:119
  86.1 3.8 %shard_map.68 = f32[2,64,1024]{2,1,0:T(8,128)S(1)} custom-call(bf16[64,1024]{1,0:T(8,128)(2,1)S(1)} %add_convert_fusion.a_ref, bf16[7168,1024]{1,0:T(8,128)(2,1)} %e_ref.11, bf16[2,7168,1024]{2,1,0:T(8,128)(2,1)} %q_ref.11), custom_call_target="tpu_custom_call" | custom-call | flops 268435456 | bytes 6815744 | tf_op jit(solution)/shard_map/pallas_call | solution.py:119
  91.1 2.8 %shard_map.69 = f32[2,64,512]{2,1,0:T(8,128)S(1)} custom-call(bf16[64,1024]{1,0:T(8,128)(2,1)S(1)} %add_convert_fusion.a_ref, bf16[7168,1024]{1,0:T(8,128)(2,1)} %e_ref.11, bf16[2,7168,1024]{2,1,0:T(8,128)(2,1)} %q_ref.11), custom_call_target="tpu_custom_call" | custom-call | flops 134217728 | bytes 3407872 | tf_op jit(solution)/shard_map/pallas_call | solution.py:119
  95.8 2.9 %collective-permute-done.19 = f32[2,64]{1,0:T(2,128)S(1)} collective-permute-done((f32[2,64]{1,0:T(2,128)S(1)}, f32[2,64]{1,0:T(2,128)S(1)}, u32[]{:S(2)}, u32[]{:S(2)}) %collective-permute-start.19) | collective-permute-done | bytes 544 | tf_op jit(solution)/shard_map/ppermute | solution.py:16
  98.7 2.0 %collective-permute-start.20 = (f32[2,64]{1,0:T(2,128)S(1)}, f32[2,64]{1,0:T(2,128)S(1)}, u32[]{:S(2)}, u32[]{:S(2)}) collective-permute-start(f32[2,64]{1,0:T(2,128)S(1)} %add.105), channel_id=1, source_target_pairs={{0,2},{1,3},{2,0},{3,1},{4,6},{5,7},{6,4},{7,5},{8,10},{9,11},{10,... | collective-permute-start | bytes 1544 | tf_op jit(solution)/shard_map/ppermute | solution.py:16
  100.8 2.4 %collective-permute-done.20 = f32[2,64]{1,0:T(2,128)S(1)} collective-permute-done((f32[2,64]{1,0:T(2,128)S(1)}, f32[2,64]{1,0:T(2,128)S(1)}, u32[]{:S(2)}, u32[]{:S(2)}) %collective-permute-start.20) | collective-permute-done | bytes 544 | tf_op jit(solution)/shard_map/ppermute | solution.py:16
  103.2 1.1 %collective-permute-done.21 = f32[2,64]{1,0:T(2,128)S(1)} collective-permute-done((f32[2,64]{1,0:T(2,128)S(1)}, f32[2,64]{1,0:T(2,128)S(1)}, u32[]{:S(2)}, u32[]{:S(2)}) %collective-permute-start.21) | collective-permute-done | bytes 544 | tf_op jit(solution)/shard_map/ppermute | solution.py:16
  104.3 1.2 %collective-permute-start.22 = (f32[2,64]{1,0:T(2,128)S(1)}, f32[2,64]{1,0:T(2,128)S(1)}, u32[]{:S(2)}, u32[]{:S(2)}) collective-permute-start(f32[2,64]{1,0:T(2,128)S(1)} %add.107), channel_id=1, source_target_pairs={{0,8},{4,12},{8,0},{12,4},{16,24},{20,28},{24,16},{28,20},{1,9},{5... | collective-permute-start | bytes 1544 | tf_op jit(solution)/shard_map/ppermute | solution.py:16
  105.5 2.4 %collective-permute-done.22 = f32[2,64]{1,0:T(2,128)S(1)} collective-permute-done((f32[2,64]{1,0:T(2,128)S(1)}, f32[2,64]{1,0:T(2,128)S(1)}, u32[]{:S(2)}, u32[]{:S(2)}) %collective-permute-start.22) | collective-permute-done | bytes 544 | tf_op jit(solution)/shard_map/ppermute | solution.py:16
  107.9 1.0 collective-permute-start.23
  108.9 2.5 %collective-permute-done.23 = f32[2,64]{1,0:T(2,128)S(1)} collective-permute-done((f32[2,64]{1,0:T(2,128)S(1)}, f32[2,64]{1,0:T(2,128)S(1)}, u32[]{:S(2)}, u32[]{:S(2)}) %collective-permute-start.23) | collective-permute-done | bytes 544 | tf_op jit(solution)/shard_map/ppermute | solution.py:16
  (67 shorter events, 11.1 us)
Async XLA Ops:
  0.0 1.5 %collective-permute-start = (bf16[8,2048]{1,0:T(8,128)(2,1)}, bf16[8,2048]{1,0:T(8,128)(2,1)S(1)}, u32[]{:S(2)}, u32[]{:S(2)}) collective-permute-start(bf16[8,2048]{1,0:T(8,128)(2,1)} %param.7), channel_id=1, source_target_pairs={{0,4},{4,0},{8,12},{12,8},{16,20},{20,16},{24,28},{28,24},{1,5},{5... | collective-permute-start | bytes 98312 | tf_op jit(solution)/shard_map/ppermute | solution.py:16
  2.4 5.5 %collective-permute-start.1 = (bf16[16,2048]{1,0:T(8,128)(2,1)S(1)}, bf16[16,2048]{1,0:T(8,128)(2,1)S(1)}, u32[]{:S(2)}, u32[]{:S(2)}) collective-permute-start(bf16[16,2048]{1,0:T(8,128)(2,1)S(1)} %maximum_select_fusion.9), channel_id=1, source_target_pairs={{0,8},{4,12},{8,0},{12,4},{16,24},{20,28},{24,16},{28,20},{1,9},{5... | collective-permute-start | bytes 196616 | tf_op jit(solution)/shard_map/ppermute | solution.py:16
  5.3 8.5 %collective-permute-start.4 = (bf16[1,16,3584]{2,1,0:T(8,128)(2,1)}, bf16[1,16,3584]{2,1,0:T(8,128)(2,1)S(1)}, u32[]{:S(2)}, u32[]{:S(2)}) collective-permute-start(bf16[1,16,3584]{2,1,0:T(8,128)(2,1)} %bitcast.29), channel_id=1, source_target_pairs={{0,2},{1,3},{2,0},{3,1},{4,6},{5,7},{6,4},{7,5},{8,10},{9,11},{10,... | collective-permute-start | bytes 344072 | tf_op jit(solution)/shard_map/ppermute | solution.py:16
  7.9 7.7 %collective-permute-start.2 = (bf16[32,2048]{1,0:T(8,128)(2,1)S(1)}, bf16[32,2048]{1,0:T(8,128)(2,1)S(1)}, u32[]{:S(2)}, u32[]{:S(2)}) collective-permute-start(bf16[32,2048]{1,0:T(8,128)(2,1)S(1)} %maximum_select_fusion.6), channel_id=1, source_target_pairs={{0,16},{4,20},{8,24},{12,28},{16,0},{20,4},{24,8},{28,12},{1,17},{... | collective-permute-start | bytes 393224 | tf_op jit(solution)/shard_map/ppermute | solution.py:16
  14.7 6.9 %collective-permute-start.5 = (bf16[2,16,3584]{2,1,0:T(8,128)(2,1)S(1)}, bf16[2,16,3584]{2,1,0:T(8,128)(2,1)S(1)}, u32[]{:S(2)}, u32[]{:S(2)}) collective-permute-start(bf16[2,16,3584]{2,1,0:T(8,128)(2,1)S(1)} %maximum_bitcast_fusion), channel_id=1, source_target_pairs={{0,1},{1,0},{2,3},{3,2},{4,5},{5,4},{6,7},{7,6},{8,9},{9,8},{10,11... | collective-permute-start | bytes 688136 | tf_op jit(solution)/shard_map/ppermute | solution.py:16
  18.6 22.9 %collective-permute-start.3 = (f32[64,1024]{1,0:T(8,128)S(1)}, f32[64,1024]{1,0:T(8,128)S(1)}, u32[]{:S(2)}, u32[]{:S(2)}) collective-permute-start(f32[64,1024]{1,0:T(8,128)S(1)} %fusion.8), channel_id=1, source_target_pairs={{0,1},{1,0},{2,3},{3,2},{4,5},{5,4},{6,7},{7,6},{8,9},{9,8},{10,11... | collective-permute-start | bytes 786440 | tf_op jit(solution)/shard_map/ppermute | solution.py:16
  41.6 14.6 %collective-permute-start.6 = (f32[64,1024]{1,0:T(8,128)S(1)}, f32[64,1024]{1,0:T(8,128)S(1)}, u32[]{:S(2)}, u32[]{:S(2)}) collective-permute-start(f32[64,1024]{1,0:T(8,128)S(1)} %add.92), channel_id=1, source_target_pairs={{0,2},{1,3},{2,0},{3,1},{4,6},{5,7},{6,4},{7,5},{8,10},{9,11},{10,... | collective-permute-start | bytes 786440 | tf_op jit(solution)/shard_map/ppermute | solution.py:16
  56.3 4.3 %collective-permute-start.7 = (f32[64,1792]{1,0:T(8,128)S(1)}, f32[64,1792]{1,0:T(8,128)S(1)}, u32[]{:S(2)}, u32[]{:S(2)}) collective-permute-start(f32[64,1792]{1,0:T(8,128)S(1)} %broadcast_select_fusion.1), channel_id=1, source_target_pairs={{0,4},{4,0},{8,12},{12,8},{16,20},{20,16},{24,28},{28,24},{1,5},{5... | collective-permute-start | bytes 1376264 | tf_op jit(solution)/shard_map/ppermute | solution.py:16
  56.4 4.3 %collective-permute-start.8 = (f32[64,1792]{1,0:T(8,128)}, f32[64,1792]{1,0:T(8,128)S(1)}, u32[]{:S(2)}, u32[]{:S(2)}) collective-permute-start(f32[64,1792]{1,0:T(8,128)} %get-tuple-element.54), channel_id=1, source_target_pairs={{0,4},{4,0},{8,12},{12,8},{16,20},{20,16},{24,28},{28,24},{1,5},{5... | collective-permute-start | bytes 1376264 | tf_op jit(solution)/shard_map/ppermute | solution.py:16
  60.9 10.6 %collective-permute-start.9 = (f32[64,896]{1,0:T(8,128)S(1)}, f32[64,896]{1,0:T(8,128)S(1)}, u32[]{:S(2)}, u32[]{:S(2)}) collective-permute-start(f32[64,896]{1,0:T(8,128)S(1)} %slice_select_fusion.1), channel_id=1, source_target_pairs={{0,8},{4,12},{8,0},{12,4},{16,24},{20,28},{24,16},{28,20},{1,9},{5... | collective-permute-start | bytes 688136 | tf_op jit(solution)/shard_map/ppermute | solution.py:16
  61.5 10.0 %collective-permute-start.10 = (f32[64,896]{1,0:T(8,128)S(1)}, f32[64,896]{1,0:T(8,128)S(1)}, u32[]{:S(2)}, u32[]{:S(2)}) collective-permute-start(f32[64,896]{1,0:T(8,128)S(1)} %slice_select_fusion), channel_id=1, source_target_pairs={{0,16},{4,20},{8,24},{12,28},{16,0},{20,4},{24,8},{28,12},{1,17},{... | collective-permute-start | bytes 688136 | tf_op jit(solution)/shard_map/ppermute | solution.py:16
  71.8 5.8 %collective-permute-start.11 = (f32[64,448]{1,0:T(8,128)S(1)}, f32[64,448]{1,0:T(8,128)S(1)}, u32[]{:S(2)}, u32[]{:S(2)}) collective-permute-start(f32[64,448]{1,0:T(8,128)S(1)} %slice_select_fusion.3), channel_id=1, source_target_pairs={{0,16},{4,20},{8,24},{12,28},{16,0},{20,4},{24,8},{28,12},{1,17},{... | collective-permute-start | bytes 344072 | tf_op jit(solution)/shard_map/ppermute | solution.py:16
  72.4 5.3 %collective-permute-start.12 = (f32[64,448]{1,0:T(8,128)S(1)}, f32[64,448]{1,0:T(8,128)S(1)}, u32[]{:S(2)}, u32[]{:S(2)}) collective-permute-start(f32[64,448]{1,0:T(8,128)S(1)} %slice_select_fusion.2), channel_id=1, source_target_pairs={{0,8},{4,12},{8,0},{12,4},{16,24},{20,28},{24,16},{28,20},{1,9},{5... | collective-permute-start | bytes 344072 | tf_op jit(solution)/shard_map/ppermute | solution.py:16
  77.9 6.5 %collective-permute-start.13 = (bf16[64,448]{1,0:T(8,128)(2,1)S(1)}, bf16[64,448]{1,0:T(8,128)(2,1)S(1)}, u32[]{:S(2)}, u32[]{:S(2)}) collective-permute-start(bf16[64,448]{1,0:T(8,128)(2,1)S(1)} %add_convert_fusion.2), channel_id=1, source_target_pairs={{0,16},{4,20},{8,24},{12,28},{16,0},{20,4},{24,8},{28,12},{1,17},{... | collective-permute-start | bytes 172040 | tf_op jit(solution)/shard_map/ppermute | solution.py:16
  79.5 5.0 %collective-permute-start.14 = (bf16[64,448]{1,0:T(8,128)(2,1)S(1)}, bf16[64,448]{1,0:T(8,128)(2,1)S(1)}, u32[]{:S(2)}, u32[]{:S(2)}) collective-permute-start(bf16[64,448]{1,0:T(8,128)(2,1)S(1)} %add_convert_fusion.1), channel_id=1, source_target_pairs={{0,8},{4,12},{8,0},{12,4},{16,24},{20,28},{24,16},{28,20},{1,9},{5... | collective-permute-start | bytes 172040 | tf_op jit(solution)/shard_map/ppermute | solution.py:16
  84.7 5.2 %collective-permute-start.15 = (bf16[64,896]{1,0:T(8,128)(2,1)S(1)}, bf16[64,896]{1,0:T(8,128)(2,1)S(1)}, u32[]{:S(2)}, u32[]{:S(2)}) collective-permute-start(bf16[64,896]{1,0:T(8,128)(2,1)S(1)} %maximum_select_fusion.7), channel_id=1, source_target_pairs={{0,8},{4,12},{8,0},{12,4},{16,24},{20,28},{24,16},{28,20},{1,9},{5... | collective-permute-start | bytes 344072 | tf_op jit(solution)/shard_map/ppermute | solution.py:16
  85.6 4.8 %collective-permute-start.16 = (bf16[64,896]{1,0:T(8,128)(2,1)S(1)}, bf16[64,896]{1,0:T(8,128)(2,1)S(1)}, u32[]{:S(2)}, u32[]{:S(2)}) collective-permute-start(bf16[64,896]{1,0:T(8,128)(2,1)S(1)} %maximum_select_fusion.8), channel_id=1, source_target_pairs={{0,16},{4,20},{8,24},{12,28},{16,0},{20,4},{24,8},{28,12},{1,17},{... | collective-permute-start | bytes 344072 | tf_op jit(solution)/shard_map/ppermute | solution.py:16
  90.5 3.4 %collective-permute-start.17 = (bf16[64,1792]{1,0:T(8,128)(2,1)S(1)}, bf16[64,1792]{1,0:T(8,128)(2,1)S(1)}, u32[]{:S(2)}, u32[]{:S(2)}) collective-permute-start(bf16[64,1792]{1,0:T(8,128)(2,1)S(1)} %maximum_select_fusion.4), channel_id=1, source_target_pairs={{0,4},{4,0},{8,12},{12,8},{16,20},{20,16},{24,28},{28,24},{1,5},{5... | collective-permute-start | bytes 688136 | tf_op jit(solution)/shard_map/ppermute | solution.py:16
  90.6 3.3 %collective-permute-start.18 = (bf16[64,1792]{1,0:T(8,128)(2,1)S(1)}, bf16[64,1792]{1,0:T(8,128)(2,1)S(1)}, u32[]{:S(2)}, u32[]{:S(2)}) collective-permute-start(bf16[64,1792]{1,0:T(8,128)(2,1)S(1)} %maximum_select_fusion.5), channel_id=1, source_target_pairs={{0,4},{4,0},{8,12},{12,8},{16,20},{20,16},{24,28},{28,24},{1,5},{5... | collective-permute-start | bytes 688136 | tf_op jit(solution)/shard_map/ppermute | solution.py:16
  95.1 3.6 %collective-permute-start.19 = (f32[2,64]{1,0:T(2,128)S(1)}, f32[2,64]{1,0:T(2,128)S(1)}, u32[]{:S(2)}, u32[]{:S(2)}) collective-permute-start(f32[2,64]{1,0:T(2,128)S(1)} %add_add_fusion), channel_id=1, source_target_pairs={{0,1},{1,0},{2,3},{3,2},{4,5},{5,4},{6,7},{7,6},{8,9},{9,8},{10,11... | collective-permute-start | bytes 1544 | tf_op jit(solution)/shard_map/ppermute | solution.py:16
  98.7 4.5 %collective-permute-start.20 = (f32[2,64]{1,0:T(2,128)S(1)}, f32[2,64]{1,0:T(2,128)S(1)}, u32[]{:S(2)}, u32[]{:S(2)}) collective-permute-start(f32[2,64]{1,0:T(2,128)S(1)} %add.105), channel_id=1, source_target_pairs={{0,2},{1,3},{2,0},{3,1},{4,6},{5,7},{6,4},{7,5},{8,10},{9,11},{10,... | collective-permute-start | bytes 1544 | tf_op jit(solution)/shard_map/ppermute | solution.py:16
  103.2 1.1 %collective-permute-start.21 = (f32[2,64]{1,0:T(2,128)S(1)}, f32[2,64]{1,0:T(2,128)S(1)}, u32[]{:S(2)}, u32[]{:S(2)}) collective-permute-start(f32[2,64]{1,0:T(2,128)S(1)} %add.106), channel_id=1, source_target_pairs={{0,4},{4,0},{8,12},{12,8},{16,20},{20,16},{24,28},{28,24},{1,5},{5... | collective-permute-start | bytes 1544 | tf_op jit(solution)/shard_map/ppermute | solution.py:16
  104.3 3.6 %collective-permute-start.22 = (f32[2,64]{1,0:T(2,128)S(1)}, f32[2,64]{1,0:T(2,128)S(1)}, u32[]{:S(2)}, u32[]{:S(2)}) collective-permute-start(f32[2,64]{1,0:T(2,128)S(1)} %add.107), channel_id=1, source_target_pairs={{0,8},{4,12},{8,0},{12,4},{16,24},{20,28},{24,16},{28,20},{1,9},{5... | collective-permute-start | bytes 1544 | tf_op jit(solution)/shard_map/ppermute | solution.py:16
  107.9 3.6 %collective-permute-start.23 = (f32[2,64]{1,0:T(2,128)S(1)}, f32[2,64]{1,0:T(2,128)S(1)}, u32[]{:S(2)}, u32[]{:S(2)}) collective-permute-start(f32[2,64]{1,0:T(2,128)S(1)} %add.108), channel_id=1, source_target_pairs={{0,16},{4,20},{8,24},{12,28},{16,0},{20,4},{24,8},{28,12},{1,17},{... | collective-permute-start | bytes 1544 | tf_op jit(solution)/shard_map/ppermute | solution.py:16

commit v11 on v9

--- a/solution.py
+++ b/solution.py
@@ -148,7 +148,7 @@
     kk = queries.shape[1]
     tk = next(c for c in (512, 256, 128, kk) if kk % c == 0)
     nt = kk // tk
-    weights = [2, 5, 2, 2, 2, 1] if nl == 6 else [1] * nl
+    weights = [2, 4, 2, 2, 2, 2] if nl == 6 else [1] * nl
     acc = [0]
     for w in weights:
         acc.append(acc[-1] + w)

time: 109 us -> 108 us (level)
  no operation moved by 1% of the time
where the time goes in v11:
time: 108 us
  starting transfers between devices  30.5 us (28%)
  matrix products  26.9 us (25%)
  Pallas kernels  25.6 us (24%)
  waiting for transfers between devices  18.6 us (17%)
  other arithmetic  5.9 us (5%)
    ppermute x26, starting transfers between devices, _swap(): return lax.ppermute(x, axis, [(i, i ^ b) for i in range(n)])  30.5 us
    pallas_call x6, Pallas kernels, _lifted(): pl.pallas_call(_lifted_kernel, grid=(t1 - t0,), in_specs=[pl.BlockSpec((t...  25.6 us
    dot_general x4, matrix products, local(): jnp.dot(g, out_basis[:, c0:c1], preferred_element_type=F32)  23.9 us
    ppermute x26, waiting for transfers between devices, _swap(): return lax.ppermute(x, axis, [(i, i ^ b) for i in range(n)])  18.6 us
    dot_general x1, matrix products, local(): act_part = jnp.dot(acts_all, in_basis, preferred_element_type=F32)  3.03 us
  transfers between devices with their start and end apart: 26, of which 9 were waited for; matrix products, arithmetic and copies ran while one was open for 26% of the time, Pallas kernels for 24%

profile of v11, /device:TPU:0, one launch (start us, length us, event | category | flops | bytes accessed | tf_op | source)
XLA Modules:
  0.0 107.9 jit_solution(14658447275952559392)
XLA Ops:
  0.5 1.1 collective-permute-done
  2.4 2.9 %collective-permute-start.1 = (bf16[16,2048]{1,0:T(8,128)(2,1)S(1)}, bf16[16,2048]{1,0:T(8,128)(2,1)S(1)}, u32[]{:S(2)}, u32[]{:S(2)}) collective-permute-start(bf16[16,2048]{1,0:T(8,128)(2,1)S(1)} %maximum_select_fusion.10), channel_id=1, source_target_pairs={{0,8},{4,12},{8,0},{12,4},{16,24},{20,28},{24,16},{28,20},{1,9},{5... | collective-permute-start | bytes 196616 | tf_op jit(solution)/shard_map/ppermute | solution.py:16
  5.3 2.6 %collective-permute-start.4 = (bf16[1,16,3584]{2,1,0:T(8,128)(2,1)}, bf16[1,16,3584]{2,1,0:T(8,128)(2,1)S(1)}, u32[]{:S(2)}, u32[]{:S(2)}) collective-permute-start(bf16[1,16,3584]{2,1,0:T(8,128)(2,1)} %bitcast.29), channel_id=1, source_target_pairs={{0,2},{1,3},{2,0},{3,1},{4,6},{5,7},{6,4},{7,5},{8,10},{9,11},{10,... | collective-permute-start | bytes 344072 | tf_op jit(solution)/shard_map/ppermute | solution.py:16
  7.9 1.8 %collective-permute-start.2 = (bf16[32,2048]{1,0:T(8,128)(2,1)S(1)}, bf16[32,2048]{1,0:T(8,128)(2,1)S(1)}, u32[]{:S(2)}, u32[]{:S(2)}) collective-permute-start(bf16[32,2048]{1,0:T(8,128)(2,1)S(1)} %maximum_select_fusion.6), channel_id=1, source_target_pairs={{0,16},{4,20},{8,24},{12,28},{16,0},{20,4},{24,8},{28,12},{1,17},{... | collective-permute-start | bytes 393224 | tf_op jit(solution)/shard_map/ppermute | solution.py:16
  9.7 4.1 %collective-permute-done.4 = bf16[1,16,3584]{2,1,0:T(8,128)(2,1)S(1)} collective-permute-done((bf16[1,16,3584]{2,1,0:T(8,128)(2,1)}, bf16[1,16,3584]{2,1,0:T(8,128)(2,1)S(1)}, u32[]{:S(2)}, u32[]{:S(2)}) %collective-permute-start.4) | collective-permute-done | bytes 114720 | tf_op jit(solution)/shard_map/ppermute | solution.py:16
  15.6 3.0 %fusion.8 = f32[64,1024]{1,0:T(8,128)S(1)} fusion(bf16[2048,1024]{1,0:T(8,128)(2,1)} %param.9, bf16[32,2048]{1,0:T(8,128)(2,1)S(1)} %collective-permute-done.2, bf16[32,2048]{1,0:T(8,128)(2,1)S(1)} %maximum_select_fusion.6, pred[]{:T(512)S(6)} %eq.65), kind=kOutput, calls=%fused_computation.21 | convolution fusion | flops 269615104 | bytes 4718593 | tf_op jit(solution)/shard_map/dot_general | solution.py:138
  18.6 1.3 %collective-permute-start.3 = (f32[64,512]{1,0:T(8,128)S(1)}, f32[64,512]{1,0:T(8,128)S(1)}, u32[]{:S(2)}, u32[]{:S(2)}) collective-permute-start(f32[64,512]{1,0:T(8,128)S(1)} %slice_select_fusion.4), channel_id=1, source_target_pairs={{0,1},{1,0},{2,3},{3,2},{4,5},{5,4},{6,7},{7,6},{8,9},{9,8},{10,11... | collective-permute-start | bytes 393224 | tf_op jit(solution)/shard_map/ppermute | solution.py:16
  20.0 1.6 %collective-permute-done.5 = bf16[2,16,3584]{2,1,0:T(8,128)(2,1)S(1)} collective-permute-done((bf16[2,16,3584]{2,1,0:T(8,128)(2,1)S(1)}, bf16[2,16,3584]{2,1,0:T(8,128)(2,1)S(1)}, u32[]{:S(2)}, u32[]{:S(2)}) %collective-permute-start.5) | collective-permute-done | bytes 229408 | tf_op jit(solution)/shard_map/ppermute | solution.py:16
  21.7 6.0 %fusion.6 = f32[64,1792]{1,0:T(8,128)S(1)} fusion(bf16[64,3584]{1,0:T(8,128)(2,1)S(1)} %bitcast.25, bf16[3584,7168]{1,0:T(8,128)(2,1)} %param.8), kind=kOutput, calls=%fused_computation.6 | convolution fusion | flops 822083584 | bytes 13762560 | tf_op jit(solution)/shard_map/dot_general | solution.py:142
  27.7 3.3 %collective-permute-start.6 = (f32[64,256]{1,0:T(8,128)S(1)}, f32[64,256]{1,0:T(8,128)S(1)}, u32[]{:S(2)}, u32[]{:S(2)}) collective-permute-start(f32[64,256]{1,0:T(8,128)S(1)} %slice_select_fusion.5), channel_id=1, source_target_pairs={{0,2},{1,3},{2,0},{3,1},{4,6},{5,7},{6,4},{7,5},{8,10},{9,11},{10,... | collective-permute-start | bytes 196616 | tf_op jit(solution)/shard_map/ppermute | solution.py:16
  31.1 6.0 %fusion.4 = f32[64,1792]{1,0:T(8,128)S(1)} fusion(bf16[64,3584]{1,0:T(8,128)(2,1)S(1)} %bitcast.26, bf16[3584,7168]{1,0:T(8,128)(2,1)} %param.8), kind=kOutput, calls=%fused_computation.4 | convolution fusion | flops 822083584 | bytes 13762560 | tf_op jit(solution)/shard_map/dot_general | solution.py:142
  37.2 6.0 %fusion.2 = f32[64,1792]{1,0:T(8,128)S(1)} fusion(bf16[64,3584]{1,0:T(8,128)(2,1)S(1)} %bitcast.27, bf16[3584,7168]{1,0:T(8,128)(2,1)} %param.8), kind=kOutput, calls=%fused_computation.2 | convolution fusion | flops 822083584 | bytes 13762560 | tf_op jit(solution)/shard_map/dot_general | solution.py:142
  43.3 2.5 %collective-permute-start.8 = (bf16[64,512]{1,0:T(8,128)(2,1)S(1)}, bf16[64,512]{1,0:T(8,128)(2,1)S(1)}, u32[]{:S(2)}, u32[]{:S(2)}) collective-permute-start(bf16[64,512]{1,0:T(8,128)(2,1)S(1)} %maximum_select_fusion.11), channel_id=1, source_target_pairs={{0,1},{1,0},{2,3},{3,2},{4,5},{5,4},{6,7},{7,6},{8,9},{9,8},{10,11... | collective-permute-start | bytes 196616 | tf_op jit(solution)/shard_map/ppermute | solution.py:16
  45.8 6.0 %fusion = f32[64,1792]{1,0:T(8,128)S(1)} fusion(bf16[64,3584]{1,0:T(8,128)(2,1)S(1)} %bitcast.28, bf16[3584,7168]{1,0:T(8,128)(2,1)} %param.8), kind=kOutput, calls=%fused_computation | convolution fusion | flops 822083584 | bytes 13762560 | tf_op jit(solution)/shard_map/dot_general | solution.py:142
  52.4 3.8 %shard_map.64 = f32[2,64,1024]{2,1,0:T(8,128)S(1)} custom-call(bf16[64,1024]{1,0:T(8,128)(2,1)S(1)} %maximum_select_fusion.7.a_ref, bf16[7168,1024]{1,0:T(8,128)(2,1)} %e_ref.11, bf16[2,7168,1024]{2,1,0:T(8,128)(2,1)} %q_ref.11), custom_call_target="tpu_custom_call" | custom-call | flops 268435456 | bytes 6815744 | tf_op jit(solution)/shard_map/pallas_call | solution.py:114
  56.2 1.1 %select_add_fusion = f32[64,1792]{1,0:T(8,128)S(1)} fusion(f32[64,1792]{1,0:T(8,128)} %collective-permute-done.10, f32[64,1792]{1,0:T(8,128)S(1)} %fusion, f32[64,1792]{1,0:T(8,128)S(1)} %fusion.2, pred[]{:T(512)S(6)} %eq.63), kind=kLoop, calls=%fused_computation.17 | loop fusion | flops 229376 | bytes 1835009 | tf_op jit(solution)/shard_map/add | solution.py:80
  58.0 1.5 %collective-permute-start.12 = (f32[64,896]{1,0:T(8,128)S(1)}, f32[64,896]{1,0:T(8,128)S(1)}, u32[]{:S(2)}, u32[]{:S(2)}) collective-permute-start(f32[64,896]{1,0:T(8,128)S(1)} %slice_select_fusion), channel_id=1, source_target_pairs={{0,16},{4,20},{8,24},{12,28},{16,0},{20,4},{24,8},{28,12},{1,17},{... | collective-permute-start | bytes 688136 | tf_op jit(solution)/shard_map/ppermute | solution.py:16
  59.6 6.8 %shard_map.65 = f32[2,64,2048]{2,1,0:T(8,128)S(1)} custom-call(bf16[64,1024]{1,0:T(8,128)(2,1)S(1)} %maximum_select_fusion.7.a_ref, bf16[7168,1024]{1,0:T(8,128)(2,1)} %e_ref.11, bf16[2,7168,1024]{2,1,0:T(8,128)(2,1)} %q_ref.11), custom_call_target="tpu_custom_call" | custom-call | flops 536870912 | bytes 13631488 | tf_op jit(solution)/shard_map/pallas_call | solution.py:114
  67.2 1.5 %collective-permute-start.14 = (f32[64,448]{1,0:T(8,128)S(1)}, f32[64,448]{1,0:T(8,128)S(1)}, u32[]{:S(2)}, u32[]{:S(2)}) collective-permute-start(f32[64,448]{1,0:T(8,128)S(1)} %slice_select_fusion.2), channel_id=1, source_target_pairs={{0,8},{4,12},{8,0},{12,4},{16,24},{20,28},{24,16},{28,20},{1,9},{5... | collective-permute-start | bytes 344072 | tf_op jit(solution)/shard_map/ppermute | solution.py:16
  68.7 3.8 %shard_map.66 = f32[2,64,1024]{2,1,0:T(8,128)S(1)} custom-call(bf16[64,1024]{1,0:T(8,128)(2,1)S(1)} %maximum_select_fusion.7.a_ref, bf16[7168,1024]{1,0:T(8,128)(2,1)} %e_ref.11, bf16[2,7168,1024]{2,1,0:T(8,128)(2,1)} %q_ref.11), custom_call_target="tpu_custom_call" | custom-call | flops 268435456 | bytes 6815744 | tf_op jit(solution)/shard_map/pallas_call | solution.py:114
  72.7 1.6 %collective-permute-start.15 = (bf16[64,448]{1,0:T(8,128)(2,1)S(1)}, bf16[64,448]{1,0:T(8,128)(2,1)S(1)}, u32[]{:S(2)}, u32[]{:S(2)}) collective-permute-start(bf16[64,448]{1,0:T(8,128)(2,1)S(1)} %add_convert_fusion.1), channel_id=1, source_target_pairs={{0,16},{4,20},{8,24},{12,28},{16,0},{20,4},{24,8},{28,12},{1,17},{... | collective-permute-start | bytes 172040 | tf_op jit(solution)/shard_map/ppermute | solution.py:16
  74.3 1.2 %collective-permute-start.16 = (bf16[64,448]{1,0:T(8,128)(2,1)S(1)}, bf16[64,448]{1,0:T(8,128)(2,1)S(1)}, u32[]{:S(2)}, u32[]{:S(2)}) collective-permute-start(bf16[64,448]{1,0:T(8,128)(2,1)S(1)} %add_convert_fusion), channel_id=1, source_target_pairs={{0,8},{4,12},{8,0},{12,4},{16,24},{20,28},{24,16},{28,20},{1,9},{5... | collective-permute-start | bytes 172040 | tf_op jit(solution)/shard_map/ppermute | solution.py:16
  75.5 3.8 %shard_map.67 = f32[2,64,1024]{2,1,0:T(8,128)S(1)} custom-call(bf16[64,1024]{1,0:T(8,128)(2,1)S(1)} %maximum_select_fusion.7.a_ref, bf16[7168,1024]{1,0:T(8,128)(2,1)} %e_ref.11, bf16[2,7168,1024]{2,1,0:T(8,128)(2,1)} %q_ref.11), custom_call_target="tpu_custom_call" | custom-call | flops 268435456 | bytes 6815744 | tf_op jit(solution)/shard_map/pallas_call | solution.py:114
  80.9 3.8 %shard_map.68 = f32[2,64,1024]{2,1,0:T(8,128)S(1)} custom-call(bf16[64,1024]{1,0:T(8,128)(2,1)S(1)} %maximum_select_fusion.7.a_ref, bf16[7168,1024]{1,0:T(8,128)(2,1)} %e_ref.11, bf16[2,7168,1024]{2,1,0:T(8,128)(2,1)} %q_ref.11), custom_call_target="tpu_custom_call" | custom-call | flops 268435456 | bytes 6815744 | tf_op jit(solution)/shard_map/pallas_call | solution.py:114
  85.9 3.8 %shard_map.69 = f32[2,64,1024]{2,1,0:T(8,128)S(1)} custom-call(bf16[64,1024]{1,0:T(8,128)(2,1)S(1)} %maximum_select_fusion.7.a_ref, bf16[7168,1024]{1,0:T(8,128)(2,1)} %e_ref.11, bf16[2,7168,1024]{2,1,0:T(8,128)(2,1)} %q_ref.11), custom_call_target="tpu_custom_call" | custom-call | flops 268435456 | bytes 6815744 | tf_op jit(solution)/shard_map/pallas_call | solution.py:114
  91.0 3.5 %collective-permute-done.21 = f32[2,64]{1,0:T(2,128)S(1)} collective-permute-done((f32[2,64]{1,0:T(2,128)S(1)}, f32[2,64]{1,0:T(2,128)S(1)}, u32[]{:S(2)}, u32[]{:S(2)}) %collective-permute-start.21) | collective-permute-done | bytes 544 | tf_op jit(solution)/shard_map/ppermute | solution.py:16
  94.6 2.9 %collective-permute-start.22 = (f32[2,64]{1,0:T(2,128)S(1)}, f32[2,64]{1,0:T(2,128)S(1)}, u32[]{:S(2)}, u32[]{:S(2)}) collective-permute-start(f32[2,64]{1,0:T(2,128)S(1)} %add.109), channel_id=1, source_target_pairs={{0,2},{1,3},{2,0},{3,1},{4,6},{5,7},{6,4},{7,5},{8,10},{9,11},{10,... | collective-permute-start | bytes 1544 | tf_op jit(solution)/shard_map/ppermute | solution.py:16
  97.5 1.6 %collective-permute-done.22 = f32[2,64]{1,0:T(2,128)S(1)} collective-permute-done((f32[2,64]{1,0:T(2,128)S(1)}, f32[2,64]{1,0:T(2,128)S(1)}, u32[]{:S(2)}, u32[]{:S(2)}) %collective-permute-start.22) | collective-permute-done | bytes 544 | tf_op jit(solution)/shard_map/ppermute | solution.py:16
  99.1 1.1 %collective-permute-done.23 = f32[2,64]{1,0:T(2,128)S(1)} collective-permute-done((f32[2,64]{1,0:T(2,128)S(1)}, f32[2,64]{1,0:T(2,128)S(1)}, u32[]{:S(2)}, u32[]{:S(2)}) %collective-permute-start.23) | collective-permute-done | bytes 544 | tf_op jit(solution)/shard_map/ppermute | solution.py:16
  100.2 1.2 %collective-permute-start.24 = (f32[2,64]{1,0:T(2,128)S(1)}, f32[2,64]{1,0:T(2,128)S(1)}, u32[]{:S(2)}, u32[]{:S(2)}) collective-permute-start(f32[2,64]{1,0:T(2,128)S(1)} %add.111), channel_id=1, source_target_pairs={{0,8},{4,12},{8,0},{12,4},{16,24},{20,28},{24,16},{28,20},{1,9},{5... | collective-permute-start | bytes 1544 | tf_op jit(solution)/shard_map/ppermute | solution.py:16
  101.4 2.4 %collective-permute-done.24 = f32[2,64]{1,0:T(2,128)S(1)} collective-permute-done((f32[2,64]{1,0:T(2,128)S(1)}, f32[2,64]{1,0:T(2,128)S(1)}, u32[]{:S(2)}, u32[]{:S(2)}) %collective-permute-start.24) | collective-permute-done | bytes 544 | tf_op jit(solution)/shard_map/ppermute | solution.py:16
  104.8 2.5 %collective-permute-done.25 = f32[2,64]{1,0:T(2,128)S(1)} collective-permute-done((f32[2,64]{1,0:T(2,128)S(1)}, f32[2,64]{1,0:T(2,128)S(1)}, u32[]{:S(2)}, u32[]{:S(2)}) %collective-permute-start.25) | collective-permute-done | bytes 544 | tf_op jit(solution)/shard_map/ppermute | solution.py:16
  (74 shorter events, 11.6 us)
Async XLA Ops:
  0.0 1.5 %collective-permute-start = (bf16[8,2048]{1,0:T(8,128)(2,1)}, bf16[8,2048]{1,0:T(8,128)(2,1)S(1)}, u32[]{:S(2)}, u32[]{:S(2)}) collective-permute-start(bf16[8,2048]{1,0:T(8,128)(2,1)} %param.7), channel_id=1, source_target_pairs={{0,4},{4,0},{8,12},{12,8},{16,20},{20,16},{24,28},{28,24},{1,5},{5... | collective-permute-start | bytes 98312 | tf_op jit(solution)/shard_map/ppermute | solution.py:16
  2.4 5.5 %collective-permute-start.1 = (bf16[16,2048]{1,0:T(8,128)(2,1)S(1)}, bf16[16,2048]{1,0:T(8,128)(2,1)S(1)}, u32[]{:S(2)}, u32[]{:S(2)}) collective-permute-start(bf16[16,2048]{1,0:T(8,128)(2,1)S(1)} %maximum_select_fusion.10), channel_id=1, source_target_pairs={{0,8},{4,12},{8,0},{12,4},{16,24},{20,28},{24,16},{28,20},{1,9},{5... | collective-permute-start | bytes 196616 | tf_op jit(solution)/shard_map/ppermute | solution.py:16
  5.3 8.5 %collective-permute-start.4 = (bf16[1,16,3584]{2,1,0:T(8,128)(2,1)}, bf16[1,16,3584]{2,1,0:T(8,128)(2,1)S(1)}, u32[]{:S(2)}, u32[]{:S(2)}) collective-permute-start(bf16[1,16,3584]{2,1,0:T(8,128)(2,1)} %bitcast.29), channel_id=1, source_target_pairs={{0,2},{1,3},{2,0},{3,1},{4,6},{5,7},{6,4},{7,5},{8,10},{9,11},{10,... | collective-permute-start | bytes 344072 | tf_op jit(solution)/shard_map/ppermute | solution.py:16
  7.9 7.7 %collective-permute-start.2 = (bf16[32,2048]{1,0:T(8,128)(2,1)S(1)}, bf16[32,2048]{1,0:T(8,128)(2,1)S(1)}, u32[]{:S(2)}, u32[]{:S(2)}) collective-permute-start(bf16[32,2048]{1,0:T(8,128)(2,1)S(1)} %maximum_select_fusion.6), channel_id=1, source_target_pairs={{0,16},{4,20},{8,24},{12,28},{16,0},{20,4},{24,8},{28,12},{1,17},{... | collective-permute-start | bytes 393224 | tf_op jit(solution)/shard_map/ppermute | solution.py:16
  14.7 6.9 %collective-permute-start.5 = (bf16[2,16,3584]{2,1,0:T(8,128)(2,1)S(1)}, bf16[2,16,3584]{2,1,0:T(8,128)(2,1)S(1)}, u32[]{:S(2)}, u32[]{:S(2)}) collective-permute-start(bf16[2,16,3584]{2,1,0:T(8,128)(2,1)S(1)} %maximum_bitcast_fusion), channel_id=1, source_target_pairs={{0,1},{1,0},{2,3},{3,2},{4,5},{5,4},{6,7},{7,6},{8,9},{9,8},{10,11... | collective-permute-start | bytes 688136 | tf_op jit(solution)/shard_map/ppermute | solution.py:16
  18.6 9.0 %collective-permute-start.3 = (f32[64,512]{1,0:T(8,128)S(1)}, f32[64,512]{1,0:T(8,128)S(1)}, u32[]{:S(2)}, u32[]{:S(2)}) collective-permute-start(f32[64,512]{1,0:T(8,128)S(1)} %slice_select_fusion.4), channel_id=1, source_target_pairs={{0,1},{1,0},{2,3},{3,2},{4,5},{5,4},{6,7},{7,6},{8,9},{9,8},{10,11... | collective-permute-start | bytes 393224 | tf_op jit(solution)/shard_map/ppermute | solution.py:16
  27.7 9.3 %collective-permute-start.6 = (f32[64,256]{1,0:T(8,128)S(1)}, f32[64,256]{1,0:T(8,128)S(1)}, u32[]{:S(2)}, u32[]{:S(2)}) collective-permute-start(f32[64,256]{1,0:T(8,128)S(1)} %slice_select_fusion.5), channel_id=1, source_target_pairs={{0,2},{1,3},{2,0},{3,1},{4,6},{5,7},{6,4},{7,5},{8,10},{9,11},{10,... | collective-permute-start | bytes 196616 | tf_op jit(solution)/shard_map/ppermute | solution.py:16
  37.1 6.2 %collective-permute-start.7 = (bf16[64,256]{1,0:T(8,128)(2,1)S(1)}, bf16[64,256]{1,0:T(8,128)(2,1)S(1)}, u32[]{:S(2)}, u32[]{:S(2)}) collective-permute-start(bf16[64,256]{1,0:T(8,128)(2,1)S(1)} %add_convert_fusion.2), channel_id=1, source_target_pairs={{0,2},{1,3},{2,0},{3,1},{4,6},{5,7},{6,4},{7,5},{8,10},{9,11},{10,... | collective-permute-start | bytes 98312 | tf_op jit(solution)/shard_map/ppermute | solution.py:16
  43.3 8.5 %collective-permute-start.8 = (bf16[64,512]{1,0:T(8,128)(2,1)S(1)}, bf16[64,512]{1,0:T(8,128)(2,1)S(1)}, u32[]{:S(2)}, u32[]{:S(2)}) collective-permute-start(bf16[64,512]{1,0:T(8,128)(2,1)S(1)} %maximum_select_fusion.11), channel_id=1, source_target_pairs={{0,1},{1,0},{2,3},{3,2},{4,5},{5,4},{6,7},{7,6},{8,9},{9,8},{10,11... | collective-permute-start | bytes 196616 | tf_op jit(solution)/shard_map/ppermute | solution.py:16
  51.8 4.3 %collective-permute-start.9 = (f32[64,1792]{1,0:T(8,128)S(1)}, f32[64,1792]{1,0:T(8,128)S(1)}, u32[]{:S(2)}, u32[]{:S(2)}) collective-permute-start(f32[64,1792]{1,0:T(8,128)S(1)} %broadcast_select_fusion.1), channel_id=1, source_target_pairs={{0,4},{4,0},{8,12},{12,8},{16,20},{20,16},{24,28},{28,24},{1,5},{5... | collective-permute-start | bytes 1376264 | tf_op jit(solution)/shard_map/ppermute | solution.py:16
  51.9 4.3 %collective-permute-start.10 = (f32[64,1792]{1,0:T(8,128)S(1)}, f32[64,1792]{1,0:T(8,128)}, u32[]{:S(2)}, u32[]{:S(2)}) collective-permute-start(f32[64,1792]{1,0:T(8,128)S(1)} %broadcast_select_fusion), channel_id=1, source_target_pairs={{0,4},{4,0},{8,12},{12,8},{16,20},{20,16},{24,28},{28,24},{1,5},{5... | collective-permute-start | bytes 1376264 | tf_op jit(solution)/shard_map/ppermute | solution.py:16
  57.4 8.9 %collective-permute-start.11 = (f32[64,896]{1,0:T(8,128)S(1)}, f32[64,896]{1,0:T(8,128)S(1)}, u32[]{:S(2)}, u32[]{:S(2)}) collective-permute-start(f32[64,896]{1,0:T(8,128)S(1)} %slice_select_fusion.1), channel_id=1, source_target_pairs={{0,8},{4,12},{8,0},{12,4},{16,24},{20,28},{24,16},{28,20},{1,9},{5... | collective-permute-start | bytes 688136 | tf_op jit(solution)/shard_map/ppermute | solution.py:16
  58.0 8.3 %collective-permute-start.12 = (f32[64,896]{1,0:T(8,128)S(1)}, f32[64,896]{1,0:T(8,128)S(1)}, u32[]{:S(2)}, u32[]{:S(2)}) collective-permute-start(f32[64,896]{1,0:T(8,128)S(1)} %slice_select_fusion), channel_id=1, source_target_pairs={{0,16},{4,20},{8,24},{12,28},{16,0},{20,4},{24,8},{28,12},{1,17},{... | collective-permute-start | bytes 688136 | tf_op jit(solution)/shard_map/ppermute | solution.py:16
  66.7 5.8 %collective-permute-start.13 = (f32[64,448]{1,0:T(8,128)S(1)}, f32[64,448]{1,0:T(8,128)S(1)}, u32[]{:S(2)}, u32[]{:S(2)}) collective-permute-start(f32[64,448]{1,0:T(8,128)S(1)} %slice_select_fusion.3), channel_id=1, source_target_pairs={{0,16},{4,20},{8,24},{12,28},{16,0},{20,4},{24,8},{28,12},{1,17},{... | collective-permute-start | bytes 344072 | tf_op jit(solution)/shard_map/ppermute | solution.py:16
  67.2 5.3 %collective-permute-start.14 = (f32[64,448]{1,0:T(8,128)S(1)}, f32[64,448]{1,0:T(8,128)S(1)}, u32[]{:S(2)}, u32[]{:S(2)}) collective-permute-start(f32[64,448]{1,0:T(8,128)S(1)} %slice_select_fusion.2), channel_id=1, source_target_pairs={{0,8},{4,12},{8,0},{12,4},{16,24},{20,28},{24,16},{28,20},{1,9},{5... | collective-permute-start | bytes 344072 | tf_op jit(solution)/shard_map/ppermute | solution.py:16
  72.7 6.5 %collective-permute-start.15 = (bf16[64,448]{1,0:T(8,128)(2,1)S(1)}, bf16[64,448]{1,0:T(8,128)(2,1)S(1)}, u32[]{:S(2)}, u32[]{:S(2)}) collective-permute-start(bf16[64,448]{1,0:T(8,128)(2,1)S(1)} %add_convert_fusion.1), channel_id=1, source_target_pairs={{0,16},{4,20},{8,24},{12,28},{16,0},{20,4},{24,8},{28,12},{1,17},{... | collective-permute-start | bytes 172040 | tf_op jit(solution)/shard_map/ppermute | solution.py:16
  74.3 5.0 %collective-permute-start.16 = (bf16[64,448]{1,0:T(8,128)(2,1)S(1)}, bf16[64,448]{1,0:T(8,128)(2,1)S(1)}, u32[]{:S(2)}, u32[]{:S(2)}) collective-permute-start(bf16[64,448]{1,0:T(8,128)(2,1)S(1)} %add_convert_fusion), channel_id=1, source_target_pairs={{0,8},{4,12},{8,0},{12,4},{16,24},{20,28},{24,16},{28,20},{1,9},{5... | collective-permute-start | bytes 172040 | tf_op jit(solution)/shard_map/ppermute | solution.py:16
  79.5 5.2 %collective-permute-start.17 = (bf16[64,896]{1,0:T(8,128)(2,1)S(1)}, bf16[64,896]{1,0:T(8,128)(2,1)S(1)}, u32[]{:S(2)}, u32[]{:S(2)}) collective-permute-start(bf16[64,896]{1,0:T(8,128)(2,1)S(1)} %maximum_select_fusion.8), channel_id=1, source_target_pairs={{0,8},{4,12},{8,0},{12,4},{16,24},{20,28},{24,16},{28,20},{1,9},{5... | collective-permute-start | bytes 344072 | tf_op jit(solution)/shard_map/ppermute | solution.py:16
  80.4 4.8 %collective-permute-start.18 = (bf16[64,896]{1,0:T(8,128)(2,1)S(1)}, bf16[64,896]{1,0:T(8,128)(2,1)S(1)}, u32[]{:S(2)}, u32[]{:S(2)}) collective-permute-start(bf16[64,896]{1,0:T(8,128)(2,1)S(1)} %maximum_select_fusion.9), channel_id=1, source_target_pairs={{0,16},{4,20},{8,24},{12,28},{16,0},{20,4},{24,8},{28,12},{1,17},{... | collective-permute-start | bytes 344072 | tf_op jit(solution)/shard_map/ppermute | solution.py:16
  85.3 4.4 %collective-permute-start.19 = (bf16[64,1792]{1,0:T(8,128)(2,1)S(1)}, bf16[64,1792]{1,0:T(8,128)(2,1)S(1)}, u32[]{:S(2)}, u32[]{:S(2)}) collective-permute-start(bf16[64,1792]{1,0:T(8,128)(2,1)S(1)} %maximum_select_fusion.4), channel_id=1, source_target_pairs={{0,4},{4,0},{8,12},{12,8},{16,20},{20,16},{24,28},{28,24},{1,5},{5... | collective-permute-start | bytes 688136 | tf_op jit(solution)/shard_map/ppermute | solution.py:16
  85.4 4.3 %collective-permute-start.20 = (bf16[64,1792]{1,0:T(8,128)(2,1)S(1)}, bf16[64,1792]{1,0:T(8,128)(2,1)S(1)}, u32[]{:S(2)}, u32[]{:S(2)}) collective-permute-start(bf16[64,1792]{1,0:T(8,128)(2,1)S(1)} %maximum_select_fusion.5), channel_id=1, source_target_pairs={{0,4},{4,0},{8,12},{12,8},{16,20},{20,16},{24,28},{28,24},{1,5},{5... | collective-permute-start | bytes 688136 | tf_op jit(solution)/shard_map/ppermute | solution.py:16
  91.0 3.6 %collective-permute-start.21 = (f32[2,64]{1,0:T(2,128)S(1)}, f32[2,64]{1,0:T(2,128)S(1)}, u32[]{:S(2)}, u32[]{:S(2)}) collective-permute-start(f32[2,64]{1,0:T(2,128)S(1)} %add_add_fusion), channel_id=1, source_target_pairs={{0,1},{1,0},{2,3},{3,2},{4,5},{5,4},{6,7},{7,6},{8,9},{9,8},{10,11... | collective-permute-start | bytes 1544 | tf_op jit(solution)/shard_map/ppermute | solution.py:16
  94.6 4.5 %collective-permute-start.22 = (f32[2,64]{1,0:T(2,128)S(1)}, f32[2,64]{1,0:T(2,128)S(1)}, u32[]{:S(2)}, u32[]{:S(2)}) collective-permute-start(f32[2,64]{1,0:T(2,128)S(1)} %add.109), channel_id=1, source_target_pairs={{0,2},{1,3},{2,0},{3,1},{4,6},{5,7},{6,4},{7,5},{8,10},{9,11},{10,... | collective-permute-start | bytes 1544 | tf_op jit(solution)/shard_map/ppermute | solution.py:16
  99.1 1.1 %collective-permute-start.23 = (f32[2,64]{1,0:T(2,128)S(1)}, f32[2,64]{1,0:T(2,128)S(1)}, u32[]{:S(2)}, u32[]{:S(2)}) collective-permute-start(f32[2,64]{1,0:T(2,128)S(1)} %add.110), channel_id=1, source_target_pairs={{0,4},{4,0},{8,12},{12,8},{16,20},{20,16},{24,28},{28,24},{1,5},{5... | collective-permute-start | bytes 1544 | tf_op jit(solution)/shard_map/ppermute | solution.py:16
  100.2 3.6 %collective-permute-start.24 = (f32[2,64]{1,0:T(2,128)S(1)}, f32[2,64]{1,0:T(2,128)S(1)}, u32[]{:S(2)}, u32[]{:S(2)}) collective-permute-start(f32[2,64]{1,0:T(2,128)S(1)} %add.111), channel_id=1, source_target_pairs={{0,8},{4,12},{8,0},{12,4},{16,24},{20,28},{24,16},{28,20},{1,9},{5... | collective-permute-start | bytes 1544 | tf_op jit(solution)/shard_map/ppermute | solution.py:16
  103.8 3.6 %collective-permute-start.25 = (f32[2,64]{1,0:T(2,128)S(1)}, f32[2,64]{1,0:T(2,128)S(1)}, u32[]{:S(2)}, u32[]{:S(2)}) collective-permute-start(f32[2,64]{1,0:T(2,128)S(1)} %add.112), channel_id=1, source_target_pairs={{0,16},{4,20},{8,24},{12,28},{16,0},{20,4},{24,8},{28,12},{1,17},{... | collective-permute-start | bytes 1544 | tf_op jit(solution)/shard_map/ppermute | solution.py:16

commit v12 on v11

--- a/solution.py
+++ b/solution.py
@@ -133,7 +133,7 @@
 
 
 def local(out_grads, in_acts, out_basis, in_basis, eigenvalues, queries, *, nr, nc, nl, ng):
-    acts_all = _gather(in_acts, "row", nr, 0)
+    acts_all = lax.all_gather(in_acts, "row", axis=0, tiled=True)
     grads_all = _gather_far_first(out_grads, "col", nc)
     act_part = jnp.dot(acts_all, in_basis, preferred_element_type=F32)
     nb = out_basis.shape[1] // 128

time: 108 us -> 114 us (1.056)
  blocking collectives: 0 us -> 9.51 us
  starting transfers between devices: 30.5 us -> 23.2 us
  other arithmetic: 5.9 us -> 8.19 us
  waiting for transfers between devices: 18.6 us -> 20.3 us
    all_gather x0 -> x1, blocking collectives: none -> 9.51 us  [local(): acts_all = lax.all_gather(in_acts, 'row', axis=0, tiled=True)]
    ppermute x26 -> x23, starting transfers between devices: 30.5 us -> 23.2 us  [_swap(): return lax.ppermute(x, axis, [(i, i ^ b) for i in range(n)])]
    select_n x7 -> x8, other arithmetic: 0.6 us -> 3.62 us  [_allreduce_bf16(): jnp.where(first, jnp.concatenate([v, other], dim), jnp.concatenate([other...]
    ppermute x26 -> x23, waiting for transfers between devices: 18.6 us -> 20.3 us  [_swap(): return lax.ppermute(x, axis, [(i, i ^ b) for i in range(n)])]
  transfers between devices with their start and end apart: 26 -> 23, of which waited for: 9 -> 7; matrix products, arithmetic and copies ran while one was open for 26% -> 24% of each run, Pallas kernels for 24% -> 22%
where the time goes in v12:
time: 114 us
  matrix products  26.7 us (23%)
  Pallas kernels  25.6 us (22%)
  starting transfers between devices  23.2 us (20%)
  waiting for transfers between devices  20.3 us (18%)
  blocking collectives  9.51 us (8%)
  other arithmetic  8.19 us (7%)
    pallas_call x6, Pallas kernels, _lifted(): pl.pallas_call(_lifted_kernel, grid=(t1 - t0,), in_specs=[pl.BlockSpec((t...  25.6 us
    dot_general x4, matrix products, local(): jnp.dot(g, out_basis[:, c0:c1], preferred_element_type=F32)  23.7 us
    ppermute x23, starting transfers between devices, _swap(): return lax.ppermute(x, axis, [(i, i ^ b) for i in range(n)])  23.2 us
    ppermute x23, waiting for transfers between devices, _swap(): return lax.ppermute(x, axis, [(i, i ^ b) for i in range(n)])  20.3 us
    all_gather x1, blocking collectives, local(): acts_all = lax.all_gather(in_acts, 'row', axis=0, tiled=True)  9.51 us
    select_n x8, other arithmetic, _allreduce_bf16(): jnp.where(first, jnp.concatenate([v, other], dim), jnp.concatenate([other...  3.62 us
    dot_general x1, matrix products, local(): act_part = jnp.dot(acts_all, in_basis, preferred_element_type=F32)  3.02 us
  transfers between devices with their start and end apart: 23, of which 7 were waited for; matrix products, arithmetic and copies ran while one was open for 24% of the time, Pallas kernels for 22%

profile of v12, /device:TPU:0, one launch (start us, length us, event | category | flops | bytes accessed | tf_op | source)
XLA Modules:
  0.0 114.0 jit_solution(11568323401575106880)
XLA Ops:
  0.0 4.0 %collective-permute-start.1 = (bf16[1,16,3584]{2,1,0:T(8,128)(2,1)}, bf16[1,16,3584]{2,1,0:T(8,128)(2,1)S(1)}, u32[]{:S(2)}, u32[]{:S(2)}) collective-permute-start(bf16[1,16,3584]{2,1,0:T(8,128)(2,1)} %bitcast.30), channel_id=1, source_target_pairs={{0,2},{1,3},{2,0},{3,1},{4,6},{5,7},{6,4},{7,5},{8,10},{9,11},{10,... | collective-permute-start | bytes 344072 | tf_op jit(solution)/shard_map/ppermute | solution.py:16
  4.0 9.5 %all_gather.3 = bf16[64,2048]{1,0:T(8,128)(2,1)S(1)} all-gather(bf16[8,2048]{1,0:T(8,128)(2,1)} %param.7), channel_id=1, replica_groups=mesh['row'=8,'col'=4] {'row'}, dimensions={0}, use_global_device_ids=true | all-gather | bytes 294912 | tf_op jit(solution)/shard_map/all_gather | solution.py:136
  13.5 3.0 %fusion.9 = f32[64,1024]{1,0:T(8,128)S(1)} fusion(bf16[64,2048]{1,0:T(8,128)(2,1)S(1)} %all_gather.3, bf16[2048,1024]{1,0:T(8,128)(2,1)} %param.9), kind=kOutput, calls=%fused_computation.52 | convolution fusion | flops 268435456 | bytes 4718592 | tf_op jit(solution)/shard_map/dot_general | solution.py:138
  16.6 0.9 select_bitcast_fusion.3
  17.6 1.6 %collective-permute-start.2 = (bf16[2,16,3584]{2,1,0:T(8,128)(2,1)S(1)}, bf16[2,16,3584]{2,1,0:T(8,128)(2,1)S(1)}, u32[]{:S(2)}, u32[]{:S(2)}) collective-permute-start(bf16[2,16,3584]{2,1,0:T(8,128)(2,1)S(1)} %maximum_bitcast_fusion), channel_id=1, source_target_pairs={{0,1},{1,0},{2,3},{3,2},{4,5},{5,4},{6,7},{7,6},{8,9},{9,8},{10,11... | collective-permute-start | bytes 688136 | tf_op jit(solution)/shard_map/ppermute | solution.py:16
  19.8 6.3 %collective-permute-done.2 = bf16[2,16,3584]{2,1,0:T(8,128)(2,1)S(1)} collective-permute-done((bf16[2,16,3584]{2,1,0:T(8,128)(2,1)S(1)}, bf16[2,16,3584]{2,1,0:T(8,128)(2,1)S(1)}, u32[]{:S(2)}, u32[]{:S(2)}) %collective-permute-start.2) | collective-permute-done | bytes 229408 | tf_op jit(solution)/shard_map/ppermute | solution.py:16
  26.2 5.9 %fusion.6 = f32[64,1792]{1,0:T(8,128)S(1)} fusion(bf16[64,3584]{1,0:T(8,128)(2,1)S(1)} %bitcast.26, bf16[3584,7168]{1,0:T(8,128)(2,1)} %param.8), kind=kOutput, calls=%fused_computation.6 | convolution fusion | flops 822083584 | bytes 13762560 | tf_op jit(solution)/shard_map/dot_general | solution.py:142
  32.6 5.9 %fusion.4 = f32[64,1792]{1,0:T(8,128)S(1)} fusion(bf16[64,3584]{1,0:T(8,128)(2,1)S(1)} %bitcast.27, bf16[3584,7168]{1,0:T(8,128)(2,1)} %param.8), kind=kOutput, calls=%fused_computation.4 | convolution fusion | flops 822083584 | bytes 13762560 | tf_op jit(solution)/shard_map/dot_general | solution.py:142
  38.5 2.7 %collective-permute-start.4 = (bf16[64,256]{1,0:T(8,128)(2,1)S(1)}, bf16[64,256]{1,0:T(8,128)(2,1)S(1)}, u32[]{:S(2)}, u32[]{:S(2)}) collective-permute-start(bf16[64,256]{1,0:T(8,128)(2,1)S(1)} %add_convert_fusion.2), channel_id=1, source_target_pairs={{0,2},{1,3},{2,0},{3,1},{4,6},{5,7},{6,4},{7,5},{8,10},{9,11},{10,... | collective-permute-start | bytes 98312 | tf_op jit(solution)/shard_map/ppermute | solution.py:16
  41.2 6.0 %fusion.2 = f32[64,1792]{1,0:T(8,128)S(1)} fusion(bf16[64,3584]{1,0:T(8,128)(2,1)S(1)} %bitcast.28, bf16[3584,7168]{1,0:T(8,128)(2,1)} %param.8), kind=kOutput, calls=%fused_computation.2 | convolution fusion | flops 822083584 | bytes 13762560 | tf_op jit(solution)/shard_map/dot_general | solution.py:142
  47.2 1.6 %collective-permute-start.5 = (bf16[64,512]{1,0:T(8,128)(2,1)S(1)}, bf16[64,512]{1,0:T(8,128)(2,1)S(1)}, u32[]{:S(2)}, u32[]{:S(2)}) collective-permute-start(bf16[64,512]{1,0:T(8,128)(2,1)S(1)} %maximum_select_fusion.7), channel_id=1, source_target_pairs={{0,1},{1,0},{2,3},{3,2},{4,5},{5,4},{6,7},{7,6},{8,9},{9,8},{10,11... | collective-permute-start | bytes 196616 | tf_op jit(solution)/shard_map/ppermute | solution.py:16
  48.9 5.9 %fusion = f32[64,1792]{1,0:T(8,128)S(1)} fusion(bf16[64,3584]{1,0:T(8,128)(2,1)S(1)} %bitcast.29, bf16[3584,7168]{1,0:T(8,128)(2,1)} %param.8), kind=kOutput, calls=%fused_computation | convolution fusion | flops 822083584 | bytes 13762560 | tf_op jit(solution)/shard_map/dot_general | solution.py:142
  55.5 3.8 %shard_map.64 = f32[2,64,1024]{2,1,0:T(8,128)S(1)} custom-call(bf16[64,1024]{1,0:T(8,128)(2,1)S(1)} %maximum_select_fusion.4.a_ref, bf16[7168,1024]{1,0:T(8,128)(2,1)} %e_ref.11, bf16[2,7168,1024]{2,1,0:T(8,128)(2,1)} %q_ref.11), custom_call_target="tpu_custom_call" | custom-call | flops 268435456 | bytes 6815744 | tf_op jit(solution)/shard_map/pallas_call | solution.py:114
  59.3 1.3 %select_add_fusion = (f32[64,1792]{1,0:T(8,128)S(1)}, f32[64,1792]{1,0:T(8,128)S(1)}) fusion(f32[64,1792]{1,0:T(8,128)} %collective-permute-done.7, f32[64,1792]{1,0:T(8,128)S(1)} %fusion, f32[64,1792]{1,0:T(8,128)S(1)} %fusion.2, pred[]{:T(512)S(6)} %eq.57, f32[64,1792]{1,0:T(8,128)} %collective-permute-done.6, f32[64,1792]{1,0:T(8,128)S(1)} %fusion.4, ...), kind=kLoop, calls=%fused_computation.17 | loop fusion | flops 458752 | bytes 3670017 | tf_op jit(solution)/shard_map/add | solution.py:80
  60.6 1.4 %collective-permute-start.8 = (f32[64,896]{1,0:T(8,128)S(1)}, f32[64,896]{1,0:T(8,128)S(1)}, u32[]{:S(2)}, u32[]{:S(2)}) collective-permute-start(f32[64,896]{1,0:T(8,128)S(1)} %slice_select_fusion.1), channel_id=1, source_target_pairs={{0,8},{4,12},{8,0},{12,4},{16,24},{20,28},{24,16},{28,20},{1,9},{5... | collective-permute-start | bytes 688136 | tf_op jit(solution)/shard_map/ppermute | solution.py:16
  62.7 6.8 %shard_map.65 = f32[2,64,2048]{2,1,0:T(8,128)S(1)} custom-call(bf16[64,1024]{1,0:T(8,128)(2,1)S(1)} %maximum_select_fusion.4.a_ref, bf16[7168,1024]{1,0:T(8,128)(2,1)} %e_ref.11, bf16[2,7168,1024]{2,1,0:T(8,128)(2,1)} %q_ref.11), custom_call_target="tpu_custom_call" | custom-call | flops 536870912 | bytes 13631488 | tf_op jit(solution)/shard_map/pallas_call | solution.py:114
  69.8 1.3 %collective-permute-start.10 = (f32[64,448]{1,0:T(8,128)S(1)}, f32[64,448]{1,0:T(8,128)S(1)}, u32[]{:S(2)}, u32[]{:S(2)}) collective-permute-start(f32[64,448]{1,0:T(8,128)S(1)} %slice_select_fusion.3), channel_id=1, source_target_pairs={{0,16},{4,20},{8,24},{12,28},{16,0},{20,4},{24,8},{28,12},{1,17},{... | collective-permute-start | bytes 344072 | tf_op jit(solution)/shard_map/ppermute | solution.py:16
  71.9 3.8 %shard_map.66 = f32[2,64,1024]{2,1,0:T(8,128)S(1)} custom-call(bf16[64,1024]{1,0:T(8,128)(2,1)S(1)} %maximum_select_fusion.4.a_ref, bf16[7168,1024]{1,0:T(8,128)(2,1)} %e_ref.11, bf16[2,7168,1024]{2,1,0:T(8,128)(2,1)} %q_ref.11), custom_call_target="tpu_custom_call" | custom-call | flops 268435456 | bytes 6815744 | tf_op jit(solution)/shard_map/pallas_call | solution.py:114
  77.3 1.2 %collective-permute-start.13 = (bf16[64,448]{1,0:T(8,128)(2,1)S(1)}, bf16[64,448]{1,0:T(8,128)(2,1)S(1)}, u32[]{:S(2)}, u32[]{:S(2)}) collective-permute-start(bf16[64,448]{1,0:T(8,128)(2,1)S(1)} %add_convert_fusion), channel_id=1, source_target_pairs={{0,8},{4,12},{8,0},{12,4},{16,24},{20,28},{24,16},{28,20},{1,9},{5... | collective-permute-start | bytes 172040 | tf_op jit(solution)/shard_map/ppermute | solution.py:16
  78.4 3.8 %shard_map.67 = f32[2,64,1024]{2,1,0:T(8,128)S(1)} custom-call(bf16[64,1024]{1,0:T(8,128)(2,1)S(1)} %maximum_select_fusion.4.a_ref, bf16[7168,1024]{1,0:T(8,128)(2,1)} %e_ref.11, bf16[2,7168,1024]{2,1,0:T(8,128)(2,1)} %q_ref.11), custom_call_target="tpu_custom_call" | custom-call | flops 268435456 | bytes 6815744 | tf_op jit(solution)/shard_map/pallas_call | solution.py:114
  83.4 1.2 %collective-permute-start.15 = (bf16[64,896]{1,0:T(8,128)(2,1)S(1)}, bf16[64,896]{1,0:T(8,128)(2,1)S(1)}, u32[]{:S(2)}, u32[]{:S(2)}) collective-permute-start(bf16[64,896]{1,0:T(8,128)(2,1)S(1)} %maximum_select_fusion.6), channel_id=1, source_target_pairs={{0,16},{4,20},{8,24},{12,28},{16,0},{20,4},{24,8},{28,12},{1,17},{... | collective-permute-start | bytes 344072 | tf_op jit(solution)/shard_map/ppermute | solution.py:16
  84.5 3.8 %shard_map.68 = f32[2,64,1024]{2,1,0:T(8,128)S(1)} custom-call(bf16[64,1024]{1,0:T(8,128)(2,1)S(1)} %maximum_select_fusion.4.a_ref, bf16[7168,1024]{1,0:T(8,128)(2,1)} %e_ref.11, bf16[2,7168,1024]{2,1,0:T(8,128)(2,1)} %q_ref.11), custom_call_target="tpu_custom_call" | custom-call | flops 268435456 | bytes 6815744 | tf_op jit(solution)/shard_map/pallas_call | solution.py:114
  89.7 3.8 %shard_map.69 = f32[2,64,1024]{2,1,0:T(8,128)S(1)} custom-call(bf16[64,1024]{1,0:T(8,128)(2,1)S(1)} %maximum_select_fusion.4.a_ref, bf16[7168,1024]{1,0:T(8,128)(2,1)} %e_ref.11, bf16[2,7168,1024]{2,1,0:T(8,128)(2,1)} %q_ref.11), custom_call_target="tpu_custom_call" | custom-call | flops 268435456 | bytes 6815744 | tf_op jit(solution)/shard_map/pallas_call | solution.py:114
  93.5 1.2 %maximum_select_fusion = bf16[64,3584]{1,0:T(8,128)(2,1)S(1)} fusion(bf16[64,1792]{1,0:T(8,128)(2,1)} %collective-permute-done.16, bf16[64,1792]{1,0:T(8,128)(2,1)S(1)} %maximum_select_fusion.2, pred[]{:T(512)S(6)} %eq.62), kind=kLoop, calls=%fused_computation.15 | loop fusion | flops 2064384 | bytes 917505 | tf_op jit(solution)/shard_map/jit(_where)/select_n | solution.py:87
  94.6 1.4 %maximum_select_fusion.1 = bf16[64,3584]{1,0:T(8,128)(2,1)S(1)} fusion(bf16[64,1792]{1,0:T(8,128)(2,1)} %collective-permute-done.17, bf16[64,1792]{1,0:T(8,128)(2,1)} %maximum_select_fusion.3, pred[]{:T(512)S(6)} %eq.62), kind=kLoop, calls=%fused_computation.16 | loop fusion | flops 2064384 | bytes 917505 | tf_op jit(solution)/shard_map/jit(_where)/select_n | solution.py:87
  97.5 3.1 %collective-permute-done.18 = f32[2,64]{1,0:T(2,128)S(1)} collective-permute-done((f32[2,64]{1,0:T(2,128)S(1)}, f32[2,64]{1,0:T(2,128)S(1)}, u32[]{:S(2)}, u32[]{:S(2)}) %collective-permute-start.18) | collective-permute-done | bytes 544 | tf_op jit(solution)/shard_map/ppermute | solution.py:16
  101.0 4.1 %collective-permute-done.19 = f32[2,64]{1,0:T(2,128)S(1)} collective-permute-done((f32[2,64]{1,0:T(2,128)S(1)}, f32[2,64]{1,0:T(2,128)S(1)}, u32[]{:S(2)}, u32[]{:S(2)}) %collective-permute-start.19) | collective-permute-done | bytes 544 | tf_op jit(solution)/shard_map/ppermute | solution.py:16
  105.1 1.1 collective-permute-done.20
  106.3 1.0 collective-permute-start.21
  107.3 2.6 %collective-permute-done.21 = f32[2,64]{1,0:T(2,128)S(1)} collective-permute-done((f32[2,64]{1,0:T(2,128)S(1)}, f32[2,64]{1,0:T(2,128)S(1)}, u32[]{:S(2)}, u32[]{:S(2)}) %collective-permute-start.21) | collective-permute-done | bytes 544 | tf_op jit(solution)/shard_map/ppermute | solution.py:16
  109.9 1.0 collective-permute-start.22
  110.9 2.6 %collective-permute-done.22 = f32[2,64]{1,0:T(2,128)S(1)} collective-permute-done((f32[2,64]{1,0:T(2,128)S(1)}, f32[2,64]{1,0:T(2,128)S(1)}, u32[]{:S(2)}, u32[]{:S(2)}) %collective-permute-start.22) | collective-permute-done | bytes 544 | tf_op jit(solution)/shard_map/ppermute | solution.py:16
  (67 shorter events, 10.1 us)
Async XLA Ops:
  0.0 16.6 %collective-permute-start.1 = (bf16[1,16,3584]{2,1,0:T(8,128)(2,1)}, bf16[1,16,3584]{2,1,0:T(8,128)(2,1)S(1)}, u32[]{:S(2)}, u32[]{:S(2)}) collective-permute-start(bf16[1,16,3584]{2,1,0:T(8,128)(2,1)} %bitcast.30), channel_id=1, source_target_pairs={{0,2},{1,3},{2,0},{3,1},{4,6},{5,7},{6,4},{7,5},{8,10},{9,11},{10,... | collective-permute-start | bytes 344072 | tf_op jit(solution)/shard_map/ppermute | solution.py:16
  17.6 8.5 %collective-permute-start.2 = (bf16[2,16,3584]{2,1,0:T(8,128)(2,1)S(1)}, bf16[2,16,3584]{2,1,0:T(8,128)(2,1)S(1)}, u32[]{:S(2)}, u32[]{:S(2)}) collective-permute-start(bf16[2,16,3584]{2,1,0:T(8,128)(2,1)S(1)} %maximum_bitcast_fusion), channel_id=1, source_target_pairs={{0,1},{1,0},{2,3},{3,2},{4,5},{5,4},{6,7},{7,6},{8,9},{9,8},{10,11... | collective-permute-start | bytes 688136 | tf_op jit(solution)/shard_map/ppermute | solution.py:16
  19.3 12.9 %collective-permute-start = (f32[64,512]{1,0:T(8,128)S(1)}, f32[64,512]{1,0:T(8,128)S(1)}, u32[]{:S(2)}, u32[]{:S(2)}) collective-permute-start(f32[64,512]{1,0:T(8,128)S(1)} %slice_select_fusion.4), channel_id=1, source_target_pairs={{0,1},{1,0},{2,3},{3,2},{4,5},{5,4},{6,7},{7,6},{8,9},{9,8},{10,11... | collective-permute-start | bytes 393224 | tf_op jit(solution)/shard_map/ppermute | solution.py:16
  32.2 6.3 %collective-permute-start.3 = (f32[64,256]{1,0:T(8,128)S(1)}, f32[64,256]{1,0:T(8,128)S(1)}, u32[]{:S(2)}, u32[]{:S(2)}) collective-permute-start(f32[64,256]{1,0:T(8,128)S(1)} %slice_select_fusion.5), channel_id=1, source_target_pairs={{0,2},{1,3},{2,0},{3,1},{4,6},{5,7},{6,4},{7,5},{8,10},{9,11},{10,... | collective-permute-start | bytes 196616 | tf_op jit(solution)/shard_map/ppermute | solution.py:16
  38.5 8.7 %collective-permute-start.4 = (bf16[64,256]{1,0:T(8,128)(2,1)S(1)}, bf16[64,256]{1,0:T(8,128)(2,1)S(1)}, u32[]{:S(2)}, u32[]{:S(2)}) collective-permute-start(bf16[64,256]{1,0:T(8,128)(2,1)S(1)} %add_convert_fusion.2), channel_id=1, source_target_pairs={{0,2},{1,3},{2,0},{3,1},{4,6},{5,7},{6,4},{7,5},{8,10},{9,11},{10,... | collective-permute-start | bytes 98312 | tf_op jit(solution)/shard_map/ppermute | solution.py:16
  47.2 7.6 %collective-permute-start.5 = (bf16[64,512]{1,0:T(8,128)(2,1)S(1)}, bf16[64,512]{1,0:T(8,128)(2,1)S(1)}, u32[]{:S(2)}, u32[]{:S(2)}) collective-permute-start(bf16[64,512]{1,0:T(8,128)(2,1)S(1)} %maximum_select_fusion.7), channel_id=1, source_target_pairs={{0,1},{1,0},{2,3},{3,2},{4,5},{5,4},{6,7},{7,6},{8,9},{9,8},{10,11... | collective-permute-start | bytes 196616 | tf_op jit(solution)/shard_map/ppermute | solution.py:16
  54.9 4.3 %collective-permute-start.6 = (f32[64,1792]{1,0:T(8,128)S(1)}, f32[64,1792]{1,0:T(8,128)}, u32[]{:S(2)}, u32[]{:S(2)}) collective-permute-start(f32[64,1792]{1,0:T(8,128)S(1)} %broadcast_select_fusion.1), channel_id=1, source_target_pairs={{0,4},{4,0},{8,12},{12,8},{16,20},{20,16},{24,28},{28,24},{1,5},{5... | collective-permute-start | bytes 1376264 | tf_op jit(solution)/shard_map/ppermute | solution.py:16
  55.0 4.3 %collective-permute-start.7 = (f32[64,1792]{1,0:T(8,128)S(1)}, f32[64,1792]{1,0:T(8,128)}, u32[]{:S(2)}, u32[]{:S(2)}) collective-permute-start(f32[64,1792]{1,0:T(8,128)S(1)} %broadcast_select_fusion), channel_id=1, source_target_pairs={{0,4},{4,0},{8,12},{12,8},{16,20},{20,16},{24,28},{28,24},{1,5},{5... | collective-permute-start | bytes 1376264 | tf_op jit(solution)/shard_map/ppermute | solution.py:16
  60.6 8.9 %collective-permute-start.8 = (f32[64,896]{1,0:T(8,128)S(1)}, f32[64,896]{1,0:T(8,128)S(1)}, u32[]{:S(2)}, u32[]{:S(2)}) collective-permute-start(f32[64,896]{1,0:T(8,128)S(1)} %slice_select_fusion.1), channel_id=1, source_target_pairs={{0,8},{4,12},{8,0},{12,4},{16,24},{20,28},{24,16},{28,20},{1,9},{5... | collective-permute-start | bytes 688136 | tf_op jit(solution)/shard_map/ppermute | solution.py:16
  62.0 7.5 %collective-permute-start.9 = (f32[64,896]{1,0:T(8,128)S(1)}, f32[64,896]{1,0:T(8,128)S(1)}, u32[]{:S(2)}, u32[]{:S(2)}) collective-permute-start(f32[64,896]{1,0:T(8,128)S(1)} %slice_select_fusion), channel_id=1, source_target_pairs={{0,16},{4,20},{8,24},{12,28},{16,0},{20,4},{24,8},{28,12},{1,17},{... | collective-permute-start | bytes 688136 | tf_op jit(solution)/shard_map/ppermute | solution.py:16
  69.8 5.9 %collective-permute-start.10 = (f32[64,448]{1,0:T(8,128)S(1)}, f32[64,448]{1,0:T(8,128)S(1)}, u32[]{:S(2)}, u32[]{:S(2)}) collective-permute-start(f32[64,448]{1,0:T(8,128)S(1)} %slice_select_fusion.3), channel_id=1, source_target_pairs={{0,16},{4,20},{8,24},{12,28},{16,0},{20,4},{24,8},{28,12},{1,17},{... | collective-permute-start | bytes 344072 | tf_op jit(solution)/shard_map/ppermute | solution.py:16
  71.2 5.0 %collective-permute-start.11 = (f32[64,448]{1,0:T(8,128)S(1)}, f32[64,448]{1,0:T(8,128)S(1)}, u32[]{:S(2)}, u32[]{:S(2)}) collective-permute-start(f32[64,448]{1,0:T(8,128)S(1)} %slice_select_fusion.2), channel_id=1, source_target_pairs={{0,8},{4,12},{8,0},{12,4},{16,24},{20,28},{24,16},{28,20},{1,9},{5... | collective-permute-start | bytes 344072 | tf_op jit(solution)/shard_map/ppermute | solution.py:16
  76.3 5.9 %collective-permute-start.12 = (bf16[64,448]{1,0:T(8,128)(2,1)S(1)}, bf16[64,448]{1,0:T(8,128)(2,1)S(1)}, u32[]{:S(2)}, u32[]{:S(2)}) collective-permute-start(bf16[64,448]{1,0:T(8,128)(2,1)S(1)} %add_convert_fusion.1), channel_id=1, source_target_pairs={{0,16},{4,20},{8,24},{12,28},{16,0},{20,4},{24,8},{28,12},{1,17},{... | collective-permute-start | bytes 172040 | tf_op jit(solution)/shard_map/ppermute | solution.py:16
  77.3 5.0 %collective-permute-start.13 = (bf16[64,448]{1,0:T(8,128)(2,1)S(1)}, bf16[64,448]{1,0:T(8,128)(2,1)S(1)}, u32[]{:S(2)}, u32[]{:S(2)}) collective-permute-start(bf16[64,448]{1,0:T(8,128)(2,1)S(1)} %add_convert_fusion), channel_id=1, source_target_pairs={{0,8},{4,12},{8,0},{12,4},{16,24},{20,28},{24,16},{28,20},{1,9},{5... | collective-permute-start | bytes 172040 | tf_op jit(solution)/shard_map/ppermute | solution.py:16
  82.5 5.9 %collective-permute-start.14 = (bf16[64,896]{1,0:T(8,128)(2,1)S(1)}, bf16[64,896]{1,0:T(8,128)(2,1)S(1)}, u32[]{:S(2)}, u32[]{:S(2)}) collective-permute-start(bf16[64,896]{1,0:T(8,128)(2,1)S(1)} %maximum_select_fusion.5), channel_id=1, source_target_pairs={{0,8},{4,12},{8,0},{12,4},{16,24},{20,28},{24,16},{28,20},{1,9},{5... | collective-permute-start | bytes 344072 | tf_op jit(solution)/shard_map/ppermute | solution.py:16
  83.4 5.0 %collective-permute-start.15 = (bf16[64,896]{1,0:T(8,128)(2,1)S(1)}, bf16[64,896]{1,0:T(8,128)(2,1)S(1)}, u32[]{:S(2)}, u32[]{:S(2)}) collective-permute-start(bf16[64,896]{1,0:T(8,128)(2,1)S(1)} %maximum_select_fusion.6), channel_id=1, source_target_pairs={{0,16},{4,20},{8,24},{12,28},{16,0},{20,4},{24,8},{28,12},{1,17},{... | collective-permute-start | bytes 344072 | tf_op jit(solution)/shard_map/ppermute | solution.py:16
  89.2 4.3 %collective-permute-start.16 = (bf16[64,1792]{1,0:T(8,128)(2,1)S(1)}, bf16[64,1792]{1,0:T(8,128)(2,1)}, u32[]{:S(2)}, u32[]{:S(2)}) collective-permute-start(bf16[64,1792]{1,0:T(8,128)(2,1)S(1)} %maximum_select_fusion.2), channel_id=1, source_target_pairs={{0,4},{4,0},{8,12},{12,8},{16,20},{20,16},{24,28},{28,24},{1,5},{5... | collective-permute-start | bytes 688136 | tf_op jit(solution)/shard_map/ppermute | solution.py:16
  89.2 4.3 %collective-permute-start.17 = (bf16[64,1792]{1,0:T(8,128)(2,1)}, bf16[64,1792]{1,0:T(8,128)(2,1)}, u32[]{:S(2)}, u32[]{:S(2)}) collective-permute-start(bf16[64,1792]{1,0:T(8,128)(2,1)} %maximum_select_fusion.3), channel_id=1, source_target_pairs={{0,4},{4,0},{8,12},{12,8},{16,20},{20,16},{24,28},{28,24},{1,5},{5... | collective-permute-start | bytes 688136 | tf_op jit(solution)/shard_map/ppermute | solution.py:16
  97.0 3.6 %collective-permute-start.18 = (f32[2,64]{1,0:T(2,128)S(1)}, f32[2,64]{1,0:T(2,128)S(1)}, u32[]{:S(2)}, u32[]{:S(2)}) collective-permute-start(f32[2,64]{1,0:T(2,128)S(1)} %add_add_fusion), channel_id=1, source_target_pairs={{0,1},{1,0},{2,3},{3,2},{4,5},{5,4},{6,7},{7,6},{8,9},{9,8},{10,11... | collective-permute-start | bytes 1544 | tf_op jit(solution)/shard_map/ppermute | solution.py:16
  100.7 4.5 %collective-permute-start.19 = (f32[2,64]{1,0:T(2,128)S(1)}, f32[2,64]{1,0:T(2,128)S(1)}, u32[]{:S(2)}, u32[]{:S(2)}) collective-permute-start(f32[2,64]{1,0:T(2,128)S(1)} %add.106), channel_id=1, source_target_pairs={{0,2},{1,3},{2,0},{3,1},{4,6},{5,7},{6,4},{7,5},{8,10},{9,11},{10,... | collective-permute-start | bytes 1544 | tf_op jit(solution)/shard_map/ppermute | solution.py:16
  105.1 1.1 collective-permute-start.20
  106.3 3.6 %collective-permute-start.21 = (f32[2,64]{1,0:T(2,128)S(1)}, f32[2,64]{1,0:T(2,128)S(1)}, u32[]{:S(2)}, u32[]{:S(2)}) collective-permute-start(f32[2,64]{1,0:T(2,128)S(1)} %add.108), channel_id=1, source_target_pairs={{0,8},{4,12},{8,0},{12,4},{16,24},{20,28},{24,16},{28,20},{1,9},{5... | collective-permute-start | bytes 1544 | tf_op jit(solution)/shard_map/ppermute | solution.py:16
  109.9 3.6 %collective-permute-start.22 = (f32[2,64]{1,0:T(2,128)S(1)}, f32[2,64]{1,0:T(2,128)S(1)}, u32[]{:S(2)}, u32[]{:S(2)}) collective-permute-start(f32[2,64]{1,0:T(2,128)S(1)} %add.109), channel_id=1, source_target_pairs={{0,16},{4,20},{8,24},{12,28},{16,0},{20,4},{24,8},{28,12},{1,17},{... | collective-permute-start | bytes 1544 | tf_op jit(solution)/shard_map/ppermute | solution.py:16

commit v13 on v12

--- a/solution.py
+++ b/solution.py
@@ -133,7 +133,7 @@
 
 
 def local(out_grads, in_acts, out_basis, in_basis, eigenvalues, queries, *, nr, nc, nl, ng):
-    acts_all = lax.all_gather(in_acts, "row", axis=0, tiled=True)
+    acts_all = _gather_far_first(in_acts, "row", nr)
     grads_all = _gather_far_first(out_grads, "col", nc)
     act_part = jnp.dot(acts_all, in_basis, preferred_element_type=F32)
     nb = out_basis.shape[1] // 128

time: 114 us -> 108 us (0.947)
  blocking collectives: 9.51 us -> 0 us
  starting transfers between devices: 23.2 us -> 29.4 us
  other arithmetic: 8.19 us -> 5.89 us
    all_gather x1 -> x0, blocking collectives: 9.51 us -> none  [local(): acts_all = lax.all_gather(in_acts, 'row', axis=0, tiled=True)]
    ppermute x23 -> x26, starting transfers between devices: 23.2 us -> 29.4 us  [_swap(): return lax.ppermute(x, axis, [(i, i ^ b) for i in range(n)])]
    select_n x8 -> x7, other arithmetic: 3.62 us -> 0.6 us  [_allreduce_bf16(): jnp.where(first, jnp.concatenate([v, other], dim), jnp.concatenate([other...]
    ppermute x23 -> x26, waiting for transfers between devices: 20.3 us -> 19.6 us  [_swap(): return lax.ppermute(x, axis, [(i, i ^ b) for i in range(n)])]
  transfers between devices with their start and end apart: 23 -> 26, of which waited for: 7 -> 9; matrix products, arithmetic and copies ran while one was open for 24% -> 26% of each run, Pallas kernels for 22% -> 24%
where the time goes in v13:
time: 108 us
  starting transfers between devices  29.4 us (27%)
  matrix products  26.9 us (25%)
  Pallas kernels  25.6 us (24%)
  waiting for transfers between devices  19.6 us (18%)
  other arithmetic  5.89 us (5%)
    ppermute x26, starting transfers between devices, _swap(): return lax.ppermute(x, axis, [(i, i ^ b) for i in range(n)])  29.4 us
    pallas_call x6, Pallas kernels, _lifted(): pl.pallas_call(_lifted_kernel, grid=(t1 - t0,), in_specs=[pl.BlockSpec((t...  25.6 us
    dot_general x4, matrix products, local(): jnp.dot(g, out_basis[:, c0:c1], preferred_element_type=F32)  23.9 us
    ppermute x26, waiting for transfers between devices, _swap(): return lax.ppermute(x, axis, [(i, i ^ b) for i in range(n)])  19.6 us
    dot_general x1, matrix products, local(): act_part = jnp.dot(acts_all, in_basis, preferred_element_type=F32)  3.03 us
  transfers between devices with their start and end apart: 26, of which 9 were waited for; matrix products, arithmetic and copies ran while one was open for 26% of the time, Pallas kernels for 24%

profile of v13, /device:TPU:0, one launch (start us, length us, event | category | flops | bytes accessed | tf_op | source)
XLA Modules:
  0.0 107.9 jit_solution(13614734417047818272)
XLA Ops:
  0.0 3.0 %collective-permute-start = (bf16[1,8,2048]{2,1,0:T(8,128)(2,1)}, bf16[1,8,2048]{2,1,0:T(8,128)(2,1)S(1)}, u32[]{:S(2)}, u32[]{:S(2)}) collective-permute-start(bf16[1,8,2048]{2,1,0:T(8,128)(2,1)} %bitcast.60), channel_id=1, source_target_pairs={{0,16},{4,20},{8,24},{12,28},{16,0},{20,4},{24,8},{28,12},{1,17},{... | collective-permute-start | bytes 98312 | tf_op jit(solution)/shard_map/ppermute | solution.py:16
  3.0 2.1 %collective-permute-done = bf16[1,8,2048]{2,1,0:T(8,128)(2,1)S(1)} collective-permute-done((bf16[1,8,2048]{2,1,0:T(8,128)(2,1)}, bf16[1,8,2048]{2,1,0:T(8,128)(2,1)S(1)}, u32[]{:S(2)}, u32[]{:S(2)}) %collective-permute-start) | collective-permute-done | bytes 32800 | tf_op jit(solution)/shard_map/ppermute | solution.py:16
  5.8 2.1 %collective-permute-start.1 = (bf16[2,8,2048]{2,1,0:T(8,128)(2,1)S(1)}, bf16[2,8,2048]{2,1,0:T(8,128)(2,1)S(1)}, u32[]{:S(2)}, u32[]{:S(2)}) collective-permute-start(bf16[2,8,2048]{2,1,0:T(8,128)(2,1)S(1)} %maximum_bitcast_fusion.1), channel_id=1, source_target_pairs={{0,8},{4,12},{8,0},{12,4},{16,24},{20,28},{24,16},{28,20},{1,9},{5... | collective-permute-start | bytes 196616 | tf_op jit(solution)/shard_map/ppermute | solution.py:16
  7.9 2.6 %collective-permute-start.4 = (bf16[1,16,3584]{2,1,0:T(8,128)(2,1)}, bf16[1,16,3584]{2,1,0:T(8,128)(2,1)S(1)}, u32[]{:S(2)}, u32[]{:S(2)}) collective-permute-start(bf16[1,16,3584]{2,1,0:T(8,128)(2,1)} %bitcast.59), channel_id=1, source_target_pairs={{0,2},{1,3},{2,0},{3,1},{4,6},{5,7},{6,4},{7,5},{8,10},{9,11},{10,... | collective-permute-start | bytes 344072 | tf_op jit(solution)/shard_map/ppermute | solution.py:16
  10.6 4.4 %collective-permute-done.4 = bf16[1,16,3584]{2,1,0:T(8,128)(2,1)S(1)} collective-permute-done((bf16[1,16,3584]{2,1,0:T(8,128)(2,1)}, bf16[1,16,3584]{2,1,0:T(8,128)(2,1)S(1)}, u32[]{:S(2)}, u32[]{:S(2)}) %collective-permute-start.4) | collective-permute-done | bytes 114720 | tf_op jit(solution)/shard_map/ppermute | solution.py:16
  16.9 3.0 %fusion.9 = f32[64,1024]{1,0:T(8,128)S(1)} fusion(bf16[64,2048]{1,0:T(8,128)(2,1)S(1)} %bitcast.53, bf16[2048,1024]{1,0:T(8,128)(2,1)} %param.9), kind=kOutput, calls=%fused_computation.61 | convolution fusion | flops 268435456 | bytes 4718592 | tf_op jit(solution)/shard_map/dot_general | solution.py:138
  20.0 1.3 %collective-permute-start.3 = (f32[64,512]{1,0:T(8,128)S(1)}, f32[64,512]{1,0:T(8,128)S(1)}, u32[]{:S(2)}, u32[]{:S(2)}) collective-permute-start(f32[64,512]{1,0:T(8,128)S(1)} %slice_select_fusion.4), channel_id=1, source_target_pairs={{0,1},{1,0},{2,3},{3,2},{4,5},{5,4},{6,7},{7,6},{8,9},{9,8},{10,11... | collective-permute-start | bytes 393224 | tf_op jit(solution)/shard_map/ppermute | solution.py:16
  21.3 2.2 %collective-permute-done.5 = bf16[2,16,3584]{2,1,0:T(8,128)(2,1)S(1)} collective-permute-done((bf16[2,16,3584]{2,1,0:T(8,128)(2,1)S(1)}, bf16[2,16,3584]{2,1,0:T(8,128)(2,1)S(1)}, u32[]{:S(2)}, u32[]{:S(2)}) %collective-permute-start.5) | collective-permute-done | bytes 229408 | tf_op jit(solution)/shard_map/ppermute | solution.py:16
  23.6 6.0 %fusion.6 = f32[64,1792]{1,0:T(8,128)S(1)} fusion(bf16[64,3584]{1,0:T(8,128)(2,1)S(1)} %bitcast.55, bf16[3584,7168]{1,0:T(8,128)(2,1)} %param.8), kind=kOutput, calls=%fused_computation.6 | convolution fusion | flops 822083584 | bytes 13762560 | tf_op jit(solution)/shard_map/dot_general | solution.py:142
  29.6 1.9 %collective-permute-start.6 = (f32[64,256]{1,0:T(8,128)S(1)}, f32[64,256]{1,0:T(8,128)S(1)}, u32[]{:S(2)}, u32[]{:S(2)}) collective-permute-start(f32[64,256]{1,0:T(8,128)S(1)} %slice_select_fusion.5), channel_id=1, source_target_pairs={{0,2},{1,3},{2,0},{3,1},{4,6},{5,7},{6,4},{7,5},{8,10},{9,11},{10,... | collective-permute-start | bytes 196616 | tf_op jit(solution)/shard_map/ppermute | solution.py:16
  31.5 6.0 %fusion.4 = f32[64,1792]{1,0:T(8,128)S(1)} fusion(bf16[64,3584]{1,0:T(8,128)(2,1)S(1)} %bitcast.56, bf16[3584,7168]{1,0:T(8,128)(2,1)} %param.8), kind=kOutput, calls=%fused_computation.4 | convolution fusion | flops 822083584 | bytes 13762560 | tf_op jit(solution)/shard_map/dot_general | solution.py:142
  37.5 1.2 %collective-permute-start.7 = (bf16[64,256]{1,0:T(8,128)(2,1)S(1)}, bf16[64,256]{1,0:T(8,128)(2,1)S(1)}, u32[]{:S(2)}, u32[]{:S(2)}) collective-permute-start(bf16[64,256]{1,0:T(8,128)(2,1)S(1)} %add_convert_fusion.2), channel_id=1, source_target_pairs={{0,2},{1,3},{2,0},{3,1},{4,6},{5,7},{6,4},{7,5},{8,10},{9,11},{10,... | collective-permute-start | bytes 98312 | tf_op jit(solution)/shard_map/ppermute | solution.py:16
  38.7 6.0 %fusion.2 = f32[64,1792]{1,0:T(8,128)S(1)} fusion(bf16[64,3584]{1,0:T(8,128)(2,1)S(1)} %bitcast.57, bf16[3584,7168]{1,0:T(8,128)(2,1)} %param.8), kind=kOutput, calls=%fused_computation.2 | convolution fusion | flops 822083584 | bytes 13762560 | tf_op jit(solution)/shard_map/dot_general | solution.py:142
  45.8 6.0 %fusion = f32[64,1792]{1,0:T(8,128)S(1)} fusion(bf16[64,3584]{1,0:T(8,128)(2,1)S(1)} %bitcast.58, bf16[3584,7168]{1,0:T(8,128)(2,1)} %param.8), kind=kOutput, calls=%fused_computation | convolution fusion | flops 822083584 | bytes 13762560 | tf_op jit(solution)/shard_map/dot_general | solution.py:142
  52.4 3.8 %shard_map.64 = f32[2,64,1024]{2,1,0:T(8,128)S(1)} custom-call(bf16[64,1024]{1,0:T(8,128)(2,1)S(1)} %maximum_select_fusion.4.a_ref, bf16[7168,1024]{1,0:T(8,128)(2,1)} %e_ref.11, bf16[2,7168,1024]{2,1,0:T(8,128)(2,1)} %q_ref.11), custom_call_target="tpu_custom_call" | custom-call | flops 268435456 | bytes 6815744 | tf_op jit(solution)/shard_map/pallas_call | solution.py:114
  58.0 1.5 %collective-permute-start.12 = (f32[64,896]{1,0:T(8,128)S(1)}, f32[64,896]{1,0:T(8,128)S(1)}, u32[]{:S(2)}, u32[]{:S(2)}) collective-permute-start(f32[64,896]{1,0:T(8,128)S(1)} %slice_select_fusion), channel_id=1, source_target_pairs={{0,16},{4,20},{8,24},{12,28},{16,0},{20,4},{24,8},{28,12},{1,17},{... | collective-permute-start | bytes 688136 | tf_op jit(solution)/shard_map/ppermute | solution.py:16
  59.5 6.8 %shard_map.65 = f32[2,64,2048]{2,1,0:T(8,128)S(1)} custom-call(bf16[64,1024]{1,0:T(8,128)(2,1)S(1)} %maximum_select_fusion.4.a_ref, bf16[7168,1024]{1,0:T(8,128)(2,1)} %e_ref.11, bf16[2,7168,1024]{2,1,0:T(8,128)(2,1)} %q_ref.11), custom_call_target="tpu_custom_call" | custom-call | flops 536870912 | bytes 13631488 | tf_op jit(solution)/shard_map/pallas_call | solution.py:114
  67.2 1.5 %collective-permute-start.14 = (f32[64,448]{1,0:T(8,128)S(1)}, f32[64,448]{1,0:T(8,128)S(1)}, u32[]{:S(2)}, u32[]{:S(2)}) collective-permute-start(f32[64,448]{1,0:T(8,128)S(1)} %slice_select_fusion.2), channel_id=1, source_target_pairs={{0,8},{4,12},{8,0},{12,4},{16,24},{20,28},{24,16},{28,20},{1,9},{5... | collective-permute-start | bytes 344072 | tf_op jit(solution)/shard_map/ppermute | solution.py:16
  68.7 3.8 %shard_map.66 = f32[2,64,1024]{2,1,0:T(8,128)S(1)} custom-call(bf16[64,1024]{1,0:T(8,128)(2,1)S(1)} %maximum_select_fusion.4.a_ref, bf16[7168,1024]{1,0:T(8,128)(2,1)} %e_ref.11, bf16[2,7168,1024]{2,1,0:T(8,128)(2,1)} %q_ref.11), custom_call_target="tpu_custom_call" | custom-call | flops 268435456 | bytes 6815744 | tf_op jit(solution)/shard_map/pallas_call | solution.py:114
  72.7 1.6 %collective-permute-start.15 = (bf16[64,448]{1,0:T(8,128)(2,1)S(1)}, bf16[64,448]{1,0:T(8,128)(2,1)S(1)}, u32[]{:S(2)}, u32[]{:S(2)}) collective-permute-start(bf16[64,448]{1,0:T(8,128)(2,1)S(1)} %add_convert_fusion.1), channel_id=1, source_target_pairs={{0,16},{4,20},{8,24},{12,28},{16,0},{20,4},{24,8},{28,12},{1,17},{... | collective-permute-start | bytes 172040 | tf_op jit(solution)/shard_map/ppermute | solution.py:16
  74.3 1.2 %collective-permute-start.16 = (bf16[64,448]{1,0:T(8,128)(2,1)S(1)}, bf16[64,448]{1,0:T(8,128)(2,1)S(1)}, u32[]{:S(2)}, u32[]{:S(2)}) collective-permute-start(bf16[64,448]{1,0:T(8,128)(2,1)S(1)} %add_convert_fusion), channel_id=1, source_target_pairs={{0,8},{4,12},{8,0},{12,4},{16,24},{20,28},{24,16},{28,20},{1,9},{5... | collective-permute-start | bytes 172040 | tf_op jit(solution)/shard_map/ppermute | solution.py:16
  75.5 3.8 %shard_map.67 = f32[2,64,1024]{2,1,0:T(8,128)S(1)} custom-call(bf16[64,1024]{1,0:T(8,128)(2,1)S(1)} %maximum_select_fusion.4.a_ref, bf16[7168,1024]{1,0:T(8,128)(2,1)} %e_ref.11, bf16[2,7168,1024]{2,1,0:T(8,128)(2,1)} %q_ref.11), custom_call_target="tpu_custom_call" | custom-call | flops 268435456 | bytes 6815744 | tf_op jit(solution)/shard_map/pallas_call | solution.py:114
  80.9 3.8 %shard_map.68 = f32[2,64,1024]{2,1,0:T(8,128)S(1)} custom-call(bf16[64,1024]{1,0:T(8,128)(2,1)S(1)} %maximum_select_fusion.4.a_ref, bf16[7168,1024]{1,0:T(8,128)(2,1)} %e_ref.11, bf16[2,7168,1024]{2,1,0:T(8,128)(2,1)} %q_ref.11), custom_call_target="tpu_custom_call" | custom-call | flops 268435456 | bytes 6815744 | tf_op jit(solution)/shard_map/pallas_call | solution.py:114
  85.9 3.8 %shard_map.69 = f32[2,64,1024]{2,1,0:T(8,128)S(1)} custom-call(bf16[64,1024]{1,0:T(8,128)(2,1)S(1)} %maximum_select_fusion.4.a_ref, bf16[7168,1024]{1,0:T(8,128)(2,1)} %e_ref.11, bf16[2,7168,1024]{2,1,0:T(8,128)(2,1)} %q_ref.11), custom_call_target="tpu_custom_call" | custom-call | flops 268435456 | bytes 6815744 | tf_op jit(solution)/shard_map/pallas_call | solution.py:114
  90.9 1.2 %collective-permute-start.21 = (f32[2,64]{1,0:T(2,128)S(1)}, f32[2,64]{1,0:T(2,128)S(1)}, u32[]{:S(2)}, u32[]{:S(2)}) collective-permute-start(f32[2,64]{1,0:T(2,128)S(1)} %add_add_fusion), channel_id=1, source_target_pairs={{0,1},{1,0},{2,3},{3,2},{4,5},{5,4},{6,7},{7,6},{8,9},{9,8},{10,11... | collective-permute-start | bytes 1544 | tf_op jit(solution)/shard_map/ppermute | solution.py:16
  92.1 2.5 %collective-permute-done.21 = f32[2,64]{1,0:T(2,128)S(1)} collective-permute-done((f32[2,64]{1,0:T(2,128)S(1)}, f32[2,64]{1,0:T(2,128)S(1)}, u32[]{:S(2)}, u32[]{:S(2)}) %collective-permute-start.21) | collective-permute-done | bytes 544 | tf_op jit(solution)/shard_map/ppermute | solution.py:16
  94.6 2.7 %collective-permute-start.22 = (f32[2,64]{1,0:T(2,128)S(1)}, f32[2,64]{1,0:T(2,128)S(1)}, u32[]{:S(2)}, u32[]{:S(2)}) collective-permute-start(f32[2,64]{1,0:T(2,128)S(1)} %add.109), channel_id=1, source_target_pairs={{0,2},{1,3},{2,0},{3,1},{4,6},{5,7},{6,4},{7,5},{8,10},{9,11},{10,... | collective-permute-start | bytes 1544 | tf_op jit(solution)/shard_map/ppermute | solution.py:16
  97.2 1.8 %collective-permute-done.22 = f32[2,64]{1,0:T(2,128)S(1)} collective-permute-done((f32[2,64]{1,0:T(2,128)S(1)}, f32[2,64]{1,0:T(2,128)S(1)}, u32[]{:S(2)}, u32[]{:S(2)}) %collective-permute-start.22) | collective-permute-done | bytes 544 | tf_op jit(solution)/shard_map/ppermute | solution.py:16
  99.1 1.1 %collective-permute-done.23 = f32[2,64]{1,0:T(2,128)S(1)} collective-permute-done((f32[2,64]{1,0:T(2,128)S(1)}, f32[2,64]{1,0:T(2,128)S(1)}, u32[]{:S(2)}, u32[]{:S(2)}) %collective-permute-start.23) | collective-permute-done | bytes 544 | tf_op jit(solution)/shard_map/ppermute | solution.py:16
  100.2 1.2 %collective-permute-start.24 = (f32[2,64]{1,0:T(2,128)S(1)}, f32[2,64]{1,0:T(2,128)S(1)}, u32[]{:S(2)}, u32[]{:S(2)}) collective-permute-start(f32[2,64]{1,0:T(2,128)S(1)} %add.111), channel_id=1, source_target_pairs={{0,8},{4,12},{8,0},{12,4},{16,24},{20,28},{24,16},{28,20},{1,9},{5... | collective-permute-start | bytes 1544 | tf_op jit(solution)/shard_map/ppermute | solution.py:16
  101.4 2.4 %collective-permute-done.24 = f32[2,64]{1,0:T(2,128)S(1)} collective-permute-done((f32[2,64]{1,0:T(2,128)S(1)}, f32[2,64]{1,0:T(2,128)S(1)}, u32[]{:S(2)}, u32[]{:S(2)}) %collective-permute-start.24) | collective-permute-done | bytes 544 | tf_op jit(solution)/shard_map/ppermute | solution.py:16
  104.8 2.5 %collective-permute-done.25 = f32[2,64]{1,0:T(2,128)S(1)} collective-permute-done((f32[2,64]{1,0:T(2,128)S(1)}, f32[2,64]{1,0:T(2,128)S(1)}, u32[]{:S(2)}, u32[]{:S(2)}) %collective-permute-start.25) | collective-permute-done | bytes 544 | tf_op jit(solution)/shard_map/ppermute | solution.py:16
  (79 shorter events, 13.1 us)
Async XLA Ops:
  0.0 5.1 %collective-permute-start = (bf16[1,8,2048]{2,1,0:T(8,128)(2,1)}, bf16[1,8,2048]{2,1,0:T(8,128)(2,1)S(1)}, u32[]{:S(2)}, u32[]{:S(2)}) collective-permute-start(bf16[1,8,2048]{2,1,0:T(8,128)(2,1)} %bitcast.60), channel_id=1, source_target_pairs={{0,16},{4,20},{8,24},{12,28},{16,0},{20,4},{24,8},{28,12},{1,17},{... | collective-permute-start | bytes 98312 | tf_op jit(solution)/shard_map/ppermute | solution.py:16
  5.8 4.7 %collective-permute-start.1 = (bf16[2,8,2048]{2,1,0:T(8,128)(2,1)S(1)}, bf16[2,8,2048]{2,1,0:T(8,128)(2,1)S(1)}, u32[]{:S(2)}, u32[]{:S(2)}) collective-permute-start(bf16[2,8,2048]{2,1,0:T(8,128)(2,1)S(1)} %maximum_bitcast_fusion.1), channel_id=1, source_target_pairs={{0,8},{4,12},{8,0},{12,4},{16,24},{20,28},{24,16},{28,20},{1,9},{5... | collective-permute-start | bytes 196616 | tf_op jit(solution)/shard_map/ppermute | solution.py:16
  7.9 7.1 %collective-permute-start.4 = (bf16[1,16,3584]{2,1,0:T(8,128)(2,1)}, bf16[1,16,3584]{2,1,0:T(8,128)(2,1)S(1)}, u32[]{:S(2)}, u32[]{:S(2)}) collective-permute-start(bf16[1,16,3584]{2,1,0:T(8,128)(2,1)} %bitcast.59), channel_id=1, source_target_pairs={{0,2},{1,3},{2,0},{3,1},{4,6},{5,7},{6,4},{7,5},{8,10},{9,11},{10,... | collective-permute-start | bytes 344072 | tf_op jit(solution)/shard_map/ppermute | solution.py:16
  10.5 6.3 %collective-permute-start.2 = (bf16[4,8,2048]{2,1,0:T(8,128)(2,1)S(1)}, bf16[4,8,2048]{2,1,0:T(8,128)(2,1)S(1)}, u32[]{:S(2)}, u32[]{:S(2)}) collective-permute-start(bf16[4,8,2048]{2,1,0:T(8,128)(2,1)S(1)} %bitcast.54), channel_id=1, source_target_pairs={{0,4},{4,0},{8,12},{12,8},{16,20},{20,16},{24,28},{28,24},{1,5},{5... | collective-permute-start | bytes 393224 | tf_op jit(solution)/shard_map/ppermute | solution.py:16
  16.0 7.5 %collective-permute-start.5 = (bf16[2,16,3584]{2,1,0:T(8,128)(2,1)S(1)}, bf16[2,16,3584]{2,1,0:T(8,128)(2,1)S(1)}, u32[]{:S(2)}, u32[]{:S(2)}) collective-permute-start(bf16[2,16,3584]{2,1,0:T(8,128)(2,1)S(1)} %maximum_bitcast_fusion), channel_id=1, source_target_pairs={{0,1},{1,0},{2,3},{3,2},{4,5},{5,4},{6,7},{7,6},{8,9},{9,8},{10,11... | collective-permute-start | bytes 688136 | tf_op jit(solution)/shard_map/ppermute | solution.py:16
  20.0 9.6 %collective-permute-start.3 = (f32[64,512]{1,0:T(8,128)S(1)}, f32[64,512]{1,0:T(8,128)S(1)}, u32[]{:S(2)}, u32[]{:S(2)}) collective-permute-start(f32[64,512]{1,0:T(8,128)S(1)} %slice_select_fusion.4), channel_id=1, source_target_pairs={{0,1},{1,0},{2,3},{3,2},{4,5},{5,4},{6,7},{7,6},{8,9},{9,8},{10,11... | collective-permute-start | bytes 393224 | tf_op jit(solution)/shard_map/ppermute | solution.py:16
  29.6 7.8 %collective-permute-start.6 = (f32[64,256]{1,0:T(8,128)S(1)}, f32[64,256]{1,0:T(8,128)S(1)}, u32[]{:S(2)}, u32[]{:S(2)}) collective-permute-start(f32[64,256]{1,0:T(8,128)S(1)} %slice_select_fusion.5), channel_id=1, source_target_pairs={{0,2},{1,3},{2,0},{3,1},{4,6},{5,7},{6,4},{7,5},{8,10},{9,11},{10,... | collective-permute-start | bytes 196616 | tf_op jit(solution)/shard_map/ppermute | solution.py:16
  37.5 7.3 %collective-permute-start.7 = (bf16[64,256]{1,0:T(8,128)(2,1)S(1)}, bf16[64,256]{1,0:T(8,128)(2,1)S(1)}, u32[]{:S(2)}, u32[]{:S(2)}) collective-permute-start(bf16[64,256]{1,0:T(8,128)(2,1)S(1)} %add_convert_fusion.2), channel_id=1, source_target_pairs={{0,2},{1,3},{2,0},{3,1},{4,6},{5,7},{6,4},{7,5},{8,10},{9,11},{10,... | collective-permute-start | bytes 98312 | tf_op jit(solution)/shard_map/ppermute | solution.py:16
  44.8 7.0 %collective-permute-start.8 = (bf16[64,512]{1,0:T(8,128)(2,1)S(1)}, bf16[64,512]{1,0:T(8,128)(2,1)S(1)}, u32[]{:S(2)}, u32[]{:S(2)}) collective-permute-start(bf16[64,512]{1,0:T(8,128)(2,1)S(1)} %maximum_select_fusion.7), channel_id=1, source_target_pairs={{0,1},{1,0},{2,3},{3,2},{4,5},{5,4},{6,7},{7,6},{8,9},{9,8},{10,11... | collective-permute-start | bytes 196616 | tf_op jit(solution)/shard_map/ppermute | solution.py:16
  51.8 4.3 %collective-permute-start.9 = (f32[64,1792]{1,0:T(8,128)S(1)}, f32[64,1792]{1,0:T(8,128)S(1)}, u32[]{:S(2)}, u32[]{:S(2)}) collective-permute-start(f32[64,1792]{1,0:T(8,128)S(1)} %broadcast_select_fusion.1), channel_id=1, source_target_pairs={{0,4},{4,0},{8,12},{12,8},{16,20},{20,16},{24,28},{28,24},{1,5},{5... | collective-permute-start | bytes 1376264 | tf_op jit(solution)/shard_map/ppermute | solution.py:16
  51.9 4.3 %collective-permute-start.10 = (f32[64,1792]{1,0:T(8,128)S(1)}, f32[64,1792]{1,0:T(8,128)}, u32[]{:S(2)}, u32[]{:S(2)}) collective-permute-start(f32[64,1792]{1,0:T(8,128)S(1)} %broadcast_select_fusion), channel_id=1, source_target_pairs={{0,4},{4,0},{8,12},{12,8},{16,20},{20,16},{24,28},{28,24},{1,5},{5... | collective-permute-start | bytes 1376264 | tf_op jit(solution)/shard_map/ppermute | solution.py:16
  57.4 8.9 %collective-permute-start.11 = (f32[64,896]{1,0:T(8,128)S(1)}, f32[64,896]{1,0:T(8,128)S(1)}, u32[]{:S(2)}, u32[]{:S(2)}) collective-permute-start(f32[64,896]{1,0:T(8,128)S(1)} %slice_select_fusion.1), channel_id=1, source_target_pairs={{0,8},{4,12},{8,0},{12,4},{16,24},{20,28},{24,16},{28,20},{1,9},{5... | collective-permute-start | bytes 688136 | tf_op jit(solution)/shard_map/ppermute | solution.py:16
  58.0 8.3 %collective-permute-start.12 = (f32[64,896]{1,0:T(8,128)S(1)}, f32[64,896]{1,0:T(8,128)S(1)}, u32[]{:S(2)}, u32[]{:S(2)}) collective-permute-start(f32[64,896]{1,0:T(8,128)S(1)} %slice_select_fusion), channel_id=1, source_target_pairs={{0,16},{4,20},{8,24},{12,28},{16,0},{20,4},{24,8},{28,12},{1,17},{... | collective-permute-start | bytes 688136 | tf_op jit(solution)/shard_map/ppermute | solution.py:16
  66.6 5.8 %collective-permute-start.13 = (f32[64,448]{1,0:T(8,128)S(1)}, f32[64,448]{1,0:T(8,128)S(1)}, u32[]{:S(2)}, u32[]{:S(2)}) collective-permute-start(f32[64,448]{1,0:T(8,128)S(1)} %slice_select_fusion.3), channel_id=1, source_target_pairs={{0,16},{4,20},{8,24},{12,28},{16,0},{20,4},{24,8},{28,12},{1,17},{... | collective-permute-start | bytes 344072 | tf_op jit(solution)/shard_map/ppermute | solution.py:16
  67.2 5.3 %collective-permute-start.14 = (f32[64,448]{1,0:T(8,128)S(1)}, f32[64,448]{1,0:T(8,128)S(1)}, u32[]{:S(2)}, u32[]{:S(2)}) collective-permute-start(f32[64,448]{1,0:T(8,128)S(1)} %slice_select_fusion.2), channel_id=1, source_target_pairs={{0,8},{4,12},{8,0},{12,4},{16,24},{20,28},{24,16},{28,20},{1,9},{5... | collective-permute-start | bytes 344072 | tf_op jit(solution)/shard_map/ppermute | solution.py:16
  72.7 6.5 %collective-permute-start.15 = (bf16[64,448]{1,0:T(8,128)(2,1)S(1)}, bf16[64,448]{1,0:T(8,128)(2,1)S(1)}, u32[]{:S(2)}, u32[]{:S(2)}) collective-permute-start(bf16[64,448]{1,0:T(8,128)(2,1)S(1)} %add_convert_fusion.1), channel_id=1, source_target_pairs={{0,16},{4,20},{8,24},{12,28},{16,0},{20,4},{24,8},{28,12},{1,17},{... | collective-permute-start | bytes 172040 | tf_op jit(solution)/shard_map/ppermute | solution.py:16
  74.3 5.0 %collective-permute-start.16 = (bf16[64,448]{1,0:T(8,128)(2,1)S(1)}, bf16[64,448]{1,0:T(8,128)(2,1)S(1)}, u32[]{:S(2)}, u32[]{:S(2)}) collective-permute-start(bf16[64,448]{1,0:T(8,128)(2,1)S(1)} %add_convert_fusion), channel_id=1, source_target_pairs={{0,8},{4,12},{8,0},{12,4},{16,24},{20,28},{24,16},{28,20},{1,9},{5... | collective-permute-start | bytes 172040 | tf_op jit(solution)/shard_map/ppermute | solution.py:16
  79.5 5.2 %collective-permute-start.17 = (bf16[64,896]{1,0:T(8,128)(2,1)S(1)}, bf16[64,896]{1,0:T(8,128)(2,1)S(1)}, u32[]{:S(2)}, u32[]{:S(2)}) collective-permute-start(bf16[64,896]{1,0:T(8,128)(2,1)S(1)} %maximum_select_fusion.5), channel_id=1, source_target_pairs={{0,8},{4,12},{8,0},{12,4},{16,24},{20,28},{24,16},{28,20},{1,9},{5... | collective-permute-start | bytes 344072 | tf_op jit(solution)/shard_map/ppermute | solution.py:16
  80.4 4.8 %collective-permute-start.18 = (bf16[64,896]{1,0:T(8,128)(2,1)S(1)}, bf16[64,896]{1,0:T(8,128)(2,1)S(1)}, u32[]{:S(2)}, u32[]{:S(2)}) collective-permute-start(bf16[64,896]{1,0:T(8,128)(2,1)S(1)} %maximum_select_fusion.6), channel_id=1, source_target_pairs={{0,16},{4,20},{8,24},{12,28},{16,0},{20,4},{24,8},{28,12},{1,17},{... | collective-permute-start | bytes 344072 | tf_op jit(solution)/shard_map/ppermute | solution.py:16
  85.3 4.4 %collective-permute-start.19 = (bf16[64,1792]{1,0:T(8,128)(2,1)S(1)}, bf16[64,1792]{1,0:T(8,128)(2,1)S(1)}, u32[]{:S(2)}, u32[]{:S(2)}) collective-permute-start(bf16[64,1792]{1,0:T(8,128)(2,1)S(1)} %maximum_select_fusion.2), channel_id=1, source_target_pairs={{0,4},{4,0},{8,12},{12,8},{16,20},{20,16},{24,28},{28,24},{1,5},{5... | collective-permute-start | bytes 688136 | tf_op jit(solution)/shard_map/ppermute | solution.py:16
  85.4 4.3 %collective-permute-start.20 = (bf16[64,1792]{1,0:T(8,128)(2,1)S(1)}, bf16[64,1792]{1,0:T(8,128)(2,1)S(1)}, u32[]{:S(2)}, u32[]{:S(2)}) collective-permute-start(bf16[64,1792]{1,0:T(8,128)(2,1)S(1)} %maximum_select_fusion.3), channel_id=1, source_target_pairs={{0,4},{4,0},{8,12},{12,8},{16,20},{20,16},{24,28},{28,24},{1,5},{5... | collective-permute-start | bytes 688136 | tf_op jit(solution)/shard_map/ppermute | solution.py:16
  90.9 3.6 %collective-permute-start.21 = (f32[2,64]{1,0:T(2,128)S(1)}, f32[2,64]{1,0:T(2,128)S(1)}, u32[]{:S(2)}, u32[]{:S(2)}) collective-permute-start(f32[2,64]{1,0:T(2,128)S(1)} %add_add_fusion), channel_id=1, source_target_pairs={{0,1},{1,0},{2,3},{3,2},{4,5},{5,4},{6,7},{7,6},{8,9},{9,8},{10,11... | collective-permute-start | bytes 1544 | tf_op jit(solution)/shard_map/ppermute | solution.py:16
  94.6 4.5 %collective-permute-start.22 = (f32[2,64]{1,0:T(2,128)S(1)}, f32[2,64]{1,0:T(2,128)S(1)}, u32[]{:S(2)}, u32[]{:S(2)}) collective-permute-start(f32[2,64]{1,0:T(2,128)S(1)} %add.109), channel_id=1, source_target_pairs={{0,2},{1,3},{2,0},{3,1},{4,6},{5,7},{6,4},{7,5},{8,10},{9,11},{10,... | collective-permute-start | bytes 1544 | tf_op jit(solution)/shard_map/ppermute | solution.py:16
  99.1 1.1 %collective-permute-start.23 = (f32[2,64]{1,0:T(2,128)S(1)}, f32[2,64]{1,0:T(2,128)S(1)}, u32[]{:S(2)}, u32[]{:S(2)}) collective-permute-start(f32[2,64]{1,0:T(2,128)S(1)} %add.110), channel_id=1, source_target_pairs={{0,4},{4,0},{8,12},{12,8},{16,20},{20,16},{24,28},{28,24},{1,5},{5... | collective-permute-start | bytes 1544 | tf_op jit(solution)/shard_map/ppermute | solution.py:16
  100.2 3.6 %collective-permute-start.24 = (f32[2,64]{1,0:T(2,128)S(1)}, f32[2,64]{1,0:T(2,128)S(1)}, u32[]{:S(2)}, u32[]{:S(2)}) collective-permute-start(f32[2,64]{1,0:T(2,128)S(1)} %add.111), channel_id=1, source_target_pairs={{0,8},{4,12},{8,0},{12,4},{16,24},{20,28},{24,16},{28,20},{1,9},{5... | collective-permute-start | bytes 1544 | tf_op jit(solution)/shard_map/ppermute | solution.py:16
  103.8 3.6 %collective-permute-start.25 = (f32[2,64]{1,0:T(2,128)S(1)}, f32[2,64]{1,0:T(2,128)S(1)}, u32[]{:S(2)}, u32[]{:S(2)}) collective-permute-start(f32[2,64]{1,0:T(2,128)S(1)} %add.112), channel_id=1, source_target_pairs={{0,16},{4,20},{8,24},{12,28},{16,0},{20,4},{24,8},{28,12},{1,17},{... | collective-permute-start | bytes 1544 | tf_op jit(solution)/shard_map/ppermute | solution.py:16

commit v14 on v13

--- a/solution.py
+++ b/solution.py
@@ -176,5 +176,5 @@
         P("col", "row"),
         P(None, "col", "row"),
     )
-    fn = functools.partial(local, nr=mesh.shape["row"], nc=mesh.shape["col"], nl=6, ng=4)
+    fn = functools.partial(local, nr=mesh.shape["row"], nc=mesh.shape["col"], nl=6, ng=3)
     return jax.shard_map(fn, mesh=mesh, in_specs=in_specs, out_specs=P(), check_vma=False)

time: 108 us -> 110 us (1.019)
  waiting for transfers between devices: 19.6 us -> 23.4 us
  starting transfers between devices: 29.4 us -> 28.1 us
    ppermute x26, waiting for transfers between devices: 19.6 us -> 23.4 us  [_swap(): return lax.ppermute(x, axis, [(i, i ^ b) for i in range(n)])]
    ppermute x26, starting transfers between devices: 29.4 us -> 28.1 us  [_swap(): return lax.ppermute(x, axis, [(i, i ^ b) for i in range(n)])]
    dot_general x4 -> x3, matrix products: 23.9 us -> 23.1 us  [local(): jnp.dot(g, out_basis[:, c0:c1], preferred_element_type=F32)]
  transfers between devices with their start and end apart: 26 -> 26, of which waited for: 9 -> 10; matrix products, arithmetic and copies ran while one was open for 26% -> 26% of each run, Pallas kernels for 24% -> 23%
where the time goes in v14:
time: 110 us; the launch traced here: 109 us
  starting transfers between devices  28.1 us (26%)
  matrix products  26.2 us (24%)
  Pallas kernels  25.6 us (23%)
  waiting for transfers between devices  23.4 us (21%)
  other arithmetic  5.63 us (5%)
    ppermute x26, starting transfers between devices, _swap(): return lax.ppermute(x, axis, [(i, i ^ b) for i in range(n)])  28.1 us
    pallas_call x6, Pallas kernels, _lifted(): pl.pallas_call(_lifted_kernel, grid=(t1 - t0,), in_specs=[pl.BlockSpec((t...  25.6 us
    ppermute x26, waiting for transfers between devices, _swap(): return lax.ppermute(x, axis, [(i, i ^ b) for i in range(n)])  23.4 us
    dot_general x3, matrix products, local(): jnp.dot(g, out_basis[:, c0:c1], preferred_element_type=F32)  23.1 us
    dot_general x1, matrix products, local(): act_part = jnp.dot(acts_all, in_basis, preferred_element_type=F32)  3.03 us
  transfers between devices with their start and end apart: 26, of which 10 were waited for; matrix products, arithmetic and copies ran while one was open for 26% of the time, Pallas kernels for 23%

profile of v14, /device:TPU:0, one launch (start us, length us, event | category | flops | bytes accessed | tf_op | source)
XLA Modules:
  0.0 109.3 jit_solution(1279241251511459374)
XLA Ops:
  0.0 3.0 %collective-permute-start = (bf16[1,8,2048]{2,1,0:T(8,128)(2,1)}, bf16[1,8,2048]{2,1,0:T(8,128)(2,1)S(1)}, u32[]{:S(2)}, u32[]{:S(2)}) collective-permute-start(bf16[1,8,2048]{2,1,0:T(8,128)(2,1)} %bitcast.58), channel_id=1, source_target_pairs={{0,16},{4,20},{8,24},{12,28},{16,0},{20,4},{24,8},{28,12},{1,17},{... | collective-permute-start | bytes 98312 | tf_op jit(solution)/shard_map/ppermute | solution.py:16
  3.0 2.1 %collective-permute-done = bf16[1,8,2048]{2,1,0:T(8,128)(2,1)S(1)} collective-permute-done((bf16[1,8,2048]{2,1,0:T(8,128)(2,1)}, bf16[1,8,2048]{2,1,0:T(8,128)(2,1)S(1)}, u32[]{:S(2)}, u32[]{:S(2)}) %collective-permute-start) | collective-permute-done | bytes 32800 | tf_op jit(solution)/shard_map/ppermute | solution.py:16
  5.8 2.1 %collective-permute-start.1 = (bf16[2,8,2048]{2,1,0:T(8,128)(2,1)S(1)}, bf16[2,8,2048]{2,1,0:T(8,128)(2,1)S(1)}, u32[]{:S(2)}, u32[]{:S(2)}) collective-permute-start(bf16[2,8,2048]{2,1,0:T(8,128)(2,1)S(1)} %maximum_bitcast_fusion.1), channel_id=1, source_target_pairs={{0,8},{4,12},{8,0},{12,4},{16,24},{20,28},{24,16},{28,20},{1,9},{5... | collective-permute-start | bytes 196616 | tf_op jit(solution)/shard_map/ppermute | solution.py:16
  7.9 2.6 %collective-permute-start.4 = (bf16[1,16,3584]{2,1,0:T(8,128)(2,1)}, bf16[1,16,3584]{2,1,0:T(8,128)(2,1)S(1)}, u32[]{:S(2)}, u32[]{:S(2)}) collective-permute-start(bf16[1,16,3584]{2,1,0:T(8,128)(2,1)} %bitcast.57), channel_id=1, source_target_pairs={{0,2},{1,3},{2,0},{3,1},{4,6},{5,7},{6,4},{7,5},{8,10},{9,11},{10,... | collective-permute-start | bytes 344072 | tf_op jit(solution)/shard_map/ppermute | solution.py:16
  10.6 4.4 %collective-permute-done.4 = bf16[1,16,3584]{2,1,0:T(8,128)(2,1)S(1)} collective-permute-done((bf16[1,16,3584]{2,1,0:T(8,128)(2,1)}, bf16[1,16,3584]{2,1,0:T(8,128)(2,1)S(1)}, u32[]{:S(2)}, u32[]{:S(2)}) %collective-permute-start.4) | collective-permute-done | bytes 114720 | tf_op jit(solution)/shard_map/ppermute | solution.py:16
  16.9 3.0 %fusion.7 = f32[64,1024]{1,0:T(8,128)S(1)} fusion(bf16[64,2048]{1,0:T(8,128)(2,1)S(1)} %bitcast.52, bf16[2048,1024]{1,0:T(8,128)(2,1)} %param.9), kind=kOutput, calls=%fused_computation.61 | convolution fusion | flops 268435456 | bytes 4718592 | tf_op jit(solution)/shard_map/dot_general | solution.py:138
  20.0 1.3 %collective-permute-start.3 = (f32[64,512]{1,0:T(8,128)S(1)}, f32[64,512]{1,0:T(8,128)S(1)}, u32[]{:S(2)}, u32[]{:S(2)}) collective-permute-start(f32[64,512]{1,0:T(8,128)S(1)} %slice_select_fusion.6), channel_id=1, source_target_pairs={{0,1},{1,0},{2,3},{3,2},{4,5},{5,4},{6,7},{7,6},{8,9},{9,8},{10,11... | collective-permute-start | bytes 393224 | tf_op jit(solution)/shard_map/ppermute | solution.py:16
  21.3 2.2 %collective-permute-done.5 = bf16[2,16,3584]{2,1,0:T(8,128)(2,1)S(1)} collective-permute-done((bf16[2,16,3584]{2,1,0:T(8,128)(2,1)S(1)}, bf16[2,16,3584]{2,1,0:T(8,128)(2,1)S(1)}, u32[]{:S(2)}, u32[]{:S(2)}) %collective-permute-start.5) | collective-permute-done | bytes 229408 | tf_op jit(solution)/shard_map/ppermute | solution.py:16
  23.6 8.0 %fusion.2 = f32[64,2432]{1,0:T(8,128)S(1)} fusion(bf16[64,3584]{1,0:T(8,128)(2,1)S(1)} %bitcast.54, bf16[3584,7168]{1,0:T(8,128)(2,1)} %param.8), kind=kOutput, calls=%fused_computation.2 | convolution fusion | flops 1115684864 | bytes 18513920 | tf_op jit(solution)/shard_map/dot_general | solution.py:142
  31.6 1.9 %collective-permute-start.6 = (f32[64,256]{1,0:T(8,128)S(1)}, f32[64,256]{1,0:T(8,128)S(1)}, u32[]{:S(2)}, u32[]{:S(2)}) collective-permute-start(f32[64,256]{1,0:T(8,128)S(1)} %slice_select_fusion.7), channel_id=1, source_target_pairs={{0,2},{1,3},{2,0},{3,1},{4,6},{5,7},{6,4},{7,5},{8,10},{9,11},{10,... | collective-permute-start | bytes 196616 | tf_op jit(solution)/shard_map/ppermute | solution.py:16
  33.5 7.3 %fusion.4 = f32[64,2304]{1,0:T(8,128)S(1)} fusion(bf16[64,3584]{1,0:T(8,128)(2,1)S(1)} %bitcast.55, bf16[3584,7168]{1,0:T(8,128)(2,1)} %param.8), kind=kOutput, calls=%fused_computation.4 | convolution fusion | flops 1056964608 | bytes 17563648 | tf_op jit(solution)/shard_map/dot_general | solution.py:142
  40.9 1.2 %collective-permute-start.7 = (bf16[64,256]{1,0:T(8,128)(2,1)S(1)}, bf16[64,256]{1,0:T(8,128)(2,1)S(1)}, u32[]{:S(2)}, u32[]{:S(2)}) collective-permute-start(bf16[64,256]{1,0:T(8,128)(2,1)S(1)} %add_convert_fusion.2), channel_id=1, source_target_pairs={{0,2},{1,3},{2,0},{3,1},{4,6},{5,7},{6,4},{7,5},{8,10},{9,11},{10,... | collective-permute-start | bytes 98312 | tf_op jit(solution)/shard_map/ppermute | solution.py:16
  42.1 7.8 %fusion = f32[64,2432]{1,0:T(8,128)S(1)} fusion(bf16[64,3584]{1,0:T(8,128)(2,1)S(1)} %bitcast.56, bf16[3584,7168]{1,0:T(8,128)(2,1)} %param.8), kind=kOutput, calls=%fused_computation | convolution fusion | flops 1115684864 | bytes 18513920 | tf_op jit(solution)/shard_map/dot_general | solution.py:142
  51.6 2.6 %collective-permute-done.8 = bf16[64,512]{1,0:T(8,128)(2,1)S(1)} collective-permute-done((bf16[64,512]{1,0:T(8,128)(2,1)S(1)}, bf16[64,512]{1,0:T(8,128)(2,1)S(1)}, u32[]{:S(2)}, u32[]{:S(2)}) %collective-permute-start.8) | collective-permute-done | bytes 65568 | tf_op jit(solution)/shard_map/ppermute | solution.py:16
  54.9 3.8 %shard_map.64 = f32[2,64,1024]{2,1,0:T(8,128)S(1)} custom-call(bf16[64,1024]{1,0:T(8,128)(2,1)S(1)} %maximum_select_fusion.4.a_ref, bf16[7168,1024]{1,0:T(8,128)(2,1)} %e_ref.11, bf16[2,7168,1024]{2,1,0:T(8,128)(2,1)} %q_ref.11), custom_call_target="tpu_custom_call" | custom-call | flops 268435456 | bytes 6815744 | tf_op jit(solution)/shard_map/pallas_call | solution.py:114
  58.9 2.0 %collective-permute-start.12 = (f32[64,896]{1,0:T(8,128)S(1)}, f32[64,896]{1,0:T(8,128)S(1)}, u32[]{:S(2)}, u32[]{:S(2)}) collective-permute-start(f32[64,896]{1,0:T(8,128)S(1)} %slice_select_fusion.2), channel_id=1, source_target_pairs={{0,16},{4,20},{8,24},{12,28},{16,0},{20,4},{24,8},{28,12},{1,17},{... | collective-permute-start | bytes 688136 | tf_op jit(solution)/shard_map/ppermute | solution.py:16
  61.0 6.8 %shard_map.65 = f32[2,64,2048]{2,1,0:T(8,128)S(1)} custom-call(bf16[64,1024]{1,0:T(8,128)(2,1)S(1)} %maximum_select_fusion.4.a_ref, bf16[7168,1024]{1,0:T(8,128)(2,1)} %e_ref.11, bf16[2,7168,1024]{2,1,0:T(8,128)(2,1)} %q_ref.11), custom_call_target="tpu_custom_call" | custom-call | flops 536870912 | bytes 13631488 | tf_op jit(solution)/shard_map/pallas_call | solution.py:114
  68.6 1.5 %collective-permute-start.14 = (f32[64,448]{1,0:T(8,128)S(1)}, f32[64,448]{1,0:T(8,128)S(1)}, u32[]{:S(2)}, u32[]{:S(2)}) collective-permute-start(f32[64,448]{1,0:T(8,128)S(1)} %slice_select_fusion.4), channel_id=1, source_target_pairs={{0,8},{4,12},{8,0},{12,4},{16,24},{20,28},{24,16},{28,20},{1,9},{5... | collective-permute-start | bytes 344072 | tf_op jit(solution)/shard_map/ppermute | solution.py:16
  70.1 3.8 %shard_map.66 = f32[2,64,1024]{2,1,0:T(8,128)S(1)} custom-call(bf16[64,1024]{1,0:T(8,128)(2,1)S(1)} %maximum_select_fusion.4.a_ref, bf16[7168,1024]{1,0:T(8,128)(2,1)} %e_ref.11, bf16[2,7168,1024]{2,1,0:T(8,128)(2,1)} %q_ref.11), custom_call_target="tpu_custom_call" | custom-call | flops 268435456 | bytes 6815744 | tf_op jit(solution)/shard_map/pallas_call | solution.py:114
  74.1 1.6 %collective-permute-start.15 = (bf16[64,448]{1,0:T(8,128)(2,1)S(1)}, bf16[64,448]{1,0:T(8,128)(2,1)S(1)}, u32[]{:S(2)}, u32[]{:S(2)}) collective-permute-start(bf16[64,448]{1,0:T(8,128)(2,1)S(1)} %add_convert_fusion.1), channel_id=1, source_target_pairs={{0,16},{4,20},{8,24},{12,28},{16,0},{20,4},{24,8},{28,12},{1,17},{... | collective-permute-start | bytes 172040 | tf_op jit(solution)/shard_map/ppermute | solution.py:16
  75.7 1.2 %collective-permute-start.16 = (bf16[64,448]{1,0:T(8,128)(2,1)S(1)}, bf16[64,448]{1,0:T(8,128)(2,1)S(1)}, u32[]{:S(2)}, u32[]{:S(2)}) collective-permute-start(bf16[64,448]{1,0:T(8,128)(2,1)S(1)} %add_convert_fusion), channel_id=1, source_target_pairs={{0,8},{4,12},{8,0},{12,4},{16,24},{20,28},{24,16},{28,20},{1,9},{5... | collective-permute-start | bytes 172040 | tf_op jit(solution)/shard_map/ppermute | solution.py:16
  76.9 3.8 %shard_map.67 = f32[2,64,1024]{2,1,0:T(8,128)S(1)} custom-call(bf16[64,1024]{1,0:T(8,128)(2,1)S(1)} %maximum_select_fusion.4.a_ref, bf16[7168,1024]{1,0:T(8,128)(2,1)} %e_ref.11, bf16[2,7168,1024]{2,1,0:T(8,128)(2,1)} %q_ref.11), custom_call_target="tpu_custom_call" | custom-call | flops 268435456 | bytes 6815744 | tf_op jit(solution)/shard_map/pallas_call | solution.py:114
  82.3 3.8 %shard_map.68 = f32[2,64,1024]{2,1,0:T(8,128)S(1)} custom-call(bf16[64,1024]{1,0:T(8,128)(2,1)S(1)} %maximum_select_fusion.4.a_ref, bf16[7168,1024]{1,0:T(8,128)(2,1)} %e_ref.11, bf16[2,7168,1024]{2,1,0:T(8,128)(2,1)} %q_ref.11), custom_call_target="tpu_custom_call" | custom-call | flops 268435456 | bytes 6815744 | tf_op jit(solution)/shard_map/pallas_call | solution.py:114
  87.3 3.8 %shard_map.69 = f32[2,64,1024]{2,1,0:T(8,128)S(1)} custom-call(bf16[64,1024]{1,0:T(8,128)(2,1)S(1)} %maximum_select_fusion.4.a_ref, bf16[7168,1024]{1,0:T(8,128)(2,1)} %e_ref.11, bf16[2,7168,1024]{2,1,0:T(8,128)(2,1)} %q_ref.11), custom_call_target="tpu_custom_call" | custom-call | flops 268435456 | bytes 6815744 | tf_op jit(solution)/shard_map/pallas_call | solution.py:114
  93.2 2.8 %collective-permute-done.21 = f32[2,64]{1,0:T(2,128)S(1)} collective-permute-done((f32[2,64]{1,0:T(2,128)S(1)}, f32[2,64]{1,0:T(2,128)S(1)}, u32[]{:S(2)}, u32[]{:S(2)}) %collective-permute-start.21) | collective-permute-done | bytes 544 | tf_op jit(solution)/shard_map/ppermute | solution.py:16
  96.0 1.8 %collective-permute-start.22 = (f32[2,64]{1,0:T(2,128)S(1)}, f32[2,64]{1,0:T(2,128)S(1)}, u32[]{:S(2)}, u32[]{:S(2)}) collective-permute-start(f32[2,64]{1,0:T(2,128)S(1)} %add.109), channel_id=1, source_target_pairs={{0,2},{1,3},{2,0},{3,1},{4,6},{5,7},{6,4},{7,5},{8,10},{9,11},{10,... | collective-permute-start | bytes 1544 | tf_op jit(solution)/shard_map/ppermute | solution.py:16
  97.8 2.7 %collective-permute-done.22 = f32[2,64]{1,0:T(2,128)S(1)} collective-permute-done((f32[2,64]{1,0:T(2,128)S(1)}, f32[2,64]{1,0:T(2,128)S(1)}, u32[]{:S(2)}, u32[]{:S(2)}) %collective-permute-start.22) | collective-permute-done | bytes 544 | tf_op jit(solution)/shard_map/ppermute | solution.py:16
  100.5 1.1 %collective-permute-done.23 = f32[2,64]{1,0:T(2,128)S(1)} collective-permute-done((f32[2,64]{1,0:T(2,128)S(1)}, f32[2,64]{1,0:T(2,128)S(1)}, u32[]{:S(2)}, u32[]{:S(2)}) %collective-permute-start.23) | collective-permute-done | bytes 544 | tf_op jit(solution)/shard_map/ppermute | solution.py:16
  101.6 1.2 %collective-permute-start.24 = (f32[2,64]{1,0:T(2,128)S(1)}, f32[2,64]{1,0:T(2,128)S(1)}, u32[]{:S(2)}, u32[]{:S(2)}) collective-permute-start(f32[2,64]{1,0:T(2,128)S(1)} %add.111), channel_id=1, source_target_pairs={{0,8},{4,12},{8,0},{12,4},{16,24},{20,28},{24,16},{28,20},{1,9},{5... | collective-permute-start | bytes 1544 | tf_op jit(solution)/shard_map/ppermute | solution.py:16
  102.8 2.4 %collective-permute-done.24 = f32[2,64]{1,0:T(2,128)S(1)} collective-permute-done((f32[2,64]{1,0:T(2,128)S(1)}, f32[2,64]{1,0:T(2,128)S(1)}, u32[]{:S(2)}, u32[]{:S(2)}) %collective-permute-start.24) | collective-permute-done | bytes 544 | tf_op jit(solution)/shard_map/ppermute | solution.py:16
  105.2 1.0 collective-permute-start.25
  106.2 2.5 %collective-permute-done.25 = f32[2,64]{1,0:T(2,128)S(1)} collective-permute-done((f32[2,64]{1,0:T(2,128)S(1)}, f32[2,64]{1,0:T(2,128)S(1)}, u32[]{:S(2)}, u32[]{:S(2)}) %collective-permute-start.25) | collective-permute-done | bytes 544 | tf_op jit(solution)/shard_map/ppermute | solution.py:16
  (76 shorter events, 12.0 us)
Async XLA Ops:
  0.0 5.1 %collective-permute-start = (bf16[1,8,2048]{2,1,0:T(8,128)(2,1)}, bf16[1,8,2048]{2,1,0:T(8,128)(2,1)S(1)}, u32[]{:S(2)}, u32[]{:S(2)}) collective-permute-start(bf16[1,8,2048]{2,1,0:T(8,128)(2,1)} %bitcast.58), channel_id=1, source_target_pairs={{0,16},{4,20},{8,24},{12,28},{16,0},{20,4},{24,8},{28,12},{1,17},{... | collective-permute-start | bytes 98312 | tf_op jit(solution)/shard_map/ppermute | solution.py:16
  5.8 4.7 %collective-permute-start.1 = (bf16[2,8,2048]{2,1,0:T(8,128)(2,1)S(1)}, bf16[2,8,2048]{2,1,0:T(8,128)(2,1)S(1)}, u32[]{:S(2)}, u32[]{:S(2)}) collective-permute-start(bf16[2,8,2048]{2,1,0:T(8,128)(2,1)S(1)} %maximum_bitcast_fusion.1), channel_id=1, source_target_pairs={{0,8},{4,12},{8,0},{12,4},{16,24},{20,28},{24,16},{28,20},{1,9},{5... | collective-permute-start | bytes 196616 | tf_op jit(solution)/shard_map/ppermute | solution.py:16
  7.9 7.1 %collective-permute-start.4 = (bf16[1,16,3584]{2,1,0:T(8,128)(2,1)}, bf16[1,16,3584]{2,1,0:T(8,128)(2,1)S(1)}, u32[]{:S(2)}, u32[]{:S(2)}) collective-permute-start(bf16[1,16,3584]{2,1,0:T(8,128)(2,1)} %bitcast.57), channel_id=1, source_target_pairs={{0,2},{1,3},{2,0},{3,1},{4,6},{5,7},{6,4},{7,5},{8,10},{9,11},{10,... | collective-permute-start | bytes 344072 | tf_op jit(solution)/shard_map/ppermute | solution.py:16
  10.5 6.3 %collective-permute-start.2 = (bf16[4,8,2048]{2,1,0:T(8,128)(2,1)S(1)}, bf16[4,8,2048]{2,1,0:T(8,128)(2,1)S(1)}, u32[]{:S(2)}, u32[]{:S(2)}) collective-permute-start(bf16[4,8,2048]{2,1,0:T(8,128)(2,1)S(1)} %bitcast.53), channel_id=1, source_target_pairs={{0,4},{4,0},{8,12},{12,8},{16,20},{20,16},{24,28},{28,24},{1,5},{5... | collective-permute-start | bytes 393224 | tf_op jit(solution)/shard_map/ppermute | solution.py:16
  16.0 7.5 %collective-permute-start.5 = (bf16[2,16,3584]{2,1,0:T(8,128)(2,1)S(1)}, bf16[2,16,3584]{2,1,0:T(8,128)(2,1)S(1)}, u32[]{:S(2)}, u32[]{:S(2)}) collective-permute-start(bf16[2,16,3584]{2,1,0:T(8,128)(2,1)S(1)} %maximum_bitcast_fusion), channel_id=1, source_target_pairs={{0,1},{1,0},{2,3},{3,2},{4,5},{5,4},{6,7},{7,6},{8,9},{9,8},{10,11... | collective-permute-start | bytes 688136 | tf_op jit(solution)/shard_map/ppermute | solution.py:16
  20.0 11.6 %collective-permute-start.3 = (f32[64,512]{1,0:T(8,128)S(1)}, f32[64,512]{1,0:T(8,128)S(1)}, u32[]{:S(2)}, u32[]{:S(2)}) collective-permute-start(f32[64,512]{1,0:T(8,128)S(1)} %slice_select_fusion.6), channel_id=1, source_target_pairs={{0,1},{1,0},{2,3},{3,2},{4,5},{5,4},{6,7},{7,6},{8,9},{9,8},{10,11... | collective-permute-start | bytes 393224 | tf_op jit(solution)/shard_map/ppermute | solution.py:16
  31.6 9.2 %collective-permute-start.6 = (f32[64,256]{1,0:T(8,128)S(1)}, f32[64,256]{1,0:T(8,128)S(1)}, u32[]{:S(2)}, u32[]{:S(2)}) collective-permute-start(f32[64,256]{1,0:T(8,128)S(1)} %slice_select_fusion.7), channel_id=1, source_target_pairs={{0,2},{1,3},{2,0},{3,1},{4,6},{5,7},{6,4},{7,5},{8,10},{9,11},{10,... | collective-permute-start | bytes 196616 | tf_op jit(solution)/shard_map/ppermute | solution.py:16
  40.9 9.0 %collective-permute-start.7 = (bf16[64,256]{1,0:T(8,128)(2,1)S(1)}, bf16[64,256]{1,0:T(8,128)(2,1)S(1)}, u32[]{:S(2)}, u32[]{:S(2)}) collective-permute-start(bf16[64,256]{1,0:T(8,128)(2,1)S(1)} %add_convert_fusion.2), channel_id=1, source_target_pairs={{0,2},{1,3},{2,0},{3,1},{4,6},{5,7},{6,4},{7,5},{8,10},{9,11},{10,... | collective-permute-start | bytes 98312 | tf_op jit(solution)/shard_map/ppermute | solution.py:16
  49.9 4.3 %collective-permute-start.8 = (bf16[64,512]{1,0:T(8,128)(2,1)S(1)}, bf16[64,512]{1,0:T(8,128)(2,1)S(1)}, u32[]{:S(2)}, u32[]{:S(2)}) collective-permute-start(bf16[64,512]{1,0:T(8,128)(2,1)S(1)} %maximum_select_fusion.7), channel_id=1, source_target_pairs={{0,1},{1,0},{2,3},{3,2},{4,5},{5,4},{6,7},{7,6},{8,9},{9,8},{10,11... | collective-permute-start | bytes 196616 | tf_op jit(solution)/shard_map/ppermute | solution.py:16
  54.3 4.3 %collective-permute-start.9 = (f32[64,1792]{1,0:T(8,128)}, f32[64,1792]{1,0:T(8,128)S(1)}, u32[]{:S(2)}, u32[]{:S(2)}) collective-permute-start(f32[64,1792]{1,0:T(8,128)} %get-tuple-element.61), channel_id=1, source_target_pairs={{0,4},{4,0},{8,12},{12,8},{16,20},{20,16},{24,28},{28,24},{1,5},{5... | collective-permute-start | bytes 1376264 | tf_op jit(solution)/shard_map/ppermute | solution.py:16
  54.4 4.3 %collective-permute-start.10 = (f32[64,1792]{1,0:T(8,128)S(1)}, f32[64,1792]{1,0:T(8,128)S(1)}, u32[]{:S(2)}, u32[]{:S(2)}) collective-permute-start(f32[64,1792]{1,0:T(8,128)S(1)} %get-tuple-element.62), channel_id=1, source_target_pairs={{0,4},{4,0},{8,12},{12,8},{16,20},{20,16},{24,28},{28,24},{1,5},{5... | collective-permute-start | bytes 1376264 | tf_op jit(solution)/shard_map/ppermute | solution.py:16
  58.9 8.9 %collective-permute-start.11 = (f32[64,896]{1,0:T(8,128)S(1)}, f32[64,896]{1,0:T(8,128)S(1)}, u32[]{:S(2)}, u32[]{:S(2)}) collective-permute-start(f32[64,896]{1,0:T(8,128)S(1)} %slice_select_fusion.3), channel_id=1, source_target_pairs={{0,8},{4,12},{8,0},{12,4},{16,24},{20,28},{24,16},{28,20},{1,9},{5... | collective-permute-start | bytes 688136 | tf_op jit(solution)/shard_map/ppermute | solution.py:16
  58.9 8.8 %collective-permute-start.12 = (f32[64,896]{1,0:T(8,128)S(1)}, f32[64,896]{1,0:T(8,128)S(1)}, u32[]{:S(2)}, u32[]{:S(2)}) collective-permute-start(f32[64,896]{1,0:T(8,128)S(1)} %slice_select_fusion.2), channel_id=1, source_target_pairs={{0,16},{4,20},{8,24},{12,28},{16,0},{20,4},{24,8},{28,12},{1,17},{... | collective-permute-start | bytes 688136 | tf_op jit(solution)/shard_map/ppermute | solution.py:16
  68.1 5.8 %collective-permute-start.13 = (f32[64,448]{1,0:T(8,128)S(1)}, f32[64,448]{1,0:T(8,128)S(1)}, u32[]{:S(2)}, u32[]{:S(2)}) collective-permute-start(f32[64,448]{1,0:T(8,128)S(1)} %slice_select_fusion.5), channel_id=1, source_target_pairs={{0,16},{4,20},{8,24},{12,28},{16,0},{20,4},{24,8},{28,12},{1,17},{... | collective-permute-start | bytes 344072 | tf_op jit(solution)/shard_map/ppermute | solution.py:16
  68.6 5.3 %collective-permute-start.14 = (f32[64,448]{1,0:T(8,128)S(1)}, f32[64,448]{1,0:T(8,128)S(1)}, u32[]{:S(2)}, u32[]{:S(2)}) collective-permute-start(f32[64,448]{1,0:T(8,128)S(1)} %slice_select_fusion.4), channel_id=1, source_target_pairs={{0,8},{4,12},{8,0},{12,4},{16,24},{20,28},{24,16},{28,20},{1,9},{5... | collective-permute-start | bytes 344072 | tf_op jit(solution)/shard_map/ppermute | solution.py:16
  74.1 6.5 %collective-permute-start.15 = (bf16[64,448]{1,0:T(8,128)(2,1)S(1)}, bf16[64,448]{1,0:T(8,128)(2,1)S(1)}, u32[]{:S(2)}, u32[]{:S(2)}) collective-permute-start(bf16[64,448]{1,0:T(8,128)(2,1)S(1)} %add_convert_fusion.1), channel_id=1, source_target_pairs={{0,16},{4,20},{8,24},{12,28},{16,0},{20,4},{24,8},{28,12},{1,17},{... | collective-permute-start | bytes 172040 | tf_op jit(solution)/shard_map/ppermute | solution.py:16
  75.7 5.0 %collective-permute-start.16 = (bf16[64,448]{1,0:T(8,128)(2,1)S(1)}, bf16[64,448]{1,0:T(8,128)(2,1)S(1)}, u32[]{:S(2)}, u32[]{:S(2)}) collective-permute-start(bf16[64,448]{1,0:T(8,128)(2,1)S(1)} %add_convert_fusion), channel_id=1, source_target_pairs={{0,8},{4,12},{8,0},{12,4},{16,24},{20,28},{24,16},{28,20},{1,9},{5... | collective-permute-start | bytes 172040 | tf_op jit(solution)/shard_map/ppermute | solution.py:16
  80.9 5.2 %collective-permute-start.17 = (bf16[64,896]{1,0:T(8,128)(2,1)S(1)}, bf16[64,896]{1,0:T(8,128)(2,1)S(1)}, u32[]{:S(2)}, u32[]{:S(2)}) collective-permute-start(bf16[64,896]{1,0:T(8,128)(2,1)S(1)} %maximum_select_fusion.5), channel_id=1, source_target_pairs={{0,8},{4,12},{8,0},{12,4},{16,24},{20,28},{24,16},{28,20},{1,9},{5... | collective-permute-start | bytes 344072 | tf_op jit(solution)/shard_map/ppermute | solution.py:16
  81.8 4.8 %collective-permute-start.18 = (bf16[64,896]{1,0:T(8,128)(2,1)S(1)}, bf16[64,896]{1,0:T(8,128)(2,1)S(1)}, u32[]{:S(2)}, u32[]{:S(2)}) collective-permute-start(bf16[64,896]{1,0:T(8,128)(2,1)S(1)} %maximum_select_fusion.6), channel_id=1, source_target_pairs={{0,16},{4,20},{8,24},{12,28},{16,0},{20,4},{24,8},{28,12},{1,17},{... | collective-permute-start | bytes 344072 | tf_op jit(solution)/shard_map/ppermute | solution.py:16
  86.8 4.4 %collective-permute-start.19 = (bf16[64,1792]{1,0:T(8,128)(2,1)S(1)}, bf16[64,1792]{1,0:T(8,128)(2,1)S(1)}, u32[]{:S(2)}, u32[]{:S(2)}) collective-permute-start(bf16[64,1792]{1,0:T(8,128)(2,1)S(1)} %maximum_select_fusion.2), channel_id=1, source_target_pairs={{0,4},{4,0},{8,12},{12,8},{16,20},{20,16},{24,28},{28,24},{1,5},{5... | collective-permute-start | bytes 688136 | tf_op jit(solution)/shard_map/ppermute | solution.py:16
  86.8 4.3 %collective-permute-start.20 = (bf16[64,1792]{1,0:T(8,128)(2,1)S(1)}, bf16[64,1792]{1,0:T(8,128)(2,1)S(1)}, u32[]{:S(2)}, u32[]{:S(2)}) collective-permute-start(bf16[64,1792]{1,0:T(8,128)(2,1)S(1)} %maximum_select_fusion.3), channel_id=1, source_target_pairs={{0,4},{4,0},{8,12},{12,8},{16,20},{20,16},{24,28},{28,24},{1,5},{5... | collective-permute-start | bytes 688136 | tf_op jit(solution)/shard_map/ppermute | solution.py:16
  92.4 3.6 %collective-permute-start.21 = (f32[2,64]{1,0:T(2,128)S(1)}, f32[2,64]{1,0:T(2,128)S(1)}, u32[]{:S(2)}, u32[]{:S(2)}) collective-permute-start(f32[2,64]{1,0:T(2,128)S(1)} %add_add_fusion), channel_id=1, source_target_pairs={{0,1},{1,0},{2,3},{3,2},{4,5},{5,4},{6,7},{7,6},{8,9},{9,8},{10,11... | collective-permute-start | bytes 1544 | tf_op jit(solution)/shard_map/ppermute | solution.py:16
  96.0 4.5 %collective-permute-start.22 = (f32[2,64]{1,0:T(2,128)S(1)}, f32[2,64]{1,0:T(2,128)S(1)}, u32[]{:S(2)}, u32[]{:S(2)}) collective-permute-start(f32[2,64]{1,0:T(2,128)S(1)} %add.109), channel_id=1, source_target_pairs={{0,2},{1,3},{2,0},{3,1},{4,6},{5,7},{6,4},{7,5},{8,10},{9,11},{10,... | collective-permute-start | bytes 1544 | tf_op jit(solution)/shard_map/ppermute | solution.py:16
  100.5 1.1 %collective-permute-start.23 = (f32[2,64]{1,0:T(2,128)S(1)}, f32[2,64]{1,0:T(2,128)S(1)}, u32[]{:S(2)}, u32[]{:S(2)}) collective-permute-start(f32[2,64]{1,0:T(2,128)S(1)} %add.110), channel_id=1, source_target_pairs={{0,4},{4,0},{8,12},{12,8},{16,20},{20,16},{24,28},{28,24},{1,5},{5... | collective-permute-start | bytes 1544 | tf_op jit(solution)/shard_map/ppermute | solution.py:16
  101.6 3.6 %collective-permute-start.24 = (f32[2,64]{1,0:T(2,128)S(1)}, f32[2,64]{1,0:T(2,128)S(1)}, u32[]{:S(2)}, u32[]{:S(2)}) collective-permute-start(f32[2,64]{1,0:T(2,128)S(1)} %add.111), channel_id=1, source_target_pairs={{0,8},{4,12},{8,0},{12,4},{16,24},{20,28},{24,16},{28,20},{1,9},{5... | collective-permute-start | bytes 1544 | tf_op jit(solution)/shard_map/ppermute | solution.py:16
  105.2 3.6 %collective-permute-start.25 = (f32[2,64]{1,0:T(2,128)S(1)}, f32[2,64]{1,0:T(2,128)S(1)}, u32[]{:S(2)}, u32[]{:S(2)}) collective-permute-start(f32[2,64]{1,0:T(2,128)S(1)} %add.112), channel_id=1, source_target_pairs={{0,16},{4,20},{8,24},{12,28},{16,0},{20,4},{24,8},{28,12},{1,17},{... | collective-permute-start | bytes 1544 | tf_op jit(solution)/shard_map/ppermute | solution.py:16

commit v15 on v13

--- a/solution.py
+++ b/solution.py
@@ -164,7 +164,7 @@
         g = grad_rot[:, t0 * tk : t1 * tk].astype(F32)
         term = jnp.sum(piece * g[None], axis=2)
         partial = term if partial is None else partial + term
-    return _allreduce_small(_allreduce_small(partial, "col", nc), "row", nr)
+    return _allreduce_small(_allreduce_small(partial, "row", nr), "col", nc)
 
 
 def solution(mesh):

time: 108 us -> 108 us (level)
  no operation moved by 1% of the time
where the time goes in v15:
time: 108 us
  starting transfers between devices  29.5 us (27%)
  matrix products  26.9 us (25%)
  Pallas kernels  25.6 us (24%)
  waiting for transfers between devices  19.5 us (18%)
  other arithmetic  5.89 us (5%)
    ppermute x26, starting transfers between devices, _swap(): return lax.ppermute(x, axis, [(i, i ^ b) for i in range(n)])  29.5 us
    pallas_call x6, Pallas kernels, _lifted(): pl.pallas_call(_lifted_kernel, grid=(t1 - t0,), in_specs=[pl.BlockSpec((t...  25.6 us
    dot_general x4, matrix products, local(): jnp.dot(g, out_basis[:, c0:c1], preferred_element_type=F32)  23.9 us
    ppermute x26, waiting for transfers between devices, _swap(): return lax.ppermute(x, axis, [(i, i ^ b) for i in range(n)])  19.5 us
    dot_general x1, matrix products, local(): act_part = jnp.dot(acts_all, in_basis, preferred_element_type=F32)  3.03 us
  transfers between devices with their start and end apart: 26, of which 9 were waited for; matrix products, arithmetic and copies ran while one was open for 26% of the time, Pallas kernels for 24%

profile of v15, /device:TPU:0, one launch (start us, length us, event | category | flops | bytes accessed | tf_op | source)
XLA Modules:
  0.0 107.9 jit_solution(508238701542328913)
XLA Ops:
  0.0 3.0 %collective-permute-start = (bf16[1,8,2048]{2,1,0:T(8,128)(2,1)}, bf16[1,8,2048]{2,1,0:T(8,128)(2,1)S(1)}, u32[]{:S(2)}, u32[]{:S(2)}) collective-permute-start(bf16[1,8,2048]{2,1,0:T(8,128)(2,1)} %bitcast.60), channel_id=1, source_target_pairs={{0,16},{4,20},{8,24},{12,28},{16,0},{20,4},{24,8},{28,12},{1,17},{... | collective-permute-start | bytes 98312 | tf_op jit(solution)/shard_map/ppermute | solution.py:16
  3.0 2.1 %collective-permute-done = bf16[1,8,2048]{2,1,0:T(8,128)(2,1)S(1)} collective-permute-done((bf16[1,8,2048]{2,1,0:T(8,128)(2,1)}, bf16[1,8,2048]{2,1,0:T(8,128)(2,1)S(1)}, u32[]{:S(2)}, u32[]{:S(2)}) %collective-permute-start) | collective-permute-done | bytes 32800 | tf_op jit(solution)/shard_map/ppermute | solution.py:16
  5.8 2.1 %collective-permute-start.1 = (bf16[2,8,2048]{2,1,0:T(8,128)(2,1)S(1)}, bf16[2,8,2048]{2,1,0:T(8,128)(2,1)S(1)}, u32[]{:S(2)}, u32[]{:S(2)}) collective-permute-start(bf16[2,8,2048]{2,1,0:T(8,128)(2,1)S(1)} %maximum_bitcast_fusion.1), channel_id=1, source_target_pairs={{0,8},{4,12},{8,0},{12,4},{16,24},{20,28},{24,16},{28,20},{1,9},{5... | collective-permute-start | bytes 196616 | tf_op jit(solution)/shard_map/ppermute | solution.py:16
  7.9 2.6 %collective-permute-start.4 = (bf16[1,16,3584]{2,1,0:T(8,128)(2,1)}, bf16[1,16,3584]{2,1,0:T(8,128)(2,1)S(1)}, u32[]{:S(2)}, u32[]{:S(2)}) collective-permute-start(bf16[1,16,3584]{2,1,0:T(8,128)(2,1)} %bitcast.59), channel_id=1, source_target_pairs={{0,2},{1,3},{2,0},{3,1},{4,6},{5,7},{6,4},{7,5},{8,10},{9,11},{10,... | collective-permute-start | bytes 344072 | tf_op jit(solution)/shard_map/ppermute | solution.py:16
  10.6 4.4 %collective-permute-done.4 = bf16[1,16,3584]{2,1,0:T(8,128)(2,1)S(1)} collective-permute-done((bf16[1,16,3584]{2,1,0:T(8,128)(2,1)}, bf16[1,16,3584]{2,1,0:T(8,128)(2,1)S(1)}, u32[]{:S(2)}, u32[]{:S(2)}) %collective-permute-start.4) | collective-permute-done | bytes 114720 | tf_op jit(solution)/shard_map/ppermute | solution.py:16
  16.9 3.0 %fusion.9 = f32[64,1024]{1,0:T(8,128)S(1)} fusion(bf16[64,2048]{1,0:T(8,128)(2,1)S(1)} %bitcast.53, bf16[2048,1024]{1,0:T(8,128)(2,1)} %param.9), kind=kOutput, calls=%fused_computation.61 | convolution fusion | flops 268435456 | bytes 4718592 | tf_op jit(solution)/shard_map/dot_general | solution.py:138
  20.0 1.3 %collective-permute-start.3 = (f32[64,512]{1,0:T(8,128)S(1)}, f32[64,512]{1,0:T(8,128)S(1)}, u32[]{:S(2)}, u32[]{:S(2)}) collective-permute-start(f32[64,512]{1,0:T(8,128)S(1)} %slice_select_fusion.4), channel_id=1, source_target_pairs={{0,1},{1,0},{2,3},{3,2},{4,5},{5,4},{6,7},{7,6},{8,9},{9,8},{10,11... | collective-permute-start | bytes 393224 | tf_op jit(solution)/shard_map/ppermute | solution.py:16
  21.3 2.2 %collective-permute-done.5 = bf16[2,16,3584]{2,1,0:T(8,128)(2,1)S(1)} collective-permute-done((bf16[2,16,3584]{2,1,0:T(8,128)(2,1)S(1)}, bf16[2,16,3584]{2,1,0:T(8,128)(2,1)S(1)}, u32[]{:S(2)}, u32[]{:S(2)}) %collective-permute-start.5) | collective-permute-done | bytes 229408 | tf_op jit(solution)/shard_map/ppermute | solution.py:16
  23.6 6.0 %fusion.6 = f32[64,1792]{1,0:T(8,128)S(1)} fusion(bf16[64,3584]{1,0:T(8,128)(2,1)S(1)} %bitcast.55, bf16[3584,7168]{1,0:T(8,128)(2,1)} %param.8), kind=kOutput, calls=%fused_computation.6 | convolution fusion | flops 822083584 | bytes 13762560 | tf_op jit(solution)/shard_map/dot_general | solution.py:142
  29.6 1.9 %collective-permute-start.6 = (f32[64,256]{1,0:T(8,128)S(1)}, f32[64,256]{1,0:T(8,128)S(1)}, u32[]{:S(2)}, u32[]{:S(2)}) collective-permute-start(f32[64,256]{1,0:T(8,128)S(1)} %slice_select_fusion.5), channel_id=1, source_target_pairs={{0,2},{1,3},{2,0},{3,1},{4,6},{5,7},{6,4},{7,5},{8,10},{9,11},{10,... | collective-permute-start | bytes 196616 | tf_op jit(solution)/shard_map/ppermute | solution.py:16
  31.5 6.0 %fusion.4 = f32[64,1792]{1,0:T(8,128)S(1)} fusion(bf16[64,3584]{1,0:T(8,128)(2,1)S(1)} %bitcast.56, bf16[3584,7168]{1,0:T(8,128)(2,1)} %param.8), kind=kOutput, calls=%fused_computation.4 | convolution fusion | flops 822083584 | bytes 13762560 | tf_op jit(solution)/shard_map/dot_general | solution.py:142
  37.5 1.2 %collective-permute-start.7 = (bf16[64,256]{1,0:T(8,128)(2,1)S(1)}, bf16[64,256]{1,0:T(8,128)(2,1)S(1)}, u32[]{:S(2)}, u32[]{:S(2)}) collective-permute-start(bf16[64,256]{1,0:T(8,128)(2,1)S(1)} %add_convert_fusion.2), channel_id=1, source_target_pairs={{0,2},{1,3},{2,0},{3,1},{4,6},{5,7},{6,4},{7,5},{8,10},{9,11},{10,... | collective-permute-start | bytes 98312 | tf_op jit(solution)/shard_map/ppermute | solution.py:16
  38.7 6.0 %fusion.2 = f32[64,1792]{1,0:T(8,128)S(1)} fusion(bf16[64,3584]{1,0:T(8,128)(2,1)S(1)} %bitcast.57, bf16[3584,7168]{1,0:T(8,128)(2,1)} %param.8), kind=kOutput, calls=%fused_computation.2 | convolution fusion | flops 822083584 | bytes 13762560 | tf_op jit(solution)/shard_map/dot_general | solution.py:142
  45.8 6.0 %fusion = f32[64,1792]{1,0:T(8,128)S(1)} fusion(bf16[64,3584]{1,0:T(8,128)(2,1)S(1)} %bitcast.58, bf16[3584,7168]{1,0:T(8,128)(2,1)} %param.8), kind=kOutput, calls=%fused_computation | convolution fusion | flops 822083584 | bytes 13762560 | tf_op jit(solution)/shard_map/dot_general | solution.py:142
  52.4 3.8 %shard_map.64 = f32[2,64,1024]{2,1,0:T(8,128)S(1)} custom-call(bf16[64,1024]{1,0:T(8,128)(2,1)S(1)} %maximum_select_fusion.4.a_ref, bf16[7168,1024]{1,0:T(8,128)(2,1)} %e_ref.11, bf16[2,7168,1024]{2,1,0:T(8,128)(2,1)} %q_ref.11), custom_call_target="tpu_custom_call" | custom-call | flops 268435456 | bytes 6815744 | tf_op jit(solution)/shard_map/pallas_call | solution.py:114
  56.2 1.1 %select_add_fusion = f32[64,1792]{1,0:T(8,128)S(1)} fusion(f32[64,1792]{1,0:T(8,128)} %collective-permute-done.10, f32[64,1792]{1,0:T(8,128)S(1)} %fusion, f32[64,1792]{1,0:T(8,128)S(1)} %fusion.2, pred[]{:T(512)S(6)} %eq.63), kind=kLoop, calls=%fused_computation.17 | loop fusion | flops 229376 | bytes 1835009 | tf_op jit(solution)/shard_map/add | solution.py:80
  58.0 1.5 %collective-permute-start.12 = (f32[64,896]{1,0:T(8,128)S(1)}, f32[64,896]{1,0:T(8,128)S(1)}, u32[]{:S(2)}, u32[]{:S(2)}) collective-permute-start(f32[64,896]{1,0:T(8,128)S(1)} %slice_select_fusion), channel_id=1, source_target_pairs={{0,16},{4,20},{8,24},{12,28},{16,0},{20,4},{24,8},{28,12},{1,17},{... | collective-permute-start | bytes 688136 | tf_op jit(solution)/shard_map/ppermute | solution.py:16
  59.5 6.8 %shard_map.65 = f32[2,64,2048]{2,1,0:T(8,128)S(1)} custom-call(bf16[64,1024]{1,0:T(8,128)(2,1)S(1)} %maximum_select_fusion.4.a_ref, bf16[7168,1024]{1,0:T(8,128)(2,1)} %e_ref.11, bf16[2,7168,1024]{2,1,0:T(8,128)(2,1)} %q_ref.11), custom_call_target="tpu_custom_call" | custom-call | flops 536870912 | bytes 13631488 | tf_op jit(solution)/shard_map/pallas_call | solution.py:114
  67.2 1.5 %collective-permute-start.14 = (f32[64,448]{1,0:T(8,128)S(1)}, f32[64,448]{1,0:T(8,128)S(1)}, u32[]{:S(2)}, u32[]{:S(2)}) collective-permute-start(f32[64,448]{1,0:T(8,128)S(1)} %slice_select_fusion.2), channel_id=1, source_target_pairs={{0,8},{4,12},{8,0},{12,4},{16,24},{20,28},{24,16},{28,20},{1,9},{5... | collective-permute-start | bytes 344072 | tf_op jit(solution)/shard_map/ppermute | solution.py:16
  68.7 3.8 %shard_map.66 = f32[2,64,1024]{2,1,0:T(8,128)S(1)} custom-call(bf16[64,1024]{1,0:T(8,128)(2,1)S(1)} %maximum_select_fusion.4.a_ref, bf16[7168,1024]{1,0:T(8,128)(2,1)} %e_ref.11, bf16[2,7168,1024]{2,1,0:T(8,128)(2,1)} %q_ref.11), custom_call_target="tpu_custom_call" | custom-call | flops 268435456 | bytes 6815744 | tf_op jit(solution)/shard_map/pallas_call | solution.py:114
  72.7 1.6 %collective-permute-start.15 = (bf16[64,448]{1,0:T(8,128)(2,1)S(1)}, bf16[64,448]{1,0:T(8,128)(2,1)S(1)}, u32[]{:S(2)}, u32[]{:S(2)}) collective-permute-start(bf16[64,448]{1,0:T(8,128)(2,1)S(1)} %add_convert_fusion.1), channel_id=1, source_target_pairs={{0,16},{4,20},{8,24},{12,28},{16,0},{20,4},{24,8},{28,12},{1,17},{... | collective-permute-start | bytes 172040 | tf_op jit(solution)/shard_map/ppermute | solution.py:16
  74.3 1.2 %collective-permute-start.16 = (bf16[64,448]{1,0:T(8,128)(2,1)S(1)}, bf16[64,448]{1,0:T(8,128)(2,1)S(1)}, u32[]{:S(2)}, u32[]{:S(2)}) collective-permute-start(bf16[64,448]{1,0:T(8,128)(2,1)S(1)} %add_convert_fusion), channel_id=1, source_target_pairs={{0,8},{4,12},{8,0},{12,4},{16,24},{20,28},{24,16},{28,20},{1,9},{5... | collective-permute-start | bytes 172040 | tf_op jit(solution)/shard_map/ppermute | solution.py:16
  75.5 3.8 %shard_map.67 = f32[2,64,1024]{2,1,0:T(8,128)S(1)} custom-call(bf16[64,1024]{1,0:T(8,128)(2,1)S(1)} %maximum_select_fusion.4.a_ref, bf16[7168,1024]{1,0:T(8,128)(2,1)} %e_ref.11, bf16[2,7168,1024]{2,1,0:T(8,128)(2,1)} %q_ref.11), custom_call_target="tpu_custom_call" | custom-call | flops 268435456 | bytes 6815744 | tf_op jit(solution)/shard_map/pallas_call | solution.py:114
  80.9 3.8 %shard_map.68 = f32[2,64,1024]{2,1,0:T(8,128)S(1)} custom-call(bf16[64,1024]{1,0:T(8,128)(2,1)S(1)} %maximum_select_fusion.4.a_ref, bf16[7168,1024]{1,0:T(8,128)(2,1)} %e_ref.11, bf16[2,7168,1024]{2,1,0:T(8,128)(2,1)} %q_ref.11), custom_call_target="tpu_custom_call" | custom-call | flops 268435456 | bytes 6815744 | tf_op jit(solution)/shard_map/pallas_call | solution.py:114
  85.9 3.8 %shard_map.69 = f32[2,64,1024]{2,1,0:T(8,128)S(1)} custom-call(bf16[64,1024]{1,0:T(8,128)(2,1)S(1)} %maximum_select_fusion.4.a_ref, bf16[7168,1024]{1,0:T(8,128)(2,1)} %e_ref.11, bf16[2,7168,1024]{2,1,0:T(8,128)(2,1)} %q_ref.11), custom_call_target="tpu_custom_call" | custom-call | flops 268435456 | bytes 6815744 | tf_op jit(solution)/shard_map/pallas_call | solution.py:114
  92.2 1.2 %collective-permute-start.22 = (f32[2,64]{1,0:T(2,128)S(1)}, f32[2,64]{1,0:T(2,128)S(1)}, u32[]{:S(2)}, u32[]{:S(2)}) collective-permute-start(f32[2,64]{1,0:T(2,128)S(1)} %add.109), channel_id=1, source_target_pairs={{0,8},{4,12},{8,0},{12,4},{16,24},{20,28},{24,16},{28,20},{1,9},{5... | collective-permute-start | bytes 1544 | tf_op jit(solution)/shard_map/ppermute | solution.py:16
  93.3 2.4 %collective-permute-done.22 = f32[2,64]{1,0:T(2,128)S(1)} collective-permute-done((f32[2,64]{1,0:T(2,128)S(1)}, f32[2,64]{1,0:T(2,128)S(1)}, u32[]{:S(2)}, u32[]{:S(2)}) %collective-permute-start.22) | collective-permute-done | bytes 544 | tf_op jit(solution)/shard_map/ppermute | solution.py:16
  96.8 2.5 %collective-permute-done.23 = f32[2,64]{1,0:T(2,128)S(1)} collective-permute-done((f32[2,64]{1,0:T(2,128)S(1)}, f32[2,64]{1,0:T(2,128)S(1)}, u32[]{:S(2)}, u32[]{:S(2)}) %collective-permute-start.23) | collective-permute-done | bytes 544 | tf_op jit(solution)/shard_map/ppermute | solution.py:16
  99.3 1.1 %collective-permute-start.24 = (f32[2,64]{1,0:T(2,128)S(1)}, f32[2,64]{1,0:T(2,128)S(1)}, u32[]{:S(2)}, u32[]{:S(2)}) collective-permute-start(f32[2,64]{1,0:T(2,128)S(1)} %add.111), channel_id=1, source_target_pairs={{0,1},{1,0},{2,3},{3,2},{4,5},{5,4},{6,7},{7,6},{8,9},{9,8},{10,11... | collective-permute-start | bytes 1544 | tf_op jit(solution)/shard_map/ppermute | solution.py:16
  100.4 2.5 %collective-permute-done.24 = f32[2,64]{1,0:T(2,128)S(1)} collective-permute-done((f32[2,64]{1,0:T(2,128)S(1)}, f32[2,64]{1,0:T(2,128)S(1)}, u32[]{:S(2)}, u32[]{:S(2)}) %collective-permute-start.24) | collective-permute-done | bytes 544 | tf_op jit(solution)/shard_map/ppermute | solution.py:16
  102.9 2.7 %collective-permute-start.25 = (f32[2,64]{1,0:T(2,128)S(1)}, f32[2,64]{1,0:T(2,128)S(1)}, u32[]{:S(2)}, u32[]{:S(2)}) collective-permute-start(f32[2,64]{1,0:T(2,128)S(1)} %add.112), channel_id=1, source_target_pairs={{0,2},{1,3},{2,0},{3,1},{4,6},{5,7},{6,4},{7,5},{8,10},{9,11},{10,... | collective-permute-start | bytes 1544 | tf_op jit(solution)/shard_map/ppermute | solution.py:16
  105.5 1.8 %collective-permute-done.25 = f32[2,64]{1,0:T(2,128)S(1)} collective-permute-done((f32[2,64]{1,0:T(2,128)S(1)}, f32[2,64]{1,0:T(2,128)S(1)}, u32[]{:S(2)}, u32[]{:S(2)}) %collective-permute-start.25) | collective-permute-done | bytes 544 | tf_op jit(solution)/shard_map/ppermute | solution.py:16
  (79 shorter events, 13.2 us)
Async XLA Ops:
  0.0 5.1 %collective-permute-start = (bf16[1,8,2048]{2,1,0:T(8,128)(2,1)}, bf16[1,8,2048]{2,1,0:T(8,128)(2,1)S(1)}, u32[]{:S(2)}, u32[]{:S(2)}) collective-permute-start(bf16[1,8,2048]{2,1,0:T(8,128)(2,1)} %bitcast.60), channel_id=1, source_target_pairs={{0,16},{4,20},{8,24},{12,28},{16,0},{20,4},{24,8},{28,12},{1,17},{... | collective-permute-start | bytes 98312 | tf_op jit(solution)/shard_map/ppermute | solution.py:16
  5.8 4.7 %collective-permute-start.1 = (bf16[2,8,2048]{2,1,0:T(8,128)(2,1)S(1)}, bf16[2,8,2048]{2,1,0:T(8,128)(2,1)S(1)}, u32[]{:S(2)}, u32[]{:S(2)}) collective-permute-start(bf16[2,8,2048]{2,1,0:T(8,128)(2,1)S(1)} %maximum_bitcast_fusion.1), channel_id=1, source_target_pairs={{0,8},{4,12},{8,0},{12,4},{16,24},{20,28},{24,16},{28,20},{1,9},{5... | collective-permute-start | bytes 196616 | tf_op jit(solution)/shard_map/ppermute | solution.py:16
  7.9 7.1 %collective-permute-start.4 = (bf16[1,16,3584]{2,1,0:T(8,128)(2,1)}, bf16[1,16,3584]{2,1,0:T(8,128)(2,1)S(1)}, u32[]{:S(2)}, u32[]{:S(2)}) collective-permute-start(bf16[1,16,3584]{2,1,0:T(8,128)(2,1)} %bitcast.59), channel_id=1, source_target_pairs={{0,2},{1,3},{2,0},{3,1},{4,6},{5,7},{6,4},{7,5},{8,10},{9,11},{10,... | collective-permute-start | bytes 344072 | tf_op jit(solution)/shard_map/ppermute | solution.py:16
  10.5 6.3 %collective-permute-start.2 = (bf16[4,8,2048]{2,1,0:T(8,128)(2,1)S(1)}, bf16[4,8,2048]{2,1,0:T(8,128)(2,1)S(1)}, u32[]{:S(2)}, u32[]{:S(2)}) collective-permute-start(bf16[4,8,2048]{2,1,0:T(8,128)(2,1)S(1)} %bitcast.54), channel_id=1, source_target_pairs={{0,4},{4,0},{8,12},{12,8},{16,20},{20,16},{24,28},{28,24},{1,5},{5... | collective-permute-start | bytes 393224 | tf_op jit(solution)/shard_map/ppermute | solution.py:16
  16.0 7.5 %collective-permute-start.5 = (bf16[2,16,3584]{2,1,0:T(8,128)(2,1)S(1)}, bf16[2,16,3584]{2,1,0:T(8,128)(2,1)S(1)}, u32[]{:S(2)}, u32[]{:S(2)}) collective-permute-start(bf16[2,16,3584]{2,1,0:T(8,128)(2,1)S(1)} %maximum_bitcast_fusion), channel_id=1, source_target_pairs={{0,1},{1,0},{2,3},{3,2},{4,5},{5,4},{6,7},{7,6},{8,9},{9,8},{10,11... | collective-permute-start | bytes 688136 | tf_op jit(solution)/shard_map/ppermute | solution.py:16
  20.0 9.6 %collective-permute-start.3 = (f32[64,512]{1,0:T(8,128)S(1)}, f32[64,512]{1,0:T(8,128)S(1)}, u32[]{:S(2)}, u32[]{:S(2)}) collective-permute-start(f32[64,512]{1,0:T(8,128)S(1)} %slice_select_fusion.4), channel_id=1, source_target_pairs={{0,1},{1,0},{2,3},{3,2},{4,5},{5,4},{6,7},{7,6},{8,9},{9,8},{10,11... | collective-permute-start | bytes 393224 | tf_op jit(solution)/shard_map/ppermute | solution.py:16
  29.6 7.8 %collective-permute-start.6 = (f32[64,256]{1,0:T(8,128)S(1)}, f32[64,256]{1,0:T(8,128)S(1)}, u32[]{:S(2)}, u32[]{:S(2)}) collective-permute-start(f32[64,256]{1,0:T(8,128)S(1)} %slice_select_fusion.5), channel_id=1, source_target_pairs={{0,2},{1,3},{2,0},{3,1},{4,6},{5,7},{6,4},{7,5},{8,10},{9,11},{10,... | collective-permute-start | bytes 196616 | tf_op jit(solution)/shard_map/ppermute | solution.py:16
  37.5 7.3 %collective-permute-start.7 = (bf16[64,256]{1,0:T(8,128)(2,1)S(1)}, bf16[64,256]{1,0:T(8,128)(2,1)S(1)}, u32[]{:S(2)}, u32[]{:S(2)}) collective-permute-start(bf16[64,256]{1,0:T(8,128)(2,1)S(1)} %add_convert_fusion.2), channel_id=1, source_target_pairs={{0,2},{1,3},{2,0},{3,1},{4,6},{5,7},{6,4},{7,5},{8,10},{9,11},{10,... | collective-permute-start | bytes 98312 | tf_op jit(solution)/shard_map/ppermute | solution.py:16
  44.8 7.0 %collective-permute-start.8 = (bf16[64,512]{1,0:T(8,128)(2,1)S(1)}, bf16[64,512]{1,0:T(8,128)(2,1)S(1)}, u32[]{:S(2)}, u32[]{:S(2)}) collective-permute-start(bf16[64,512]{1,0:T(8,128)(2,1)S(1)} %maximum_select_fusion.7), channel_id=1, source_target_pairs={{0,1},{1,0},{2,3},{3,2},{4,5},{5,4},{6,7},{7,6},{8,9},{9,8},{10,11... | collective-permute-start | bytes 196616 | tf_op jit(solution)/shard_map/ppermute | solution.py:16
  51.8 4.3 %collective-permute-start.9 = (f32[64,1792]{1,0:T(8,128)S(1)}, f32[64,1792]{1,0:T(8,128)S(1)}, u32[]{:S(2)}, u32[]{:S(2)}) collective-permute-start(f32[64,1792]{1,0:T(8,128)S(1)} %broadcast_select_fusion.1), channel_id=1, source_target_pairs={{0,4},{4,0},{8,12},{12,8},{16,20},{20,16},{24,28},{28,24},{1,5},{5... | collective-permute-start | bytes 1376264 | tf_op jit(solution)/shard_map/ppermute | solution.py:16
  51.9 4.3 %collective-permute-start.10 = (f32[64,1792]{1,0:T(8,128)S(1)}, f32[64,1792]{1,0:T(8,128)}, u32[]{:S(2)}, u32[]{:S(2)}) collective-permute-start(f32[64,1792]{1,0:T(8,128)S(1)} %broadcast_select_fusion), channel_id=1, source_target_pairs={{0,4},{4,0},{8,12},{12,8},{16,20},{20,16},{24,28},{28,24},{1,5},{5... | collective-permute-start | bytes 1376264 | tf_op jit(solution)/shard_map/ppermute | solution.py:16
  57.4 8.9 %collective-permute-start.11 = (f32[64,896]{1,0:T(8,128)S(1)}, f32[64,896]{1,0:T(8,128)S(1)}, u32[]{:S(2)}, u32[]{:S(2)}) collective-permute-start(f32[64,896]{1,0:T(8,128)S(1)} %slice_select_fusion.1), channel_id=1, source_target_pairs={{0,8},{4,12},{8,0},{12,4},{16,24},{20,28},{24,16},{28,20},{1,9},{5... | collective-permute-start | bytes 688136 | tf_op jit(solution)/shard_map/ppermute | solution.py:16
  58.0 8.3 %collective-permute-start.12 = (f32[64,896]{1,0:T(8,128)S(1)}, f32[64,896]{1,0:T(8,128)S(1)}, u32[]{:S(2)}, u32[]{:S(2)}) collective-permute-start(f32[64,896]{1,0:T(8,128)S(1)} %slice_select_fusion), channel_id=1, source_target_pairs={{0,16},{4,20},{8,24},{12,28},{16,0},{20,4},{24,8},{28,12},{1,17},{... | collective-permute-start | bytes 688136 | tf_op jit(solution)/shard_map/ppermute | solution.py:16
  66.6 5.8 %collective-permute-start.13 = (f32[64,448]{1,0:T(8,128)S(1)}, f32[64,448]{1,0:T(8,128)S(1)}, u32[]{:S(2)}, u32[]{:S(2)}) collective-permute-start(f32[64,448]{1,0:T(8,128)S(1)} %slice_select_fusion.3), channel_id=1, source_target_pairs={{0,16},{4,20},{8,24},{12,28},{16,0},{20,4},{24,8},{28,12},{1,17},{... | collective-permute-start | bytes 344072 | tf_op jit(solution)/shard_map/ppermute | solution.py:16
  67.2 5.3 %collective-permute-start.14 = (f32[64,448]{1,0:T(8,128)S(1)}, f32[64,448]{1,0:T(8,128)S(1)}, u32[]{:S(2)}, u32[]{:S(2)}) collective-permute-start(f32[64,448]{1,0:T(8,128)S(1)} %slice_select_fusion.2), channel_id=1, source_target_pairs={{0,8},{4,12},{8,0},{12,4},{16,24},{20,28},{24,16},{28,20},{1,9},{5... | collective-permute-start | bytes 344072 | tf_op jit(solution)/shard_map/ppermute | solution.py:16
  72.7 6.5 %collective-permute-start.15 = (bf16[64,448]{1,0:T(8,128)(2,1)S(1)}, bf16[64,448]{1,0:T(8,128)(2,1)S(1)}, u32[]{:S(2)}, u32[]{:S(2)}) collective-permute-start(bf16[64,448]{1,0:T(8,128)(2,1)S(1)} %add_convert_fusion.1), channel_id=1, source_target_pairs={{0,16},{4,20},{8,24},{12,28},{16,0},{20,4},{24,8},{28,12},{1,17},{... | collective-permute-start | bytes 172040 | tf_op jit(solution)/shard_map/ppermute | solution.py:16
  74.3 5.0 %collective-permute-start.16 = (bf16[64,448]{1,0:T(8,128)(2,1)S(1)}, bf16[64,448]{1,0:T(8,128)(2,1)S(1)}, u32[]{:S(2)}, u32[]{:S(2)}) collective-permute-start(bf16[64,448]{1,0:T(8,128)(2,1)S(1)} %add_convert_fusion), channel_id=1, source_target_pairs={{0,8},{4,12},{8,0},{12,4},{16,24},{20,28},{24,16},{28,20},{1,9},{5... | collective-permute-start | bytes 172040 | tf_op jit(solution)/shard_map/ppermute | solution.py:16
  79.5 5.2 %collective-permute-start.17 = (bf16[64,896]{1,0:T(8,128)(2,1)S(1)}, bf16[64,896]{1,0:T(8,128)(2,1)S(1)}, u32[]{:S(2)}, u32[]{:S(2)}) collective-permute-start(bf16[64,896]{1,0:T(8,128)(2,1)S(1)} %maximum_select_fusion.5), channel_id=1, source_target_pairs={{0,8},{4,12},{8,0},{12,4},{16,24},{20,28},{24,16},{28,20},{1,9},{5... | collective-permute-start | bytes 344072 | tf_op jit(solution)/shard_map/ppermute | solution.py:16
  80.4 4.8 %collective-permute-start.18 = (bf16[64,896]{1,0:T(8,128)(2,1)S(1)}, bf16[64,896]{1,0:T(8,128)(2,1)S(1)}, u32[]{:S(2)}, u32[]{:S(2)}) collective-permute-start(bf16[64,896]{1,0:T(8,128)(2,1)S(1)} %maximum_select_fusion.6), channel_id=1, source_target_pairs={{0,16},{4,20},{8,24},{12,28},{16,0},{20,4},{24,8},{28,12},{1,17},{... | collective-permute-start | bytes 344072 | tf_op jit(solution)/shard_map/ppermute | solution.py:16
  85.3 4.4 %collective-permute-start.19 = (bf16[64,1792]{1,0:T(8,128)(2,1)S(1)}, bf16[64,1792]{1,0:T(8,128)(2,1)S(1)}, u32[]{:S(2)}, u32[]{:S(2)}) collective-permute-start(bf16[64,1792]{1,0:T(8,128)(2,1)S(1)} %maximum_select_fusion.2), channel_id=1, source_target_pairs={{0,4},{4,0},{8,12},{12,8},{16,20},{20,16},{24,28},{28,24},{1,5},{5... | collective-permute-start | bytes 688136 | tf_op jit(solution)/shard_map/ppermute | solution.py:16
  85.4 4.3 %collective-permute-start.20 = (bf16[64,1792]{1,0:T(8,128)(2,1)S(1)}, bf16[64,1792]{1,0:T(8,128)(2,1)S(1)}, u32[]{:S(2)}, u32[]{:S(2)}) collective-permute-start(bf16[64,1792]{1,0:T(8,128)(2,1)S(1)} %maximum_select_fusion.3), channel_id=1, source_target_pairs={{0,4},{4,0},{8,12},{12,8},{16,20},{20,16},{24,28},{28,24},{1,5},{5... | collective-permute-start | bytes 688136 | tf_op jit(solution)/shard_map/ppermute | solution.py:16
  90.9 1.2 %collective-permute-start.21 = (f32[2,64]{1,0:T(2,128)S(1)}, f32[2,64]{1,0:T(2,128)S(1)}, u32[]{:S(2)}, u32[]{:S(2)}) collective-permute-start(f32[2,64]{1,0:T(2,128)S(1)} %add_add_fusion), channel_id=1, source_target_pairs={{0,4},{4,0},{8,12},{12,8},{16,20},{20,16},{24,28},{28,24},{1,5},{5... | collective-permute-start | bytes 1544 | tf_op jit(solution)/shard_map/ppermute | solution.py:16
  92.2 3.6 %collective-permute-start.22 = (f32[2,64]{1,0:T(2,128)S(1)}, f32[2,64]{1,0:T(2,128)S(1)}, u32[]{:S(2)}, u32[]{:S(2)}) collective-permute-start(f32[2,64]{1,0:T(2,128)S(1)} %add.109), channel_id=1, source_target_pairs={{0,8},{4,12},{8,0},{12,4},{16,24},{20,28},{24,16},{28,20},{1,9},{5... | collective-permute-start | bytes 1544 | tf_op jit(solution)/shard_map/ppermute | solution.py:16
  95.7 3.6 %collective-permute-start.23 = (f32[2,64]{1,0:T(2,128)S(1)}, f32[2,64]{1,0:T(2,128)S(1)}, u32[]{:S(2)}, u32[]{:S(2)}) collective-permute-start(f32[2,64]{1,0:T(2,128)S(1)} %add.110), channel_id=1, source_target_pairs={{0,16},{4,20},{8,24},{12,28},{16,0},{20,4},{24,8},{28,12},{1,17},{... | collective-permute-start | bytes 1544 | tf_op jit(solution)/shard_map/ppermute | solution.py:16
  99.3 3.6 %collective-permute-start.24 = (f32[2,64]{1,0:T(2,128)S(1)}, f32[2,64]{1,0:T(2,128)S(1)}, u32[]{:S(2)}, u32[]{:S(2)}) collective-permute-start(f32[2,64]{1,0:T(2,128)S(1)} %add.111), channel_id=1, source_target_pairs={{0,1},{1,0},{2,3},{3,2},{4,5},{5,4},{6,7},{7,6},{8,9},{9,8},{10,11... | collective-permute-start | bytes 1544 | tf_op jit(solution)/shard_map/ppermute | solution.py:16
  102.9 4.5 %collective-permute-start.25 = (f32[2,64]{1,0:T(2,128)S(1)}, f32[2,64]{1,0:T(2,128)S(1)}, u32[]{:S(2)}, u32[]{:S(2)}) collective-permute-start(f32[2,64]{1,0:T(2,128)S(1)} %add.112), channel_id=1, source_target_pairs={{0,2},{1,3},{2,0},{3,1},{4,6},{5,7},{6,4},{7,5},{8,10},{9,11},{10,... | collective-permute-start | bytes 1544 | tf_op jit(solution)/shard_map/ppermute | solution.py:16
